TPU v7x, 128 devices: a whole 4x4x4 slice. The times are simulated.
128 devices in a mesh: blk: 4 (over y_hi, core), feat: 32 (over y_lo, z, x).
Axes of the slice: x: 4, y: 4 (y_hi: 2, y_lo: 2; y = y_hi * 2 + y_lo), z: 4, core: 2. Of those that a mesh axis runs over, the one named last changes fastest.
Arguments:
- features_t: bfloat16 [128, 32768], P('feat', 'blk'), may hold values from -6 to 6
- weight: bfloat16 [128, 128], replicated, may hold values from -0.5 to 0.5
- tile_values: bfloat16 [32768, 128, 128], P(('blk', 'feat')), may hold values from -0.0625 to 0.0625
- tile_col: int32 [32768], P(('blk', 'feat')), may hold values from 0 to 255, as said below
- tile_count: int32 [1024], P(('blk', 'feat')), may hold values from 1 to 32, as said below
- grad_out: bfloat16 [32768, 128], P(('blk', 'feat')), may hold values from -6 to 6
Outputs:
- activations: bfloat16 [32768, 128], P(('blk', 'feat'))
- grad_features: bfloat16 [128, 32768], P('feat', 'blk')
- grad_weight: float32 [128, 128], P('feat')
Inputs may be any that keep to these rules, and one draw needn't show every extreme that they name: `tile_count`: live slots of one tile row of one device for one column block; the first that many slots are live, and in every draw some entry equals 32. `tile_col`: the slots of column block c hold tile columns c * 64 to c * 64 + 63; columns may repeat within a tile row.
All inputs are finite; a program needn't handle non-finite values.
Results may differ from a plain program's by a relative error of at most 0.013.
Values may be sent and summed in bfloat16 or wider, within the bound.
No kernel may reach another device: no remote copies, remote signals or barrier semaphores. Data moves between devices by JAX's collectives and lax.ppermute only.
A program may use at most 128 MiB of HBM per device.

v0:
```python
import jax
import jax.numpy as jnp
from jax import lax
from jax.sharding import PartitionSpec as P


def shifted(block, axis, distance):
    devices = range(lax.axis_size(axis))
    route = [((i - distance) % len(devices), i) for i in devices]
    return lax.ppermute(block, axis, route)


def body(features_t, weight, tile_values, tile_col, tile_count, grad_out):
    cycle_size = lax.axis_size("blk")
    hidden_width = weight.shape[1]
    tile_size = tile_values.shape[1]
    rows_own = grad_out.shape[0]
    tile_rows = rows_own // tile_size
    block_rows = features_t.shape[1]
    block_tiles = block_rows // tile_size
    slot_count = tile_values.shape[0] // (cycle_size * tile_rows)
    part_cols = features_t.shape[0]
    feat_id = lax.axis_index("feat")
    blk_id = lax.axis_index("blk")
    weight_part = lax.dynamic_slice_in_dim(weight, feat_id * part_cols, part_cols, 0)
    slot_index = lax.broadcasted_iota(jnp.int32, (cycle_size, tile_rows, slot_count), 2)
    live_mask = slot_index < tile_count.reshape(cycle_size, tile_rows, 1)
    tile_stack = tile_values.reshape(cycle_size, tile_rows, slot_count, tile_size, tile_size)
    tile_stack = jnp.where(live_mask[..., None, None], tile_stack, jnp.zeros((), jnp.bfloat16))
    local_cols = (tile_col % block_tiles).reshape(cycle_size, tile_rows, slot_count)
    projected = lax.dot_general(
        lax.all_gather(features_t, "feat", axis=0, tiled=True),
        weight,
        (((0,), (0,)), ((), ())),
        preferred_element_type=jnp.float32,
    ).astype(jnp.bfloat16)

    def aggregate(block_value, block_id):
        block_tiles_view = block_value.reshape(block_tiles, tile_size, hidden_width)
        cols_here = lax.dynamic_index_in_dim(local_cols, block_id, 0, keepdims=False)
        tiles_here = lax.dynamic_index_in_dim(tile_stack, block_id, 0, keepdims=False)
        picked = jnp.take(block_tiles_view, cols_here, axis=0)
        return jnp.einsum("rsij,rsjh->rih", tiles_here, picked, preferred_element_type=jnp.float32)

    aggregate_sum = aggregate(projected, blk_id)
    moving = projected
    for turn_index in range(cycle_size - 1):
        moving = shifted(moving, "blk", 1)
        aggregate_sum = aggregate_sum + aggregate(moving, (blk_id - turn_index - 1) % cycle_size)
    pre_act = aggregate_sum.reshape(rows_own, hidden_width)
    sigmoid_y = jax.nn.sigmoid(pre_act)
    activations = (pre_act * sigmoid_y).astype(jnp.bfloat16)
    grad_pre = (
        grad_out.astype(jnp.float32) * sigmoid_y * (1.0 + pre_act * (1.0 - sigmoid_y))
    ).astype(jnp.bfloat16)
    grad_tiles = grad_pre.reshape(tile_rows, tile_size, hidden_width)

    def spread(block_id):
        tiles_here = lax.dynamic_index_in_dim(tile_stack, block_id, 0, keepdims=False)
        cols_here = lax.dynamic_index_in_dim(local_cols, block_id, 0, keepdims=False)
        contrib = jnp.einsum(
            "rsij,rih->rsjh", tiles_here, grad_tiles, preferred_element_type=jnp.float32
        )
        empty_block = jnp.zeros((block_tiles, tile_size, hidden_width), jnp.float32)
        return empty_block.at[cols_here.reshape(-1)].add(
            contrib.reshape(-1, tile_size, hidden_width)
        )

    whole_term = jnp.concatenate([spread(block_id) for block_id in range(cycle_size)], axis=0)
    whole_term = whole_term.reshape(cycle_size * block_rows, hidden_width)
    grad_own = lax.psum_scatter(whole_term, ("blk", "feat"), scatter_dimension=0, tiled=True)
    grad_hidden = lax.all_gather(grad_own.astype(jnp.bfloat16), "feat", axis=0, tiled=True)
    weight_term = jnp.dot(features_t, grad_hidden, preferred_element_type=jnp.float32)
    grad_weight = lax.psum(weight_term, "blk") * lax.rsqrt(jnp.float32(block_rows * cycle_size))
    grad_features = lax.dot_general(
        weight_part, grad_hidden, (((1,), (1,)), ((), ())), preferred_element_type=jnp.float32
    ).astype(jnp.bfloat16)
    return (activations, grad_features, grad_weight)


def solution(mesh):
    placed = (
        P("feat", "blk"),
        P(),
        P(("blk", "feat"), None, None),
        P(("blk", "feat")),
        P(("blk", "feat")),
        P(("blk", "feat"), None),
    )
    return jax.shard_map(
        body,
        mesh=mesh,
        in_specs=placed,
        out_specs=(P(("blk", "feat"), None), P("feat", "blk"), P("feat", None)),
        check_vma=False,
    )
```

profile of v0, /device:TPU:0, one launch (start us, length us, event | category | flops | bytes accessed | tf_op | source)
XLA Modules:
  0.0 1190.6 jit_solution(1916217125052492609)
XLA Ops:
  8.0 157.5 %all-gather.6.cloned.1.call-done = bf16[32,4,8192]{2,1,0:T(4,128)(2,1)} async-done(((bf16[1,4,8192]{2,1,0:T(4,128)(2,1)}), bf16[32,4,8192]{2,1,0:T(4,128)(2,1)}) %all-gather.6.cloned.1.call-update) | async-done | bytes 2097168 | tf_op jit(solution)/shard_map/all_gather | solution.py:32
  165.5 3.9 reshape.178
  169.4 2.4 convolution_convert_fusion
  171.8 27.1 %collective-permute-done = bf16[8192,128]{1,0:T(8,128)(2,1)} collective-permute-done((bf16[8192,128]{1,0:T(8,128)(2,1)S(1)}, bf16[8192,128]{1,0:T(8,128)(2,1)}, u32[]{:S(2)}, u32[]{:S(2)}) %collective-permute-start) | collective-permute-done | bytes 2097184 | tf_op jit(solution)/shard_map/ppermute | solution.py:10
  199.1 11.9 %copy.19 = bf16[256,128,128]{1,2,0:T(8,128)(2,1)} copy(bf16[256,128,128]{2,1,0:T(8,128)(2,1)} %param.10) | data formatting | bytes 16777216 | tf_op args[2]
  211.5 14.6 %collective-permute-done.1 = bf16[8192,128]{1,0:T(8,128)(2,1)} collective-permute-done((bf16[8192,128]{1,0:T(8,128)(2,1)}, bf16[8192,128]{1,0:T(8,128)(2,1)}, u32[]{:S(2)}, u32[]{:S(2)}) %collective-permute-start.1) | collective-permute-done | bytes 2097184 | tf_op jit(solution)/shard_map/ppermute | solution.py:10
  226.2 7.3 broadcast_select_fusion
  233.5 2.2 gather_fusion
  235.6 3.1 fusion.24
  238.8 2.5 gather_fusion.1
  241.3 2.5 fusion.54
  243.8 2.5 gather_fusion.2
  246.4 2.5 fusion.49
  248.9 4.6 collective-permute-done.2
  253.5 2.5 gather_fusion.3
  256.0 2.7 fusion.44
  259.4 4.4 fusion
  263.8 4.2 fusion.1
  268.0 2.7 fusion.2
  270.7 2.6 fusion.3
  273.3 2.5 broadcast.46.clone
  275.8 13.8 %scatter_fusion.3 = f32[64,128,128]{2,1,0:T(8,128)} fusion(f32[64,128,128]{2,1,0:T(8,128)} %broadcast.46.clone, s32[64]{0:T(128)S(1)} %get-tuple-element.21, f32[64,128,128]{2,1,0:T(8,128)} %bitcast.140), kind=kCustom, calls=%fused_computation.7 | custom fusion | flops 1048576 | bytes 12583168 | tf_op jit(solution)/shard_map/scatter-add | solution.py:65
  289.6 2.5 broadcast.46.clone.1
  292.1 13.5 %scatter_fusion.2 = f32[64,128,128]{2,1,0:T(8,128)} fusion(f32[64,128,128]{2,1,0:T(8,128)} %broadcast.46.clone.1, s32[64]{0:T(128)S(1)} %get-tuple-element.22, f32[64,128,128]{2,1,0:T(8,128)} %bitcast.139), kind=kCustom, calls=%fused_computation.6 | custom fusion | flops 1048576 | bytes 12583168 | tf_op jit(solution)/shard_map/scatter-add | solution.py:65
  305.6 2.5 broadcast.46.clone.2
  308.1 13.6 %scatter_fusion.1 = f32[64,128,128]{2,1,0:T(8,128)} fusion(f32[64,128,128]{2,1,0:T(8,128)} %broadcast.46.clone.2, s32[64]{0:T(128)S(1)} %get-tuple-element.23, f32[64,128,128]{2,1,0:T(8,128)} %bitcast.138), kind=kCustom, calls=%fused_computation.5 | custom fusion | flops 1048576 | bytes 12583168 | tf_op jit(solution)/shard_map/scatter-add | solution.py:65
  321.6 2.4 broadcast.46.clone.3
  324.0 13.6 %scatter_fusion = f32[64,128,128]{2,1,0:T(8,128)} fusion(f32[64,128,128]{2,1,0:T(8,128)} %broadcast.46.clone.3, s32[64]{0:T(128)S(1)} %get-tuple-element.20, f32[64,128,128]{2,1,0:T(8,128)} %bitcast.137), kind=kCustom, calls=%fused_computation.4 | custom fusion | flops 1048576 | bytes 12583168 | tf_op jit(solution)/shard_map/scatter-add | solution.py:65
  337.6 11.6 pad_maximum_fusion
  349.3 673.9 %reduce-scatter.2.cloned.1.call-done = f32[256,128]{1,0:T(8,128)} async-done(((f32[32768,128]{1,0:T(8,128)}), f32[256,128]{1,0:T(8,128)}) %reduce-scatter.2.cloned.1.call-update) | async-done | bytes 131088 | tf_op jit(solution)/shard_map/reduce_scatter | solution.py:71
  1024.8 148.2 %all-gather.4.cloned.1.call-done = bf16[8192,128]{1,0:T(8,128)(2,1)} async-done(((bf16[256,128]{1,0:T(8,128)(2,1)}), bf16[8192,128]{1,0:T(8,128)(2,1)}) %all-gather.4.cloned.1.call-update) | async-done | bytes 2097168 | tf_op jit(solution)/shard_map/all_gather | solution.py:72
  1175.1 7.2 psum.7
  (45 shorter events, 7.9 us)
Async XLA Ops:
  7.2 162.2 %copy-start = (bf16[128,128]{1,0:T(8,128)(2,1)S(1)}, bf16[128,128]{1,0:T(8,128)(2,1)}, u32[]{:S(2)}) copy-start(bf16[128,128]{1,0:T(8,128)(2,1)} %param.9) | copy-start | bytes 98308
  7.2 158.3 %all-gather.6.cloned.1.call-start = ((), (), s32[]{:S(2)}) async-start(), calls=%async_computation.3 | async-start | bytes 2162688 | tf_op jit(solution)/shard_map/all_gather | solution.py:32
  7.9 1015.3 %reduce-scatter.2.cloned.1.call-start = ((), (), s32[]{:S(2)}) async-start(), calls=%async_computation.1 | async-start | bytes 16908288 | tf_op jit(solution)/shard_map/reduce_scatter | solution.py:71
  169.4 29.5 %copy-start.4 = (s32[256]{0:T(256)S(1)}, s32[256]{0:T(256)}, u32[]{:S(2)}) copy-start(s32[256]{0:T(256)} %param.11) | copy-start | bytes 3076
  171.8 27.1 %collective-permute-start = (bf16[8192,128]{1,0:T(8,128)(2,1)S(1)}, bf16[8192,128]{1,0:T(8,128)(2,1)}, u32[]{:S(2)}, u32[]{:S(2)}) collective-permute-start(bf16[8192,128]{1,0:T(8,128)(2,1)S(1)} %convolution_convert_fusion), channel_id=1, source_target_pairs={{96,0},{0,32},{32,64},{64,96},{97,1},{1,33},{33,65},{65,97},{98,2}... | collective-permute-start | bytes 6291464 | tf_op jit(solution)/shard_map/ppermute | solution.py:10
  198.9 27.3 %collective-permute-start.1 = (bf16[8192,128]{1,0:T(8,128)(2,1)}, bf16[8192,128]{1,0:T(8,128)(2,1)}, u32[]{:S(2)}, u32[]{:S(2)}) collective-permute-start(bf16[8192,128]{1,0:T(8,128)(2,1)} %collective-permute-done), channel_id=1, source_target_pairs={{96,0},{0,32},{32,64},{64,96},{97,1},{1,33},{33,65},{65,97},{98,2}... | collective-permute-start | bytes 6291464 | tf_op jit(solution)/shard_map/ppermute | solution.py:10
  199.1 11.9 %copy-start.5 = (s32[8]{0:T(128)S(1)}, s32[8]{0:T(128)}, u32[]{:S(2)}) copy-start(s32[8]{0:T(128)} %param.12) | copy-start | bytes 100
  226.2 27.3 %collective-permute-start.2 = (bf16[8192,128]{1,0:T(8,128)(2,1)}, bf16[8192,128]{1,0:T(8,128)(2,1)}, u32[]{:S(2)}, u32[]{:S(2)}) collective-permute-start(bf16[8192,128]{1,0:T(8,128)(2,1)} %collective-permute-done.1), channel_id=1, source_target_pairs={{96,0},{0,32},{32,64},{64,96},{97,1},{1,33},{33,65},{65,97},{98,2}... | collective-permute-start | bytes 6291464 | tf_op jit(solution)/shard_map/ppermute | solution.py:10
  256.0 2.7 copy-start.3
  256.0 12.0 %slice-start = ((s8[8388608]{0:T(1024)(128)(4,1)}), s8[4194304]{0:T(1024)(128)(4,1)S(1)}, s32[]{:S(2)}) async-start(s8[8388608]{0:T(1024)(128)(4,1)} %bitcast.134), calls=%async_computation.4 | async-start | bytes 8388608
  259.4 8.6 slice-start.1
  349.2 823.7 %copy-start.2 = (bf16[4,8192]{1,0:T(4,128)(2,1)S(1)}, bf16[4,8192]{1,0:T(4,128)(2,1)}, u32[]{:S(2)}) copy-start(bf16[4,8192]{1,0:T(4,128)(2,1)} %param.8) | copy-start | bytes 196612
  349.3 823.7 %all-gather.4.cloned.1.call-start = ((), (), s32[]{:S(2)}) async-start(), calls=%async_computation.2 | async-start | bytes 2162688 | tf_op jit(solution)/shard_map/all_gather | solution.py:72
  1172.9 9.9 copy-start.1
Sparse Core Ops, SparseCore 0:
  9.7 155.7 all-gather.5
  349.4 673.7 reduce-scatter.1
  1025.4 147.4 all-gather.3
where the time goes:
time: 1190 us
  waiting for transfers between devices  1030 us (87%)
  other arithmetic  76.3 us (6%)
  local copies, waits for them, and re-layouts  36 us (3%)
  matrix products  30.5 us (3%)
  between operations  13.9 us (1%)
    reduce_scatter x1, waiting for transfers between devices, body(): lax.psum_scatter(whole_term, ('blk', 'feat'), scatter_dimension=0, tiled=...  674 us
    all_gather x1, waiting for transfers between devices, body(): lax.all_gather(features_t, 'feat', axis=0, tiled=True)  157 us
    all_gather x1, waiting for transfers between devices, body(): lax.all_gather(grad_own.astype(jnp.bfloat16), 'feat', axis=0, tiled=True)  148 us
    scatter-add x4, other arithmetic, spread(): empty_block.at[cols_here.reshape(-1)]  54.4 us
    ppermute x3, waiting for transfers between devices, shifted(): return lax.ppermute(block, axis, route)  46.3 us
  transfers between devices with their start and end apart: 6, of which 6 were waited for; matrix products, arithmetic and copies ran while one was open for 3% of the time, Pallas kernels for 0%

commit v1 on v0

--- a/solution.py
+++ b/solution.py
@@ -10,6 +10,43 @@
     return lax.ppermute(block, axis, route)
 
 
+def swapped(block, axis, mask):
+    count = lax.axis_size(axis)
+    return lax.ppermute(block, axis, [(i, i ^ mask) for i in range(count)])
+
+
+def gather_rows(block, axis):
+    count = lax.axis_size(axis)
+    index = lax.axis_index(axis)
+    mask = 1
+    while mask < count:
+        other = swapped(block, axis, mask)
+        upper = (index // mask) % 2 == 1
+        block = jnp.where(
+            upper,
+            jnp.concatenate([other, block], axis=0),
+            jnp.concatenate([block, other], axis=0),
+        )
+        mask *= 2
+    return block
+
+
+def scatter_rows(total, axis, wire_type):
+    count = lax.axis_size(axis)
+    index = lax.axis_index(axis)
+    mask = count // 2
+    while mask >= 1:
+        half = total.shape[0] // 2
+        lower, upper_part = total[:half], total[half:]
+        upper = (index // mask) % 2 == 1
+        keep = jnp.where(upper, upper_part, lower)
+        send = jnp.where(upper, lower, upper_part)
+        got = swapped(send.astype(wire_type), axis, mask)
+        total = keep + got.astype(jnp.float32)
+        mask //= 2
+    return total
+
+
 def body(features_t, weight, tile_values, tile_col, tile_count, grad_out):
     cycle_size = lax.axis_size("blk")
     hidden_width = weight.shape[1]
@@ -19,17 +56,16 @@
     block_rows = features_t.shape[1]
     block_tiles = block_rows // tile_size
     slot_count = tile_values.shape[0] // (cycle_size * tile_rows)
-    part_cols = features_t.shape[0]
     feat_id = lax.axis_index("feat")
     blk_id = lax.axis_index("blk")
-    weight_part = lax.dynamic_slice_in_dim(weight, feat_id * part_cols, part_cols, 0)
     slot_index = lax.broadcasted_iota(jnp.int32, (cycle_size, tile_rows, slot_count), 2)
     live_mask = slot_index < tile_count.reshape(cycle_size, tile_rows, 1)
     tile_stack = tile_values.reshape(cycle_size, tile_rows, slot_count, tile_size, tile_size)
     tile_stack = jnp.where(live_mask[..., None, None], tile_stack, jnp.zeros((), jnp.bfloat16))
     local_cols = (tile_col % block_tiles).reshape(cycle_size, tile_rows, slot_count)
+    features_block = gather_rows(features_t, "feat")
     projected = lax.dot_general(
-        lax.all_gather(features_t, "feat", axis=0, tiled=True),
+        features_block,
         weight,
         (((0,), (0,)), ((), ())),
         preferred_element_type=jnp.float32,
@@ -64,17 +100,28 @@
         empty_block = jnp.zeros((block_tiles, tile_size, hidden_width), jnp.float32)
         return empty_block.at[cols_here.reshape(-1)].add(
             contrib.reshape(-1, tile_size, hidden_width)
-        )
+        ).reshape(block_rows, hidden_width)
 
-    whole_term = jnp.concatenate([spread(block_id) for block_id in range(cycle_size)], axis=0)
-    whole_term = whole_term.reshape(cycle_size * block_rows, hidden_width)
-    grad_own = lax.psum_scatter(whole_term, ("blk", "feat"), scatter_dimension=0, tiled=True)
-    grad_hidden = lax.all_gather(grad_own.astype(jnp.bfloat16), "feat", axis=0, tiled=True)
-    weight_term = jnp.dot(features_t, grad_hidden, preferred_element_type=jnp.float32)
-    grad_weight = lax.psum(weight_term, "blk") * lax.rsqrt(jnp.float32(block_rows * cycle_size))
-    grad_features = lax.dot_general(
-        weight_part, grad_hidden, (((1,), (1,)), ((), ())), preferred_element_type=jnp.float32
+    block_total = spread(blk_id)
+    for distance in range(1, cycle_size):
+        outgoing = spread((blk_id + distance) % cycle_size).astype(jnp.bfloat16)
+        block_total = block_total + shifted(outgoing, "blk", distance).astype(jnp.float32)
+    grad_own = scatter_rows(block_total, "feat", jnp.bfloat16)
+    grad_hidden = grad_own.astype(jnp.bfloat16)
+
+    features_own = lax.dynamic_slice_in_dim(features_block, feat_id * rows_own, rows_own, 1)
+    weight_term = jnp.dot(features_own, grad_hidden, preferred_element_type=jnp.float32)
+    weight_part = scatter_rows(weight_term, "feat", jnp.float32)
+    weight_part = weight_part + swapped(weight_part, "blk", 1)
+    weight_part = weight_part + swapped(weight_part, "blk", 2)
+    grad_weight = weight_part * lax.rsqrt(jnp.float32(block_rows * cycle_size))
+
+    features_grad_local = lax.dot_general(
+        weight, grad_hidden, (((1,), (1,)), ((), ())), preferred_element_type=jnp.float32
     ).astype(jnp.bfloat16)
+    grad_features = lax.all_to_all(
+        features_grad_local, "feat", split_axis=0, concat_axis=1, tiled=True
+    )
     return (activations, grad_features, grad_weight)
 
 

time: 1190 us -> 379 us (0.32)
  waiting for transfers between devices: 1030 us -> 195 us
  starting transfers between devices: 0.2 us -> 38.9 us
  between operations: 13.9 us -> 0.95 us
    reduce_scatter x1 -> x0, waiting for transfers between devices: 674 us -> none  [body(): lax.psum_scatter(whole_term, ('blk', 'feat'), scatter_dimension=0, tiled=...]
    all_gather x2 -> x0, waiting for transfers between devices: 306 us -> none  [the longest x1 157 us: body(): lax.all_gather(features_t, 'feat', axis=0, tiled=True)]
    ppermute x0 -> x17, waiting for transfers between devices: none -> 109 us  [swapped(): return lax.ppermute(block, axis, [(i, i ^ mask) for i in range(count)])]
    ppermute x3 -> x6, waiting for transfers between devices: 46.3 us -> 80.6 us  [shifted(): return lax.ppermute(block, axis, route)]
    ppermute x0 -> x17, starting transfers between devices: none -> 28 us  [swapped(): return lax.ppermute(block, axis, [(i, i ^ mask) for i in range(count)])]
    unnamed x18 -> x11, local copies, waits for them, and re-layouts: 15.9 us -> 1.96 us
  transfers between devices with their start and end apart: 6 -> 24, of which waited for: 6 -> 20; matrix products, arithmetic and copies ran while one was open for 3% -> 24% of each run, Pallas kernels for 0% -> 0%
where the time goes in v1:
time: 379 us; the launch traced here: 378 us
  waiting for transfers between devices  195 us (51%)
  other arithmetic  83.9 us (22%)
  starting transfers between devices  38.9 us (10%)
  matrix products  31.2 us (8%)
  local copies, waits for them, and re-layouts  28.4 us (7%)
    ppermute x17, waiting for transfers between devices, swapped(): return lax.ppermute(block, axis, [(i, i ^ mask) for i in range(count)])  109 us
    ppermute x6, waiting for transfers between devices, shifted(): return lax.ppermute(block, axis, route)  80.6 us
    scatter-add x4, other arithmetic, spread(): empty_block.at[cols_here.reshape(-1)]  54.2 us
    ppermute x17, starting transfers between devices, swapped(): return lax.ppermute(block, axis, [(i, i ^ mask) for i in range(count)])  28 us
    dot_general x4, matrix products, spread(): jnp.einsum('rsij,rih->rsjh', tiles_here, grad_tiles, preferred_element_ty...  18.1 us
    gather x4, local copies, waits for them, and re-layouts, aggregate(): picked = jnp.take(block_tiles_view, cols_here, axis=0)  14.9 us
    dot_general x4, matrix products, aggregate(): jnp.einsum('rsij,rsjh->rih', tiles_here, picked, preferred_element_type=j...  12 us
    convert_element_type x3, other arithmetic, body(): outgoing = spread((blk_id + distance) % cycle_size).astype(jnp.bfloat16)  11.7 us
  transfers between devices with their start and end apart: 24, of which 20 were waited for; matrix products, arithmetic and copies ran while one was open for 24% of the time, Pallas kernels for 0%

profile of v1, /device:TPU:0, one launch (start us, length us, event | category | flops | bytes accessed | tf_op | source)
XLA Modules:
  0.0 378.0 jit_solution(10236930792944145629)
XLA Ops:
  14.9 4.4 %collective-permute-done.2 = bf16[16,8192]{1,0:T(8,128)(2,1)S(1)} collective-permute-done((bf16[16,8192]{1,0:T(8,128)(2,1)S(1)}, bf16[16,8192]{1,0:T(8,128)(2,1)S(1)}, u32[]{:S(2)}, u32[]{:S(2)}) %collective-permute-start.2) | collective-permute-done | bytes 262176 | tf_op jit(solution)/shard_map/ppermute | solution.py:15
  19.4 5.4 %collective-permute-start.3 = (bf16[32,8192]{1,0:T(8,128)(2,1)S(1)}, bf16[32,8192]{1,0:T(8,128)(2,1)S(1)}, u32[]{:S(2)}, u32[]{:S(2)}) collective-permute-start(bf16[32,8192]{1,0:T(8,128)(2,1)S(1)} %maximum_select_fusion.2), channel_id=1, source_target_pairs={{0,8},{1,9},{2,10},{3,11},{4,12},{5,13},{6,14},{7,15},{8,0},{9,1},... | collective-permute-start | bytes 1572872 | tf_op jit(solution)/shard_map/ppermute | solution.py:15
  24.8 9.3 %collective-permute-done.3 = bf16[32,8192]{1,0:T(8,128)(2,1)S(1)} collective-permute-done((bf16[32,8192]{1,0:T(8,128)(2,1)S(1)}, bf16[32,8192]{1,0:T(8,128)(2,1)S(1)}, u32[]{:S(2)}, u32[]{:S(2)}) %collective-permute-start.3) | collective-permute-done | bytes 524320 | tf_op jit(solution)/shard_map/ppermute | solution.py:15
  35.9 20.1 %collective-permute-done.4 = bf16[64,8192]{1,0:T(8,128)(2,1)} collective-permute-done((bf16[64,8192]{1,0:T(8,128)(2,1)S(1)}, bf16[64,8192]{1,0:T(8,128)(2,1)}, u32[]{:S(2)}, u32[]{:S(2)}) %collective-permute-start.4) | collective-permute-done | bytes 1048608 | tf_op jit(solution)/shard_map/ppermute | solution.py:15
  60.2 27.1 %collective-permute-done.5 = bf16[8192,128]{1,0:T(8,128)(2,1)} collective-permute-done((bf16[8192,128]{1,0:T(8,128)(2,1)S(1)}, bf16[8192,128]{1,0:T(8,128)(2,1)}, u32[]{:S(2)}, u32[]{:S(2)}) %collective-permute-start.5) | collective-permute-done | bytes 2097184 | tf_op jit(solution)/shard_map/ppermute | solution.py:10
  88.2 26.4 %collective-permute-done.6 = bf16[8192,128]{1,0:T(8,128)(2,1)} collective-permute-done((bf16[8192,128]{1,0:T(8,128)(2,1)}, bf16[8192,128]{1,0:T(8,128)(2,1)}, u32[]{:S(2)}, u32[]{:S(2)}) %collective-permute-start.6) | collective-permute-done | bytes 2097184 | tf_op jit(solution)/shard_map/ppermute | solution.py:10
  114.5 7.3 %broadcast_select_fusion = bf16[4,2,32,128,128]{4,3,2,1,0:T(8,128)(2,1)} fusion(bf16[4,2,32,128,128]{4,3,2,1,0:T(8,128)(2,1)} %bitcast.153, pred[4,2,32]{2,1,0:T(4,128)(4,1)S(1)} %iota_compare_fusion), kind=kLoop, calls=%fused_computation.9 | loop fusion | flops 4194304 | bytes 16777472 | tf_op jit(solution)/shard_map/jit(_where)/select_n | solution.py:64
  121.8 3.7 gather_fusion
  128.6 3.7 gather_fusion.1
  135.3 3.7 gather_fusion.2
  142.0 3.7 gather_fusion.3
  149.5 4.5 %fusion.6 = f32[2,32,128,128]{3,2,1,0:T(8,128)} fusion(bf16[2,128,128,1]{2,1,3,0:T(8,128)(2,1)S(1)} %bitcast.158, bf16[4,2,32,128,128]{4,3,2,1,0:T(8,128)(2,1)} %broadcast_select_fusion, s32[]{:T(128)S(6)} %select_n.378), kind=kOutput, calls=%fused_computation.18 | convolution fusion | flops 268435456 | bytes 6356996 | tf_op jit(solution)/shard_map/rsij,rih->rsjh/dot_general | solution.py:97
  154.0 4.6 %fusion.4 = f32[2,32,128,128]{3,2,1,0:T(8,128)} fusion(bf16[2,128,128,1]{2,1,3,0:T(8,128)(2,1)S(1)} %bitcast.159, bf16[4,2,32,128,128]{4,3,2,1,0:T(8,128)(2,1)} %broadcast_select_fusion, s32[]{:T(128)S(6)} %select_n.381), kind=kOutput, calls=%fused_computation.16 | convolution fusion | flops 268435456 | bytes 6356996 | tf_op jit(solution)/shard_map/rsij,rih->rsjh/dot_general | solution.py:97
  158.6 4.5 %fusion.2 = f32[2,32,128,128]{3,2,1,0:T(8,128)} fusion(bf16[2,128,128,1]{2,1,3,0:T(8,128)(2,1)S(1)} %bitcast.160, bf16[4,2,32,128,128]{4,3,2,1,0:T(8,128)(2,1)} %broadcast_select_fusion, s32[]{:T(128)S(6)} %select_n.384), kind=kOutput, calls=%fused_computation.14 | convolution fusion | flops 268435456 | bytes 6356996 | tf_op jit(solution)/shard_map/rsij,rih->rsjh/dot_general | solution.py:97
  165.7 13.6 %scatter_fusion.1 = f32[64,128,128]{2,1,0:T(8,128)} fusion(f32[64,128,128]{2,1,0:T(8,128)} %broadcast.99.clone.3, s32[64]{0:T(128)S(1)} %get-tuple-element.23, f32[64,128,128]{2,1,0:T(8,128)} %bitcast.150), kind=kCustom, calls=%fused_computation.5 | custom fusion | flops 1048576 | bytes 12583168 | tf_op jit(solution)/shard_map/scatter-add | solution.py:101
  179.3 3.9 %convert_element_type.82 = bf16[64,128,128]{2,1,0:T(8,128)(2,1)} convert(f32[64,128,128]{2,1,0:T(8,128)} %scatter_fusion.1) | non-fusion elementwise | flops 1048576 | bytes 6291456 | tf_op jit(solution)/shard_map/convert_element_type | solution.py:107
  189.0 13.5 %scatter_fusion.2 = f32[64,128,128]{2,1,0:T(8,128)} fusion(f32[64,128,128]{2,1,0:T(8,128)} %broadcast.99.clone.2, s32[64]{0:T(128)S(1)} %get-tuple-element.24, f32[64,128,128]{2,1,0:T(8,128)} %bitcast.149), kind=kCustom, calls=%fused_computation.6 | custom fusion | flops 1048576 | bytes 12583168 | tf_op jit(solution)/shard_map/scatter-add | solution.py:101
  202.5 3.9 %convert_element_type.85 = bf16[64,128,128]{2,1,0:T(8,128)(2,1)} convert(f32[64,128,128]{2,1,0:T(8,128)} %scatter_fusion.2) | non-fusion elementwise | flops 1048576 | bytes 6291456 | tf_op jit(solution)/shard_map/convert_element_type | solution.py:107
  209.5 13.5 %scatter_fusion.3 = f32[64,128,128]{2,1,0:T(8,128)} fusion(f32[64,128,128]{2,1,0:T(8,128)} %broadcast.99.clone.1, s32[64]{0:T(128)S(1)} %fusion.99, f32[64,128,128]{2,1,0:T(8,128)} %bitcast.148), kind=kCustom, calls=%fused_computation.7 | custom fusion | flops 1048576 | bytes 12583168 | tf_op jit(solution)/shard_map/scatter-add | solution.py:101
  223.1 3.9 %convert_element_type.88 = bf16[64,128,128]{2,1,0:T(8,128)(2,1)} convert(f32[64,128,128]{2,1,0:T(8,128)} %scatter_fusion.3) | non-fusion elementwise | flops 1048576 | bytes 6291456 | tf_op jit(solution)/shard_map/convert_element_type | solution.py:107
  229.4 4.5 %fusion.14 = f32[2,32,128,128]{3,2,1,0:T(8,128)} fusion(bf16[2,128,128,1]{2,1,3,0:T(8,128)(2,1)S(1)} %bitcast.161, bf16[4,2,32,128,128]{4,3,2,1,0:T(8,128)(2,1)} %broadcast_select_fusion, s32[]{:T(128)S(6)} %select_n.344), kind=kOutput, calls=%fused_computation.26 | convolution fusion | flops 268435456 | bytes 6356996 | tf_op jit(solution)/shard_map/rsij,rih->rsjh/dot_general | solution.py:97
  236.4 13.5 %scatter_fusion = f32[64,128,128]{2,1,0:T(8,128)} fusion(f32[64,128,128]{2,1,0:T(8,128)} %broadcast.99.clone, s32[64]{0:T(128)S(1)} %fusion.96, f32[64,128,128]{2,1,0:T(8,128)} %bitcast.151), kind=kCustom, calls=%fused_computation.4 | custom fusion | flops 1048576 | bytes 12583168 | tf_op jit(solution)/shard_map/scatter-add | solution.py:101
  249.9 5.9 %collective-permute-done.9 = bf16[8192,128]{1,0:T(8,128)(2,1)} collective-permute-done((bf16[8192,128]{1,0:T(8,128)(2,1)}, bf16[8192,128]{1,0:T(8,128)(2,1)}, u32[]{:S(2)}, u32[]{:S(2)}) %collective-permute-start.9) | collective-permute-done | bytes 2097184 | tf_op jit(solution)/shard_map/ppermute | solution.py:10
  255.8 21.2 %collective-permute-done.10 = bf16[8192,128]{1,0:T(8,128)(2,1)} collective-permute-done((bf16[8192,128]{1,0:T(8,128)(2,1)}, bf16[8192,128]{1,0:T(8,128)(2,1)}, u32[]{:S(2)}, u32[]{:S(2)}) %collective-permute-start.10) | collective-permute-done | bytes 2097184 | tf_op jit(solution)/shard_map/ppermute | solution.py:10
  277.0 4.8 %fusion.1 = f32[8192,128]{1,0:T(8,128)S(1)} fusion(f32[64,128,128]{2,1,0:T(8,128)} %scatter_fusion, bf16[8192,128]{1,0:T(8,128)(2,1)} %collective-permute-done.10, bf16[8192,128]{1,0:T(8,128)(2,1)} %collective-permute-done.9, bf16[8192,128]{1,0:T(8,128)(2,1)} %collective-permute-done.8), kind=kLoop, calls=%fused_computation.12 | loop fusion | flops 6291456 | bytes 14680064 | tf_op jit(solution)/shard_map/add | solution.py:108
  282.9 25.2 %collective-permute-done.11 = bf16[4096,128]{1,0:T(8,128)(2,1)S(1)} collective-permute-done((bf16[4096,128]{1,0:T(8,128)(2,1)S(1)}, bf16[4096,128]{1,0:T(8,128)(2,1)S(1)}, u32[]{:S(2)}, u32[]{:S(2)}) %collective-permute-start.11) | collective-permute-done | bytes 1048608 | tf_op jit(solution)/shard_map/ppermute | solution.py:15
  308.6 15.4 %collective-permute-done.12 = bf16[2048,128]{1,0:T(8,128)(2,1)S(1)} collective-permute-done((bf16[2048,128]{1,0:T(8,128)(2,1)S(1)}, bf16[2048,128]{1,0:T(8,128)(2,1)S(1)}, u32[]{:S(2)}, u32[]{:S(2)}) %collective-permute-start.12) | collective-permute-done | bytes 524320 | tf_op jit(solution)/shard_map/ppermute | solution.py:15
  324.4 7.5 %collective-permute-done.13 = bf16[1024,128]{1,0:T(8,128)(2,1)S(1)} collective-permute-done((bf16[1024,128]{1,0:T(8,128)(2,1)S(1)}, bf16[1024,128]{1,0:T(8,128)(2,1)S(1)}, u32[]{:S(2)}, u32[]{:S(2)}) %collective-permute-start.13) | collective-permute-done | bytes 262176 | tf_op jit(solution)/shard_map/ppermute | solution.py:15
  335.1 3.4 collective-permute-done.14
  347.8 4.6 %collective-permute-done.17 = f32[32,128]{1,0:T(8,128)S(1)} collective-permute-done((f32[32,128]{1,0:T(8,128)S(1)}, f32[32,128]{1,0:T(8,128)S(1)}, u32[]{:S(2)}, u32[]{:S(2)}) %collective-permute-start.17) | collective-permute-done | bytes 16416 | tf_op jit(solution)/shard_map/ppermute | solution.py:15
  363.8 4.7 %all-to-all-start = ((bf16[32,4,256]{2,1,0:T(4,128)(2,1)}), bf16[32,4,256]{2,1,0:T(4,128)(2,1)S(1)}, u32[]{:S(2)}, u32[]{:S(2)}) async-start(bf16[32,4,256]{2,1,0:T(4,128)(2,1)} %all_to_all.14), calls=%async_computation | async-start | bytes 131072 | tf_op jit(solution)/shard_map/all_to_all | solution.py:122
  371.4 5.5 %all-to-all-done = bf16[32,4,256]{2,1,0:T(4,128)(2,1)S(1)} async-done(((bf16[32,4,256]{2,1,0:T(4,128)(2,1)}), bf16[32,4,256]{2,1,0:T(4,128)(2,1)S(1)}, u32[]{:S(2)}, u32[]{:S(2)}) %all-to-all-start) | async-done | bytes 65568 | tf_op jit(solution)/shard_map/all_to_all | solution.py:122
  (106 shorter events, 80.0 us)
Async XLA Ops:
  0.6 57.5 %copy-start = (bf16[128,128]{1,0:T(8,128)(2,1)S(1)}, bf16[128,128]{1,0:T(8,128)(2,1)}, u32[]{:S(2)}) copy-start(bf16[128,128]{1,0:T(8,128)(2,1)} %param.9) | copy-start | bytes 98308
  0.6 4.6 %collective-permute-start = (bf16[4,8192]{1,0:T(4,128)(2,1)}, bf16[4,8192]{1,0:T(4,128)(2,1)S(1)}, u32[]{:S(2)}, u32[]{:S(2)}) collective-permute-start(bf16[4,8192]{1,0:T(4,128)(2,1)} %param.8), channel_id=1, source_target_pairs={{0,1},{1,0},{2,3},{3,2},{4,5},{5,4},{6,7},{7,6},{8,9},{9,8},{10,11... | collective-permute-start | bytes 196616 | tf_op jit(solution)/shard_map/ppermute | solution.py:15
  6.2 6.6 %collective-permute-start.1 = (bf16[8,8192]{1,0:T(8,128)(2,1)S(1)}, bf16[8,8192]{1,0:T(8,128)(2,1)S(1)}, u32[]{:S(2)}, u32[]{:S(2)}) collective-permute-start(bf16[8,8192]{1,0:T(8,128)(2,1)S(1)} %maximum_select_fusion.4), channel_id=1, source_target_pairs={{0,2},{1,3},{2,0},{3,1},{4,6},{5,7},{6,4},{7,5},{8,10},{9,11},{10,... | collective-permute-start | bytes 393224 | tf_op jit(solution)/shard_map/ppermute | solution.py:15
  12.8 6.5 %collective-permute-start.2 = (bf16[16,8192]{1,0:T(8,128)(2,1)S(1)}, bf16[16,8192]{1,0:T(8,128)(2,1)S(1)}, u32[]{:S(2)}, u32[]{:S(2)}) collective-permute-start(bf16[16,8192]{1,0:T(8,128)(2,1)S(1)} %maximum_select_fusion.3), channel_id=1, source_target_pairs={{0,4},{1,5},{2,6},{3,7},{4,0},{5,1},{6,2},{7,3},{8,12},{9,13},{10,... | collective-permute-start | bytes 786440 | tf_op jit(solution)/shard_map/ppermute | solution.py:15
  19.4 14.7 %collective-permute-start.3 = (bf16[32,8192]{1,0:T(8,128)(2,1)S(1)}, bf16[32,8192]{1,0:T(8,128)(2,1)S(1)}, u32[]{:S(2)}, u32[]{:S(2)}) collective-permute-start(bf16[32,8192]{1,0:T(8,128)(2,1)S(1)} %maximum_select_fusion.2), channel_id=1, source_target_pairs={{0,8},{1,9},{2,10},{3,11},{4,12},{5,13},{6,14},{7,15},{8,0},{9,1},... | collective-permute-start | bytes 1572872 | tf_op jit(solution)/shard_map/ppermute | solution.py:15
  34.3 21.8 %collective-permute-start.4 = (bf16[64,8192]{1,0:T(8,128)(2,1)S(1)}, bf16[64,8192]{1,0:T(8,128)(2,1)}, u32[]{:S(2)}, u32[]{:S(2)}) collective-permute-start(bf16[64,8192]{1,0:T(8,128)(2,1)S(1)} %maximum_select_fusion.1), channel_id=1, source_target_pairs={{0,16},{1,17},{2,18},{3,19},{4,20},{5,21},{6,22},{7,23},{8,24},{9,... | collective-permute-start | bytes 3145736 | tf_op jit(solution)/shard_map/ppermute | solution.py:15
  58.1 29.2 %copy-start.3 = (s32[256]{0:T(256)S(1)}, s32[256]{0:T(256)}, u32[]{:S(2)}) copy-start(s32[256]{0:T(256)} %param.11) | copy-start | bytes 3076
  58.1 29.4 %copy-start.4 = (s32[8]{0:T(128)S(1)}, s32[8]{0:T(128)}, u32[]{:S(2)}) copy-start(s32[8]{0:T(128)} %param.12) | copy-start | bytes 100
  58.9 1.3 copy-start.1
  60.2 27.1 %collective-permute-start.5 = (bf16[8192,128]{1,0:T(8,128)(2,1)S(1)}, bf16[8192,128]{1,0:T(8,128)(2,1)}, u32[]{:S(2)}, u32[]{:S(2)}) collective-permute-start(bf16[8192,128]{1,0:T(8,128)(2,1)S(1)} %convolution_convert_fusion), channel_id=1, source_target_pairs={{96,0},{0,32},{32,64},{64,96},{97,1},{1,33},{33,65},{65,97},{98,2}... | collective-permute-start | bytes 6291464 | tf_op jit(solution)/shard_map/ppermute | solution.py:10
  87.3 27.3 %collective-permute-start.6 = (bf16[8192,128]{1,0:T(8,128)(2,1)}, bf16[8192,128]{1,0:T(8,128)(2,1)}, u32[]{:S(2)}, u32[]{:S(2)}) collective-permute-start(bf16[8192,128]{1,0:T(8,128)(2,1)} %collective-permute-done.5), channel_id=1, source_target_pairs={{96,0},{0,32},{32,64},{64,96},{97,1},{1,33},{33,65},{65,97},{98,2}... | collective-permute-start | bytes 6291464 | tf_op jit(solution)/shard_map/ppermute | solution.py:10
  114.5 27.5 %collective-permute-start.7 = (bf16[8192,128]{1,0:T(8,128)(2,1)}, bf16[8192,128]{1,0:T(8,128)(2,1)}, u32[]{:S(2)}, u32[]{:S(2)}) collective-permute-start(bf16[8192,128]{1,0:T(8,128)(2,1)} %collective-permute-done.6), channel_id=1, source_target_pairs={{96,0},{0,32},{32,64},{64,96},{97,1},{1,33},{33,65},{65,97},{98,2}... | collective-permute-start | bytes 6291464 | tf_op jit(solution)/shard_map/ppermute | solution.py:10
  145.8 3.0 copy-start.2
  183.2 66.7 %collective-permute-start.8 = (bf16[8192,128]{1,0:T(8,128)(2,1)}, bf16[8192,128]{1,0:T(8,128)(2,1)}, u32[]{:S(2)}, u32[]{:S(2)}) collective-permute-start(bf16[8192,128]{1,0:T(8,128)(2,1)} %bitcast.37), channel_id=1, source_target_pairs={{96,0},{0,32},{32,64},{64,96},{97,1},{1,33},{33,65},{65,97},{98,2}... | collective-permute-start | bytes 6291464 | tf_op jit(solution)/shard_map/ppermute | solution.py:10
  206.4 49.4 %collective-permute-start.9 = (bf16[8192,128]{1,0:T(8,128)(2,1)}, bf16[8192,128]{1,0:T(8,128)(2,1)}, u32[]{:S(2)}, u32[]{:S(2)}) collective-permute-start(bf16[8192,128]{1,0:T(8,128)(2,1)} %bitcast.41), channel_id=1, source_target_pairs={{64,0},{96,32},{0,64},{32,96},{65,1},{97,33},{1,65},{33,97},{66,2}... | collective-permute-start | bytes 6291464 | tf_op jit(solution)/shard_map/ppermute | solution.py:10
  227.0 50.0 %collective-permute-start.10 = (bf16[8192,128]{1,0:T(8,128)(2,1)}, bf16[8192,128]{1,0:T(8,128)(2,1)}, u32[]{:S(2)}, u32[]{:S(2)}) collective-permute-start(bf16[8192,128]{1,0:T(8,128)(2,1)} %bitcast.45), channel_id=1, source_target_pairs={{32,0},{64,32},{96,64},{0,96},{33,1},{65,33},{97,65},{1,97},{34,2}... | collective-permute-start | bytes 6291464 | tf_op jit(solution)/shard_map/ppermute | solution.py:10
  282.1 26.0 %collective-permute-start.11 = (bf16[4096,128]{1,0:T(8,128)(2,1)S(1)}, bf16[4096,128]{1,0:T(8,128)(2,1)S(1)}, u32[]{:S(2)}, u32[]{:S(2)}) collective-permute-start(bf16[4096,128]{1,0:T(8,128)(2,1)S(1)} %select_convert_fusion), channel_id=1, source_target_pairs={{0,16},{1,17},{2,18},{3,19},{4,20},{5,21},{6,22},{7,23},{8,24},{9,... | collective-permute-start | bytes 3145736 | tf_op jit(solution)/shard_map/ppermute | solution.py:15
  308.5 15.5 %collective-permute-start.12 = (bf16[2048,128]{1,0:T(8,128)(2,1)S(1)}, bf16[2048,128]{1,0:T(8,128)(2,1)S(1)}, u32[]{:S(2)}, u32[]{:S(2)}) collective-permute-start(bf16[2048,128]{1,0:T(8,128)(2,1)S(1)} %select_convert_fusion.1), channel_id=1, source_target_pairs={{0,8},{1,9},{2,10},{3,11},{4,12},{5,13},{6,14},{7,15},{8,0},{9,1},... | collective-permute-start | bytes 1572872 | tf_op jit(solution)/shard_map/ppermute | solution.py:15
  324.3 7.6 %collective-permute-start.13 = (bf16[1024,128]{1,0:T(8,128)(2,1)S(1)}, bf16[1024,128]{1,0:T(8,128)(2,1)S(1)}, u32[]{:S(2)}, u32[]{:S(2)}) collective-permute-start(bf16[1024,128]{1,0:T(8,128)(2,1)S(1)} %select_convert_fusion.2), channel_id=1, source_target_pairs={{0,4},{1,5},{2,6},{3,7},{4,0},{5,1},{6,2},{7,3},{8,12},{9,13},{10,... | collective-permute-start | bytes 786440 | tf_op jit(solution)/shard_map/ppermute | solution.py:15
  332.0 6.6 %collective-permute-start.14 = (bf16[512,128]{1,0:T(8,128)(2,1)S(1)}, bf16[512,128]{1,0:T(8,128)(2,1)S(1)}, u32[]{:S(2)}, u32[]{:S(2)}) collective-permute-start(bf16[512,128]{1,0:T(8,128)(2,1)S(1)} %select_convert_fusion.3), channel_id=1, source_target_pairs={{0,2},{1,3},{2,0},{3,1},{4,6},{5,7},{6,4},{7,5},{8,10},{9,11},{10,... | collective-permute-start | bytes 393224 | tf_op jit(solution)/shard_map/ppermute | solution.py:15
  338.6 4.3 %collective-permute-start.15 = (bf16[256,128]{1,0:T(8,128)(2,1)S(1)}, bf16[256,128]{1,0:T(8,128)(2,1)S(1)}, u32[]{:S(2)}, u32[]{:S(2)}) collective-permute-start(bf16[256,128]{1,0:T(8,128)(2,1)S(1)} %select_convert_fusion.4), channel_id=1, source_target_pairs={{0,1},{1,0},{2,3},{3,2},{4,5},{5,4},{6,7},{7,6},{8,9},{9,8},{10,11... | collective-permute-start | bytes 196616 | tf_op jit(solution)/shard_map/ppermute | solution.py:15
  343.1 4.0 %collective-permute-start.16 = (f32[64,128]{1,0:T(8,128)S(1)}, f32[64,128]{1,0:T(8,128)S(1)}, u32[]{:S(2)}, u32[]{:S(2)}) collective-permute-start(f32[64,128]{1,0:T(8,128)S(1)} %slice_select_fusion), channel_id=1, source_target_pairs={{0,16},{1,17},{2,18},{3,19},{4,20},{5,21},{6,22},{7,23},{8,24},{9,... | collective-permute-start | bytes 98312 | tf_op jit(solution)/shard_map/ppermute | solution.py:15
  347.1 5.3 %collective-permute-start.17 = (f32[32,128]{1,0:T(8,128)S(1)}, f32[32,128]{1,0:T(8,128)S(1)}, u32[]{:S(2)}, u32[]{:S(2)}) collective-permute-start(f32[32,128]{1,0:T(8,128)S(1)} %slice_select_fusion.1), channel_id=1, source_target_pairs={{0,8},{1,9},{2,10},{3,11},{4,12},{5,13},{6,14},{7,15},{8,0},{9,1},... | collective-permute-start | bytes 49160 | tf_op jit(solution)/shard_map/ppermute | solution.py:15
  352.5 3.7 collective-permute-start.18
  356.2 5.2 %collective-permute-start.19 = (f32[8,128]{1,0:T(8,128)S(1)}, f32[8,128]{1,0:T(8,128)S(1)}, u32[]{:S(2)}, u32[]{:S(2)}) collective-permute-start(f32[8,128]{1,0:T(8,128)S(1)} %slice_select_fusion.3), channel_id=1, source_target_pairs={{0,2},{1,3},{2,0},{3,1},{4,6},{5,7},{6,4},{7,5},{8,10},{9,11},{10,... | collective-permute-start | bytes 12296 | tf_op jit(solution)/shard_map/ppermute | solution.py:15
  361.4 7.1 %collective-permute-start.20 = (f32[4,128]{1,0:T(4,128)S(1)}, f32[4,128]{1,0:T(4,128)S(1)}, u32[]{:S(2)}, u32[]{:S(2)}) collective-permute-start(f32[4,128]{1,0:T(4,128)S(1)} %slice_select_fusion.4), channel_id=1, source_target_pairs={{0,1},{1,0},{2,3},{3,2},{4,5},{5,4},{6,7},{7,6},{8,9},{9,8},{10,11... | collective-permute-start | bytes 6152 | tf_op jit(solution)/shard_map/ppermute | solution.py:15
  363.8 13.0 %all-to-all-start = ((bf16[32,4,256]{2,1,0:T(4,128)(2,1)}), bf16[32,4,256]{2,1,0:T(4,128)(2,1)S(1)}, u32[]{:S(2)}, u32[]{:S(2)}) async-start(bf16[32,4,256]{2,1,0:T(4,128)(2,1)} %all_to_all.14), calls=%async_computation | async-start | bytes 131072 | tf_op jit(solution)/shard_map/all_to_all | solution.py:122
  368.5 1.2 collective-permute-start.21
  369.8 7.1 %collective-permute-start.22 = (f32[4,128]{1,0:T(4,128)S(1)}, f32[4,128]{1,0:T(4,128)S(1)}, u32[]{:S(2)}, u32[]{:S(2)}) collective-permute-start(f32[4,128]{1,0:T(4,128)S(1)} %add.266), channel_id=1, source_target_pairs={{0,64},{32,96},{64,0},{96,32},{1,65},{33,97},{65,1},{97,33},{2,66}... | collective-permute-start | bytes 6152 | tf_op jit(solution)/shard_map/ppermute | solution.py:15

commit v2 on v1

--- a/solution.py
+++ b/solution.py
@@ -2,6 +2,8 @@
 import jax.numpy as jnp
 from jax import lax
 from jax.sharding import PartitionSpec as P
+from jax.experimental import pallas as pl
+from jax.experimental.pallas import tpu as pltpu
 
 
 def shifted(block, axis, distance):
@@ -47,6 +49,113 @@
     return total
 
 
+def aggregate_kernel(block_ref, cols_ref, count_ref, tiles_ref, proj_ref, out_ref):
+    row = pl.program_id(0)
+    tile_rows = pl.num_programs(0)
+    slot_count = tiles_ref.shape[0]
+    base = block_ref[0] * tile_rows + row
+    live = count_ref[base]
+
+    def step(slot, total):
+        col = cols_ref[base * slot_count + slot]
+        return total + jnp.dot(tiles_ref[slot], proj_ref[col], preferred_element_type=jnp.float32)
+
+    out_ref[...] = lax.fori_loop(0, live, step, jnp.zeros(out_ref.shape, jnp.float32))
+
+
+def aggregate_block(block_id, cols, counts, tile_stack, block_value):
+    blocks, tile_rows, slot_count, tile_size, _ = tile_stack.shape
+    hidden_width = block_value.shape[-1]
+    block_tiles = block_value.shape[0] // tile_size
+    grid_spec = pltpu.PrefetchScalarGridSpec(
+        num_scalar_prefetch=3,
+        grid=(tile_rows,),
+        in_specs=[
+            pl.BlockSpec(
+                (None, None, slot_count, tile_size, tile_size),
+                lambda r, b, c, n: (b[0], r, 0, 0, 0),
+            ),
+            pl.BlockSpec(
+                (block_tiles, tile_size, hidden_width), lambda r, b, c, n: (0, 0, 0)
+            ),
+        ],
+        out_specs=pl.BlockSpec((None, tile_size, hidden_width), lambda r, b, c, n: (r, 0, 0)),
+    )
+    return pl.pallas_call(
+        aggregate_kernel,
+        grid_spec=grid_spec,
+        out_shape=jax.ShapeDtypeStruct((tile_rows, tile_size, hidden_width), jnp.float32),
+        compiler_params=pltpu.CompilerParams(dimension_semantics=("arbitrary",)),
+    )(
+        jnp.reshape(block_id, (1,)).astype(jnp.int32),
+        cols,
+        counts,
+        tile_stack,
+        block_value.reshape(block_tiles, tile_size, hidden_width),
+    )
+
+
+def spread_kernel(block_ref, cols_ref, count_ref, tiles_ref, grad_ref, out_ref, total_ref):
+    row = pl.program_id(0)
+    tile_rows = pl.num_programs(0)
+    slot_count = tiles_ref.shape[0]
+    base = block_ref[0] * tile_rows + row
+    live = count_ref[base]
+
+    @pl.when(row == 0)
+    def _():
+        total_ref[...] = jnp.zeros(total_ref.shape, jnp.float32)
+
+    grad_rows = grad_ref[...]
+
+    def step(slot, carry):
+        col = cols_ref[base * slot_count + slot]
+        total_ref[col] += lax.dot_general(
+            tiles_ref[slot], grad_rows, (((0,), (0,)), ((), ())),
+            preferred_element_type=jnp.float32,
+        )
+        return carry
+
+    lax.fori_loop(0, live, step, 0)
+
+    @pl.when(row == tile_rows - 1)
+    def _():
+        out_ref[...] = total_ref[...].astype(out_ref.dtype)
+
+
+def spread_block(block_id, cols, counts, tile_stack, grad_tiles, block_tiles, out_type):
+    blocks, tile_rows, slot_count, tile_size, _ = tile_stack.shape
+    hidden_width = grad_tiles.shape[-1]
+    grid_spec = pltpu.PrefetchScalarGridSpec(
+        num_scalar_prefetch=3,
+        grid=(tile_rows,),
+        in_specs=[
+            pl.BlockSpec(
+                (None, None, slot_count, tile_size, tile_size),
+                lambda r, b, c, n: (b[0], r, 0, 0, 0),
+            ),
+            pl.BlockSpec((None, tile_size, hidden_width), lambda r, b, c, n: (r, 0, 0)),
+        ],
+        out_specs=pl.BlockSpec(
+            (block_tiles, tile_size, hidden_width), lambda r, b, c, n: (0, 0, 0)
+        ),
+        scratch_shapes=[pltpu.VMEM((block_tiles, tile_size, hidden_width), jnp.float32)],
+    )
+    out = pl.pallas_call(
+        spread_kernel,
+        grid_spec=grid_spec,
+        out_shape=jax.ShapeDtypeStruct((block_tiles, tile_size, hidden_width), out_type),
+        compiler_params=pltpu.CompilerParams(dimension_semantics=("arbitrary",)),
+    )(
+        jnp.reshape(block_id, (1,)).astype(jnp.int32),
+        cols,
+        counts,
+        tile_stack,
+        grad_tiles,
+    )
+    return out.reshape(block_tiles * tile_size, hidden_width)
+
+
 def body(features_t, weight, tile_values, tile_col, tile_count, grad_out):
     cycle_size = lax.axis_size("blk")
     hidden_width = weight.shape[1]
@@ -58,11 +167,9 @@
     slot_count = tile_values.shape[0] // (cycle_size * tile_rows)
     feat_id = lax.axis_index("feat")
     blk_id = lax.axis_index("blk")
-    slot_index = lax.broadcasted_iota(jnp.int32, (cycle_size, tile_rows, slot_count), 2)
-    live_mask = slot_index < tile_count.reshape(cycle_size, tile_rows, 1)
     tile_stack = tile_values.reshape(cycle_size, tile_rows, slot_count, tile_size, tile_size)
-    tile_stack = jnp.where(live_mask[..., None, None], tile_stack, jnp.zeros((), jnp.bfloat16))
-    local_cols = (tile_col % block_tiles).reshape(cycle_size, tile_rows, slot_count)
+    local_cols = tile_col % block_tiles
+    counts = tile_count
     features_block = gather_rows(features_t, "feat")
     projected = lax.dot_general(
         features_block,
@@ -71,18 +178,12 @@
         preferred_element_type=jnp.float32,
     ).astype(jnp.bfloat16)
 
-    def aggregate(block_value, block_id):
-        block_tiles_view = block_value.reshape(block_tiles, tile_size, hidden_width)
-        cols_here = lax.dynamic_index_in_dim(local_cols, block_id, 0, keepdims=False)
-        tiles_here = lax.dynamic_index_in_dim(tile_stack, block_id, 0, keepdims=False)
-        picked = jnp.take(block_tiles_view, cols_here, axis=0)
-        return jnp.einsum("rsij,rsjh->rih", tiles_here, picked, preferred_element_type=jnp.float32)
-
-    aggregate_sum = aggregate(projected, blk_id)
-    moving = projected
-    for turn_index in range(cycle_size - 1):
-        moving = shifted(moving, "blk", 1)
-        aggregate_sum = aggregate_sum + aggregate(moving, (blk_id - turn_index - 1) % cycle_size)
+    aggregate_sum = aggregate_block(blk_id, local_cols, counts, tile_stack, projected)
+    for distance in range(1, cycle_size):
+        moving = shifted(projected, "blk", distance)
+        aggregate_sum = aggregate_sum + aggregate_block(
+            (blk_id - distance) % cycle_size, local_cols, counts, tile_stack, moving
+        )
     pre_act = aggregate_sum.reshape(rows_own, hidden_width)
     sigmoid_y = jax.nn.sigmoid(pre_act)
     activations = (pre_act * sigmoid_y).astype(jnp.bfloat16)
@@ -91,21 +192,17 @@
     ).astype(jnp.bfloat16)
     grad_tiles = grad_pre.reshape(tile_rows, tile_size, hidden_width)
 
-    def spread(block_id):
-        tiles_here = lax.dynamic_index_in_dim(tile_stack, block_id, 0, keepdims=False)
-        cols_here = lax.dynamic_index_in_dim(local_cols, block_id, 0, keepdims=False)
-        contrib = jnp.einsum(
-            "rsij,rih->rsjh", tiles_here, grad_tiles, preferred_element_type=jnp.float32
-        )
-        empty_block = jnp.zeros((block_tiles, tile_size, hidden_width), jnp.float32)
-        return empty_block.at[cols_here.reshape(-1)].add(
-            contrib.reshape(-1, tile_size, hidden_width)
-        ).reshape(block_rows, hidden_width)
-
-    block_total = spread(blk_id)
+    block_total = None
     for distance in range(1, cycle_size):
-        outgoing = spread((blk_id + distance) % cycle_size).astype(jnp.bfloat16)
-        block_total = block_total + shifted(outgoing, "blk", distance).astype(jnp.float32)
+        outgoing = spread_block(
+            (blk_id + distance) % cycle_size, local_cols, counts, tile_stack, grad_tiles,
+            block_tiles, jnp.bfloat16,
+        )
+        arrived = shifted(outgoing, "blk", distance).astype(jnp.float32)
+        block_total = arrived if block_total is None else block_total + arrived
+    block_total = block_total + spread_block(
+        blk_id, local_cols, counts, tile_stack, grad_tiles, block_tiles, jnp.float32
+    )
     grad_own = scatter_rows(block_total, "feat", jnp.bfloat16)
     grad_hidden = grad_own.astype(jnp.bfloat16)
 

time: 379 us -> 410 us (1.082)
  other arithmetic: 83.9 us -> 12.1 us
  waiting for transfers between devices: 195 us -> 262 us
  starting transfers between devices: 38.9 us -> 86.2 us
  Pallas kernels: 0 us -> 43.6 us
  matrix products: 31.2 us -> 2.4 us
  local copies, waits for them, and re-layouts: 28.4 us -> 1.32 us
    ppermute x6, waiting for transfers between devices: 80.6 us -> 160 us  [shifted(): return lax.ppermute(block, axis, route)]
    scatter-add x4 -> x0, other arithmetic: 54.2 us -> none  [spread(): empty_block.at[cols_here.reshape(-1)]]
    ppermute x17, starting transfers between devices: 28 us -> 73.3 us  [swapped(): return lax.ppermute(block, axis, [(i, i ^ mask) for i in range(count)])]
    pallas_call x0 -> x8, Pallas kernels: none -> 43.6 us  [the longest x4 24.1 us: spread_block(): pl.pallas_call(spread_kernel, grid_spec=grid_spec, out_shape=jax.ShapeDty...]
    dot_general x8 -> x0, matrix products: 30.1 us -> none  [the longest x4 18.1 us: spread(): jnp.einsum('rsij,rih->rsjh', tiles_here, grad_tiles, preferred_element_ty...]
    gather x4 -> x0, local copies, waits for them, and re-layouts: 14.9 us -> none  [aggregate(): picked = jnp.take(block_tiles_view, cols_here, axis=0)]
    ppermute x17, waiting for transfers between devices: 109 us -> 94.8 us  [swapped(): return lax.ppermute(block, axis, [(i, i ^ mask) for i in range(count)])]
    convert_element_type x3 -> x0, other arithmetic: 11.7 us -> none  [body(): outgoing = spread((blk_id + distance) % cycle_size).astype(jnp.bfloat16)]
  transfers between devices with their start and end apart: 24 -> 24, of which waited for: 20 -> 21; matrix products, arithmetic and copies ran while one was open for 24% -> 0% of each run, Pallas kernels for 0% -> 5%
where the time goes in v2:
time: 410 us; the launch traced here: 409 us
  waiting for transfers between devices  262 us (64%)
  starting transfers between devices  86.2 us (21%)
  Pallas kernels  43.6 us (11%)
  other arithmetic  12.1 us (3%)
    ppermute x6, waiting for transfers between devices, shifted(): return lax.ppermute(block, axis, route)  160 us
    ppermute x17, waiting for transfers between devices, swapped(): return lax.ppermute(block, axis, [(i, i ^ mask) for i in range(count)])  94.8 us
    ppermute x17, starting transfers between devices, swapped(): return lax.ppermute(block, axis, [(i, i ^ mask) for i in range(count)])  73.3 us
    pallas_call x4, Pallas kernels, spread_block(): pl.pallas_call(spread_kernel, grid_spec=grid_spec, out_shape=jax.ShapeDty...  24.1 us
    pallas_call x4, Pallas kernels, aggregate_block(): pl.pallas_call(aggregate_kernel, grid_spec=grid_spec, out_shape=jax.Shape...  19.5 us
  transfers between devices with their start and end apart: 24, of which 21 were waited for; matrix products, arithmetic and copies ran while one was open for 0% of the time, Pallas kernels for 5%

profile of v2, /device:TPU:0, one launch (start us, length us, event | category | flops | bytes accessed | tf_op | source)
XLA Modules:
  0.0 408.6 jit_solution(9214558707233962318)
XLA Ops:
  6.2 3.2 collective-permute-start.1
  9.4 3.4 collective-permute-done.1
  14.9 4.4 %collective-permute-done.2 = bf16[16,8192]{1,0:T(8,128)(2,1)S(1)} collective-permute-done((bf16[16,8192]{1,0:T(8,128)(2,1)S(1)}, bf16[16,8192]{1,0:T(8,128)(2,1)S(1)}, u32[]{:S(2)}, u32[]{:S(2)}) %collective-permute-start.2) | collective-permute-done | bytes 262176 | tf_op jit(solution)/shard_map/ppermute | solution.py:17
  19.4 5.4 %collective-permute-start.3 = (bf16[32,8192]{1,0:T(8,128)(2,1)S(1)}, bf16[32,8192]{1,0:T(8,128)(2,1)S(1)}, u32[]{:S(2)}, u32[]{:S(2)}) collective-permute-start(bf16[32,8192]{1,0:T(8,128)(2,1)S(1)} %maximum_select_fusion.2), channel_id=1, source_target_pairs={{0,8},{1,9},{2,10},{3,11},{4,12},{5,13},{6,14},{7,15},{8,0},{9,1},... | collective-permute-start | bytes 1572872 | tf_op jit(solution)/shard_map/ppermute | solution.py:17
  24.8 9.3 %collective-permute-done.3 = bf16[32,8192]{1,0:T(8,128)(2,1)S(1)} collective-permute-done((bf16[32,8192]{1,0:T(8,128)(2,1)S(1)}, bf16[32,8192]{1,0:T(8,128)(2,1)S(1)}, u32[]{:S(2)}, u32[]{:S(2)}) %collective-permute-start.3) | collective-permute-done | bytes 524320 | tf_op jit(solution)/shard_map/ppermute | solution.py:17
  35.9 20.1 %collective-permute-done.4 = bf16[64,8192]{1,0:T(8,128)(2,1)} collective-permute-done((bf16[64,8192]{1,0:T(8,128)(2,1)S(1)}, bf16[64,8192]{1,0:T(8,128)(2,1)}, u32[]{:S(2)}, u32[]{:S(2)}) %collective-permute-start.4) | collective-permute-done | bytes 1048608 | tf_op jit(solution)/shard_map/ppermute | solution.py:17
  60.3 3.2 collective-permute-start.6
  64.3 4.8 %shard_map.85 = f32[2,128,128]{2,1,0:T(8,128)} custom-call(s32[1]{0:T(128)} %bitcast.block_ref, s32[256]{0:T(256)} %and_select_fusion.cols_ref, s32[8]{0:T(128)} %count_ref.15, bf16[4,2,32,128,128]{4,3,2,1,0:T(8,128)(2,1)} %bitcast.50, bf16[64,128,128]{2,1,0:T(8,128)(2,1)} %bitcast.2.proj_ref), custom_call_target="tpu_custom_call" | custom-call | tf_op jit(solution)/shard_map/pallas_call | solution.py:84
  69.1 34.7 %collective-permute-done.7 = bf16[8192,128]{1,0:T(8,128)(2,1)} collective-permute-done((bf16[8192,128]{1,0:T(8,128)(2,1)}, bf16[8192,128]{1,0:T(8,128)(2,1)}, u32[]{:S(2)}, u32[]{:S(2)}) %collective-permute-start.7) | collective-permute-done | bytes 2097184 | tf_op jit(solution)/shard_map/ppermute | solution.py:12
  103.8 5.5 %shard_map.88 = f32[2,128,128]{2,1,0:T(8,128)} custom-call(s32[1]{0:T(128)} %bitcast.7.block_ref, s32[256]{0:T(256)} %and_select_fusion.cols_ref, s32[8]{0:T(128)} %count_ref.15, bf16[4,2,32,128,128]{4,3,2,1,0:T(8,128)(2,1)} %bitcast.51, bf16[64,128,128]{2,1,0:T(8,128)(2,1)} %bitcast.8.proj_ref), custom_call_target="tpu_custom_call" | custom-call | tf_op jit(solution)/shard_map/pallas_call | solution.py:84
  109.3 45.7 %collective-permute-done.6 = bf16[8192,128]{1,0:T(8,128)(2,1)} collective-permute-done((bf16[8192,128]{1,0:T(8,128)(2,1)}, bf16[8192,128]{1,0:T(8,128)(2,1)}, u32[]{:S(2)}, u32[]{:S(2)}) %collective-permute-start.6) | collective-permute-done | bytes 2097184 | tf_op jit(solution)/shard_map/ppermute | solution.py:12
  155.1 4.1 %shard_map.87 = f32[2,128,128]{2,1,0:T(8,128)} custom-call(s32[1]{0:T(128)} %bitcast.5.block_ref, s32[256]{0:T(256)} %and_select_fusion.cols_ref, s32[8]{0:T(128)} %count_ref.15, bf16[4,2,32,128,128]{4,3,2,1,0:T(8,128)(2,1)} %bitcast.52, bf16[64,128,128]{2,1,0:T(8,128)(2,1)} %bitcast.6.proj_ref), custom_call_target="tpu_custom_call" | custom-call | tf_op jit(solution)/shard_map/pallas_call | solution.py:84
  159.2 5.0 %shard_map.86 = f32[2,128,128]{2,1,0:T(8,128)} custom-call(s32[1]{0:T(128)} %bitcast.3.block_ref, s32[256]{0:T(256)} %and_select_fusion.cols_ref, s32[8]{0:T(128)} %count_ref.15, bf16[4,2,32,128,128]{4,3,2,1,0:T(8,128)(2,1)} %bitcast.53, bf16[64,128,128]{2,1,0:T(8,128)(2,1)} %bitcast.4.proj_ref), custom_call_target="tpu_custom_call" | custom-call | tf_op jit(solution)/shard_map/pallas_call | solution.py:84
  165.9 5.9 %shard_map.91 = bf16[64,128,128]{2,1,0:T(8,128)(2,1)} custom-call(s32[1]{0:T(128)} %bitcast.15.block_ref, s32[256]{0:T(256)} %and_select_fusion.cols_ref, s32[8]{0:T(128)} %count_ref.15, bf16[4,2,32,128,128]{4,3,2,1,0:T(8,128)(2,1)} %bitcast.54, bf16[2,128,128]{2,1,0:T(8,128)(2,1)} %bitcast.61), custom_call_target="tpu_custom_call" | custom-call | tf_op jit(solution)/shard_map/pallas_call | solution.py:144
  171.8 5.0 %shard_map.90 = bf16[64,128,128]{2,1,0:T(8,128)(2,1)} custom-call(s32[1]{0:T(128)} %bitcast.13.block_ref, s32[256]{0:T(256)} %and_select_fusion.cols_ref, s32[8]{0:T(128)} %count_ref.15, bf16[4,2,32,128,128]{4,3,2,1,0:T(8,128)(2,1)} %bitcast.55, bf16[2,128,128]{2,1,0:T(8,128)(2,1)} %bitcast.62), custom_call_target="tpu_custom_call" | custom-call | tf_op jit(solution)/shard_map/pallas_call | solution.py:144
  176.7 6.8 %shard_map.89 = bf16[64,128,128]{2,1,0:T(8,128)(2,1)} custom-call(s32[1]{0:T(128)} %bitcast.10.block_ref, s32[256]{0:T(256)} %and_select_fusion.cols_ref, s32[8]{0:T(128)} %count_ref.15, bf16[4,2,32,128,128]{4,3,2,1,0:T(8,128)(2,1)} %bitcast.56, bf16[2,128,128]{2,1,0:T(8,128)(2,1)} %bitcast.63), custom_call_target="tpu_custom_call" | custom-call | tf_op jit(solution)/shard_map/pallas_call | solution.py:144
  183.5 3.3 collective-permute-start.10
  186.7 6.5 %shard_map.92 = f32[64,128,128]{2,1,0:T(8,128)} custom-call(s32[1]{0:T(128)} %bitcast.block_ref, s32[256]{0:T(256)} %and_select_fusion.cols_ref, s32[8]{0:T(128)} %count_ref.15, bf16[4,2,32,128,128]{4,3,2,1,0:T(8,128)(2,1)} %bitcast.57, bf16[2,128,128]{2,1,0:T(8,128)(2,1)} %bitcast.64), custom_call_target="tpu_custom_call" | custom-call | tf_op jit(solution)/shard_map/pallas_call | solution.py:144
  193.3 39.4 %collective-permute-done.8 = bf16[8192,128]{1,0:T(8,128)(2,1)} collective-permute-done((bf16[8192,128]{1,0:T(8,128)(2,1)}, bf16[8192,128]{1,0:T(8,128)(2,1)}, u32[]{:S(2)}, u32[]{:S(2)}) %collective-permute-start.8) | collective-permute-done | bytes 2097184 | tf_op jit(solution)/shard_map/ppermute | solution.py:12
  233.8 39.3 %collective-permute-done.10 = bf16[8192,128]{1,0:T(8,128)(2,1)} collective-permute-done((bf16[8192,128]{1,0:T(8,128)(2,1)}, bf16[8192,128]{1,0:T(8,128)(2,1)}, u32[]{:S(2)}, u32[]{:S(2)}) %collective-permute-start.10) | collective-permute-done | bytes 2097184 | tf_op jit(solution)/shard_map/ppermute | solution.py:12
  273.1 4.8 %bitcast_add_fusion = f32[8192,128]{1,0:T(8,128)S(1)} fusion(f32[64,128,128]{2,1,0:T(8,128)} %shard_map.92, bf16[8192,128]{1,0:T(8,128)(2,1)} %collective-permute-done.10, bf16[8192,128]{1,0:T(8,128)(2,1)} %collective-permute-done.9, bf16[8192,128]{1,0:T(8,128)(2,1)} %collective-permute-done.8), kind=kLoop, calls=%fused_computation.1 | loop fusion | flops 6291456 | bytes 14680064 | tf_op jit(solution)/shard_map/add | solution.py:203
  278.4 21.8 %collective-permute-done.11 = bf16[4096,128]{1,0:T(8,128)(2,1)S(1)} collective-permute-done((bf16[4096,128]{1,0:T(8,128)(2,1)S(1)}, bf16[4096,128]{1,0:T(8,128)(2,1)S(1)}, u32[]{:S(2)}, u32[]{:S(2)}) %collective-permute-start.11) | collective-permute-done | bytes 1048608 | tf_op jit(solution)/shard_map/ppermute | solution.py:17
  300.6 28.8 %collective-permute-start.12 = (bf16[2048,128]{1,0:T(8,128)(2,1)S(1)}, bf16[2048,128]{1,0:T(8,128)(2,1)S(1)}, u32[]{:S(2)}, u32[]{:S(2)}) collective-permute-start(bf16[2048,128]{1,0:T(8,128)(2,1)S(1)} %select_convert_fusion.1), channel_id=1, source_target_pairs={{0,8},{1,9},{2,10},{3,11},{4,12},{5,13},{6,14},{7,15},{8,0},{9,1},... | collective-permute-start | bytes 1572872 | tf_op jit(solution)/shard_map/ppermute | solution.py:17
  329.4 11.1 %collective-permute-done.12 = bf16[2048,128]{1,0:T(8,128)(2,1)S(1)} collective-permute-done((bf16[2048,128]{1,0:T(8,128)(2,1)S(1)}, bf16[2048,128]{1,0:T(8,128)(2,1)S(1)}, u32[]{:S(2)}, u32[]{:S(2)}) %collective-permute-start.12) | collective-permute-done | bytes 524320 | tf_op jit(solution)/shard_map/ppermute | solution.py:17
  340.7 9.6 %collective-permute-start.13 = (bf16[1024,128]{1,0:T(8,128)(2,1)S(1)}, bf16[1024,128]{1,0:T(8,128)(2,1)S(1)}, u32[]{:S(2)}, u32[]{:S(2)}) collective-permute-start(bf16[1024,128]{1,0:T(8,128)(2,1)S(1)} %select_convert_fusion.2), channel_id=1, source_target_pairs={{0,4},{1,5},{2,6},{3,7},{4,0},{5,1},{6,2},{7,3},{8,12},{9,13},{10,... | collective-permute-start | bytes 786440 | tf_op jit(solution)/shard_map/ppermute | solution.py:17
  350.3 4.9 %collective-permute-done.13 = bf16[1024,128]{1,0:T(8,128)(2,1)S(1)} collective-permute-done((bf16[1024,128]{1,0:T(8,128)(2,1)S(1)}, bf16[1024,128]{1,0:T(8,128)(2,1)S(1)}, u32[]{:S(2)}, u32[]{:S(2)}) %collective-permute-start.13) | collective-permute-done | bytes 262176 | tf_op jit(solution)/shard_map/ppermute | solution.py:17
  355.4 6.5 %collective-permute-done.14 = bf16[512,128]{1,0:T(8,128)(2,1)S(1)} collective-permute-done((bf16[512,128]{1,0:T(8,128)(2,1)S(1)}, bf16[512,128]{1,0:T(8,128)(2,1)S(1)}, u32[]{:S(2)}, u32[]{:S(2)}) %collective-permute-start.14) | collective-permute-done | bytes 131104 | tf_op jit(solution)/shard_map/ppermute | solution.py:17
  362.0 6.7 %collective-permute-start.15 = (bf16[256,128]{1,0:T(8,128)(2,1)S(1)}, bf16[256,128]{1,0:T(8,128)(2,1)S(1)}, u32[]{:S(2)}, u32[]{:S(2)}) collective-permute-start(bf16[256,128]{1,0:T(8,128)(2,1)S(1)} %select_convert_fusion.4), channel_id=1, source_target_pairs={{0,1},{1,0},{2,3},{3,2},{4,5},{5,4},{6,7},{7,6},{8,9},{9,8},{10,11... | collective-permute-start | bytes 196616 | tf_op jit(solution)/shard_map/ppermute | solution.py:17
  375.1 4.1 %collective-permute-start.17 = (f32[32,128]{1,0:T(8,128)S(1)}, f32[32,128]{1,0:T(8,128)S(1)}, u32[]{:S(2)}, u32[]{:S(2)}) collective-permute-start(f32[32,128]{1,0:T(8,128)S(1)} %slice_select_fusion.1), channel_id=1, source_target_pairs={{0,8},{1,9},{2,10},{3,11},{4,12},{5,13},{6,14},{7,15},{8,0},{9,1},... | collective-permute-start | bytes 49160 | tf_op jit(solution)/shard_map/ppermute | solution.py:17
  384.7 4.2 %collective-permute-start.19 = (f32[8,128]{1,0:T(8,128)S(1)}, f32[8,128]{1,0:T(8,128)S(1)}, u32[]{:S(2)}, u32[]{:S(2)}) collective-permute-start(f32[8,128]{1,0:T(8,128)S(1)} %slice_select_fusion.3), channel_id=1, source_target_pairs={{0,2},{1,3},{2,0},{3,1},{4,6},{5,7},{6,4},{7,5},{8,10},{9,11},{10,... | collective-permute-start | bytes 12296 | tf_op jit(solution)/shard_map/ppermute | solution.py:17
  392.8 6.2 %all-to-all-start = ((bf16[32,4,256]{2,1,0:T(4,128)(2,1)}), bf16[32,4,256]{2,1,0:T(4,128)(2,1)S(1)}, u32[]{:S(2)}, u32[]{:S(2)}) async-start(bf16[32,4,256]{2,1,0:T(4,128)(2,1)} %all_to_all.14), calls=%async_computation | async-start | bytes 131072 | tf_op jit(solution)/shard_map/all_to_all | solution.py:219
  400.3 7.1 %all-to-all-done = bf16[32,4,256]{2,1,0:T(4,128)(2,1)S(1)} async-done(((bf16[32,4,256]{2,1,0:T(4,128)(2,1)}), bf16[32,4,256]{2,1,0:T(4,128)(2,1)S(1)}, u32[]{:S(2)}, u32[]{:S(2)}) %all-to-all-start) | async-done | bytes 65568 | tf_op jit(solution)/shard_map/all_to_all | solution.py:219
  (72 shorter events, 37.1 us)
Async XLA Ops:
  0.6 57.5 %copy-start = (bf16[128,128]{1,0:T(8,128)(2,1)S(1)}, bf16[128,128]{1,0:T(8,128)(2,1)}, u32[]{:S(2)}) copy-start(bf16[128,128]{1,0:T(8,128)(2,1)} %param.7) | copy-start | bytes 98308
  0.6 4.6 %collective-permute-start = (bf16[4,8192]{1,0:T(4,128)(2,1)}, bf16[4,8192]{1,0:T(4,128)(2,1)S(1)}, u32[]{:S(2)}, u32[]{:S(2)}) collective-permute-start(bf16[4,8192]{1,0:T(4,128)(2,1)} %param.6), channel_id=1, source_target_pairs={{0,1},{1,0},{2,3},{3,2},{4,5},{5,4},{6,7},{7,6},{8,9},{9,8},{10,11... | collective-permute-start | bytes 196616 | tf_op jit(solution)/shard_map/ppermute | solution.py:17
  6.2 6.6 %collective-permute-start.1 = (bf16[8,8192]{1,0:T(8,128)(2,1)S(1)}, bf16[8,8192]{1,0:T(8,128)(2,1)S(1)}, u32[]{:S(2)}, u32[]{:S(2)}) collective-permute-start(bf16[8,8192]{1,0:T(8,128)(2,1)S(1)} %maximum_select_fusion.4), channel_id=1, source_target_pairs={{0,2},{1,3},{2,0},{3,1},{4,6},{5,7},{6,4},{7,5},{8,10},{9,11},{10,... | collective-permute-start | bytes 393224 | tf_op jit(solution)/shard_map/ppermute | solution.py:17
  12.8 6.5 %collective-permute-start.2 = (bf16[16,8192]{1,0:T(8,128)(2,1)S(1)}, bf16[16,8192]{1,0:T(8,128)(2,1)S(1)}, u32[]{:S(2)}, u32[]{:S(2)}) collective-permute-start(bf16[16,8192]{1,0:T(8,128)(2,1)S(1)} %maximum_select_fusion.3), channel_id=1, source_target_pairs={{0,4},{1,5},{2,6},{3,7},{4,0},{5,1},{6,2},{7,3},{8,12},{9,13},{10,... | collective-permute-start | bytes 786440 | tf_op jit(solution)/shard_map/ppermute | solution.py:17
  19.4 14.7 %collective-permute-start.3 = (bf16[32,8192]{1,0:T(8,128)(2,1)S(1)}, bf16[32,8192]{1,0:T(8,128)(2,1)S(1)}, u32[]{:S(2)}, u32[]{:S(2)}) collective-permute-start(bf16[32,8192]{1,0:T(8,128)(2,1)S(1)} %maximum_select_fusion.2), channel_id=1, source_target_pairs={{0,8},{1,9},{2,10},{3,11},{4,12},{5,13},{6,14},{7,15},{8,0},{9,1},... | collective-permute-start | bytes 1572872 | tf_op jit(solution)/shard_map/ppermute | solution.py:17
  34.3 21.8 %collective-permute-start.4 = (bf16[64,8192]{1,0:T(8,128)(2,1)S(1)}, bf16[64,8192]{1,0:T(8,128)(2,1)}, u32[]{:S(2)}, u32[]{:S(2)}) collective-permute-start(bf16[64,8192]{1,0:T(8,128)(2,1)S(1)} %maximum_select_fusion.1), channel_id=1, source_target_pairs={{0,16},{1,17},{2,18},{3,19},{4,20},{5,21},{6,22},{7,23},{8,24},{9,... | collective-permute-start | bytes 3145736 | tf_op jit(solution)/shard_map/ppermute | solution.py:17
  58.1 5.5 %copy-start.5 = (s32[256]{0:T(256)S(1)}, s32[256]{0:T(256)}, u32[]{:S(2)}) copy-start(s32[256]{0:T(256)} %param.9) | copy-start | bytes 3076
  60.3 43.5 %collective-permute-start.7 = (bf16[8192,128]{1,0:T(8,128)(2,1)}, bf16[8192,128]{1,0:T(8,128)(2,1)}, u32[]{:S(2)}, u32[]{:S(2)}) collective-permute-start(bf16[8192,128]{1,0:T(8,128)(2,1)} %convolution_convert_fusion), channel_id=1, source_target_pairs={{32,0},{64,32},{96,64},{0,96},{33,1},{65,33},{97,65},{1,97},{34,2}... | collective-permute-start | bytes 6291464 | tf_op jit(solution)/shard_map/ppermute | solution.py:12
  60.3 94.8 %collective-permute-start.6 = (bf16[8192,128]{1,0:T(8,128)(2,1)}, bf16[8192,128]{1,0:T(8,128)(2,1)}, u32[]{:S(2)}, u32[]{:S(2)}) collective-permute-start(bf16[8192,128]{1,0:T(8,128)(2,1)} %convolution_convert_fusion), channel_id=1, source_target_pairs={{64,0},{96,32},{0,64},{32,96},{65,1},{97,33},{1,65},{33,97},{66,2}... | collective-permute-start | bytes 6291464 | tf_op jit(solution)/shard_map/ppermute | solution.py:12
  63.4 95.8 %collective-permute-start.5 = (bf16[8192,128]{1,0:T(8,128)(2,1)}, bf16[8192,128]{1,0:T(8,128)(2,1)}, u32[]{:S(2)}, u32[]{:S(2)}) collective-permute-start(bf16[8192,128]{1,0:T(8,128)(2,1)} %convolution_convert_fusion), channel_id=1, source_target_pairs={{96,0},{0,32},{32,64},{64,96},{97,1},{1,33},{33,65},{65,97},{98,2}... | collective-permute-start | bytes 6291464 | tf_op jit(solution)/shard_map/ppermute | solution.py:12
  159.2 5.0 %copy-start.1 = (f32[2,128,128]{2,1,0:T(8,128)S(1)}, f32[2,128,128]{2,1,0:T(8,128)}, u32[]{:S(2)}) copy-start(f32[2,128,128]{2,1,0:T(8,128)} %shard_map.85) | copy-start | bytes 393220
  159.2 5.0 %copy-start.2 = (f32[2,128,128]{2,1,0:T(8,128)S(1)}, f32[2,128,128]{2,1,0:T(8,128)}, u32[]{:S(2)}) copy-start(f32[2,128,128]{2,1,0:T(8,128)} %shard_map.88) | copy-start | bytes 393220
  159.2 5.0 %copy-start.3 = (f32[2,128,128]{2,1,0:T(8,128)S(1)}, f32[2,128,128]{2,1,0:T(8,128)}, u32[]{:S(2)}) copy-start(f32[2,128,128]{2,1,0:T(8,128)} %shard_map.87) | copy-start | bytes 393220
  159.2 5.9 %copy-start.4 = (bf16[256,128]{1,0:T(8,128)(2,1)S(1)}, bf16[256,128]{1,0:T(8,128)(2,1)}, u32[]{:S(2)}) copy-start(bf16[256,128]{1,0:T(8,128)(2,1)} %param.11) | copy-start | bytes 196612
  183.5 49.2 %collective-permute-start.8 = (bf16[8192,128]{1,0:T(8,128)(2,1)}, bf16[8192,128]{1,0:T(8,128)(2,1)}, u32[]{:S(2)}, u32[]{:S(2)}) collective-permute-start(bf16[8192,128]{1,0:T(8,128)(2,1)} %bitcast.60), channel_id=1, source_target_pairs={{96,0},{0,32},{32,64},{64,96},{97,1},{1,33},{33,65},{65,97},{98,2}... | collective-permute-start | bytes 6291464 | tf_op jit(solution)/shard_map/ppermute | solution.py:12
  183.5 50.3 %collective-permute-start.9 = (bf16[8192,128]{1,0:T(8,128)(2,1)}, bf16[8192,128]{1,0:T(8,128)(2,1)}, u32[]{:S(2)}, u32[]{:S(2)}) collective-permute-start(bf16[8192,128]{1,0:T(8,128)(2,1)} %bitcast.59), channel_id=1, source_target_pairs={{64,0},{96,32},{0,64},{32,96},{65,1},{97,33},{1,65},{33,97},{66,2}... | collective-permute-start | bytes 6291464 | tf_op jit(solution)/shard_map/ppermute | solution.py:12
  183.5 89.6 %collective-permute-start.10 = (bf16[8192,128]{1,0:T(8,128)(2,1)}, bf16[8192,128]{1,0:T(8,128)(2,1)}, u32[]{:S(2)}, u32[]{:S(2)}) collective-permute-start(bf16[8192,128]{1,0:T(8,128)(2,1)} %bitcast.58), channel_id=1, source_target_pairs={{32,0},{64,32},{96,64},{0,96},{33,1},{65,33},{97,65},{1,97},{34,2}... | collective-permute-start | bytes 6291464 | tf_op jit(solution)/shard_map/ppermute | solution.py:12
  278.1 22.1 %collective-permute-start.11 = (bf16[4096,128]{1,0:T(8,128)(2,1)S(1)}, bf16[4096,128]{1,0:T(8,128)(2,1)S(1)}, u32[]{:S(2)}, u32[]{:S(2)}) collective-permute-start(bf16[4096,128]{1,0:T(8,128)(2,1)S(1)} %select_convert_fusion), channel_id=1, source_target_pairs={{0,16},{1,17},{2,18},{3,19},{4,20},{5,21},{6,22},{7,23},{8,24},{9,... | collective-permute-start | bytes 3145736 | tf_op jit(solution)/shard_map/ppermute | solution.py:17
  300.6 39.9 %collective-permute-start.12 = (bf16[2048,128]{1,0:T(8,128)(2,1)S(1)}, bf16[2048,128]{1,0:T(8,128)(2,1)S(1)}, u32[]{:S(2)}, u32[]{:S(2)}) collective-permute-start(bf16[2048,128]{1,0:T(8,128)(2,1)S(1)} %select_convert_fusion.1), channel_id=1, source_target_pairs={{0,8},{1,9},{2,10},{3,11},{4,12},{5,13},{6,14},{7,15},{8,0},{9,1},... | collective-permute-start | bytes 1572872 | tf_op jit(solution)/shard_map/ppermute | solution.py:17
  340.7 14.5 %collective-permute-start.13 = (bf16[1024,128]{1,0:T(8,128)(2,1)S(1)}, bf16[1024,128]{1,0:T(8,128)(2,1)S(1)}, u32[]{:S(2)}, u32[]{:S(2)}) collective-permute-start(bf16[1024,128]{1,0:T(8,128)(2,1)S(1)} %select_convert_fusion.2), channel_id=1, source_target_pairs={{0,4},{1,5},{2,6},{3,7},{4,0},{5,1},{6,2},{7,3},{8,12},{9,13},{10,... | collective-permute-start | bytes 786440 | tf_op jit(solution)/shard_map/ppermute | solution.py:17
  355.3 6.6 %collective-permute-start.14 = (bf16[512,128]{1,0:T(8,128)(2,1)S(1)}, bf16[512,128]{1,0:T(8,128)(2,1)S(1)}, u32[]{:S(2)}, u32[]{:S(2)}) collective-permute-start(bf16[512,128]{1,0:T(8,128)(2,1)S(1)} %select_convert_fusion.3), channel_id=1, source_target_pairs={{0,2},{1,3},{2,0},{3,1},{4,6},{5,7},{6,4},{7,5},{8,10},{9,11},{10,... | collective-permute-start | bytes 393224 | tf_op jit(solution)/shard_map/ppermute | solution.py:17
  362.0 8.9 %collective-permute-start.15 = (bf16[256,128]{1,0:T(8,128)(2,1)S(1)}, bf16[256,128]{1,0:T(8,128)(2,1)S(1)}, u32[]{:S(2)}, u32[]{:S(2)}) collective-permute-start(bf16[256,128]{1,0:T(8,128)(2,1)S(1)} %select_convert_fusion.4), channel_id=1, source_target_pairs={{0,1},{1,0},{2,3},{3,2},{4,5},{5,4},{6,7},{7,6},{8,9},{9,8},{10,11... | collective-permute-start | bytes 196616 | tf_op jit(solution)/shard_map/ppermute | solution.py:17
  371.1 4.0 collective-permute-start.16
  375.1 5.8 %collective-permute-start.17 = (f32[32,128]{1,0:T(8,128)S(1)}, f32[32,128]{1,0:T(8,128)S(1)}, u32[]{:S(2)}, u32[]{:S(2)}) collective-permute-start(f32[32,128]{1,0:T(8,128)S(1)} %slice_select_fusion.1), channel_id=1, source_target_pairs={{0,8},{1,9},{2,10},{3,11},{4,12},{5,13},{6,14},{7,15},{8,0},{9,1},... | collective-permute-start | bytes 49160 | tf_op jit(solution)/shard_map/ppermute | solution.py:17
  381.0 3.7 collective-permute-start.18
  384.7 5.7 %collective-permute-start.19 = (f32[8,128]{1,0:T(8,128)S(1)}, f32[8,128]{1,0:T(8,128)S(1)}, u32[]{:S(2)}, u32[]{:S(2)}) collective-permute-start(f32[8,128]{1,0:T(8,128)S(1)} %slice_select_fusion.3), channel_id=1, source_target_pairs={{0,2},{1,3},{2,0},{3,1},{4,6},{5,7},{6,4},{7,5},{8,10},{9,11},{10,... | collective-permute-start | bytes 12296 | tf_op jit(solution)/shard_map/ppermute | solution.py:17
  390.5 8.6 %collective-permute-start.20 = (f32[4,128]{1,0:T(4,128)S(1)}, f32[4,128]{1,0:T(4,128)S(1)}, u32[]{:S(2)}, u32[]{:S(2)}) collective-permute-start(f32[4,128]{1,0:T(4,128)S(1)} %slice_select_fusion.4), channel_id=1, source_target_pairs={{0,1},{1,0},{2,3},{3,2},{4,5},{5,4},{6,7},{7,6},{8,9},{9,8},{10,11... | collective-permute-start | bytes 6152 | tf_op jit(solution)/shard_map/ppermute | solution.py:17
  392.8 14.6 %all-to-all-start = ((bf16[32,4,256]{2,1,0:T(4,128)(2,1)}), bf16[32,4,256]{2,1,0:T(4,128)(2,1)S(1)}, u32[]{:S(2)}, u32[]{:S(2)}) async-start(bf16[32,4,256]{2,1,0:T(4,128)(2,1)} %all_to_all.14), calls=%async_computation | async-start | bytes 131072 | tf_op jit(solution)/shard_map/all_to_all | solution.py:219
  399.1 1.2 collective-permute-start.21
  400.3 7.1 %collective-permute-start.22 = (f32[4,128]{1,0:T(4,128)S(1)}, f32[4,128]{1,0:T(4,128)S(1)}, u32[]{:S(2)}, u32[]{:S(2)}) collective-permute-start(f32[4,128]{1,0:T(4,128)S(1)} %add.164), channel_id=1, source_target_pairs={{0,64},{32,96},{64,0},{96,32},{1,65},{33,97},{65,1},{97,33},{2,66}... | collective-permute-start | bytes 6152 | tf_op jit(solution)/shard_map/ppermute | solution.py:17

commit v3 on v2

v3 whole, which is shorter than its diff:
```python
import jax
import jax.numpy as jnp
from jax import lax
from jax.sharding import PartitionSpec as P
from jax.experimental import pallas as pl
from jax.experimental.pallas import tpu as pltpu

RING = 4
GATHER_ORDER = (("x", "z", "y"), ("y", "z", "x"))
BOTH = ("blk", "feat")


def place_of(blk, feat):
    return {
        "core": blk % 2,
        "y": (blk // 2) * 2 + feat // 16,
        "z": (feat // 4) % 4,
        "x": feat % 4,
    }


def linear_of(place):
    blk = (place["y"] // 2) * 2 + place["core"]
    feat = (place["y"] % 2) * 16 + place["z"] * 4 + place["x"]
    return blk * 32 + feat


def ring_shift(block, phase, distance):
    route = []
    for blk in range(4):
        for feat in range(32):
            place = place_of(blk, feat)
            axis = GATHER_ORDER[place["core"]][phase]
            target = dict(place)
            target[axis] = (place[axis] + distance) % RING
            route.append((linear_of(place), linear_of(target)))
    return lax.ppermute(block, BOTH, route)


def sibling(block):
    return lax.ppermute(block, "blk", [(i, i ^ 1) for i in range(lax.axis_size("blk"))])


def swapped(block, axis, mask):
    count = lax.axis_size(axis)
    return lax.ppermute(block, axis, [(i, i ^ mask) for i in range(count)])


def gather_phase(block, phase):
    half = block.shape[-2] // 2
    from_minus = ring_shift(block, phase, 1)
    from_plus = ring_shift(block, phase, -1)
    far_low = ring_shift(from_minus[..., :half, :], phase, 1)
    far_high = ring_shift(from_plus[..., half:, :], phase, -1)
    far = jnp.concatenate([far_low, far_high], axis=-2)
    return jnp.stack([block, from_plus, far, from_minus])


def reduce_phase(total, phase, wire_type):
    half = total.shape[-2] // 2
    far = total[2]
    got_minus = ring_shift(far[..., :half, :].astype(wire_type), phase, 1)
    got_plus = ring_shift(far[..., half:, :].astype(wire_type), phase, -1)
    ahead = total[1]
    ahead = jnp.concatenate(
        [ahead[..., :half, :] + got_minus.astype(jnp.float32), ahead[..., half:, :]], axis=-2
    )
    behind = total[3]
    behind = jnp.concatenate(
        [behind[..., :half, :], behind[..., half:, :] + got_plus.astype(jnp.float32)], axis=-2
    )
    from_minus = ring_shift(ahead.astype(wire_type), phase, 1)
    from_plus = ring_shift(behind.astype(wire_type), phase, -1)
    return total[0] + from_minus.astype(jnp.float32) + from_plus.astype(jnp.float32)


def scatter_rows(total, axis, wire_type):
    count = lax.axis_size(axis)
    index = lax.axis_index(axis)
    mask = count // 2
    while mask >= 1:
        half = total.shape[0] // 2
        lower, upper_part = total[:half], total[half:]
        upper = (index // mask) % 2 == 1
        keep = jnp.where(upper, upper_part, lower)
        send = jnp.where(upper, lower, upper_part)
        got = swapped(send.astype(wire_type), axis, mask)
        total = keep + got.astype(jnp.float32)
        mask //= 2
    return total


def aggregate_kernel(core_ref, where_ref, count_ref, tiles_ref, proj_ref, out_ref):
    row = pl.program_id(0)
    half_id = pl.program_id(1)
    tile_rows = pl.num_programs(0)
    slot_count = tiles_ref.shape[0]
    base = (half_id * 2 + core_ref[0]) * tile_rows + row
    live = count_ref[base]

    def step(slot, total):
        spot = where_ref[base * slot_count + slot]
        return total + jnp.dot(tiles_ref[slot], proj_ref[spot], preferred_element_type=jnp.float32)

    part = lax.fori_loop(0, live, step, jnp.zeros(out_ref.shape, jnp.float32))

    @pl.when(half_id == 0)
    def _():
        out_ref[...] = part

    @pl.when(half_id != 0)
    def _():
        out_ref[...] += part


def aggregate_pair(core_id, spots, counts, tile_stack, buffer):
    blocks, tile_rows, slot_count, tile_size, _ = tile_stack.shape
    hidden_width = buffer.shape[-1]
    grid_spec = pltpu.PrefetchScalarGridSpec(
        num_scalar_prefetch=3,
        grid=(tile_rows, blocks // 2),
        in_specs=[
            pl.BlockSpec(
                (None, None, slot_count, tile_size, tile_size),
                lambda r, h, c, w, n: (h * 2 + c[0], r, 0, 0, 0),
            ),
            pl.BlockSpec(buffer.shape, lambda r, h, c, w, n: (0, 0, 0)),
        ],
        out_specs=pl.BlockSpec((None, tile_size, hidden_width), lambda r, h, c, w, n: (r, 0, 0)),
    )
    return pl.pallas_call(
        aggregate_kernel,
        grid_spec=grid_spec,
        out_shape=jax.ShapeDtypeStruct((tile_rows, tile_size, hidden_width), jnp.float32),
        compiler_params=pltpu.CompilerParams(dimension_semantics=("arbitrary", "arbitrary")),
    )(jnp.reshape(core_id, (1,)).astype(jnp.int32), spots, counts, tile_stack, buffer)


def spread_kernel(core_ref, where_ref, count_ref, tiles_ref, grad_ref, out_ref, total_ref):
    row = pl.program_id(0)
    half_id = pl.program_id(1)
    tile_rows = pl.num_programs(0)
    halves = pl.num_programs(1)
    slot_count = tiles_ref.shape[0]
    base = (half_id * 2 + core_ref[0]) * tile_rows + row
    live = count_ref[base]

    @pl.when((row == 0) & (half_id == 0))
    def _():
        total_ref[...] = jnp.zeros(total_ref.shape, jnp.float32)

    grad_rows = grad_ref[...]

    def step(slot, carry):
        spot = where_ref[base * slot_count + slot]
        total_ref[spot] += lax.dot_general(
            tiles_ref[slot], grad_rows, (((0,), (0,)), ((), ())),
            preferred_element_type=jnp.float32,
        )
        return carry

    lax.fori_loop(0, live, step, 0)

    @pl.when((row == tile_rows - 1) & (half_id == halves - 1))
    def _():
        out_ref[...] = total_ref[...].astype(out_ref.dtype)


def spread_pair(core_id, spots, counts, tile_stack, grad_tiles, buffer_tiles, out_type):
    blocks, tile_rows, slot_count, tile_size, _ = tile_stack.shape
    hidden_width = grad_tiles.shape[-1]
    grid_spec = pltpu.PrefetchScalarGridSpec(
        num_scalar_prefetch=3,
        grid=(tile_rows, blocks // 2),
        in_specs=[
            pl.BlockSpec(
                (None, None, slot_count, tile_size, tile_size),
                lambda r, h, c, w, n: (h * 2 + c[0], r, 0, 0, 0),
            ),
            pl.BlockSpec((None, tile_size, hidden_width), lambda r, h, c, w, n: (r, 0, 0)),
        ],
        out_specs=pl.BlockSpec(
            (buffer_tiles, tile_size, hidden_width), lambda r, h, c, w, n: (0, 0, 0)
        ),
        scratch_shapes=[pltpu.VMEM((buffer_tiles, tile_size, hidden_width), jnp.float32)],
    )
    return pl.pallas_call(
        spread_kernel,
        grid_spec=grid_spec,
        out_shape=jax.ShapeDtypeStruct((buffer_tiles, tile_size, hidden_width), out_type),
        compiler_params=pltpu.CompilerParams(dimension_semantics=("arbitrary", "arbitrary")),
    )(jnp.reshape(core_id, (1,)).astype(jnp.int32), spots, counts, tile_stack, grad_tiles)


def buffer_spots(tile_col, blk_id, feat_id, block_tiles, tiles_per_device):
    own = place_of(blk_id, feat_id)
    block = tile_col // block_tiles
    local = tile_col % block_tiles
    source_feat = local // tiles_per_device
    part = local % tiles_per_device
    source = place_of(block, source_feat)
    rel = {axis: (source[axis] - own[axis]) % RING for axis in ("y", "z", "x")}
    chunk = jnp.where(
        source["core"] == 0,
        rel["y"] * 16 + rel["z"] * 4 + rel["x"],
        rel["x"] * 16 + rel["z"] * 4 + rel["y"],
    )
    return (chunk * tiles_per_device + part).astype(jnp.int32)


def body(features_t, weight, tile_values, tile_col, tile_count, grad_out):
    cycle_size = lax.axis_size("blk")
    hidden_width = weight.shape[1]
    tile_size = tile_values.shape[1]
    rows_own = grad_out.shape[0]
    tile_rows = rows_own // tile_size
    block_rows = features_t.shape[1]
    block_tiles = block_rows // tile_size
    slot_count = tile_values.shape[0] // (cycle_size * tile_rows)
    feat_id = lax.axis_index("feat")
    blk_id = lax.axis_index("blk")
    core_id = blk_id % 2
    tile_stack = tile_values.reshape(cycle_size, tile_rows, slot_count, tile_size, tile_size)
    spots = buffer_spots(tile_col, blk_id, feat_id, block_tiles, tile_rows)
    buffer_tiles = block_tiles * 2

    features_own = lax.all_to_all(features_t, "feat", split_axis=1, concat_axis=0, tiled=True)
    projected = lax.dot_general(
        features_own, weight, (((0,), (0,)), ((), ())), preferred_element_type=jnp.float32
    ).astype(jnp.bfloat16)

    gathered = projected
    for phase in range(3):
        gathered = gather_phase(gathered, phase)
    own_buffer = gathered.reshape(buffer_tiles, tile_size, hidden_width)
    other_buffer = sibling(own_buffer)
    aggregate_sum = aggregate_pair(core_id, spots, tile_count, tile_stack, own_buffer)
    aggregate_sum = aggregate_sum + aggregate_pair(
        1 - core_id, spots, tile_count, tile_stack, other_buffer
    )

    pre_act = aggregate_sum.reshape(rows_own, hidden_width)
    sigmoid_y = jax.nn.sigmoid(pre_act)
    activations = (pre_act * sigmoid_y).astype(jnp.bfloat16)
    grad_pre = (
        grad_out.astype(jnp.float32) * sigmoid_y * (1.0 + pre_act * (1.0 - sigmoid_y))
    ).astype(jnp.bfloat16)
    grad_tiles = grad_pre.reshape(tile_rows, tile_size, hidden_width)

    outgoing = spread_pair(
        1 - core_id, spots, tile_count, tile_stack, grad_tiles, buffer_tiles, jnp.bfloat16
    )
    arrived = sibling(outgoing)
    total = spread_pair(
        core_id, spots, tile_count, tile_stack, grad_tiles, buffer_tiles, jnp.float32
    )
    total = total + arrived.astype(jnp.float32)
    total = total.reshape(RING, RING, RING, rows_own, hidden_width)
    for phase in (2, 1, 0):
        total = reduce_phase(total, phase, jnp.bfloat16)
    grad_hidden = total.astype(jnp.bfloat16)

    weight_term = jnp.dot(features_own, grad_hidden, preferred_element_type=jnp.float32)
    weight_part = scatter_rows(weight_term, "feat", jnp.float32)
    weight_part = weight_part + swapped(weight_part, "blk", 1)
    weight_part = weight_part + swapped(weight_part, "blk", 2)
    grad_weight = weight_part * lax.rsqrt(jnp.float32(block_rows * cycle_size))

    features_grad_local = lax.dot_general(
        weight, grad_hidden, (((1,), (1,)), ((), ())), preferred_element_type=jnp.float32
    ).astype(jnp.bfloat16)
    grad_features = lax.all_to_all(
        features_grad_local, "feat", split_axis=0, concat_axis=1, tiled=True
    )
    return (activations, grad_features, grad_weight)


def solution(mesh):
    placed = (
        P("feat", "blk"),
        P(),
        P(("blk", "feat"), None, None),
        P(("blk", "feat")),
        P(("blk", "feat")),
        P(("blk", "feat"), None),
    )
    return jax.shard_map(
        body,
        mesh=mesh,
        in_specs=placed,
        out_specs=(P(("blk", "feat"), None), P("feat", "blk"), P("feat", None)),
        check_vma=False,
    )
```

time: 410 us -> 264 us (0.64)
  waiting for transfers between devices: 262 us -> 101 us
  blocking collectives: 0 us -> 17.6 us
  Pallas kernels: 43.6 us -> 34.9 us
  starting transfers between devices: 86.2 us -> 92.2 us
    ppermute x6 -> x26, waiting for transfers between devices: 160 us -> 78.9 us  [the longest x24 78.9 us: ring_shift(): return lax.ppermute(block, BOTH, route)]
    ppermute x6 -> x26, starting transfers between devices: 6.71 us -> 84.4 us  [the longest x24 84.4 us: ring_shift(): return lax.ppermute(block, BOTH, route)]
    ppermute x17 -> x7, waiting for transfers between devices: 94.8 us -> 18.9 us  [swapped(): return lax.ppermute(block, axis, [(i, i ^ mask) for i in range(count)])]
    ppermute x17 -> x7, starting transfers between devices: 73.3 us -> 3.92 us  [swapped(): return lax.ppermute(block, axis, [(i, i ^ mask) for i in range(count)])]
    all_to_all x0 -> x1, blocking collectives: none -> 17.6 us  [body(): lax.all_to_all(features_t, 'feat', split_axis=1, concat_axis=0, tiled=True)]
    pallas_call x8 -> x4, Pallas kernels: 43.6 us -> 34.9 us  [the longest x2 19.8 us: spread_pair(): pl.pallas_call(spread_kernel, grid_spec=grid_spec, out_shape=jax.ShapeDty...]
  transfers between devices with their start and end apart: 24 -> 34, of which waited for: 21 -> 24; matrix products, arithmetic and copies ran while one was open for 0% -> 1% of each run, Pallas kernels for 5% -> 7%
where the time goes in v3:
time: 264 us; the launch traced here: 263 us
  waiting for transfers between devices  101 us (38%)
  starting transfers between devices  92.2 us (35%)
  Pallas kernels  34.9 us (13%)
  blocking collectives  17.6 us (7%)
  other arithmetic  12.4 us (5%)
    ppermute x24, starting transfers between devices, ring_shift(): return lax.ppermute(block, BOTH, route)  84.4 us
    ppermute x24, waiting for transfers between devices, ring_shift(): return lax.ppermute(block, BOTH, route)  78.9 us
    pallas_call x2, Pallas kernels, spread_pair(): pl.pallas_call(spread_kernel, grid_spec=grid_spec, out_shape=jax.ShapeDty...  19.8 us
    ppermute x7, waiting for transfers between devices, swapped(): return lax.ppermute(block, axis, [(i, i ^ mask) for i in range(count)])  18.9 us
    all_to_all x1, blocking collectives, body(): lax.all_to_all(features_t, 'feat', split_axis=1, concat_axis=0, tiled=True)  17.6 us
    pallas_call x2, Pallas kernels, aggregate_pair(): pl.pallas_call(aggregate_kernel, grid_spec=grid_spec, out_shape=jax.Shape...  15.1 us
    add x1, other arithmetic, body(): total = total + arrived.astype(jnp.float32)  5.84 us
  transfers between devices with their start and end apart: 34, of which 24 were waited for; matrix products, arithmetic and copies ran while one was open for 1% of the time, Pallas kernels for 7%

profile of v3, /device:TPU:0, one launch (start us, length us, event | category | flops | bytes accessed | tf_op | source)
XLA Modules:
  0.0 262.9 jit_solution(18274032163594818419)
XLA Ops:
  0.6 17.6 %all_to_all.38 = bf16[4,32,256]{2,0,1:T(4,128)(2,1)S(1)} all-to-all(bf16[4,32,256]{2,0,1:T(4,128)(2,1)} %bitcast.125), channel_id=1, replica_groups=mesh['blk'=4,'feat'=32] {'feat'}, dimensions={1} | all-to-all | bytes 131072 | tf_op jit(solution)/shard_map/all_to_all | solution.py:227
  19.1 2.7 %collective-permute-start = (bf16[256,128]{1,0:T(8,128)(2,1)S(1)}, bf16[256,128]{1,0:T(8,128)(2,1)S(1)}, u32[]{:S(2)}, u32[]{:S(2)}) collective-permute-start(bf16[256,128]{1,0:T(8,128)(2,1)S(1)} %convolution_convert_fusion.1), channel_id=1, source_target_pairs={{0,3},{1,0},{2,1},{3,2},{4,7},{5,4},{6,5},{7,6},{8,11},{9,8},{10,9... | collective-permute-start | bytes 196616 | tf_op jit(solution)/shard_map/ppermute | solution.py:37
  24.0 3.2 %collective-permute-start.3 = (bf16[128,128]{1,0:T(8,128)(2,1)S(1)}, bf16[128,128]{1,0:T(8,128)(2,1)S(1)}, u32[]{:S(2)}, u32[]{:S(2)}) collective-permute-start(bf16[128,128]{1,0:T(8,128)(2,1)S(1)} %slice.216), channel_id=1, source_target_pairs={{0,3},{1,0},{2,1},{3,2},{4,7},{5,4},{6,5},{7,6},{8,11},{9,8},{10,9... | collective-permute-start | bytes 98312 | tf_op jit(solution)/shard_map/ppermute | solution.py:37
  31.3 5.8 %collective-permute-done.4 = bf16[4,256,128]{2,1,0:T(8,128)(2,1)S(1)} collective-permute-done((bf16[4,256,128]{2,1,0:T(8,128)(2,1)S(1)}, bf16[4,256,128]{2,1,0:T(8,128)(2,1)S(1)}, u32[]{:S(2)}, u32[]{:S(2)}) %collective-permute-start.4) | collective-permute-done | bytes 262176 | tf_op jit(solution)/shard_map/ppermute | solution.py:37
  42.1 3.5 %collective-permute-done.6 = bf16[4,128,128]{2,1,0:T(8,128)(2,1)S(1)} collective-permute-done((bf16[4,128,128]{2,1,0:T(8,128)(2,1)S(1)}, bf16[4,128,128]{2,1,0:T(8,128)(2,1)S(1)}, u32[]{:S(2)}, u32[]{:S(2)}) %collective-permute-start.6) | collective-permute-done | bytes 131104 | tf_op jit(solution)/shard_map/ppermute | solution.py:37
  47.9 12.8 %collective-permute-done.8 = bf16[4,4,256,128]{3,2,1,0:T(8,128)(2,1)S(1)} collective-permute-done((bf16[4,4,256,128]{3,2,1,0:T(8,128)(2,1)S(1)}, bf16[4,4,256,128]{3,2,1,0:T(8,128)(2,1)S(1)}, u32[]{:S(2)}, u32[]{:S(2)}) %collective-permute-start.8) | collective-permute-done | bytes 1048608 | tf_op jit(solution)/shard_map/ppermute | solution.py:37
  63.1 6.8 %collective-permute-done.11 = bf16[4,4,128,128]{3,2,1,0:T(8,128)(2,1)S(1)} collective-permute-done((bf16[4,4,128,128]{3,2,1,0:T(8,128)(2,1)S(1)}, bf16[4,4,128,128]{3,2,1,0:T(8,128)(2,1)S(1)}, u32[]{:S(2)}, u32[]{:S(2)}) %collective-permute-start.11) | collective-permute-done | bytes 524320 | tf_op jit(solution)/shard_map/ppermute | solution.py:37
  70.0 3.5 %collective-permute-done.10 = bf16[4,4,128,128]{3,2,1,0:T(8,128)(2,1)S(1)} collective-permute-done((bf16[4,4,128,128]{3,2,1,0:T(8,128)(2,1)S(1)}, bf16[4,4,128,128]{3,2,1,0:T(8,128)(2,1)S(1)}, u32[]{:S(2)}, u32[]{:S(2)}) %collective-permute-start.10) | collective-permute-done | bytes 524320 | tf_op jit(solution)/shard_map/ppermute | solution.py:37
  76.6 7.6 %shard_map.85 = f32[2,128,128]{2,1,0:T(8,128)} custom-call(s32[1]{0:T(128)} %bitcast.core_ref, s32[256]{0:T(256)} %fusion.25.where_ref, s32[8]{0:T(128)} %count_ref.7, bf16[4,2,32,128,128]{4,3,2,1,0:T(8,128)(2,1)} %bitcast.104, bf16[128,128,128]{2,1,0:T(8,128)(2,1)} %bitcast.16.proj_ref), custom_call_target="tpu_custom_call" | custom-call | tf_op jit(solution)/shard_map/pallas_call | solution.py:131
  84.2 7.5 %shard_map.86 = f32[2,128,128]{2,1,0:T(8,128)} custom-call(s32[1]{0:T(128)} %bitcast.17.core_ref, s32[256]{0:T(256)} %fusion.25.where_ref, s32[8]{0:T(128)} %count_ref.7, bf16[4,2,32,128,128]{4,3,2,1,0:T(8,128)(2,1)} %bitcast.105, bf16[128,128,128]{2,1,0:T(8,128)(2,1)} %collective-permute-done.12.proj_ref), custom_call_target="tpu_custom_call" | custom-call | tf_op jit(solution)/shard_map/pallas_call | solution.py:131
  93.3 9.1 %shard_map.88 = bf16[128,128,128]{2,1,0:T(8,128)(2,1)} custom-call(s32[1]{0:T(128)} %bitcast.17.core_ref, s32[256]{0:T(256)} %fusion.25.where_ref, s32[8]{0:T(128)} %count_ref.7, bf16[4,2,32,128,128]{4,3,2,1,0:T(8,128)(2,1)} %bitcast.106, bf16[2,128,128]{2,1,0:T(8,128)(2,1)} %bitcast.116), custom_call_target="tpu_custom_call" | custom-call | tf_op jit(solution)/shard_map/pallas_call | solution.py:187
  102.4 10.8 %shard_map.87 = f32[128,128,128]{2,1,0:T(8,128)} custom-call(s32[1]{0:T(128)} %bitcast.core_ref, s32[256]{0:T(256)} %fusion.25.where_ref, s32[8]{0:T(128)} %count_ref.7, bf16[4,2,32,128,128]{4,3,2,1,0:T(8,128)(2,1)} %bitcast.107, bf16[2,128,128]{2,1,0:T(8,128)(2,1)} %bitcast.117), custom_call_target="tpu_custom_call" | custom-call | tf_op jit(solution)/shard_map/pallas_call | solution.py:187
  113.2 5.8 %convert_add_fusion = f32[128,128,128]{2,1,0:T(8,128)S(1)} fusion(f32[128,128,128]{2,1,0:T(8,128)} %shard_map.87, bf16[128,128,128]{2,1,0:T(8,128)(2,1)} %collective-permute-done.13), kind=kLoop, calls=%fused_computation | loop fusion | flops 4194304 | bytes 20971520 | tf_op jit(solution)/shard_map/add | solution.py:257
  119.3 53.2 %collective-permute-start.16 = (bf16[4,4,128,128]{3,2,1,0:T(8,128)(2,1)S(1)}, bf16[4,4,128,128]{3,2,1,0:T(8,128)(2,1)S(1)}, u32[]{:S(2)}, u32[]{:S(2)}) collective-permute-start(bf16[4,4,128,128]{3,2,1,0:T(8,128)(2,1)S(1)} %get-tuple-element.11), channel_id=1, source_target_pairs={{0,80},{1,81},{2,82},{3,83},{4,84},{5,85},{6,86},{7,87},{8,88},{9,... | collective-permute-start | bytes 1572872 | tf_op jit(solution)/shard_map/ppermute | solution.py:37
  173.2 6.0 %collective-permute-done.16 = bf16[4,4,128,128]{3,2,1,0:T(8,128)(2,1)S(1)} collective-permute-done((bf16[4,4,128,128]{3,2,1,0:T(8,128)(2,1)S(1)}, bf16[4,4,128,128]{3,2,1,0:T(8,128)(2,1)S(1)}, u32[]{:S(2)}, u32[]{:S(2)}) %collective-permute-start.16) | collective-permute-done | bytes 524320 | tf_op jit(solution)/shard_map/ppermute | solution.py:37
  179.4 3.8 %collective-permute-start.17 = (bf16[4,4,256,128]{3,2,1,0:T(8,128)(2,1)S(1)}, bf16[4,4,256,128]{3,2,1,0:T(8,128)(2,1)S(1)}, u32[]{:S(2)}, u32[]{:S(2)}) collective-permute-start(bf16[4,4,256,128]{3,2,1,0:T(8,128)(2,1)S(1)} %pad_maximum_fusion.3), channel_id=1, source_target_pairs={{0,80},{1,81},{2,82},{3,83},{4,84},{5,85},{6,86},{7,87},{8,88},{9,... | collective-permute-start | bytes 3145736 | tf_op jit(solution)/shard_map/ppermute | solution.py:37
  183.5 12.0 %collective-permute-done.17 = bf16[4,4,256,128]{3,2,1,0:T(8,128)(2,1)S(1)} collective-permute-done((bf16[4,4,256,128]{3,2,1,0:T(8,128)(2,1)S(1)}, bf16[4,4,256,128]{3,2,1,0:T(8,128)(2,1)S(1)}, u32[]{:S(2)}, u32[]{:S(2)}) %collective-permute-start.17) | collective-permute-done | bytes 1048608 | tf_op jit(solution)/shard_map/ppermute | solution.py:37
  195.5 4.0 %collective-permute-done.15 = bf16[4,4,256,128]{3,2,1,0:T(8,128)(2,1)S(1)} collective-permute-done((bf16[4,4,256,128]{3,2,1,0:T(8,128)(2,1)S(1)}, bf16[4,4,256,128]{3,2,1,0:T(8,128)(2,1)S(1)}, u32[]{:S(2)}, u32[]{:S(2)}) %collective-permute-start.15) | collective-permute-done | bytes 1048608 | tf_op jit(solution)/shard_map/ppermute | solution.py:37
  202.2 2.7 %collective-permute-done.20 = bf16[4,128,128]{2,1,0:T(8,128)(2,1)S(1)} collective-permute-done((bf16[4,128,128]{2,1,0:T(8,128)(2,1)S(1)}, bf16[4,128,128]{2,1,0:T(8,128)(2,1)S(1)}, u32[]{:S(2)}, u32[]{:S(2)}) %collective-permute-start.20) | collective-permute-done | bytes 131104 | tf_op jit(solution)/shard_map/ppermute | solution.py:37
  205.0 3.1 %collective-permute-start.21 = (bf16[4,256,128]{2,1,0:T(8,128)(2,1)S(1)}, bf16[4,256,128]{2,1,0:T(8,128)(2,1)S(1)}, u32[]{:S(2)}, u32[]{:S(2)}) collective-permute-start(bf16[4,256,128]{2,1,0:T(8,128)(2,1)S(1)} %pad_maximum_fusion.6), channel_id=1, source_target_pairs={{0,12},{1,13},{2,14},{3,15},{4,0},{5,1},{6,2},{7,3},{8,4},{9,5},{1... | collective-permute-start | bytes 786440 | tf_op jit(solution)/shard_map/ppermute | solution.py:37
  208.3 3.7 %collective-permute-done.21 = bf16[4,256,128]{2,1,0:T(8,128)(2,1)S(1)} collective-permute-done((bf16[4,256,128]{2,1,0:T(8,128)(2,1)S(1)}, bf16[4,256,128]{2,1,0:T(8,128)(2,1)S(1)}, u32[]{:S(2)}, u32[]{:S(2)}) %collective-permute-start.21) | collective-permute-done | bytes 262176 | tf_op jit(solution)/shard_map/ppermute | solution.py:37
  212.0 3.9 %collective-permute-done.19 = bf16[4,256,128]{2,1,0:T(8,128)(2,1)S(1)} collective-permute-done((bf16[4,256,128]{2,1,0:T(8,128)(2,1)S(1)}, bf16[4,256,128]{2,1,0:T(8,128)(2,1)S(1)}, u32[]{:S(2)}, u32[]{:S(2)}) %collective-permute-start.19) | collective-permute-done | bytes 262176 | tf_op jit(solution)/shard_map/ppermute | solution.py:37
  216.1 3.3 %collective-permute-start.24 = (bf16[128,128]{1,0:T(8,128)(2,1)S(1)}, bf16[128,128]{1,0:T(8,128)(2,1)S(1)}, u32[]{:S(2)}, u32[]{:S(2)}) collective-permute-start(bf16[128,128]{1,0:T(8,128)(2,1)S(1)} %get-tuple-element.17), channel_id=1, source_target_pairs={{0,3},{1,0},{2,1},{3,2},{4,7},{5,4},{6,5},{7,6},{8,11},{9,8},{10,9... | collective-permute-start | bytes 98312 | tf_op jit(solution)/shard_map/ppermute | solution.py:37
  221.2 3.4 %collective-permute-start.25 = (bf16[256,128]{1,0:T(8,128)(2,1)S(1)}, bf16[256,128]{1,0:T(8,128)(2,1)S(1)}, u32[]{:S(2)}, u32[]{:S(2)}) collective-permute-start(bf16[256,128]{1,0:T(8,128)(2,1)S(1)} %pad_maximum_fusion.8), channel_id=1, source_target_pairs={{0,3},{1,0},{2,1},{3,2},{4,7},{5,4},{6,5},{7,6},{8,11},{9,8},{10,9... | collective-permute-start | bytes 196616 | tf_op jit(solution)/shard_map/ppermute | solution.py:37
  226.5 3.6 %collective-permute-done.23 = bf16[256,128]{1,0:T(8,128)(2,1)S(1)} collective-permute-done((bf16[256,128]{1,0:T(8,128)(2,1)S(1)}, bf16[256,128]{1,0:T(8,128)(2,1)S(1)}, u32[]{:S(2)}, u32[]{:S(2)}) %collective-permute-start.23) | collective-permute-done | bytes 65568 | tf_op jit(solution)/shard_map/ppermute | solution.py:37
  230.4 3.9 %collective-permute-done.26 = f32[64,128]{1,0:T(8,128)S(1)} collective-permute-done((f32[64,128]{1,0:T(8,128)S(1)}, f32[64,128]{1,0:T(8,128)S(1)}, u32[]{:S(2)}, u32[]{:S(2)}) %collective-permute-start.26) | collective-permute-done | bytes 32800 | tf_op jit(solution)/shard_map/ppermute | solution.py:46
  234.4 5.2 %collective-permute-done.27 = f32[32,128]{1,0:T(8,128)S(1)} collective-permute-done((f32[32,128]{1,0:T(8,128)S(1)}, f32[32,128]{1,0:T(8,128)S(1)}, u32[]{:S(2)}, u32[]{:S(2)}) %collective-permute-start.27) | collective-permute-done | bytes 16416 | tf_op jit(solution)/shard_map/ppermute | solution.py:46
  239.7 3.6 %collective-permute-done.28 = f32[16,128]{1,0:T(8,128)S(1)} collective-permute-done((f32[16,128]{1,0:T(8,128)S(1)}, f32[16,128]{1,0:T(8,128)S(1)}, u32[]{:S(2)}, u32[]{:S(2)}) %collective-permute-start.28) | collective-permute-done | bytes 8224 | tf_op jit(solution)/shard_map/ppermute | solution.py:46
  243.5 5.1 %collective-permute-done.29 = f32[8,128]{1,0:T(8,128)S(1)} collective-permute-done((f32[8,128]{1,0:T(8,128)S(1)}, f32[8,128]{1,0:T(8,128)S(1)}, u32[]{:S(2)}, u32[]{:S(2)}) %collective-permute-start.29) | collective-permute-done | bytes 4128 | tf_op jit(solution)/shard_map/ppermute | solution.py:46
  249.5 3.9 %all-to-all-start.1 = ((bf16[32,4,256]{2,1,0:T(4,128)(2,1)}), bf16[32,4,256]{2,1,0:T(4,128)(2,1)S(1)}, u32[]{:S(2)}, u32[]{:S(2)}) async-start(bf16[32,4,256]{2,1,0:T(4,128)(2,1)} %all_to_all.32), calls=%async_computation.1 | async-start | bytes 131072 | tf_op jit(solution)/shard_map/all_to_all | solution.py:272
  254.6 3.4 %collective-permute-start.32 = (f32[4,128]{1,0:T(4,128)S(1)}, f32[4,128]{1,0:T(4,128)S(1)}, u32[]{:S(2)}, u32[]{:S(2)}) collective-permute-start(f32[4,128]{1,0:T(4,128)S(1)} %add.204), channel_id=1, source_target_pairs={{0,64},{32,96},{64,0},{96,32},{1,65},{33,97},{65,1},{97,33},{2,66}... | collective-permute-start | bytes 6152 | tf_op jit(solution)/shard_map/ppermute | solution.py:46
  258.0 3.6 %all-to-all-done.1 = bf16[32,4,256]{2,1,0:T(4,128)(2,1)S(1)} async-done(((bf16[32,4,256]{2,1,0:T(4,128)(2,1)}), bf16[32,4,256]{2,1,0:T(4,128)(2,1)S(1)}, u32[]{:S(2)}, u32[]{:S(2)}) %all-to-all-start.1) | async-done | bytes 65568 | tf_op jit(solution)/shard_map/all_to_all | solution.py:272
  (108 shorter events, 33.7 us)
Async XLA Ops:
  18.5 5.5 %collective-permute-start.1 = (bf16[256,128]{1,0:T(8,128)(2,1)S(1)}, bf16[256,128]{1,0:T(8,128)(2,1)S(1)}, u32[]{:S(2)}, u32[]{:S(2)}) collective-permute-start(bf16[256,128]{1,0:T(8,128)(2,1)S(1)} %convolution_convert_fusion.1), channel_id=1, source_target_pairs={{0,1},{1,2},{2,3},{3,0},{4,5},{5,6},{6,7},{7,4},{8,9},{9,10},{10,1... | collective-permute-start | bytes 196616 | tf_op jit(solution)/shard_map/ppermute | solution.py:37
  19.1 4.9 %collective-permute-start = (bf16[256,128]{1,0:T(8,128)(2,1)S(1)}, bf16[256,128]{1,0:T(8,128)(2,1)S(1)}, u32[]{:S(2)}, u32[]{:S(2)}) collective-permute-start(bf16[256,128]{1,0:T(8,128)(2,1)S(1)} %convolution_convert_fusion.1), channel_id=1, source_target_pairs={{0,3},{1,0},{2,1},{3,2},{4,7},{5,4},{6,5},{7,6},{8,11},{9,8},{10,9... | collective-permute-start | bytes 196616 | tf_op jit(solution)/shard_map/ppermute | solution.py:37
  24.0 5.1 %collective-permute-start.2 = (bf16[128,128]{1,0:T(8,128)(2,1)S(1)}, bf16[128,128]{1,0:T(8,128)(2,1)S(1)}, u32[]{:S(2)}, u32[]{:S(2)}) collective-permute-start(bf16[128,128]{1,0:T(8,128)(2,1)S(1)} %slice.215), channel_id=1, source_target_pairs={{0,1},{1,2},{2,3},{3,0},{4,5},{5,6},{6,7},{7,4},{8,9},{9,10},{10,1... | collective-permute-start | bytes 98312 | tf_op jit(solution)/shard_map/ppermute | solution.py:37
  24.0 5.1 %collective-permute-start.3 = (bf16[128,128]{1,0:T(8,128)(2,1)S(1)}, bf16[128,128]{1,0:T(8,128)(2,1)S(1)}, u32[]{:S(2)}, u32[]{:S(2)}) collective-permute-start(bf16[128,128]{1,0:T(8,128)(2,1)S(1)} %slice.216), channel_id=1, source_target_pairs={{0,3},{1,0},{2,1},{3,2},{4,7},{5,4},{6,5},{7,6},{8,11},{9,8},{10,9... | collective-permute-start | bytes 98312 | tf_op jit(solution)/shard_map/ppermute | solution.py:37
  29.2 7.8 %collective-permute-start.4 = (bf16[4,256,128]{2,1,0:T(8,128)(2,1)S(1)}, bf16[4,256,128]{2,1,0:T(8,128)(2,1)S(1)}, u32[]{:S(2)}, u32[]{:S(2)}) collective-permute-start(bf16[4,256,128]{2,1,0:T(8,128)(2,1)S(1)} %get-tuple-element.23), channel_id=1, source_target_pairs={{0,12},{1,13},{2,14},{3,15},{4,0},{5,1},{6,2},{7,3},{8,4},{9,5},{1... | collective-permute-start | bytes 786440 | tf_op jit(solution)/shard_map/ppermute | solution.py:37
  30.5 8.8 %collective-permute-start.5 = (bf16[4,256,128]{2,1,0:T(8,128)(2,1)S(1)}, bf16[4,256,128]{2,1,0:T(8,128)(2,1)S(1)}, u32[]{:S(2)}, u32[]{:S(2)}) collective-permute-start(bf16[4,256,128]{2,1,0:T(8,128)(2,1)S(1)} %get-tuple-element.23), channel_id=1, source_target_pairs={{0,4},{1,5},{2,6},{3,7},{4,8},{5,9},{6,10},{7,11},{8,12},{9,13},{1... | collective-permute-start | bytes 786440 | tf_op jit(solution)/shard_map/ppermute | solution.py:37
  37.1 5.0 %collective-permute-start.7 = (bf16[4,128,128]{2,1,0:T(8,128)(2,1)S(1)}, bf16[4,128,128]{2,1,0:T(8,128)(2,1)S(1)}, u32[]{:S(2)}, u32[]{:S(2)}) collective-permute-start(bf16[4,128,128]{2,1,0:T(8,128)(2,1)S(1)} %slice.218), channel_id=1, source_target_pairs={{0,12},{1,13},{2,14},{3,15},{4,0},{5,1},{6,2},{7,3},{8,4},{9,5},{1... | collective-permute-start | bytes 393224 | tf_op jit(solution)/shard_map/ppermute | solution.py:37
  39.4 6.2 %collective-permute-start.6 = (bf16[4,128,128]{2,1,0:T(8,128)(2,1)S(1)}, bf16[4,128,128]{2,1,0:T(8,128)(2,1)S(1)}, u32[]{:S(2)}, u32[]{:S(2)}) collective-permute-start(bf16[4,128,128]{2,1,0:T(8,128)(2,1)S(1)} %slice.217), channel_id=1, source_target_pairs={{0,4},{1,5},{2,6},{3,7},{4,8},{5,9},{6,10},{7,11},{8,12},{9,13},{1... | collective-permute-start | bytes 393224 | tf_op jit(solution)/shard_map/ppermute | solution.py:37
  45.8 14.9 %collective-permute-start.8 = (bf16[4,4,256,128]{3,2,1,0:T(8,128)(2,1)S(1)}, bf16[4,4,256,128]{3,2,1,0:T(8,128)(2,1)S(1)}, u32[]{:S(2)}, u32[]{:S(2)}) collective-permute-start(bf16[4,4,256,128]{3,2,1,0:T(8,128)(2,1)S(1)} %get-tuple-element.13), channel_id=1, source_target_pairs={{0,80},{1,81},{2,82},{3,83},{4,84},{5,85},{6,86},{7,87},{8,88},{9,... | collective-permute-start | bytes 3145736 | tf_op jit(solution)/shard_map/ppermute | solution.py:37
  46.9 16.1 %collective-permute-start.9 = (bf16[4,4,256,128]{3,2,1,0:T(8,128)(2,1)S(1)}, bf16[4,4,256,128]{3,2,1,0:T(8,128)(2,1)S(1)}, u32[]{:S(2)}, u32[]{:S(2)}) collective-permute-start(bf16[4,4,256,128]{3,2,1,0:T(8,128)(2,1)S(1)} %get-tuple-element.13), channel_id=1, source_target_pairs={{0,16},{1,17},{2,18},{3,19},{4,20},{5,21},{6,22},{7,23},{8,24},{9,... | collective-permute-start | bytes 3145736 | tf_op jit(solution)/shard_map/ppermute | solution.py:37
  60.7 9.2 %collective-permute-start.11 = (bf16[4,4,128,128]{3,2,1,0:T(8,128)(2,1)S(1)}, bf16[4,4,128,128]{3,2,1,0:T(8,128)(2,1)S(1)}, u32[]{:S(2)}, u32[]{:S(2)}) collective-permute-start(bf16[4,4,128,128]{3,2,1,0:T(8,128)(2,1)S(1)} %slice.220), channel_id=1, source_target_pairs={{0,80},{1,81},{2,82},{3,83},{4,84},{5,85},{6,86},{7,87},{8,88},{9,... | collective-permute-start | bytes 1572872 | tf_op jit(solution)/shard_map/ppermute | solution.py:37
  63.1 10.5 %collective-permute-start.10 = (bf16[4,4,128,128]{3,2,1,0:T(8,128)(2,1)S(1)}, bf16[4,4,128,128]{3,2,1,0:T(8,128)(2,1)S(1)}, u32[]{:S(2)}, u32[]{:S(2)}) collective-permute-start(bf16[4,4,128,128]{3,2,1,0:T(8,128)(2,1)S(1)} %slice.219), channel_id=1, source_target_pairs={{0,16},{1,17},{2,18},{3,19},{4,20},{5,21},{6,22},{7,23},{8,24},{9,... | collective-permute-start | bytes 1572872 | tf_op jit(solution)/shard_map/ppermute | solution.py:37
  75.9 8.2 %collective-permute-start.12 = (bf16[128,128,128]{2,1,0:T(8,128)(2,1)}, bf16[128,128,128]{2,1,0:T(8,128)(2,1)}, u32[]{:S(2)}, u32[]{:S(2)}) collective-permute-start(bf16[128,128,128]{2,1,0:T(8,128)(2,1)} %bitcast.16.proj_ref), channel_id=1, source_target_pairs={{0,32},{32,0},{64,96},{96,64},{1,33},{33,1},{65,97},{97,65},{2,34}... | collective-permute-start | bytes 12582920 | tf_op jit(solution)/shard_map/ppermute | solution.py:41
  102.4 10.8 %collective-permute-start.13 = (bf16[128,128,128]{2,1,0:T(8,128)(2,1)}, bf16[128,128,128]{2,1,0:T(8,128)(2,1)}, u32[]{:S(2)}, u32[]{:S(2)}) collective-permute-start(bf16[128,128,128]{2,1,0:T(8,128)(2,1)} %shard_map.88), channel_id=1, source_target_pairs={{0,32},{32,0},{64,96},{96,64},{1,33},{33,1},{65,97},{97,65},{2,34}... | collective-permute-start | bytes 12582920 | tf_op jit(solution)/shard_map/ppermute | solution.py:41
  119.3 59.9 %collective-permute-start.16 = (bf16[4,4,128,128]{3,2,1,0:T(8,128)(2,1)S(1)}, bf16[4,4,128,128]{3,2,1,0:T(8,128)(2,1)S(1)}, u32[]{:S(2)}, u32[]{:S(2)}) collective-permute-start(bf16[4,4,128,128]{3,2,1,0:T(8,128)(2,1)S(1)} %get-tuple-element.11), channel_id=1, source_target_pairs={{0,80},{1,81},{2,82},{3,83},{4,84},{5,85},{6,86},{7,87},{8,88},{9,... | collective-permute-start | bytes 1572872 | tf_op jit(solution)/shard_map/ppermute | solution.py:37
  172.5 10.7 %collective-permute-start.14 = (bf16[4,4,128,128]{3,2,1,0:T(8,128)(2,1)S(1)}, bf16[4,4,128,128]{3,2,1,0:T(8,128)(2,1)S(1)}, u32[]{:S(2)}, u32[]{:S(2)}) collective-permute-start(bf16[4,4,128,128]{3,2,1,0:T(8,128)(2,1)S(1)} %get-tuple-element.10), channel_id=1, source_target_pairs={{0,16},{1,17},{2,18},{3,19},{4,20},{5,21},{6,22},{7,23},{8,24},{9,... | collective-permute-start | bytes 1572872 | tf_op jit(solution)/shard_map/ppermute | solution.py:37
  179.4 16.1 %collective-permute-start.17 = (bf16[4,4,256,128]{3,2,1,0:T(8,128)(2,1)S(1)}, bf16[4,4,256,128]{3,2,1,0:T(8,128)(2,1)S(1)}, u32[]{:S(2)}, u32[]{:S(2)}) collective-permute-start(bf16[4,4,256,128]{3,2,1,0:T(8,128)(2,1)S(1)} %pad_maximum_fusion.3), channel_id=1, source_target_pairs={{0,80},{1,81},{2,82},{3,83},{4,84},{5,85},{6,86},{7,87},{8,88},{9,... | collective-permute-start | bytes 3145736 | tf_op jit(solution)/shard_map/ppermute | solution.py:37
  183.4 16.1 %collective-permute-start.15 = (bf16[4,4,256,128]{3,2,1,0:T(8,128)(2,1)S(1)}, bf16[4,4,256,128]{3,2,1,0:T(8,128)(2,1)S(1)}, u32[]{:S(2)}, u32[]{:S(2)}) collective-permute-start(bf16[4,4,256,128]{3,2,1,0:T(8,128)(2,1)S(1)} %pad_maximum_fusion.2), channel_id=1, source_target_pairs={{0,16},{1,17},{2,18},{3,19},{4,20},{5,21},{6,22},{7,23},{8,24},{9,... | collective-permute-start | bytes 3145736 | tf_op jit(solution)/shard_map/ppermute | solution.py:37
  199.9 5.0 %collective-permute-start.20 = (bf16[4,128,128]{2,1,0:T(8,128)(2,1)S(1)}, bf16[4,128,128]{2,1,0:T(8,128)(2,1)S(1)}, u32[]{:S(2)}, u32[]{:S(2)}) collective-permute-start(bf16[4,128,128]{2,1,0:T(8,128)(2,1)S(1)} %get-tuple-element.21), channel_id=1, source_target_pairs={{0,12},{1,13},{2,14},{3,15},{4,0},{5,1},{6,2},{7,3},{8,4},{9,5},{1... | collective-permute-start | bytes 393224 | tf_op jit(solution)/shard_map/ppermute | solution.py:37
  201.9 6.3 %collective-permute-start.18 = (bf16[4,128,128]{2,1,0:T(8,128)(2,1)S(1)}, bf16[4,128,128]{2,1,0:T(8,128)(2,1)S(1)}, u32[]{:S(2)}, u32[]{:S(2)}) collective-permute-start(bf16[4,128,128]{2,1,0:T(8,128)(2,1)S(1)} %get-tuple-element.20), channel_id=1, source_target_pairs={{0,4},{1,5},{2,6},{3,7},{4,8},{5,9},{6,10},{7,11},{8,12},{9,13},{1... | collective-permute-start | bytes 393224 | tf_op jit(solution)/shard_map/ppermute | solution.py:37
  205.0 7.0 %collective-permute-start.21 = (bf16[4,256,128]{2,1,0:T(8,128)(2,1)S(1)}, bf16[4,256,128]{2,1,0:T(8,128)(2,1)S(1)}, u32[]{:S(2)}, u32[]{:S(2)}) collective-permute-start(bf16[4,256,128]{2,1,0:T(8,128)(2,1)S(1)} %pad_maximum_fusion.6), channel_id=1, source_target_pairs={{0,12},{1,13},{2,14},{3,15},{4,0},{5,1},{6,2},{7,3},{8,4},{9,5},{1... | collective-permute-start | bytes 786440 | tf_op jit(solution)/shard_map/ppermute | solution.py:37
  208.2 7.7 %collective-permute-start.19 = (bf16[4,256,128]{2,1,0:T(8,128)(2,1)S(1)}, bf16[4,256,128]{2,1,0:T(8,128)(2,1)S(1)}, u32[]{:S(2)}, u32[]{:S(2)}) collective-permute-start(bf16[4,256,128]{2,1,0:T(8,128)(2,1)S(1)} %pad_maximum_fusion.5), channel_id=1, source_target_pairs={{0,4},{1,5},{2,6},{3,7},{4,8},{5,9},{6,10},{7,11},{8,12},{9,13},{1... | collective-permute-start | bytes 786440 | tf_op jit(solution)/shard_map/ppermute | solution.py:37
  216.0 5.2 %collective-permute-start.22 = (bf16[128,128]{1,0:T(8,128)(2,1)S(1)}, bf16[128,128]{1,0:T(8,128)(2,1)S(1)}, u32[]{:S(2)}, u32[]{:S(2)}) collective-permute-start(bf16[128,128]{1,0:T(8,128)(2,1)S(1)} %get-tuple-element.16), channel_id=1, source_target_pairs={{0,1},{1,2},{2,3},{3,0},{4,5},{5,6},{6,7},{7,4},{8,9},{9,10},{10,1... | collective-permute-start | bytes 98312 | tf_op jit(solution)/shard_map/ppermute | solution.py:37
  216.1 5.1 %collective-permute-start.24 = (bf16[128,128]{1,0:T(8,128)(2,1)S(1)}, bf16[128,128]{1,0:T(8,128)(2,1)S(1)}, u32[]{:S(2)}, u32[]{:S(2)}) collective-permute-start(bf16[128,128]{1,0:T(8,128)(2,1)S(1)} %get-tuple-element.17), channel_id=1, source_target_pairs={{0,3},{1,0},{2,1},{3,2},{4,7},{5,4},{6,5},{7,6},{8,11},{9,8},{10,9... | collective-permute-start | bytes 98312 | tf_op jit(solution)/shard_map/ppermute | solution.py:37
  221.2 5.3 %collective-permute-start.25 = (bf16[256,128]{1,0:T(8,128)(2,1)S(1)}, bf16[256,128]{1,0:T(8,128)(2,1)S(1)}, u32[]{:S(2)}, u32[]{:S(2)}) collective-permute-start(bf16[256,128]{1,0:T(8,128)(2,1)S(1)} %pad_maximum_fusion.8), channel_id=1, source_target_pairs={{0,3},{1,0},{2,1},{3,2},{4,7},{5,4},{6,5},{7,6},{8,11},{9,8},{10,9... | collective-permute-start | bytes 196616 | tf_op jit(solution)/shard_map/ppermute | solution.py:37
  224.6 5.5 %collective-permute-start.23 = (bf16[256,128]{1,0:T(8,128)(2,1)S(1)}, bf16[256,128]{1,0:T(8,128)(2,1)S(1)}, u32[]{:S(2)}, u32[]{:S(2)}) collective-permute-start(bf16[256,128]{1,0:T(8,128)(2,1)S(1)} %pad_maximum_fusion.7), channel_id=1, source_target_pairs={{0,1},{1,2},{2,3},{3,0},{4,5},{5,6},{6,7},{7,4},{8,9},{9,10},{10,1... | collective-permute-start | bytes 196616 | tf_op jit(solution)/shard_map/ppermute | solution.py:37
  230.3 4.0 %collective-permute-start.26 = (f32[64,128]{1,0:T(8,128)S(1)}, f32[64,128]{1,0:T(8,128)S(1)}, u32[]{:S(2)}, u32[]{:S(2)}) collective-permute-start(f32[64,128]{1,0:T(8,128)S(1)} %slice_select_fusion), channel_id=1, source_target_pairs={{0,16},{1,17},{2,18},{3,19},{4,20},{5,21},{6,22},{7,23},{8,24},{9,... | collective-permute-start | bytes 98312 | tf_op jit(solution)/shard_map/ppermute | solution.py:46
  234.3 5.3 %collective-permute-start.27 = (f32[32,128]{1,0:T(8,128)S(1)}, f32[32,128]{1,0:T(8,128)S(1)}, u32[]{:S(2)}, u32[]{:S(2)}) collective-permute-start(f32[32,128]{1,0:T(8,128)S(1)} %slice_select_fusion.1), channel_id=1, source_target_pairs={{0,8},{1,9},{2,10},{3,11},{4,12},{5,13},{6,14},{7,15},{8,0},{9,1},... | collective-permute-start | bytes 49160 | tf_op jit(solution)/shard_map/ppermute | solution.py:46
  243.4 5.2 %collective-permute-start.29 = (f32[8,128]{1,0:T(8,128)S(1)}, f32[8,128]{1,0:T(8,128)S(1)}, u32[]{:S(2)}, u32[]{:S(2)}) collective-permute-start(f32[8,128]{1,0:T(8,128)S(1)} %slice_select_fusion.3), channel_id=1, source_target_pairs={{0,2},{1,3},{2,0},{3,1},{4,6},{5,7},{6,4},{7,5},{8,10},{9,11},{10,... | collective-permute-start | bytes 12296 | tf_op jit(solution)/shard_map/ppermute | solution.py:46
  248.6 4.8 %collective-permute-start.30 = (f32[4,128]{1,0:T(4,128)S(1)}, f32[4,128]{1,0:T(4,128)S(1)}, u32[]{:S(2)}, u32[]{:S(2)}) collective-permute-start(f32[4,128]{1,0:T(4,128)S(1)} %slice_select_fusion.4), channel_id=1, source_target_pairs={{0,1},{1,0},{2,3},{3,2},{4,5},{5,4},{6,7},{7,6},{8,9},{9,8},{10,11... | collective-permute-start | bytes 6152 | tf_op jit(solution)/shard_map/ppermute | solution.py:46
  249.5 12.2 %all-to-all-start.1 = ((bf16[32,4,256]{2,1,0:T(4,128)(2,1)}), bf16[32,4,256]{2,1,0:T(4,128)(2,1)S(1)}, u32[]{:S(2)}, u32[]{:S(2)}) async-start(bf16[32,4,256]{2,1,0:T(4,128)(2,1)} %all_to_all.32), calls=%async_computation.1 | async-start | bytes 131072 | tf_op jit(solution)/shard_map/all_to_all | solution.py:272
  254.6 7.1 %collective-permute-start.32 = (f32[4,128]{1,0:T(4,128)S(1)}, f32[4,128]{1,0:T(4,128)S(1)}, u32[]{:S(2)}, u32[]{:S(2)}) collective-permute-start(f32[4,128]{1,0:T(4,128)S(1)} %add.204), channel_id=1, source_target_pairs={{0,64},{32,96},{64,0},{96,32},{1,65},{33,97},{65,1},{97,33},{2,66}... | collective-permute-start | bytes 6152 | tf_op jit(solution)/shard_map/ppermute | solution.py:46
  (6 other events, 40.9 us)

commit v4 on v3

--- a/solution.py
+++ b/solution.py
@@ -90,19 +90,20 @@
     return total
 
 
-def aggregate_kernel(core_ref, where_ref, count_ref, tiles_ref, proj_ref, out_ref):
+def aggregate_kernel(core_ref, where_ref, count_ref, tiles_ref, proj_ref, out_ref, picked_ref):
     row = pl.program_id(0)
     half_id = pl.program_id(1)
     tile_rows = pl.num_programs(0)
-    slot_count = tiles_ref.shape[0]
+    tile_size = proj_ref.shape[1]
+    slot_count = tiles_ref.shape[1] // tile_size
     base = (half_id * 2 + core_ref[0]) * tile_rows + row
     live = count_ref[base]
-
-    def step(slot, total):
-        spot = where_ref[base * slot_count + slot]
-        return total + jnp.dot(tiles_ref[slot], proj_ref[spot], preferred_element_type=jnp.float32)
-
-    part = lax.fori_loop(0, live, step, jnp.zeros(out_ref.shape, jnp.float32))
+    for slot in range(slot_count):
+        piece = proj_ref[where_ref[base * slot_count + slot]]
+        picked_ref[slot * tile_size:(slot + 1) * tile_size, :] = jnp.where(
+            slot < live, piece, jnp.zeros_like(piece)
+        )
+    part = jnp.dot(tiles_ref[...], picked_ref[...], preferred_element_type=jnp.float32)
 
     @pl.when(half_id == 0)
     def _():
@@ -113,35 +114,34 @@
         out_ref[...] += part
 
 
-def aggregate_pair(core_id, spots, counts, tile_stack, buffer):
-    blocks, tile_rows, slot_count, tile_size, _ = tile_stack.shape
+def aggregate_pair(core_id, spots, counts, tiles_wide, buffer):
+    blocks, tile_rows, tile_size, wide = tiles_wide.shape
     hidden_width = buffer.shape[-1]
     grid_spec = pltpu.PrefetchScalarGridSpec(
         num_scalar_prefetch=3,
         grid=(tile_rows, blocks // 2),
         in_specs=[
-            pl.BlockSpec(
-                (None, None, slot_count, tile_size, tile_size),
-                lambda r, h, c, w, n: (h * 2 + c[0], r, 0, 0, 0),
-            ),
+            pl.BlockSpec((None, None, tile_size, wide), lambda r, h, c, w, n: (h * 2 + c[0], r, 0, 0)),
             pl.BlockSpec(buffer.shape, lambda r, h, c, w, n: (0, 0, 0)),
         ],
         out_specs=pl.BlockSpec((None, tile_size, hidden_width), lambda r, h, c, w, n: (r, 0, 0)),
+        scratch_shapes=[pltpu.VMEM((wide, hidden_width), buffer.dtype)],
     )
     return pl.pallas_call(
         aggregate_kernel,
         grid_spec=grid_spec,
         out_shape=jax.ShapeDtypeStruct((tile_rows, tile_size, hidden_width), jnp.float32),
         compiler_params=pltpu.CompilerParams(dimension_semantics=("arbitrary", "arbitrary")),
-    )(jnp.reshape(core_id, (1,)).astype(jnp.int32), spots, counts, tile_stack, buffer)
-
-
-def spread_kernel(core_ref, where_ref, count_ref, tiles_ref, grad_ref, out_ref, total_ref):
+    )(jnp.reshape(core_id, (1,)).astype(jnp.int32), spots, counts, tiles_wide, buffer)
+
+
+def spread_kernel(core_ref, where_ref, count_ref, tiles_ref, grad_ref, out_ref, total_ref, terms_ref):
     row = pl.program_id(0)
     half_id = pl.program_id(1)
     tile_rows = pl.num_programs(0)
     halves = pl.num_programs(1)
-    slot_count = tiles_ref.shape[0]
+    tile_size = grad_ref.shape[0]
+    slot_count = tiles_ref.shape[0] // tile_size
     base = (half_id * 2 + core_ref[0]) * tile_rows + row
     live = count_ref[base]
 
@@ -149,14 +149,12 @@
     def _():
         total_ref[...] = jnp.zeros(total_ref.shape, jnp.float32)
 
-    grad_rows = grad_ref[...]
+    terms_ref[...] = jnp.dot(tiles_ref[...], grad_ref[...], preferred_element_type=jnp.float32)
 
     def step(slot, carry):
         spot = where_ref[base * slot_count + slot]
-        total_ref[spot] += lax.dot_general(
-            tiles_ref[slot], grad_rows, (((0,), (0,)), ((), ())),
-            preferred_element_type=jnp.float32,
-        )
+        start = pl.multiple_of(slot * tile_size, tile_size)
+        total_ref[spot] += terms_ref[pl.ds(start, tile_size), :]
         return carry
 
     lax.fori_loop(0, live, step, 0)
@@ -166,30 +164,30 @@
         out_ref[...] = total_ref[...].astype(out_ref.dtype)
 
 
-def spread_pair(core_id, spots, counts, tile_stack, grad_tiles, buffer_tiles, out_type):
-    blocks, tile_rows, slot_count, tile_size, _ = tile_stack.shape
+def spread_pair(core_id, spots, counts, tiles_tall, grad_tiles, buffer_tiles, out_type):
+    blocks, tile_rows, tall, tile_size = tiles_tall.shape
     hidden_width = grad_tiles.shape[-1]
     grid_spec = pltpu.PrefetchScalarGridSpec(
         num_scalar_prefetch=3,
         grid=(tile_rows, blocks // 2),
         in_specs=[
-            pl.BlockSpec(
-                (None, None, slot_count, tile_size, tile_size),
-                lambda r, h, c, w, n: (h * 2 + c[0], r, 0, 0, 0),
-            ),
+            pl.BlockSpec((None, None, tall, tile_size), lambda r, h, c, w, n: (h * 2 + c[0], r, 0, 0)),
             pl.BlockSpec((None, tile_size, hidden_width), lambda r, h, c, w, n: (r, 0, 0)),
         ],
         out_specs=pl.BlockSpec(
             (buffer_tiles, tile_size, hidden_width), lambda r, h, c, w, n: (0, 0, 0)
         ),
-        scratch_shapes=[pltpu.VMEM((buffer_tiles, tile_size, hidden_width), jnp.float32)],
+        scratch_shapes=[
+            pltpu.VMEM((buffer_tiles, tile_size, hidden_width), jnp.float32),
+            pltpu.VMEM((tall, hidden_width), jnp.float32),
+        ],
     )
     return pl.pallas_call(
         spread_kernel,
         grid_spec=grid_spec,
         out_shape=jax.ShapeDtypeStruct((buffer_tiles, tile_size, hidden_width), out_type),
         compiler_params=pltpu.CompilerParams(dimension_semantics=("arbitrary", "arbitrary")),
-    )(jnp.reshape(core_id, (1,)).astype(jnp.int32), spots, counts, tile_stack, grad_tiles)
+    )(jnp.reshape(core_id, (1,)).astype(jnp.int32), spots, counts, tiles_tall, grad_tiles)
 
 
 def buffer_spots(tile_col, blk_id, feat_id, block_tiles, tiles_per_device):
@@ -221,6 +219,12 @@
     blk_id = lax.axis_index("blk")
     core_id = blk_id % 2
     tile_stack = tile_values.reshape(cycle_size, tile_rows, slot_count, tile_size, tile_size)
+    tiles_wide = tile_stack.transpose(0, 1, 3, 2, 4).reshape(
+        cycle_size, tile_rows, tile_size, slot_count * tile_size
+    )
+    tiles_tall = tile_stack.transpose(0, 1, 2, 4, 3).reshape(
+        cycle_size, tile_rows, slot_count * tile_size, tile_size
+    )
     spots = buffer_spots(tile_col, blk_id, feat_id, block_tiles, tile_rows)
     buffer_tiles = block_tiles * 2
 
@@ -234,9 +238,9 @@
         gathered = gather_phase(gathered, phase)
     own_buffer = gathered.reshape(buffer_tiles, tile_size, hidden_width)
     other_buffer = sibling(own_buffer)
-    aggregate_sum = aggregate_pair(core_id, spots, tile_count, tile_stack, own_buffer)
+    aggregate_sum = aggregate_pair(core_id, spots, tile_count, tiles_wide, own_buffer)
     aggregate_sum = aggregate_sum + aggregate_pair(
-        1 - core_id, spots, tile_count, tile_stack, other_buffer
+        1 - core_id, spots, tile_count, tiles_wide, other_buffer
     )
 
     pre_act = aggregate_sum.reshape(rows_own, hidden_width)
@@ -248,11 +252,11 @@
     grad_tiles = grad_pre.reshape(tile_rows, tile_size, hidden_width)
 
     outgoing = spread_pair(
-        1 - core_id, spots, tile_count, tile_stack, grad_tiles, buffer_tiles, jnp.bfloat16
+        1 - core_id, spots, tile_count, tiles_tall, grad_tiles, buffer_tiles, jnp.bfloat16
     )
     arrived = sibling(outgoing)
     total = spread_pair(
-        core_id, spots, tile_count, tile_stack, grad_tiles, buffer_tiles, jnp.float32
+        core_id, spots, tile_count, tiles_tall, grad_tiles, buffer_tiles, jnp.float32
     )
     total = total + arrived.astype(jnp.float32)
     total = total.reshape(RING, RING, RING, rows_own, hidden_width)

time: 264 us -> 246 us (0.932)
  starting transfers between devices: 92.2 us -> 35.7 us
  local copies, waits for them, and re-layouts: 2.55 us -> 40 us
  waiting for transfers between devices: 101 us -> 106 us
  Pallas kernels: 34.9 us -> 30.8 us
    ppermute x24, starting transfers between devices: 84.4 us -> 30.4 us  [ring_shift(): return lax.ppermute(block, BOTH, route)]
    reshape x0 -> x3, local copies, waits for them, and re-layouts: none -> 37.4 us  [the longest x2 24.1 us: body(): tile_values.reshape(cycle_size, tile_rows, slot_count, tile_size, tile_size)]
    pallas_call x2, Pallas kernels: 19.8 us -> 16.6 us  [spread_pair(): pl.pallas_call(spread_kernel, grid_spec=grid_spec, out_shape=jax.ShapeDty...]
    all_to_all x1, waiting for transfers between devices: 3.65 us -> 6.66 us  [body(): lax.all_to_all(features_grad_local, 'feat', split_axis=0, concat_axis=1,...]
    ppermute x7, starting transfers between devices: 3.92 us -> 0.92 us  [swapped(): return lax.ppermute(block, axis, [(i, i ^ mask) for i in range(count)])]
  transfers between devices with their start and end apart: 34 -> 34, of which waited for: 24 -> 26; matrix products, arithmetic and copies ran while one was open for 1% -> 16% of each run, Pallas kernels for 7% -> 7%
where the time goes in v4:
time: 246 us; the launch traced here: 244 us
  waiting for transfers between devices  106 us (43%)
  local copies, waits for them, and re-layouts  40 us (16%)
  starting transfers between devices  35.7 us (15%)
  Pallas kernels  30.8 us (13%)
  blocking collectives  17.6 us (7%)
  other arithmetic  12.4 us (5%)
    ppermute x24, waiting for transfers between devices, ring_shift(): return lax.ppermute(block, BOTH, route)  80.5 us
    ppermute x24, starting transfers between devices, ring_shift(): return lax.ppermute(block, BOTH, route)  30.4 us
    reshape x2, local copies, waits for them, and re-layouts, body(): tile_values.reshape(cycle_size, tile_rows, slot_count, tile_size, tile_size)  24.1 us
    ppermute x7, waiting for transfers between devices, swapped(): return lax.ppermute(block, axis, [(i, i ^ mask) for i in range(count)])  18.9 us
    all_to_all x1, blocking collectives, body(): lax.all_to_all(features_t, 'feat', split_axis=1, concat_axis=0, tiled=True)  17.6 us
    pallas_call x2, Pallas kernels, spread_pair(): pl.pallas_call(spread_kernel, grid_spec=grid_spec, out_shape=jax.ShapeDty...  16.6 us
    pallas_call x2, Pallas kernels, aggregate_pair(): pl.pallas_call(aggregate_kernel, grid_spec=grid_spec, out_shape=jax.Shape...  14.2 us
    reshape x1, local copies, waits for them, and re-layouts, body(): tile_stack.transpose(0, 1, 3, 2, 4)  13.3 us
  transfers between devices with their start and end apart: 34, of which 26 were waited for; matrix products, arithmetic and copies ran while one was open for 16% of the time, Pallas kernels for 7%

profile of v4, /device:TPU:0, one launch (start us, length us, event | category | flops | bytes accessed | tf_op | source)
XLA Modules:
  0.0 244.3 jit_solution(7292066145482891767)
XLA Ops:
  0.6 17.6 %all_to_all.38 = bf16[4,32,256]{2,0,1:T(4,128)(2,1)S(1)} all-to-all(bf16[4,32,256]{2,0,1:T(4,128)(2,1)} %bitcast.134), channel_id=1, replica_groups=mesh['blk'=4,'feat'=32] {'feat'}, dimensions={1} | all-to-all | bytes 131072 | tf_op jit(solution)/shard_map/all_to_all | solution.py:231
  27.0 3.5 %collective-permute-done.2 = bf16[128,128]{1,0:T(8,128)(2,1)S(1)} collective-permute-done((bf16[128,128]{1,0:T(8,128)(2,1)S(1)}, bf16[128,128]{1,0:T(8,128)(2,1)S(1)}, u32[]{:S(2)}, u32[]{:S(2)}) %collective-permute-start.2) | collective-permute-done | bytes 32800 | tf_op jit(solution)/shard_map/ppermute | solution.py:37
  32.7 5.8 %collective-permute-done.4 = bf16[4,256,128]{2,1,0:T(8,128)(2,1)S(1)} collective-permute-done((bf16[4,256,128]{2,1,0:T(8,128)(2,1)S(1)}, bf16[4,256,128]{2,1,0:T(8,128)(2,1)S(1)}, u32[]{:S(2)}, u32[]{:S(2)}) %collective-permute-start.4) | collective-permute-done | bytes 262176 | tf_op jit(solution)/shard_map/ppermute | solution.py:37
  40.6 2.9 %collective-permute-done.7 = bf16[4,128,128]{2,1,0:T(8,128)(2,1)S(1)} collective-permute-done((bf16[4,128,128]{2,1,0:T(8,128)(2,1)S(1)}, bf16[4,128,128]{2,1,0:T(8,128)(2,1)S(1)}, u32[]{:S(2)}, u32[]{:S(2)}) %collective-permute-start.7) | collective-permute-done | bytes 131104 | tf_op jit(solution)/shard_map/ppermute | solution.py:37
  43.5 3.2 %collective-permute-done.6 = bf16[4,128,128]{2,1,0:T(8,128)(2,1)S(1)} collective-permute-done((bf16[4,128,128]{2,1,0:T(8,128)(2,1)S(1)}, bf16[4,128,128]{2,1,0:T(8,128)(2,1)S(1)}, u32[]{:S(2)}, u32[]{:S(2)}) %collective-permute-start.6) | collective-permute-done | bytes 131104 | tf_op jit(solution)/shard_map/ppermute | solution.py:37
  46.8 2.6 %collective-permute-start.8 = (bf16[4,4,256,128]{3,2,1,0:T(8,128)(2,1)S(1)}, bf16[4,4,256,128]{3,2,1,0:T(8,128)(2,1)S(1)}, u32[]{:S(2)}, u32[]{:S(2)}) collective-permute-start(bf16[4,4,256,128]{3,2,1,0:T(8,128)(2,1)S(1)} %get-tuple-element.13), channel_id=1, source_target_pairs={{0,80},{1,81},{2,82},{3,83},{4,84},{5,85},{6,86},{7,87},{8,88},{9,... | collective-permute-start | bytes 3145736 | tf_op jit(solution)/shard_map/ppermute | solution.py:37
  49.5 12.3 %collective-permute-done.8 = bf16[4,4,256,128]{3,2,1,0:T(8,128)(2,1)S(1)} collective-permute-done((bf16[4,4,256,128]{3,2,1,0:T(8,128)(2,1)S(1)}, bf16[4,4,256,128]{3,2,1,0:T(8,128)(2,1)S(1)}, u32[]{:S(2)}, u32[]{:S(2)}) %collective-permute-start.8) | collective-permute-done | bytes 1048608 | tf_op jit(solution)/shard_map/ppermute | solution.py:37
  61.8 3.8 %collective-permute-start.11 = (bf16[4,4,128,128]{3,2,1,0:T(8,128)(2,1)S(1)}, bf16[4,4,128,128]{3,2,1,0:T(8,128)(2,1)S(1)}, u32[]{:S(2)}, u32[]{:S(2)}) collective-permute-start(bf16[4,4,128,128]{3,2,1,0:T(8,128)(2,1)S(1)} %slice.220), channel_id=1, source_target_pairs={{0,80},{1,81},{2,82},{3,83},{4,84},{5,85},{6,86},{7,87},{8,88},{9,... | collective-permute-start | bytes 1572872 | tf_op jit(solution)/shard_map/ppermute | solution.py:37
  65.7 6.6 %collective-permute-done.11 = bf16[4,4,128,128]{3,2,1,0:T(8,128)(2,1)S(1)} collective-permute-done((bf16[4,4,128,128]{3,2,1,0:T(8,128)(2,1)S(1)}, bf16[4,4,128,128]{3,2,1,0:T(8,128)(2,1)S(1)}, u32[]{:S(2)}, u32[]{:S(2)}) %collective-permute-start.11) | collective-permute-done | bytes 524320 | tf_op jit(solution)/shard_map/ppermute | solution.py:37
  72.3 3.8 %collective-permute-done.10 = bf16[4,4,128,128]{3,2,1,0:T(8,128)(2,1)S(1)} collective-permute-done((bf16[4,4,128,128]{3,2,1,0:T(8,128)(2,1)S(1)}, bf16[4,4,128,128]{3,2,1,0:T(8,128)(2,1)S(1)}, u32[]{:S(2)}, u32[]{:S(2)}) %collective-permute-start.10) | collective-permute-done | bytes 524320 | tf_op jit(solution)/shard_map/ppermute | solution.py:37
  78.4 12.1 %copy.17 = bf16[4,2,32,128,128]{4,2,3,1,0:T(8,128)(2,1)} copy(bf16[4,2,32,128,128]{4,3,2,1,0:T(8,128)(2,1)} %bitcast.114) | data formatting | bytes 16777216 | tf_op jit(solution)/shard_map/reshape | solution.py:221
  90.5 12.0 %copy.14 = bf16[4,2,32,128,128]{3,4,2,1,0:T(8,128)(2,1)} copy(bf16[4,2,32,128,128]{4,3,2,1,0:T(8,128)(2,1)} %bitcast.115) | data formatting | bytes 16777216 | tf_op jit(solution)/shard_map/reshape | solution.py:221
  102.6 13.3 %reshape.59.tiles_ref = bf16[4,2,128,4096]{3,2,1,0:T(8,128)(2,1)} reshape(bf16[4,2,128,32,128]{4,3,2,1,0:T(8,128)(2,1)} %bitcast.116) | data formatting | bytes 16777216 | tf_op jit(solution)/shard_map/reshape | solution.py:222
  116.5 7.0 %shard_map.85 = f32[2,128,128]{2,1,0:T(8,128)} custom-call(s32[1]{0:T(128)} %bitcast.core_ref, s32[256]{0:T(256)} %fusion.25.where_ref, s32[8]{0:T(128)} %count_ref.7, bf16[4,2,128,4096]{3,2,1,0:T(8,128)(2,1)} %reshape.59.tiles_ref, bf16[128,128,128]{2,1,0:T(8,128)(2,1)} %bitcast.17.proj_ref), custom_call_target="tpu_custom_call" | custom-call | tf_op jit(solution)/shard_map/pallas_call | solution.py:130
  123.5 7.2 %shard_map.86 = f32[2,128,128]{2,1,0:T(8,128)} custom-call(s32[1]{0:T(128)} %bitcast.18.core_ref, s32[256]{0:T(256)} %fusion.25.where_ref, s32[8]{0:T(128)} %count_ref.7, bf16[4,2,128,4096]{3,2,1,0:T(8,128)(2,1)} %reshape.59.tiles_ref, bf16[128,128,128]{2,1,0:T(8,128)(2,1)} %collective-permute-done.12.proj_ref), custom_call_target="tpu_custom_call" | custom-call | tf_op jit(solution)/shard_map/pallas_call | solution.py:130
  132.4 7.6 %shard_map.88 = bf16[128,128,128]{2,1,0:T(8,128)(2,1)} custom-call(s32[1]{0:T(128)} %bitcast.18.core_ref, s32[256]{0:T(256)} %fusion.25.where_ref, s32[8]{0:T(128)} %count_ref.7, bf16[4,2,4096,128]{3,2,1,0:T(8,128)(2,1)} %bitcast.112, bf16[2,128,128]{2,1,0:T(8,128)(2,1)} %bitcast.125), custom_call_target="tpu_custom_call" | custom-call | tf_op jit(solution)/shard_map/pallas_call | solution.py:185
  140.5 9.0 %shard_map.87 = f32[128,128,128]{2,1,0:T(8,128)} custom-call(s32[1]{0:T(128)} %bitcast.core_ref, s32[256]{0:T(256)} %fusion.25.where_ref, s32[8]{0:T(128)} %count_ref.7, bf16[4,2,4096,128]{3,2,1,0:T(8,128)(2,1)} %bitcast.113, bf16[2,128,128]{2,1,0:T(8,128)(2,1)} %bitcast.126), custom_call_target="tpu_custom_call" | custom-call | tf_op jit(solution)/shard_map/pallas_call | solution.py:185
  149.5 5.8 %convert_add_fusion = f32[128,128,128]{2,1,0:T(8,128)S(1)} fusion(f32[128,128,128]{2,1,0:T(8,128)} %shard_map.87, bf16[128,128,128]{2,1,0:T(8,128)(2,1)} %collective-permute-done.13), kind=kLoop, calls=%fused_computation.1 | loop fusion | flops 4194304 | bytes 20971520 | tf_op jit(solution)/shard_map/add | solution.py:261
  158.4 6.4 %collective-permute-done.16 = bf16[4,4,128,128]{3,2,1,0:T(8,128)(2,1)S(1)} collective-permute-done((bf16[4,4,128,128]{3,2,1,0:T(8,128)(2,1)S(1)}, bf16[4,4,128,128]{3,2,1,0:T(8,128)(2,1)S(1)}, u32[]{:S(2)}, u32[]{:S(2)}) %collective-permute-start.16) | collective-permute-done | bytes 524320 | tf_op jit(solution)/shard_map/ppermute | solution.py:37
  167.5 12.5 %collective-permute-done.17 = bf16[4,4,256,128]{3,2,1,0:T(8,128)(2,1)S(1)} collective-permute-done((bf16[4,4,256,128]{3,2,1,0:T(8,128)(2,1)S(1)}, bf16[4,4,256,128]{3,2,1,0:T(8,128)(2,1)S(1)}, u32[]{:S(2)}, u32[]{:S(2)}) %collective-permute-start.17) | collective-permute-done | bytes 1048608 | tf_op jit(solution)/shard_map/ppermute | solution.py:37
  180.0 2.7 %collective-permute-done.15 = bf16[4,4,256,128]{3,2,1,0:T(8,128)(2,1)S(1)} collective-permute-done((bf16[4,4,256,128]{3,2,1,0:T(8,128)(2,1)S(1)}, bf16[4,4,256,128]{3,2,1,0:T(8,128)(2,1)S(1)}, u32[]{:S(2)}, u32[]{:S(2)}) %collective-permute-start.15) | collective-permute-done | bytes 1048608 | tf_op jit(solution)/shard_map/ppermute | solution.py:37
  185.4 2.9 %collective-permute-done.20 = bf16[4,128,128]{2,1,0:T(8,128)(2,1)S(1)} collective-permute-done((bf16[4,128,128]{2,1,0:T(8,128)(2,1)S(1)}, bf16[4,128,128]{2,1,0:T(8,128)(2,1)S(1)}, u32[]{:S(2)}, u32[]{:S(2)}) %collective-permute-start.20) | collective-permute-done | bytes 131104 | tf_op jit(solution)/shard_map/ppermute | solution.py:37
  190.7 4.2 %collective-permute-done.21 = bf16[4,256,128]{2,1,0:T(8,128)(2,1)S(1)} collective-permute-done((bf16[4,256,128]{2,1,0:T(8,128)(2,1)S(1)}, bf16[4,256,128]{2,1,0:T(8,128)(2,1)S(1)}, u32[]{:S(2)}, u32[]{:S(2)}) %collective-permute-start.21) | collective-permute-done | bytes 262176 | tf_op jit(solution)/shard_map/ppermute | solution.py:37
  197.5 3.2 %collective-permute-start.24 = (bf16[128,128]{1,0:T(8,128)(2,1)S(1)}, bf16[128,128]{1,0:T(8,128)(2,1)S(1)}, u32[]{:S(2)}, u32[]{:S(2)}) collective-permute-start(bf16[128,128]{1,0:T(8,128)(2,1)S(1)} %get-tuple-element.17), channel_id=1, source_target_pairs={{0,3},{1,0},{2,1},{3,2},{4,7},{5,4},{6,5},{7,6},{8,11},{9,8},{10,9... | collective-permute-start | bytes 98312 | tf_op jit(solution)/shard_map/ppermute | solution.py:37
  202.7 3.3 %collective-permute-start.25 = (bf16[256,128]{1,0:T(8,128)(2,1)S(1)}, bf16[256,128]{1,0:T(8,128)(2,1)S(1)}, u32[]{:S(2)}, u32[]{:S(2)}) collective-permute-start(bf16[256,128]{1,0:T(8,128)(2,1)S(1)} %pad_maximum_fusion.8), channel_id=1, source_target_pairs={{0,3},{1,0},{2,1},{3,2},{4,7},{5,4},{6,5},{7,6},{8,11},{9,8},{10,9... | collective-permute-start | bytes 196616 | tf_op jit(solution)/shard_map/ppermute | solution.py:37
  207.9 3.6 %collective-permute-done.23 = bf16[256,128]{1,0:T(8,128)(2,1)S(1)} collective-permute-done((bf16[256,128]{1,0:T(8,128)(2,1)S(1)}, bf16[256,128]{1,0:T(8,128)(2,1)S(1)}, u32[]{:S(2)}, u32[]{:S(2)}) %collective-permute-start.23) | collective-permute-done | bytes 65568 | tf_op jit(solution)/shard_map/ppermute | solution.py:37
  211.8 3.9 %collective-permute-done.26 = f32[64,128]{1,0:T(8,128)S(1)} collective-permute-done((f32[64,128]{1,0:T(8,128)S(1)}, f32[64,128]{1,0:T(8,128)S(1)}, u32[]{:S(2)}, u32[]{:S(2)}) %collective-permute-start.26) | collective-permute-done | bytes 32800 | tf_op jit(solution)/shard_map/ppermute | solution.py:46
  215.8 5.2 %collective-permute-done.27 = f32[32,128]{1,0:T(8,128)S(1)} collective-permute-done((f32[32,128]{1,0:T(8,128)S(1)}, f32[32,128]{1,0:T(8,128)S(1)}, u32[]{:S(2)}, u32[]{:S(2)}) %collective-permute-start.27) | collective-permute-done | bytes 16416 | tf_op jit(solution)/shard_map/ppermute | solution.py:46
  221.1 3.6 %collective-permute-done.28 = f32[16,128]{1,0:T(8,128)S(1)} collective-permute-done((f32[16,128]{1,0:T(8,128)S(1)}, f32[16,128]{1,0:T(8,128)S(1)}, u32[]{:S(2)}, u32[]{:S(2)}) %collective-permute-start.28) | collective-permute-done | bytes 8224 | tf_op jit(solution)/shard_map/ppermute | solution.py:46
  224.8 5.1 %collective-permute-done.29 = f32[8,128]{1,0:T(8,128)S(1)} collective-permute-done((f32[8,128]{1,0:T(8,128)S(1)}, f32[8,128]{1,0:T(8,128)S(1)}, u32[]{:S(2)}, u32[]{:S(2)}) %collective-permute-start.29) | collective-permute-done | bytes 4128 | tf_op jit(solution)/shard_map/ppermute | solution.py:46
  230.9 3.9 %all-to-all-start.1 = ((bf16[32,4,256]{2,1,0:T(4,128)(2,1)}), bf16[32,4,256]{2,1,0:T(4,128)(2,1)S(1)}, u32[]{:S(2)}, u32[]{:S(2)}) async-start(bf16[32,4,256]{2,1,0:T(4,128)(2,1)} %all_to_all.32), calls=%async_computation.1 | async-start | bytes 131072 | tf_op jit(solution)/shard_map/all_to_all | solution.py:276
  236.4 6.7 %all-to-all-done.1 = bf16[32,4,256]{2,1,0:T(4,128)(2,1)S(1)} async-done(((bf16[32,4,256]{2,1,0:T(4,128)(2,1)}), bf16[32,4,256]{2,1,0:T(4,128)(2,1)S(1)}, u32[]{:S(2)}, u32[]{:S(2)}) %all-to-all-start.1) | async-done | bytes 65568 | tf_op jit(solution)/shard_map/all_to_all | solution.py:276
  (111 shorter events, 40.0 us)
Async XLA Ops:
  18.5 4.3 %collective-permute-start = (bf16[256,128]{1,0:T(8,128)(2,1)S(1)}, bf16[256,128]{1,0:T(8,128)(2,1)S(1)}, u32[]{:S(2)}, u32[]{:S(2)}) collective-permute-start(bf16[256,128]{1,0:T(8,128)(2,1)S(1)} %convolution_convert_fusion.1), channel_id=1, source_target_pairs={{0,3},{1,0},{2,1},{3,2},{4,7},{5,4},{6,5},{7,6},{8,11},{9,8},{10,9... | collective-permute-start | bytes 196616 | tf_op jit(solution)/shard_map/ppermute | solution.py:37
  19.9 5.5 %collective-permute-start.1 = (bf16[256,128]{1,0:T(8,128)(2,1)S(1)}, bf16[256,128]{1,0:T(8,128)(2,1)S(1)}, u32[]{:S(2)}, u32[]{:S(2)}) collective-permute-start(bf16[256,128]{1,0:T(8,128)(2,1)S(1)} %convolution_convert_fusion.1), channel_id=1, source_target_pairs={{0,1},{1,2},{2,3},{3,0},{4,5},{5,6},{6,7},{7,4},{8,9},{9,10},{10,1... | collective-permute-start | bytes 196616 | tf_op jit(solution)/shard_map/ppermute | solution.py:37
  22.8 4.2 %collective-permute-start.3 = (bf16[128,128]{1,0:T(8,128)(2,1)S(1)}, bf16[128,128]{1,0:T(8,128)(2,1)S(1)}, u32[]{:S(2)}, u32[]{:S(2)}) collective-permute-start(bf16[128,128]{1,0:T(8,128)(2,1)S(1)} %slice.216), channel_id=1, source_target_pairs={{0,3},{1,0},{2,1},{3,2},{4,7},{5,4},{6,5},{7,6},{8,11},{9,8},{10,9... | collective-permute-start | bytes 98312 | tf_op jit(solution)/shard_map/ppermute | solution.py:37
  25.4 5.1 %collective-permute-start.2 = (bf16[128,128]{1,0:T(8,128)(2,1)S(1)}, bf16[128,128]{1,0:T(8,128)(2,1)S(1)}, u32[]{:S(2)}, u32[]{:S(2)}) collective-permute-start(bf16[128,128]{1,0:T(8,128)(2,1)S(1)} %slice.215), channel_id=1, source_target_pairs={{0,1},{1,2},{2,3},{3,0},{4,5},{5,6},{6,7},{7,4},{8,9},{9,10},{10,1... | collective-permute-start | bytes 98312 | tf_op jit(solution)/shard_map/ppermute | solution.py:37
  30.6 7.8 %collective-permute-start.4 = (bf16[4,256,128]{2,1,0:T(8,128)(2,1)S(1)}, bf16[4,256,128]{2,1,0:T(8,128)(2,1)S(1)}, u32[]{:S(2)}, u32[]{:S(2)}) collective-permute-start(bf16[4,256,128]{2,1,0:T(8,128)(2,1)S(1)} %get-tuple-element.23), channel_id=1, source_target_pairs={{0,12},{1,13},{2,14},{3,15},{4,0},{5,1},{6,2},{7,3},{8,4},{9,5},{1... | collective-permute-start | bytes 786440 | tf_op jit(solution)/shard_map/ppermute | solution.py:37
  31.9 8.5 %collective-permute-start.5 = (bf16[4,256,128]{2,1,0:T(8,128)(2,1)S(1)}, bf16[4,256,128]{2,1,0:T(8,128)(2,1)S(1)}, u32[]{:S(2)}, u32[]{:S(2)}) collective-permute-start(bf16[4,256,128]{2,1,0:T(8,128)(2,1)S(1)} %get-tuple-element.23), channel_id=1, source_target_pairs={{0,4},{1,5},{2,6},{3,7},{4,8},{5,9},{6,10},{7,11},{8,12},{9,13},{1... | collective-permute-start | bytes 786440 | tf_op jit(solution)/shard_map/ppermute | solution.py:37
  38.4 5.0 %collective-permute-start.7 = (bf16[4,128,128]{2,1,0:T(8,128)(2,1)S(1)}, bf16[4,128,128]{2,1,0:T(8,128)(2,1)S(1)}, u32[]{:S(2)}, u32[]{:S(2)}) collective-permute-start(bf16[4,128,128]{2,1,0:T(8,128)(2,1)S(1)} %slice.218), channel_id=1, source_target_pairs={{0,12},{1,13},{2,14},{3,15},{4,0},{5,1},{6,2},{7,3},{8,4},{9,5},{1... | collective-permute-start | bytes 393224 | tf_op jit(solution)/shard_map/ppermute | solution.py:37
  40.4 6.2 %collective-permute-start.6 = (bf16[4,128,128]{2,1,0:T(8,128)(2,1)S(1)}, bf16[4,128,128]{2,1,0:T(8,128)(2,1)S(1)}, u32[]{:S(2)}, u32[]{:S(2)}) collective-permute-start(bf16[4,128,128]{2,1,0:T(8,128)(2,1)S(1)} %slice.217), channel_id=1, source_target_pairs={{0,4},{1,5},{2,6},{3,7},{4,8},{5,9},{6,10},{7,11},{8,12},{9,13},{1... | collective-permute-start | bytes 393224 | tf_op jit(solution)/shard_map/ppermute | solution.py:37
  46.8 14.9 %collective-permute-start.8 = (bf16[4,4,256,128]{3,2,1,0:T(8,128)(2,1)S(1)}, bf16[4,4,256,128]{3,2,1,0:T(8,128)(2,1)S(1)}, u32[]{:S(2)}, u32[]{:S(2)}) collective-permute-start(bf16[4,4,256,128]{3,2,1,0:T(8,128)(2,1)S(1)} %get-tuple-element.13), channel_id=1, source_target_pairs={{0,80},{1,81},{2,82},{3,83},{4,84},{5,85},{6,86},{7,87},{8,88},{9,... | collective-permute-start | bytes 3145736 | tf_op jit(solution)/shard_map/ppermute | solution.py:37
  49.4 16.1 %collective-permute-start.9 = (bf16[4,4,256,128]{3,2,1,0:T(8,128)(2,1)S(1)}, bf16[4,4,256,128]{3,2,1,0:T(8,128)(2,1)S(1)}, u32[]{:S(2)}, u32[]{:S(2)}) collective-permute-start(bf16[4,4,256,128]{3,2,1,0:T(8,128)(2,1)S(1)} %get-tuple-element.13), channel_id=1, source_target_pairs={{0,16},{1,17},{2,18},{3,19},{4,20},{5,21},{6,22},{7,23},{8,24},{9,... | collective-permute-start | bytes 3145736 | tf_op jit(solution)/shard_map/ppermute | solution.py:37
  61.8 10.5 %collective-permute-start.11 = (bf16[4,4,128,128]{3,2,1,0:T(8,128)(2,1)S(1)}, bf16[4,4,128,128]{3,2,1,0:T(8,128)(2,1)S(1)}, u32[]{:S(2)}, u32[]{:S(2)}) collective-permute-start(bf16[4,4,128,128]{3,2,1,0:T(8,128)(2,1)S(1)} %slice.220), channel_id=1, source_target_pairs={{0,80},{1,81},{2,82},{3,83},{4,84},{5,85},{6,86},{7,87},{8,88},{9,... | collective-permute-start | bytes 1572872 | tf_op jit(solution)/shard_map/ppermute | solution.py:37
  65.6 10.5 %collective-permute-start.10 = (bf16[4,4,128,128]{3,2,1,0:T(8,128)(2,1)S(1)}, bf16[4,4,128,128]{3,2,1,0:T(8,128)(2,1)S(1)}, u32[]{:S(2)}, u32[]{:S(2)}) collective-permute-start(bf16[4,4,128,128]{3,2,1,0:T(8,128)(2,1)S(1)} %slice.219), channel_id=1, source_target_pairs={{0,16},{1,17},{2,18},{3,19},{4,20},{5,21},{6,22},{7,23},{8,24},{9,... | collective-permute-start | bytes 1572872 | tf_op jit(solution)/shard_map/ppermute | solution.py:37
  78.4 45.1 %collective-permute-start.12 = (bf16[128,128,128]{2,1,0:T(8,128)(2,1)}, bf16[128,128,128]{2,1,0:T(8,128)(2,1)}, u32[]{:S(2)}, u32[]{:S(2)}) collective-permute-start(bf16[128,128,128]{2,1,0:T(8,128)(2,1)} %bitcast.17.proj_ref), channel_id=1, source_target_pairs={{0,32},{32,0},{64,96},{96,64},{1,33},{33,1},{65,97},{97,65},{2,34}... | collective-permute-start | bytes 12582920 | tf_op jit(solution)/shard_map/ppermute | solution.py:41
  139.9 9.6 %collective-permute-start.13 = (bf16[128,128,128]{2,1,0:T(8,128)(2,1)}, bf16[128,128,128]{2,1,0:T(8,128)(2,1)}, u32[]{:S(2)}, u32[]{:S(2)}) collective-permute-start(bf16[128,128,128]{2,1,0:T(8,128)(2,1)} %shard_map.88), channel_id=1, source_target_pairs={{0,32},{32,0},{64,96},{96,64},{1,33},{33,1},{65,97},{97,65},{2,34}... | collective-permute-start | bytes 12582920 | tf_op jit(solution)/shard_map/ppermute | solution.py:41
  155.6 9.2 %collective-permute-start.16 = (bf16[4,4,128,128]{3,2,1,0:T(8,128)(2,1)S(1)}, bf16[4,4,128,128]{3,2,1,0:T(8,128)(2,1)S(1)}, u32[]{:S(2)}, u32[]{:S(2)}) collective-permute-start(bf16[4,4,128,128]{3,2,1,0:T(8,128)(2,1)S(1)} %get-tuple-element.11), channel_id=1, source_target_pairs={{0,80},{1,81},{2,82},{3,83},{4,84},{5,85},{6,86},{7,87},{8,88},{9,... | collective-permute-start | bytes 1572872 | tf_op jit(solution)/shard_map/ppermute | solution.py:37
  155.7 10.7 %collective-permute-start.14 = (bf16[4,4,128,128]{3,2,1,0:T(8,128)(2,1)S(1)}, bf16[4,4,128,128]{3,2,1,0:T(8,128)(2,1)S(1)}, u32[]{:S(2)}, u32[]{:S(2)}) collective-permute-start(bf16[4,4,128,128]{3,2,1,0:T(8,128)(2,1)S(1)} %get-tuple-element.10), channel_id=1, source_target_pairs={{0,16},{1,17},{2,18},{3,19},{4,20},{5,21},{6,22},{7,23},{8,24},{9,... | collective-permute-start | bytes 1572872 | tf_op jit(solution)/shard_map/ppermute | solution.py:37
  165.1 14.9 %collective-permute-start.17 = (bf16[4,4,256,128]{3,2,1,0:T(8,128)(2,1)S(1)}, bf16[4,4,256,128]{3,2,1,0:T(8,128)(2,1)S(1)}, u32[]{:S(2)}, u32[]{:S(2)}) collective-permute-start(bf16[4,4,256,128]{3,2,1,0:T(8,128)(2,1)S(1)} %pad_maximum_fusion.3), channel_id=1, source_target_pairs={{0,80},{1,81},{2,82},{3,83},{4,84},{5,85},{6,86},{7,87},{8,88},{9,... | collective-permute-start | bytes 3145736 | tf_op jit(solution)/shard_map/ppermute | solution.py:37
  166.6 16.1 %collective-permute-start.15 = (bf16[4,4,256,128]{3,2,1,0:T(8,128)(2,1)S(1)}, bf16[4,4,256,128]{3,2,1,0:T(8,128)(2,1)S(1)}, u32[]{:S(2)}, u32[]{:S(2)}) collective-permute-start(bf16[4,4,256,128]{3,2,1,0:T(8,128)(2,1)S(1)} %pad_maximum_fusion.2), channel_id=1, source_target_pairs={{0,16},{1,17},{2,18},{3,19},{4,20},{5,21},{6,22},{7,23},{8,24},{9,... | collective-permute-start | bytes 3145736 | tf_op jit(solution)/shard_map/ppermute | solution.py:37
  183.1 5.2 %collective-permute-start.20 = (bf16[4,128,128]{2,1,0:T(8,128)(2,1)S(1)}, bf16[4,128,128]{2,1,0:T(8,128)(2,1)S(1)}, u32[]{:S(2)}, u32[]{:S(2)}) collective-permute-start(bf16[4,128,128]{2,1,0:T(8,128)(2,1)S(1)} %get-tuple-element.21), channel_id=1, source_target_pairs={{0,12},{1,13},{2,14},{3,15},{4,0},{5,1},{6,2},{7,3},{8,4},{9,5},{1... | collective-permute-start | bytes 393224 | tf_op jit(solution)/shard_map/ppermute | solution.py:37
  183.3 6.2 %collective-permute-start.18 = (bf16[4,128,128]{2,1,0:T(8,128)(2,1)S(1)}, bf16[4,128,128]{2,1,0:T(8,128)(2,1)S(1)}, u32[]{:S(2)}, u32[]{:S(2)}) collective-permute-start(bf16[4,128,128]{2,1,0:T(8,128)(2,1)S(1)} %get-tuple-element.20), channel_id=1, source_target_pairs={{0,4},{1,5},{2,6},{3,7},{4,8},{5,9},{6,10},{7,11},{8,12},{9,13},{1... | collective-permute-start | bytes 393224 | tf_op jit(solution)/shard_map/ppermute | solution.py:37
  188.4 6.4 %collective-permute-start.21 = (bf16[4,256,128]{2,1,0:T(8,128)(2,1)S(1)}, bf16[4,256,128]{2,1,0:T(8,128)(2,1)S(1)}, u32[]{:S(2)}, u32[]{:S(2)}) collective-permute-start(bf16[4,256,128]{2,1,0:T(8,128)(2,1)S(1)} %pad_maximum_fusion.6), channel_id=1, source_target_pairs={{0,12},{1,13},{2,14},{3,15},{4,0},{5,1},{6,2},{7,3},{8,4},{9,5},{1... | collective-permute-start | bytes 786440 | tf_op jit(solution)/shard_map/ppermute | solution.py:37
  189.7 7.7 %collective-permute-start.19 = (bf16[4,256,128]{2,1,0:T(8,128)(2,1)S(1)}, bf16[4,256,128]{2,1,0:T(8,128)(2,1)S(1)}, u32[]{:S(2)}, u32[]{:S(2)}) collective-permute-start(bf16[4,256,128]{2,1,0:T(8,128)(2,1)S(1)} %pad_maximum_fusion.5), channel_id=1, source_target_pairs={{0,4},{1,5},{2,6},{3,7},{4,8},{5,9},{6,10},{7,11},{8,12},{9,13},{1... | collective-permute-start | bytes 786440 | tf_op jit(solution)/shard_map/ppermute | solution.py:37
  197.4 5.2 %collective-permute-start.22 = (bf16[128,128]{1,0:T(8,128)(2,1)S(1)}, bf16[128,128]{1,0:T(8,128)(2,1)S(1)}, u32[]{:S(2)}, u32[]{:S(2)}) collective-permute-start(bf16[128,128]{1,0:T(8,128)(2,1)S(1)} %get-tuple-element.16), channel_id=1, source_target_pairs={{0,1},{1,2},{2,3},{3,0},{4,5},{5,6},{6,7},{7,4},{8,9},{9,10},{10,1... | collective-permute-start | bytes 98312 | tf_op jit(solution)/shard_map/ppermute | solution.py:37
  197.5 5.1 %collective-permute-start.24 = (bf16[128,128]{1,0:T(8,128)(2,1)S(1)}, bf16[128,128]{1,0:T(8,128)(2,1)S(1)}, u32[]{:S(2)}, u32[]{:S(2)}) collective-permute-start(bf16[128,128]{1,0:T(8,128)(2,1)S(1)} %get-tuple-element.17), channel_id=1, source_target_pairs={{0,3},{1,0},{2,1},{3,2},{4,7},{5,4},{6,5},{7,6},{8,11},{9,8},{10,9... | collective-permute-start | bytes 98312 | tf_op jit(solution)/shard_map/ppermute | solution.py:37
  202.7 5.2 %collective-permute-start.25 = (bf16[256,128]{1,0:T(8,128)(2,1)S(1)}, bf16[256,128]{1,0:T(8,128)(2,1)S(1)}, u32[]{:S(2)}, u32[]{:S(2)}) collective-permute-start(bf16[256,128]{1,0:T(8,128)(2,1)S(1)} %pad_maximum_fusion.8), channel_id=1, source_target_pairs={{0,3},{1,0},{2,1},{3,2},{4,7},{5,4},{6,5},{7,6},{8,11},{9,8},{10,9... | collective-permute-start | bytes 196616 | tf_op jit(solution)/shard_map/ppermute | solution.py:37
  206.0 5.5 %collective-permute-start.23 = (bf16[256,128]{1,0:T(8,128)(2,1)S(1)}, bf16[256,128]{1,0:T(8,128)(2,1)S(1)}, u32[]{:S(2)}, u32[]{:S(2)}) collective-permute-start(bf16[256,128]{1,0:T(8,128)(2,1)S(1)} %pad_maximum_fusion.7), channel_id=1, source_target_pairs={{0,1},{1,2},{2,3},{3,0},{4,5},{5,6},{6,7},{7,4},{8,9},{9,10},{10,1... | collective-permute-start | bytes 196616 | tf_op jit(solution)/shard_map/ppermute | solution.py:37
  211.7 4.0 %collective-permute-start.26 = (f32[64,128]{1,0:T(8,128)S(1)}, f32[64,128]{1,0:T(8,128)S(1)}, u32[]{:S(2)}, u32[]{:S(2)}) collective-permute-start(f32[64,128]{1,0:T(8,128)S(1)} %slice_select_fusion), channel_id=1, source_target_pairs={{0,16},{1,17},{2,18},{3,19},{4,20},{5,21},{6,22},{7,23},{8,24},{9,... | collective-permute-start | bytes 98312 | tf_op jit(solution)/shard_map/ppermute | solution.py:46
  215.7 5.3 %collective-permute-start.27 = (f32[32,128]{1,0:T(8,128)S(1)}, f32[32,128]{1,0:T(8,128)S(1)}, u32[]{:S(2)}, u32[]{:S(2)}) collective-permute-start(f32[32,128]{1,0:T(8,128)S(1)} %slice_select_fusion.1), channel_id=1, source_target_pairs={{0,8},{1,9},{2,10},{3,11},{4,12},{5,13},{6,14},{7,15},{8,0},{9,1},... | collective-permute-start | bytes 49160 | tf_op jit(solution)/shard_map/ppermute | solution.py:46
  224.7 5.2 %collective-permute-start.29 = (f32[8,128]{1,0:T(8,128)S(1)}, f32[8,128]{1,0:T(8,128)S(1)}, u32[]{:S(2)}, u32[]{:S(2)}) collective-permute-start(f32[8,128]{1,0:T(8,128)S(1)} %slice_select_fusion.3), channel_id=1, source_target_pairs={{0,2},{1,3},{2,0},{3,1},{4,6},{5,7},{6,4},{7,5},{8,10},{9,11},{10,... | collective-permute-start | bytes 12296 | tf_op jit(solution)/shard_map/ppermute | solution.py:46
  229.9 4.8 %collective-permute-start.30 = (f32[4,128]{1,0:T(4,128)S(1)}, f32[4,128]{1,0:T(4,128)S(1)}, u32[]{:S(2)}, u32[]{:S(2)}) collective-permute-start(f32[4,128]{1,0:T(4,128)S(1)} %slice_select_fusion.4), channel_id=1, source_target_pairs={{0,1},{1,0},{2,3},{3,2},{4,5},{5,4},{6,7},{7,6},{8,9},{9,8},{10,11... | collective-permute-start | bytes 6152 | tf_op jit(solution)/shard_map/ppermute | solution.py:46
  230.9 12.2 %all-to-all-start.1 = ((bf16[32,4,256]{2,1,0:T(4,128)(2,1)}), bf16[32,4,256]{2,1,0:T(4,128)(2,1)S(1)}, u32[]{:S(2)}, u32[]{:S(2)}) async-start(bf16[32,4,256]{2,1,0:T(4,128)(2,1)} %all_to_all.32), calls=%async_computation.1 | async-start | bytes 131072 | tf_op jit(solution)/shard_map/all_to_all | solution.py:276
  236.0 7.1 %collective-permute-start.32 = (f32[4,128]{1,0:T(4,128)S(1)}, f32[4,128]{1,0:T(4,128)S(1)}, u32[]{:S(2)}, u32[]{:S(2)}) collective-permute-start(f32[4,128]{1,0:T(4,128)S(1)} %add.204), channel_id=1, source_target_pairs={{0,64},{32,96},{64,0},{96,32},{1,65},{33,97},{65,1},{97,33},{2,66}... | collective-permute-start | bytes 6152 | tf_op jit(solution)/shard_map/ppermute | solution.py:46
  (6 other events, 51.2 us)

commit v5 on v3

--- a/solution.py
+++ b/solution.py
@@ -90,19 +90,20 @@
     return total
 
 
-def aggregate_kernel(core_ref, where_ref, count_ref, tiles_ref, proj_ref, out_ref):
+def aggregate_kernel(core_ref, where_ref, count_ref, tiles_ref, proj_ref, out_ref, wide_ref, picked_ref):
     row = pl.program_id(0)
     half_id = pl.program_id(1)
     tile_rows = pl.num_programs(0)
-    slot_count = tiles_ref.shape[0]
+    slot_count, tile_size, _ = tiles_ref.shape
     base = (half_id * 2 + core_ref[0]) * tile_rows + row
     live = count_ref[base]
-
-    def step(slot, total):
-        spot = where_ref[base * slot_count + slot]
-        return total + jnp.dot(tiles_ref[slot], proj_ref[spot], preferred_element_type=jnp.float32)
-
-    part = lax.fori_loop(0, live, step, jnp.zeros(out_ref.shape, jnp.float32))
+    for slot in range(slot_count):
+        wide_ref[:, slot * tile_size:(slot + 1) * tile_size] = tiles_ref[slot]
+        piece = proj_ref[where_ref[base * slot_count + slot]]
+        picked_ref[slot * tile_size:(slot + 1) * tile_size, :] = jnp.where(
+            slot < live, piece, jnp.zeros_like(piece)
+        )
+    part = jnp.dot(wide_ref[...], picked_ref[...], preferred_element_type=jnp.float32)
 
     @pl.when(half_id == 0)
     def _():
@@ -127,6 +128,10 @@
             pl.BlockSpec(buffer.shape, lambda r, h, c, w, n: (0, 0, 0)),
         ],
         out_specs=pl.BlockSpec((None, tile_size, hidden_width), lambda r, h, c, w, n: (r, 0, 0)),
+        scratch_shapes=[
+            pltpu.VMEM((tile_size, slot_count * tile_size), tile_stack.dtype),
+            pltpu.VMEM((slot_count * tile_size, hidden_width), buffer.dtype),
+        ],
     )
     return pl.pallas_call(
         aggregate_kernel,
@@ -136,12 +141,14 @@
     )(jnp.reshape(core_id, (1,)).astype(jnp.int32), spots, counts, tile_stack, buffer)
 
 
-def spread_kernel(core_ref, where_ref, count_ref, tiles_ref, grad_ref, out_ref, total_ref):
+def spread_kernel(
+    core_ref, where_ref, count_ref, tiles_ref, grad_ref, out_ref, total_ref, wide_ref, terms_ref
+):
     row = pl.program_id(0)
     half_id = pl.program_id(1)
     tile_rows = pl.num_programs(0)
     halves = pl.num_programs(1)
-    slot_count = tiles_ref.shape[0]
+    slot_count, tile_size, _ = tiles_ref.shape
     base = (half_id * 2 + core_ref[0]) * tile_rows + row
     live = count_ref[base]
 
@@ -149,26 +156,24 @@
     def _():
         total_ref[...] = jnp.zeros(total_ref.shape, jnp.float32)
 
-    grad_rows = grad_ref[...]
-
-    def step(slot, carry):
+    for slot in range(slot_count):
+        wide_ref[:, slot * tile_size:(slot + 1) * tile_size] = tiles_ref[slot]
+    terms_ref[...] = jnp.dot(grad_ref[...], wide_ref[...], preferred_element_type=jnp.float32)
+    for slot in range(slot_count):
         spot = where_ref[base * slot_count + slot]
-        total_ref[spot] += lax.dot_general(
-            tiles_ref[slot], grad_rows, (((0,), (0,)), ((), ())),
-            preferred_element_type=jnp.float32,
-        )
-        return carry
-
-    lax.fori_loop(0, live, step, 0)
+
+        @pl.when(slot < live)
+        def _():
+            total_ref[spot] += terms_ref[:, slot * tile_size:(slot + 1) * tile_size]
 
     @pl.when((row == tile_rows - 1) & (half_id == halves - 1))
     def _():
         out_ref[...] = total_ref[...].astype(out_ref.dtype)
 
 
-def spread_pair(core_id, spots, counts, tile_stack, grad_tiles, buffer_tiles, out_type):
+def spread_pair(core_id, spots, counts, tile_stack, grad_turned, buffer_tiles, out_type):
     blocks, tile_rows, slot_count, tile_size, _ = tile_stack.shape
-    hidden_width = grad_tiles.shape[-1]
+    hidden_width = grad_turned.shape[1]
     grid_spec = pltpu.PrefetchScalarGridSpec(
         num_scalar_prefetch=3,
         grid=(tile_rows, blocks // 2),
@@ -177,19 +182,23 @@
                 (None, None, slot_count, tile_size, tile_size),
                 lambda r, h, c, w, n: (h * 2 + c[0], r, 0, 0, 0),
             ),
-            pl.BlockSpec((None, tile_size, hidden_width), lambda r, h, c, w, n: (r, 0, 0)),
+            pl.BlockSpec((None, hidden_width, tile_size), lambda r, h, c, w, n: (r, 0, 0)),
         ],
         out_specs=pl.BlockSpec(
-            (buffer_tiles, tile_size, hidden_width), lambda r, h, c, w, n: (0, 0, 0)
+            (buffer_tiles, hidden_width, tile_size), lambda r, h, c, w, n: (0, 0, 0)
         ),
-        scratch_shapes=[pltpu.VMEM((buffer_tiles, tile_size, hidden_width), jnp.float32)],
+        scratch_shapes=[
+            pltpu.VMEM((buffer_tiles, hidden_width, tile_size), jnp.float32),
+            pltpu.VMEM((tile_size, slot_count * tile_size), tile_stack.dtype),
+            pltpu.VMEM((hidden_width, slot_count * tile_size), jnp.float32),
+        ],
     )
     return pl.pallas_call(
         spread_kernel,
         grid_spec=grid_spec,
-        out_shape=jax.ShapeDtypeStruct((buffer_tiles, tile_size, hidden_width), out_type),
+        out_shape=jax.ShapeDtypeStruct((buffer_tiles, hidden_width, tile_size), out_type),
         compiler_params=pltpu.CompilerParams(dimension_semantics=("arbitrary", "arbitrary")),
-    )(jnp.reshape(core_id, (1,)).astype(jnp.int32), spots, counts, tile_stack, grad_tiles)
+    )(jnp.reshape(core_id, (1,)).astype(jnp.int32), spots, counts, tile_stack, grad_turned)
 
 
 def buffer_spots(tile_col, blk_id, feat_id, block_tiles, tiles_per_device):
@@ -245,20 +254,25 @@
     grad_pre = (
         grad_out.astype(jnp.float32) * sigmoid_y * (1.0 + pre_act * (1.0 - sigmoid_y))
     ).astype(jnp.bfloat16)
-    grad_tiles = grad_pre.reshape(tile_rows, tile_size, hidden_width)
+    grad_turned = grad_pre.reshape(tile_rows, tile_size, hidden_width).transpose(0, 2, 1)
 
     outgoing = spread_pair(
-        1 - core_id, spots, tile_count, tile_stack, grad_tiles, buffer_tiles, jnp.bfloat16
+        1 - core_id, spots, tile_count, tile_stack, grad_turned, buffer_tiles, jnp.bfloat16
     )
     arrived = sibling(outgoing)
     total = spread_pair(
-        core_id, spots, tile_count, tile_stack, grad_tiles, buffer_tiles, jnp.float32
+        core_id, spots, tile_count, tile_stack, grad_turned, buffer_tiles, jnp.float32
     )
     total = total + arrived.astype(jnp.float32)
     total = total.reshape(RING, RING, RING, rows_own, hidden_width)
     for phase in (2, 1, 0):
         total = reduce_phase(total, phase, jnp.bfloat16)
-    grad_hidden = total.astype(jnp.bfloat16)
+    grad_hidden = (
+        total.reshape(tile_rows, hidden_width, tile_size)
+        .transpose(0, 2, 1)
+        .reshape(rows_own, hidden_width)
+        .astype(jnp.bfloat16)
+    )
 
     weight_term = jnp.dot(features_own, grad_hidden, preferred_element_type=jnp.float32)
     weight_part = scatter_rows(weight_term, "feat", jnp.float32)

time: 264 us -> 211 us (0.80)
  starting transfers between devices: 92.2 us -> 36.7 us
  waiting for transfers between devices: 101 us -> 106 us
    ppermute x24, starting transfers between devices: 84.4 us -> 30.7 us  [ring_shift(): return lax.ppermute(block, BOTH, route)]
    all_to_all x1, waiting for transfers between devices: 3.65 us -> 6.3 us  [body(): lax.all_to_all(features_grad_local, 'feat', split_axis=0, concat_axis=1,...]
  transfers between devices with their start and end apart: 34 -> 34, of which waited for: 24 -> 25; matrix products, arithmetic and copies ran while one was open for 1% -> 1% of each run, Pallas kernels for 7% -> 8%
where the time goes in v5:
time: 211 us
  waiting for transfers between devices  106 us (50%)
  starting transfers between devices  36.7 us (17%)
  Pallas kernels  33.4 us (16%)
  blocking collectives  17.6 us (8%)
  other arithmetic  12.4 us (6%)
  local copies, waits for them, and re-layouts  3.41 us (2%)
    ppermute x24, waiting for transfers between devices, ring_shift(): return lax.ppermute(block, BOTH, route)  81.1 us
    ppermute x24, starting transfers between devices, ring_shift(): return lax.ppermute(block, BOTH, route)  30.7 us
    ppermute x7, waiting for transfers between devices, swapped(): return lax.ppermute(block, axis, [(i, i ^ mask) for i in range(count)])  18.7 us
    pallas_call x2, Pallas kernels, spread_pair(): pl.pallas_call(spread_kernel, grid_spec=grid_spec, out_shape=jax.ShapeDty...  18.1 us
    all_to_all x1, blocking collectives, body(): lax.all_to_all(features_t, 'feat', split_axis=1, concat_axis=0, tiled=True)  17.6 us
    pallas_call x2, Pallas kernels, aggregate_pair(): pl.pallas_call(aggregate_kernel, grid_spec=grid_spec, out_shape=jax.Shape...  15.3 us
    all_to_all x1, waiting for transfers between devices, body(): lax.all_to_all(features_grad_local, 'feat', split_axis=0, concat_axis=1,...  6.3 us
    add x1, other arithmetic, body(): total = total + arrived.astype(jnp.float32)  5.84 us
  transfers between devices with their start and end apart: 34, of which 25 were waited for; matrix products, arithmetic and copies ran while one was open for 1% of the time, Pallas kernels for 8%

profile of v5, /device:TPU:0, one launch (start us, length us, event | category | flops | bytes accessed | tf_op | source)
XLA Modules:
  0.0 211.3 jit_solution(1009837472226632241)
XLA Ops:
  0.6 17.6 %all_to_all.38 = bf16[4,32,256]{2,0,1:T(4,128)(2,1)S(1)} all-to-all(bf16[4,32,256]{2,0,1:T(4,128)(2,1)} %bitcast.134), channel_id=1, replica_groups=mesh['blk'=4,'feat'=32] {'feat'}, dimensions={1} | all-to-all | bytes 131072 | tf_op jit(solution)/shard_map/all_to_all | solution.py:236
  19.1 2.7 %collective-permute-start = (bf16[256,128]{1,0:T(8,128)(2,1)S(1)}, bf16[256,128]{1,0:T(8,128)(2,1)S(1)}, u32[]{:S(2)}, u32[]{:S(2)}) collective-permute-start(bf16[256,128]{1,0:T(8,128)(2,1)S(1)} %convolution_convert_fusion.1), channel_id=1, source_target_pairs={{0,3},{1,0},{2,1},{3,2},{4,7},{5,4},{6,5},{7,6},{8,11},{9,8},{10,9... | collective-permute-start | bytes 196616 | tf_op jit(solution)/shard_map/ppermute | solution.py:37
  21.8 2.2 %collective-permute-done.1 = bf16[256,128]{1,0:T(8,128)(2,1)S(1)} collective-permute-done((bf16[256,128]{1,0:T(8,128)(2,1)S(1)}, bf16[256,128]{1,0:T(8,128)(2,1)S(1)}, u32[]{:S(2)}, u32[]{:S(2)}) %collective-permute-start.1) | collective-permute-done | bytes 65568 | tf_op jit(solution)/shard_map/ppermute | solution.py:37
  24.0 3.2 %collective-permute-start.3 = (bf16[128,128]{1,0:T(8,128)(2,1)S(1)}, bf16[128,128]{1,0:T(8,128)(2,1)S(1)}, u32[]{:S(2)}, u32[]{:S(2)}) collective-permute-start(bf16[128,128]{1,0:T(8,128)(2,1)S(1)} %slice.216), channel_id=1, source_target_pairs={{0,3},{1,0},{2,1},{3,2},{4,7},{5,4},{6,5},{7,6},{8,11},{9,8},{10,9... | collective-permute-start | bytes 98312 | tf_op jit(solution)/shard_map/ppermute | solution.py:37
  31.3 5.8 %collective-permute-done.4 = bf16[4,256,128]{2,1,0:T(8,128)(2,1)S(1)} collective-permute-done((bf16[4,256,128]{2,1,0:T(8,128)(2,1)S(1)}, bf16[4,256,128]{2,1,0:T(8,128)(2,1)S(1)}, u32[]{:S(2)}, u32[]{:S(2)}) %collective-permute-start.4) | collective-permute-done | bytes 262176 | tf_op jit(solution)/shard_map/ppermute | solution.py:37
  39.5 2.7 %collective-permute-done.7 = bf16[4,128,128]{2,1,0:T(8,128)(2,1)S(1)} collective-permute-done((bf16[4,128,128]{2,1,0:T(8,128)(2,1)S(1)}, bf16[4,128,128]{2,1,0:T(8,128)(2,1)S(1)}, u32[]{:S(2)}, u32[]{:S(2)}) %collective-permute-start.7) | collective-permute-done | bytes 131104 | tf_op jit(solution)/shard_map/ppermute | solution.py:37
  42.1 3.5 %collective-permute-done.6 = bf16[4,128,128]{2,1,0:T(8,128)(2,1)S(1)} collective-permute-done((bf16[4,128,128]{2,1,0:T(8,128)(2,1)S(1)}, bf16[4,128,128]{2,1,0:T(8,128)(2,1)S(1)}, u32[]{:S(2)}, u32[]{:S(2)}) %collective-permute-start.6) | collective-permute-done | bytes 131104 | tf_op jit(solution)/shard_map/ppermute | solution.py:37
  47.9 12.8 %collective-permute-done.8 = bf16[4,4,256,128]{3,2,1,0:T(8,128)(2,1)S(1)} collective-permute-done((bf16[4,4,256,128]{3,2,1,0:T(8,128)(2,1)S(1)}, bf16[4,4,256,128]{3,2,1,0:T(8,128)(2,1)S(1)}, u32[]{:S(2)}, u32[]{:S(2)}) %collective-permute-start.8) | collective-permute-done | bytes 1048608 | tf_op jit(solution)/shard_map/ppermute | solution.py:37
  60.7 2.3 %collective-permute-start.11 = (bf16[4,4,128,128]{3,2,1,0:T(8,128)(2,1)S(1)}, bf16[4,4,128,128]{3,2,1,0:T(8,128)(2,1)S(1)}, u32[]{:S(2)}, u32[]{:S(2)}) collective-permute-start(bf16[4,4,128,128]{3,2,1,0:T(8,128)(2,1)S(1)} %slice.220), channel_id=1, source_target_pairs={{0,80},{1,81},{2,82},{3,83},{4,84},{5,85},{6,86},{7,87},{8,88},{9,... | collective-permute-start | bytes 1572872 | tf_op jit(solution)/shard_map/ppermute | solution.py:37
  63.1 6.8 %collective-permute-done.11 = bf16[4,4,128,128]{3,2,1,0:T(8,128)(2,1)S(1)} collective-permute-done((bf16[4,4,128,128]{3,2,1,0:T(8,128)(2,1)S(1)}, bf16[4,4,128,128]{3,2,1,0:T(8,128)(2,1)S(1)}, u32[]{:S(2)}, u32[]{:S(2)}) %collective-permute-start.11) | collective-permute-done | bytes 524320 | tf_op jit(solution)/shard_map/ppermute | solution.py:37
  70.0 3.5 %collective-permute-done.10 = bf16[4,4,128,128]{3,2,1,0:T(8,128)(2,1)S(1)} collective-permute-done((bf16[4,4,128,128]{3,2,1,0:T(8,128)(2,1)S(1)}, bf16[4,4,128,128]{3,2,1,0:T(8,128)(2,1)S(1)}, u32[]{:S(2)}, u32[]{:S(2)}) %collective-permute-start.10) | collective-permute-done | bytes 524320 | tf_op jit(solution)/shard_map/ppermute | solution.py:37
  73.6 2.3 %pad_maximum_fusion = bf16[4,4,4,256,128]{4,3,2,1,0:T(8,128)(2,1)} fusion(bf16[1,4,4,256,128]{4,3,2,1,0:T(8,128)(2,1)S(1)} %bitcast.120, bf16[1,4,4,256,128]{4,3,2,1,0:T(8,128)(2,1)S(1)} %maximum_bitcast_fusion, bf16[1,4,4,256,128]{4,3,2,1,0:T(8,128)(2,1)S(1)} %bitcast.119, bf16[1,4,4,256,128]{4,3,2,1,0:T(8,128)(2,1)S(1)} %get-tuple-element.12), kind=kLoop, calls=%fused_computation.1 | loop fusion | flops 6291456 | bytes 8388608 | tf_op jit(solution)/shard_map/stack | solution.py:56
  76.6 7.6 %shard_map.85 = f32[2,128,128]{2,1,0:T(8,128)} custom-call(s32[1]{0:T(128)} %bitcast.core_ref, s32[256]{0:T(256)} %fusion.25.where_ref, s32[8]{0:T(128)} %count_ref.7, bf16[4,2,32,128,128]{4,3,2,1,0:T(8,128)(2,1)} %bitcast.109, bf16[128,128,128]{2,1,0:T(8,128)(2,1)} %bitcast.16.proj_ref), custom_call_target="tpu_custom_call" | custom-call | tf_op jit(solution)/shard_map/pallas_call | solution.py:136
  84.2 7.7 %shard_map.86 = f32[2,128,128]{2,1,0:T(8,128)} custom-call(s32[1]{0:T(128)} %bitcast.17.core_ref, s32[256]{0:T(256)} %fusion.25.where_ref, s32[8]{0:T(128)} %count_ref.7, bf16[4,2,32,128,128]{4,3,2,1,0:T(8,128)(2,1)} %bitcast.110, bf16[128,128,128]{2,1,0:T(8,128)(2,1)} %collective-permute-done.12.proj_ref), custom_call_target="tpu_custom_call" | custom-call | tf_op jit(solution)/shard_map/pallas_call | solution.py:136
  94.2 8.3 %shard_map.88 = bf16[128,128,128]{2,1,0:T(8,128)(2,1)} custom-call(s32[1]{0:T(128)} %bitcast.17.core_ref, s32[256]{0:T(256)} %fusion.25.where_ref, s32[8]{0:T(128)} %count_ref.7, bf16[4,2,32,128,128]{4,3,2,1,0:T(8,128)(2,1)} %bitcast.111, bf16[2,128,128]{2,1,0:T(8,128)(2,1)} %bitcast.121), custom_call_target="tpu_custom_call" | custom-call | tf_op jit(solution)/shard_map/pallas_call | solution.py:196
  103.2 9.7 %shard_map.87 = f32[128,128,128]{2,1,0:T(8,128)} custom-call(s32[1]{0:T(128)} %bitcast.core_ref, s32[256]{0:T(256)} %fusion.25.where_ref, s32[8]{0:T(128)} %count_ref.7, bf16[4,2,32,128,128]{4,3,2,1,0:T(8,128)(2,1)} %bitcast.112, bf16[2,128,128]{2,1,0:T(8,128)(2,1)} %bitcast.122), custom_call_target="tpu_custom_call" | custom-call | tf_op jit(solution)/shard_map/pallas_call | solution.py:196
  112.9 5.8 %convert_add_fusion = f32[128,128,128]{2,1,0:T(8,128)S(1)} fusion(f32[128,128,128]{2,1,0:T(8,128)} %shard_map.87, bf16[128,128,128]{2,1,0:T(8,128)(2,1)} %collective-permute-done.13), kind=kLoop, calls=%fused_computation | loop fusion | flops 4194304 | bytes 20971520 | tf_op jit(solution)/shard_map/add | solution.py:266
  121.8 6.4 %collective-permute-done.16 = bf16[4,4,128,128]{3,2,1,0:T(8,128)(2,1)S(1)} collective-permute-done((bf16[4,4,128,128]{3,2,1,0:T(8,128)(2,1)S(1)}, bf16[4,4,128,128]{3,2,1,0:T(8,128)(2,1)S(1)}, u32[]{:S(2)}, u32[]{:S(2)}) %collective-permute-start.16) | collective-permute-done | bytes 524320 | tf_op jit(solution)/shard_map/ppermute | solution.py:37
  130.9 12.4 %collective-permute-done.17 = bf16[4,4,256,128]{3,2,1,0:T(8,128)(2,1)S(1)} collective-permute-done((bf16[4,4,256,128]{3,2,1,0:T(8,128)(2,1)S(1)}, bf16[4,4,256,128]{3,2,1,0:T(8,128)(2,1)S(1)}, u32[]{:S(2)}, u32[]{:S(2)}) %collective-permute-start.17) | collective-permute-done | bytes 1048608 | tf_op jit(solution)/shard_map/ppermute | solution.py:37
  143.4 3.6 %collective-permute-done.15 = bf16[4,4,256,128]{3,2,1,0:T(8,128)(2,1)S(1)} collective-permute-done((bf16[4,4,256,128]{3,2,1,0:T(8,128)(2,1)S(1)}, bf16[4,4,256,128]{3,2,1,0:T(8,128)(2,1)S(1)}, u32[]{:S(2)}, u32[]{:S(2)}) %collective-permute-start.15) | collective-permute-done | bytes 1048608 | tf_op jit(solution)/shard_map/ppermute | solution.py:37
  149.6 2.8 %collective-permute-done.20 = bf16[4,128,128]{2,1,0:T(8,128)(2,1)S(1)} collective-permute-done((bf16[4,128,128]{2,1,0:T(8,128)(2,1)S(1)}, bf16[4,128,128]{2,1,0:T(8,128)(2,1)S(1)}, u32[]{:S(2)}, u32[]{:S(2)}) %collective-permute-start.20) | collective-permute-done | bytes 131104 | tf_op jit(solution)/shard_map/ppermute | solution.py:37
  155.1 6.3 %collective-permute-done.21 = bf16[4,256,128]{2,1,0:T(8,128)(2,1)S(1)} collective-permute-done((bf16[4,256,128]{2,1,0:T(8,128)(2,1)S(1)}, bf16[4,256,128]{2,1,0:T(8,128)(2,1)S(1)}, u32[]{:S(2)}, u32[]{:S(2)}) %collective-permute-start.21) | collective-permute-done | bytes 262176 | tf_op jit(solution)/shard_map/ppermute | solution.py:37
  161.4 2.8 %collective-permute-done.19 = bf16[4,256,128]{2,1,0:T(8,128)(2,1)S(1)} collective-permute-done((bf16[4,256,128]{2,1,0:T(8,128)(2,1)S(1)}, bf16[4,256,128]{2,1,0:T(8,128)(2,1)S(1)}, u32[]{:S(2)}, u32[]{:S(2)}) %collective-permute-start.19) | collective-permute-done | bytes 262176 | tf_op jit(solution)/shard_map/ppermute | solution.py:37
  164.4 3.2 %collective-permute-start.24 = (bf16[128,128]{1,0:T(8,128)(2,1)S(1)}, bf16[128,128]{1,0:T(8,128)(2,1)S(1)}, u32[]{:S(2)}, u32[]{:S(2)}) collective-permute-start(bf16[128,128]{1,0:T(8,128)(2,1)S(1)} %get-tuple-element.17), channel_id=1, source_target_pairs={{0,3},{1,0},{2,1},{3,2},{4,7},{5,4},{6,5},{7,6},{8,11},{9,8},{10,9... | collective-permute-start | bytes 98312 | tf_op jit(solution)/shard_map/ppermute | solution.py:37
  169.5 3.3 %collective-permute-start.25 = (bf16[256,128]{1,0:T(8,128)(2,1)S(1)}, bf16[256,128]{1,0:T(8,128)(2,1)S(1)}, u32[]{:S(2)}, u32[]{:S(2)}) collective-permute-start(bf16[256,128]{1,0:T(8,128)(2,1)S(1)} %pad_maximum_fusion.8), channel_id=1, source_target_pairs={{0,3},{1,0},{2,1},{3,2},{4,7},{5,4},{6,5},{7,6},{8,11},{9,8},{10,9... | collective-permute-start | bytes 196616 | tf_op jit(solution)/shard_map/ppermute | solution.py:37
  174.7 3.6 %collective-permute-done.23 = bf16[256,128]{1,0:T(8,128)(2,1)S(1)} collective-permute-done((bf16[256,128]{1,0:T(8,128)(2,1)S(1)}, bf16[256,128]{1,0:T(8,128)(2,1)S(1)}, u32[]{:S(2)}, u32[]{:S(2)}) %collective-permute-start.23) | collective-permute-done | bytes 65568 | tf_op jit(solution)/shard_map/ppermute | solution.py:37
  178.8 3.9 %collective-permute-done.26 = f32[64,128]{1,0:T(8,128)S(1)} collective-permute-done((f32[64,128]{1,0:T(8,128)S(1)}, f32[64,128]{1,0:T(8,128)S(1)}, u32[]{:S(2)}, u32[]{:S(2)}) %collective-permute-start.26) | collective-permute-done | bytes 32800 | tf_op jit(solution)/shard_map/ppermute | solution.py:46
  183.0 5.0 %collective-permute-done.27 = f32[32,128]{1,0:T(8,128)S(1)} collective-permute-done((f32[32,128]{1,0:T(8,128)S(1)}, f32[32,128]{1,0:T(8,128)S(1)}, u32[]{:S(2)}, u32[]{:S(2)}) %collective-permute-start.27) | collective-permute-done | bytes 16416 | tf_op jit(solution)/shard_map/ppermute | solution.py:46
  188.1 3.6 %collective-permute-done.28 = f32[16,128]{1,0:T(8,128)S(1)} collective-permute-done((f32[16,128]{1,0:T(8,128)S(1)}, f32[16,128]{1,0:T(8,128)S(1)}, u32[]{:S(2)}, u32[]{:S(2)}) %collective-permute-start.28) | collective-permute-done | bytes 8224 | tf_op jit(solution)/shard_map/ppermute | solution.py:46
  191.8 5.1 %collective-permute-done.29 = f32[8,128]{1,0:T(8,128)S(1)} collective-permute-done((f32[8,128]{1,0:T(8,128)S(1)}, f32[8,128]{1,0:T(8,128)S(1)}, u32[]{:S(2)}, u32[]{:S(2)}) %collective-permute-start.29) | collective-permute-done | bytes 4128 | tf_op jit(solution)/shard_map/ppermute | solution.py:46
  197.8 3.9 %all-to-all-start.1 = ((bf16[32,4,256]{2,1,0:T(4,128)(2,1)}), bf16[32,4,256]{2,1,0:T(4,128)(2,1)S(1)}, u32[]{:S(2)}, u32[]{:S(2)}) async-start(bf16[32,4,256]{2,1,0:T(4,128)(2,1)} %all_to_all.32), calls=%async_computation.1 | async-start | bytes 131072 | tf_op jit(solution)/shard_map/all_to_all | solution.py:286
  203.7 6.3 %all-to-all-done.1 = bf16[32,4,256]{2,1,0:T(4,128)(2,1)S(1)} async-done(((bf16[32,4,256]{2,1,0:T(4,128)(2,1)}), bf16[32,4,256]{2,1,0:T(4,128)(2,1)S(1)}, u32[]{:S(2)}, u32[]{:S(2)}) %all-to-all-start.1) | async-done | bytes 65568 | tf_op jit(solution)/shard_map/all_to_all | solution.py:286
  (110 shorter events, 33.3 us)
Async XLA Ops:
  18.5 5.5 %collective-permute-start.1 = (bf16[256,128]{1,0:T(8,128)(2,1)S(1)}, bf16[256,128]{1,0:T(8,128)(2,1)S(1)}, u32[]{:S(2)}, u32[]{:S(2)}) collective-permute-start(bf16[256,128]{1,0:T(8,128)(2,1)S(1)} %convolution_convert_fusion.1), channel_id=1, source_target_pairs={{0,1},{1,2},{2,3},{3,0},{4,5},{5,6},{6,7},{7,4},{8,9},{9,10},{10,1... | collective-permute-start | bytes 196616 | tf_op jit(solution)/shard_map/ppermute | solution.py:37
  19.1 4.9 %collective-permute-start = (bf16[256,128]{1,0:T(8,128)(2,1)S(1)}, bf16[256,128]{1,0:T(8,128)(2,1)S(1)}, u32[]{:S(2)}, u32[]{:S(2)}) collective-permute-start(bf16[256,128]{1,0:T(8,128)(2,1)S(1)} %convolution_convert_fusion.1), channel_id=1, source_target_pairs={{0,3},{1,0},{2,1},{3,2},{4,7},{5,4},{6,5},{7,6},{8,11},{9,8},{10,9... | collective-permute-start | bytes 196616 | tf_op jit(solution)/shard_map/ppermute | solution.py:37
  24.0 5.1 %collective-permute-start.2 = (bf16[128,128]{1,0:T(8,128)(2,1)S(1)}, bf16[128,128]{1,0:T(8,128)(2,1)S(1)}, u32[]{:S(2)}, u32[]{:S(2)}) collective-permute-start(bf16[128,128]{1,0:T(8,128)(2,1)S(1)} %slice.215), channel_id=1, source_target_pairs={{0,1},{1,2},{2,3},{3,0},{4,5},{5,6},{6,7},{7,4},{8,9},{9,10},{10,1... | collective-permute-start | bytes 98312 | tf_op jit(solution)/shard_map/ppermute | solution.py:37
  24.0 5.1 %collective-permute-start.3 = (bf16[128,128]{1,0:T(8,128)(2,1)S(1)}, bf16[128,128]{1,0:T(8,128)(2,1)S(1)}, u32[]{:S(2)}, u32[]{:S(2)}) collective-permute-start(bf16[128,128]{1,0:T(8,128)(2,1)S(1)} %slice.216), channel_id=1, source_target_pairs={{0,3},{1,0},{2,1},{3,2},{4,7},{5,4},{6,5},{7,6},{8,11},{9,8},{10,9... | collective-permute-start | bytes 98312 | tf_op jit(solution)/shard_map/ppermute | solution.py:37
  29.2 7.8 %collective-permute-start.4 = (bf16[4,256,128]{2,1,0:T(8,128)(2,1)S(1)}, bf16[4,256,128]{2,1,0:T(8,128)(2,1)S(1)}, u32[]{:S(2)}, u32[]{:S(2)}) collective-permute-start(bf16[4,256,128]{2,1,0:T(8,128)(2,1)S(1)} %get-tuple-element.23), channel_id=1, source_target_pairs={{0,12},{1,13},{2,14},{3,15},{4,0},{5,1},{6,2},{7,3},{8,4},{9,5},{1... | collective-permute-start | bytes 786440 | tf_op jit(solution)/shard_map/ppermute | solution.py:37
  30.5 8.8 %collective-permute-start.5 = (bf16[4,256,128]{2,1,0:T(8,128)(2,1)S(1)}, bf16[4,256,128]{2,1,0:T(8,128)(2,1)S(1)}, u32[]{:S(2)}, u32[]{:S(2)}) collective-permute-start(bf16[4,256,128]{2,1,0:T(8,128)(2,1)S(1)} %get-tuple-element.23), channel_id=1, source_target_pairs={{0,4},{1,5},{2,6},{3,7},{4,8},{5,9},{6,10},{7,11},{8,12},{9,13},{1... | collective-permute-start | bytes 786440 | tf_op jit(solution)/shard_map/ppermute | solution.py:37
  37.1 5.0 %collective-permute-start.7 = (bf16[4,128,128]{2,1,0:T(8,128)(2,1)S(1)}, bf16[4,128,128]{2,1,0:T(8,128)(2,1)S(1)}, u32[]{:S(2)}, u32[]{:S(2)}) collective-permute-start(bf16[4,128,128]{2,1,0:T(8,128)(2,1)S(1)} %slice.218), channel_id=1, source_target_pairs={{0,12},{1,13},{2,14},{3,15},{4,0},{5,1},{6,2},{7,3},{8,4},{9,5},{1... | collective-permute-start | bytes 393224 | tf_op jit(solution)/shard_map/ppermute | solution.py:37
  39.4 6.2 %collective-permute-start.6 = (bf16[4,128,128]{2,1,0:T(8,128)(2,1)S(1)}, bf16[4,128,128]{2,1,0:T(8,128)(2,1)S(1)}, u32[]{:S(2)}, u32[]{:S(2)}) collective-permute-start(bf16[4,128,128]{2,1,0:T(8,128)(2,1)S(1)} %slice.217), channel_id=1, source_target_pairs={{0,4},{1,5},{2,6},{3,7},{4,8},{5,9},{6,10},{7,11},{8,12},{9,13},{1... | collective-permute-start | bytes 393224 | tf_op jit(solution)/shard_map/ppermute | solution.py:37
  45.8 14.9 %collective-permute-start.8 = (bf16[4,4,256,128]{3,2,1,0:T(8,128)(2,1)S(1)}, bf16[4,4,256,128]{3,2,1,0:T(8,128)(2,1)S(1)}, u32[]{:S(2)}, u32[]{:S(2)}) collective-permute-start(bf16[4,4,256,128]{3,2,1,0:T(8,128)(2,1)S(1)} %get-tuple-element.13), channel_id=1, source_target_pairs={{0,80},{1,81},{2,82},{3,83},{4,84},{5,85},{6,86},{7,87},{8,88},{9,... | collective-permute-start | bytes 3145736 | tf_op jit(solution)/shard_map/ppermute | solution.py:37
  46.9 16.1 %collective-permute-start.9 = (bf16[4,4,256,128]{3,2,1,0:T(8,128)(2,1)S(1)}, bf16[4,4,256,128]{3,2,1,0:T(8,128)(2,1)S(1)}, u32[]{:S(2)}, u32[]{:S(2)}) collective-permute-start(bf16[4,4,256,128]{3,2,1,0:T(8,128)(2,1)S(1)} %get-tuple-element.13), channel_id=1, source_target_pairs={{0,16},{1,17},{2,18},{3,19},{4,20},{5,21},{6,22},{7,23},{8,24},{9,... | collective-permute-start | bytes 3145736 | tf_op jit(solution)/shard_map/ppermute | solution.py:37
  60.7 9.2 %collective-permute-start.11 = (bf16[4,4,128,128]{3,2,1,0:T(8,128)(2,1)S(1)}, bf16[4,4,128,128]{3,2,1,0:T(8,128)(2,1)S(1)}, u32[]{:S(2)}, u32[]{:S(2)}) collective-permute-start(bf16[4,4,128,128]{3,2,1,0:T(8,128)(2,1)S(1)} %slice.220), channel_id=1, source_target_pairs={{0,80},{1,81},{2,82},{3,83},{4,84},{5,85},{6,86},{7,87},{8,88},{9,... | collective-permute-start | bytes 1572872 | tf_op jit(solution)/shard_map/ppermute | solution.py:37
  63.1 10.5 %collective-permute-start.10 = (bf16[4,4,128,128]{3,2,1,0:T(8,128)(2,1)S(1)}, bf16[4,4,128,128]{3,2,1,0:T(8,128)(2,1)S(1)}, u32[]{:S(2)}, u32[]{:S(2)}) collective-permute-start(bf16[4,4,128,128]{3,2,1,0:T(8,128)(2,1)S(1)} %slice.219), channel_id=1, source_target_pairs={{0,16},{1,17},{2,18},{3,19},{4,20},{5,21},{6,22},{7,23},{8,24},{9,... | collective-permute-start | bytes 1572872 | tf_op jit(solution)/shard_map/ppermute | solution.py:37
  75.9 8.2 %collective-permute-start.12 = (bf16[128,128,128]{2,1,0:T(8,128)(2,1)}, bf16[128,128,128]{2,1,0:T(8,128)(2,1)}, u32[]{:S(2)}, u32[]{:S(2)}) collective-permute-start(bf16[128,128,128]{2,1,0:T(8,128)(2,1)} %bitcast.16.proj_ref), channel_id=1, source_target_pairs={{0,32},{32,0},{64,96},{96,64},{1,33},{33,1},{65,97},{97,65},{2,34}... | collective-permute-start | bytes 12582920 | tf_op jit(solution)/shard_map/ppermute | solution.py:41
  102.6 10.3 %collective-permute-start.13 = (bf16[128,128,128]{2,1,0:T(8,128)(2,1)}, bf16[128,128,128]{2,1,0:T(8,128)(2,1)}, u32[]{:S(2)}, u32[]{:S(2)}) collective-permute-start(bf16[128,128,128]{2,1,0:T(8,128)(2,1)} %shard_map.88), channel_id=1, source_target_pairs={{0,32},{32,0},{64,96},{96,64},{1,33},{33,1},{65,97},{97,65},{2,34}... | collective-permute-start | bytes 12582920 | tf_op jit(solution)/shard_map/ppermute | solution.py:41
  119.0 9.2 %collective-permute-start.16 = (bf16[4,4,128,128]{3,2,1,0:T(8,128)(2,1)S(1)}, bf16[4,4,128,128]{3,2,1,0:T(8,128)(2,1)S(1)}, u32[]{:S(2)}, u32[]{:S(2)}) collective-permute-start(bf16[4,4,128,128]{3,2,1,0:T(8,128)(2,1)S(1)} %get-tuple-element.11), channel_id=1, source_target_pairs={{0,80},{1,81},{2,82},{3,83},{4,84},{5,85},{6,86},{7,87},{8,88},{9,... | collective-permute-start | bytes 1572872 | tf_op jit(solution)/shard_map/ppermute | solution.py:37
  119.9 10.7 %collective-permute-start.14 = (bf16[4,4,128,128]{3,2,1,0:T(8,128)(2,1)S(1)}, bf16[4,4,128,128]{3,2,1,0:T(8,128)(2,1)S(1)}, u32[]{:S(2)}, u32[]{:S(2)}) collective-permute-start(bf16[4,4,128,128]{3,2,1,0:T(8,128)(2,1)S(1)} %get-tuple-element.10), channel_id=1, source_target_pairs={{0,16},{1,17},{2,18},{3,19},{4,20},{5,21},{6,22},{7,23},{8,24},{9,... | collective-permute-start | bytes 1572872 | tf_op jit(solution)/shard_map/ppermute | solution.py:37
  128.5 14.9 %collective-permute-start.17 = (bf16[4,4,256,128]{3,2,1,0:T(8,128)(2,1)S(1)}, bf16[4,4,256,128]{3,2,1,0:T(8,128)(2,1)S(1)}, u32[]{:S(2)}, u32[]{:S(2)}) collective-permute-start(bf16[4,4,256,128]{3,2,1,0:T(8,128)(2,1)S(1)} %pad_maximum_fusion.3), channel_id=1, source_target_pairs={{0,80},{1,81},{2,82},{3,83},{4,84},{5,85},{6,86},{7,87},{8,88},{9,... | collective-permute-start | bytes 3145736 | tf_op jit(solution)/shard_map/ppermute | solution.py:37
  130.9 16.1 %collective-permute-start.15 = (bf16[4,4,256,128]{3,2,1,0:T(8,128)(2,1)S(1)}, bf16[4,4,256,128]{3,2,1,0:T(8,128)(2,1)S(1)}, u32[]{:S(2)}, u32[]{:S(2)}) collective-permute-start(bf16[4,4,256,128]{3,2,1,0:T(8,128)(2,1)S(1)} %pad_maximum_fusion.2), channel_id=1, source_target_pairs={{0,16},{1,17},{2,18},{3,19},{4,20},{5,21},{6,22},{7,23},{8,24},{9,... | collective-permute-start | bytes 3145736 | tf_op jit(solution)/shard_map/ppermute | solution.py:37
  147.3 5.1 %collective-permute-start.20 = (bf16[4,128,128]{2,1,0:T(8,128)(2,1)S(1)}, bf16[4,128,128]{2,1,0:T(8,128)(2,1)S(1)}, u32[]{:S(2)}, u32[]{:S(2)}) collective-permute-start(bf16[4,128,128]{2,1,0:T(8,128)(2,1)S(1)} %get-tuple-element.21), channel_id=1, source_target_pairs={{0,12},{1,13},{2,14},{3,15},{4,0},{5,1},{6,2},{7,3},{8,4},{9,5},{1... | collective-permute-start | bytes 393224 | tf_op jit(solution)/shard_map/ppermute | solution.py:37
  147.5 6.3 %collective-permute-start.18 = (bf16[4,128,128]{2,1,0:T(8,128)(2,1)S(1)}, bf16[4,128,128]{2,1,0:T(8,128)(2,1)S(1)}, u32[]{:S(2)}, u32[]{:S(2)}) collective-permute-start(bf16[4,128,128]{2,1,0:T(8,128)(2,1)S(1)} %get-tuple-element.20), channel_id=1, source_target_pairs={{0,4},{1,5},{2,6},{3,7},{4,8},{5,9},{6,10},{7,11},{8,12},{9,13},{1... | collective-permute-start | bytes 393224 | tf_op jit(solution)/shard_map/ppermute | solution.py:37
  152.5 8.8 %collective-permute-start.21 = (bf16[4,256,128]{2,1,0:T(8,128)(2,1)S(1)}, bf16[4,256,128]{2,1,0:T(8,128)(2,1)S(1)}, u32[]{:S(2)}, u32[]{:S(2)}) collective-permute-start(bf16[4,256,128]{2,1,0:T(8,128)(2,1)S(1)} %pad_maximum_fusion.6), channel_id=1, source_target_pairs={{0,12},{1,13},{2,14},{3,15},{4,0},{5,1},{6,2},{7,3},{8,4},{9,5},{1... | collective-permute-start | bytes 786440 | tf_op jit(solution)/shard_map/ppermute | solution.py:37
  153.9 10.3 %collective-permute-start.19 = (bf16[4,256,128]{2,1,0:T(8,128)(2,1)S(1)}, bf16[4,256,128]{2,1,0:T(8,128)(2,1)S(1)}, u32[]{:S(2)}, u32[]{:S(2)}) collective-permute-start(bf16[4,256,128]{2,1,0:T(8,128)(2,1)S(1)} %pad_maximum_fusion.5), channel_id=1, source_target_pairs={{0,4},{1,5},{2,6},{3,7},{4,8},{5,9},{6,10},{7,11},{8,12},{9,13},{1... | collective-permute-start | bytes 786440 | tf_op jit(solution)/shard_map/ppermute | solution.py:37
  164.3 5.2 %collective-permute-start.22 = (bf16[128,128]{1,0:T(8,128)(2,1)S(1)}, bf16[128,128]{1,0:T(8,128)(2,1)S(1)}, u32[]{:S(2)}, u32[]{:S(2)}) collective-permute-start(bf16[128,128]{1,0:T(8,128)(2,1)S(1)} %get-tuple-element.16), channel_id=1, source_target_pairs={{0,1},{1,2},{2,3},{3,0},{4,5},{5,6},{6,7},{7,4},{8,9},{9,10},{10,1... | collective-permute-start | bytes 98312 | tf_op jit(solution)/shard_map/ppermute | solution.py:37
  164.4 5.1 %collective-permute-start.24 = (bf16[128,128]{1,0:T(8,128)(2,1)S(1)}, bf16[128,128]{1,0:T(8,128)(2,1)S(1)}, u32[]{:S(2)}, u32[]{:S(2)}) collective-permute-start(bf16[128,128]{1,0:T(8,128)(2,1)S(1)} %get-tuple-element.17), channel_id=1, source_target_pairs={{0,3},{1,0},{2,1},{3,2},{4,7},{5,4},{6,5},{7,6},{8,11},{9,8},{10,9... | collective-permute-start | bytes 98312 | tf_op jit(solution)/shard_map/ppermute | solution.py:37
  169.5 5.2 %collective-permute-start.25 = (bf16[256,128]{1,0:T(8,128)(2,1)S(1)}, bf16[256,128]{1,0:T(8,128)(2,1)S(1)}, u32[]{:S(2)}, u32[]{:S(2)}) collective-permute-start(bf16[256,128]{1,0:T(8,128)(2,1)S(1)} %pad_maximum_fusion.8), channel_id=1, source_target_pairs={{0,3},{1,0},{2,1},{3,2},{4,7},{5,4},{6,5},{7,6},{8,11},{9,8},{10,9... | collective-permute-start | bytes 196616 | tf_op jit(solution)/shard_map/ppermute | solution.py:37
  172.8 5.5 %collective-permute-start.23 = (bf16[256,128]{1,0:T(8,128)(2,1)S(1)}, bf16[256,128]{1,0:T(8,128)(2,1)S(1)}, u32[]{:S(2)}, u32[]{:S(2)}) collective-permute-start(bf16[256,128]{1,0:T(8,128)(2,1)S(1)} %pad_maximum_fusion.7), channel_id=1, source_target_pairs={{0,1},{1,2},{2,3},{3,0},{4,5},{5,6},{6,7},{7,4},{8,9},{9,10},{10,1... | collective-permute-start | bytes 196616 | tf_op jit(solution)/shard_map/ppermute | solution.py:37
  178.6 4.0 %collective-permute-start.26 = (f32[64,128]{1,0:T(8,128)S(1)}, f32[64,128]{1,0:T(8,128)S(1)}, u32[]{:S(2)}, u32[]{:S(2)}) collective-permute-start(f32[64,128]{1,0:T(8,128)S(1)} %slice_select_fusion), channel_id=1, source_target_pairs={{0,16},{1,17},{2,18},{3,19},{4,20},{5,21},{6,22},{7,23},{8,24},{9,... | collective-permute-start | bytes 98312 | tf_op jit(solution)/shard_map/ppermute | solution.py:46
  182.6 5.3 %collective-permute-start.27 = (f32[32,128]{1,0:T(8,128)S(1)}, f32[32,128]{1,0:T(8,128)S(1)}, u32[]{:S(2)}, u32[]{:S(2)}) collective-permute-start(f32[32,128]{1,0:T(8,128)S(1)} %slice_select_fusion.1), channel_id=1, source_target_pairs={{0,8},{1,9},{2,10},{3,11},{4,12},{5,13},{6,14},{7,15},{8,0},{9,1},... | collective-permute-start | bytes 49160 | tf_op jit(solution)/shard_map/ppermute | solution.py:46
  191.7 5.2 %collective-permute-start.29 = (f32[8,128]{1,0:T(8,128)S(1)}, f32[8,128]{1,0:T(8,128)S(1)}, u32[]{:S(2)}, u32[]{:S(2)}) collective-permute-start(f32[8,128]{1,0:T(8,128)S(1)} %slice_select_fusion.3), channel_id=1, source_target_pairs={{0,2},{1,3},{2,0},{3,1},{4,6},{5,7},{6,4},{7,5},{8,10},{9,11},{10,... | collective-permute-start | bytes 12296 | tf_op jit(solution)/shard_map/ppermute | solution.py:46
  196.9 4.8 %collective-permute-start.30 = (f32[4,128]{1,0:T(4,128)S(1)}, f32[4,128]{1,0:T(4,128)S(1)}, u32[]{:S(2)}, u32[]{:S(2)}) collective-permute-start(f32[4,128]{1,0:T(4,128)S(1)} %slice_select_fusion.4), channel_id=1, source_target_pairs={{0,1},{1,0},{2,3},{3,2},{4,5},{5,4},{6,7},{7,6},{8,9},{9,8},{10,11... | collective-permute-start | bytes 6152 | tf_op jit(solution)/shard_map/ppermute | solution.py:46
  197.8 12.2 %all-to-all-start.1 = ((bf16[32,4,256]{2,1,0:T(4,128)(2,1)}), bf16[32,4,256]{2,1,0:T(4,128)(2,1)S(1)}, u32[]{:S(2)}, u32[]{:S(2)}) async-start(bf16[32,4,256]{2,1,0:T(4,128)(2,1)} %all_to_all.32), calls=%async_computation.1 | async-start | bytes 131072 | tf_op jit(solution)/shard_map/all_to_all | solution.py:286
  203.0 7.1 %collective-permute-start.32 = (f32[4,128]{1,0:T(4,128)S(1)}, f32[4,128]{1,0:T(4,128)S(1)}, u32[]{:S(2)}, u32[]{:S(2)}) collective-permute-start(f32[4,128]{1,0:T(4,128)S(1)} %add.204), channel_id=1, source_target_pairs={{0,64},{32,96},{64,0},{96,32},{1,65},{33,97},{65,1},{97,33},{2,66}... | collective-permute-start | bytes 6152 | tf_op jit(solution)/shard_map/ppermute | solution.py:46
  (6 other events, 41.3 us)

commit v6 on v5

--- a/solution.py
+++ b/solution.py
@@ -56,22 +56,47 @@
     return jnp.stack([block, from_plus, far, from_minus])
 
 
-def reduce_phase(total, phase, wire_type):
+def gather_phase_direct(block, phase):
+    from_minus = ring_shift(block, phase, 1)
+    from_plus = ring_shift(block, phase, -1)
+    far = ring_shift(block, phase, 2)
+    return jnp.stack([block, from_plus, far, from_minus])
+
+
+def reduce_phase_direct(total, phase, wire_type):
+    from_minus = ring_shift(total[1].astype(wire_type), phase, 1)
+    from_plus = ring_shift(total[3].astype(wire_type), phase, -1)
+    far = ring_shift(total[2].astype(wire_type), phase, 2)
+    return (
+        total[0]
+        + from_minus.astype(jnp.float32)
+        + from_plus.astype(jnp.float32)
+        + far.astype(jnp.float32)
+    )
+
+
+def reduce_phase(total, phase, wire_type, extra=None):
     half = total.shape[-2] // 2
-    far = total[2]
+
+    def term(k):
+        if extra is None:
+            return total[k]
+        return total[k] + extra[k].astype(jnp.float32)
+
+    far = term(2)
     got_minus = ring_shift(far[..., :half, :].astype(wire_type), phase, 1)
     got_plus = ring_shift(far[..., half:, :].astype(wire_type), phase, -1)
-    ahead = total[1]
+    ahead = term(1)
     ahead = jnp.concatenate(
         [ahead[..., :half, :] + got_minus.astype(jnp.float32), ahead[..., half:, :]], axis=-2
     )
-    behind = total[3]
+    behind = term(3)
     behind = jnp.concatenate(
         [behind[..., :half, :], behind[..., half:, :] + got_plus.astype(jnp.float32)], axis=-2
     )
     from_minus = ring_shift(ahead.astype(wire_type), phase, 1)
     from_plus = ring_shift(behind.astype(wire_type), phase, -1)
-    return total[0] + from_minus.astype(jnp.float32) + from_plus.astype(jnp.float32)
+    return term(0) + from_minus.astype(jnp.float32) + from_plus.astype(jnp.float32)
 
 
 def scatter_rows(total, axis, wire_type):
@@ -238,9 +263,9 @@
         features_own, weight, (((0,), (0,)), ((), ())), preferred_element_type=jnp.float32
     ).astype(jnp.bfloat16)
 
-    gathered = projected
-    for phase in range(3):
-        gathered = gather_phase(gathered, phase)
+    gathered = gather_phase_direct(projected, 0)
+    gathered = gather_phase_direct(gathered, 1)
+    gathered = gather_phase(gathered, 2)
     own_buffer = gathered.reshape(buffer_tiles, tile_size, hidden_width)
     other_buffer = sibling(own_buffer)
     aggregate_sum = aggregate_pair(core_id, spots, tile_count, tile_stack, own_buffer)
@@ -263,10 +288,10 @@
     total = spread_pair(
         core_id, spots, tile_count, tile_stack, grad_turned, buffer_tiles, jnp.float32
     )
-    total = total + arrived.astype(jnp.float32)
-    total = total.reshape(RING, RING, RING, rows_own, hidden_width)
-    for phase in (2, 1, 0):
-        total = reduce_phase(total, phase, jnp.bfloat16)
+    shape = (RING, RING, RING, rows_own, hidden_width)
+    total = reduce_phase(total.reshape(shape), 2, jnp.bfloat16, arrived.reshape(shape))
+    total = reduce_phase_direct(total, 1, jnp.bfloat16)
+    total = reduce_phase_direct(total, 0, jnp.bfloat16)
     grad_hidden = (
         total.reshape(tile_rows, hidden_width, tile_size)
         .transpose(0, 2, 1)
@@ -275,10 +300,12 @@
     )
 
     weight_term = jnp.dot(features_own, grad_hidden, preferred_element_type=jnp.float32)
-    weight_part = scatter_rows(weight_term, "feat", jnp.float32)
-    weight_part = weight_part + swapped(weight_part, "blk", 1)
-    weight_part = weight_part + swapped(weight_part, "blk", 2)
-    grad_weight = weight_part * lax.rsqrt(jnp.float32(block_rows * cycle_size))
+    feat_count = lax.axis_size("feat")
+    weight_rows = weight_term.reshape(1, feat_count, -1, hidden_width)
+    weight_rows = jnp.broadcast_to(weight_rows, (cycle_size,) + weight_rows.shape[1:])
+    weight_rows = weight_rows.reshape(cycle_size * feat_count, -1, hidden_width)
+    weight_got = lax.all_to_all(weight_rows, BOTH, split_axis=0, concat_axis=0, tiled=True)
+    grad_weight = jnp.sum(weight_got, axis=0) * lax.rsqrt(jnp.float32(block_rows * cycle_size))
 
     features_grad_local = lax.dot_general(
         weight, grad_hidden, (((1,), (1,)), ((), ())), preferred_element_type=jnp.float32

time: 211 us -> 199 us (0.943)
  waiting for transfers between devices: 106 us -> 92 us
    ppermute x7 -> x0, waiting for transfers between devices: 18.7 us -> none  [swapped(): return lax.ppermute(block, axis, [(i, i ^ mask) for i in range(count)])]
    all_to_all x0 -> x1, waiting for transfers between devices: none -> 10.9 us  [body(): lax.all_to_all(weight_rows, BOTH, split_axis=0, concat_axis=0, tiled=True)]
    ppermute x24 -> x20, waiting for transfers between devices: 81.1 us -> 72.9 us  [ring_shift(): return lax.ppermute(block, BOTH, route)]
    ppermute x24 -> x20, starting transfers between devices: 30.7 us -> 25.5 us  [ring_shift(): return lax.ppermute(block, BOTH, route)]
    all_to_all x0 -> x1, starting transfers between devices: none -> 4.6 us  [body(): lax.all_to_all(weight_rows, BOTH, split_axis=0, concat_axis=0, tiled=True)]
    add x8 -> x1, other arithmetic: 6.2 us -> 5.99 us  [term(): return total[k] + extra[k].astype(jnp.float32)]
  transfers between devices with their start and end apart: 34 -> 24, of which waited for: 25 -> 18; matrix products, arithmetic and copies ran while one was open for 1% -> 1% of each run, Pallas kernels for 8% -> 9%
where the time goes in v6:
time: 199 us; the launch traced here: 198 us
  waiting for transfers between devices  92 us (46%)
  starting transfers between devices  36.2 us (18%)
  Pallas kernels  34.4 us (17%)
  blocking collectives  17.6 us (9%)
  other arithmetic  12.7 us (6%)
  local copies, waits for them, and re-layouts  3.32 us (2%)
    ppermute x20, waiting for transfers between devices, ring_shift(): return lax.ppermute(block, BOTH, route)  72.9 us
    ppermute x20, starting transfers between devices, ring_shift(): return lax.ppermute(block, BOTH, route)  25.5 us
    pallas_call x2, Pallas kernels, spread_pair(): pl.pallas_call(spread_kernel, grid_spec=grid_spec, out_shape=jax.ShapeDty...  19.1 us
    all_to_all x1, blocking collectives, body(): lax.all_to_all(features_t, 'feat', split_axis=1, concat_axis=0, tiled=True)  17.6 us
    pallas_call x2, Pallas kernels, aggregate_pair(): pl.pallas_call(aggregate_kernel, grid_spec=grid_spec, out_shape=jax.Shape...  15.3 us
    all_to_all x1, waiting for transfers between devices, body(): lax.all_to_all(weight_rows, BOTH, split_axis=0, concat_axis=0, tiled=True)  10.9 us
    all_to_all x1, waiting for transfers between devices, body(): lax.all_to_all(features_grad_local, 'feat', split_axis=0, concat_axis=1,...  8.18 us
    add x1, other arithmetic, term(): return total[k] + extra[k].astype(jnp.float32)  5.99 us
  transfers between devices with their start and end apart: 24, of which 18 were waited for; matrix products, arithmetic and copies ran while one was open for 1% of the time, Pallas kernels for 9%

profile of v6, /device:TPU:0, one launch (start us, length us, event | category | flops | bytes accessed | tf_op | source)
XLA Modules:
  0.0 197.6 jit_solution(14114112907382106956)
XLA Ops:
  0.6 17.6 %all_to_all.43 = bf16[4,32,256]{2,0,1:T(4,128)(2,1)S(1)} all-to-all(bf16[4,32,256]{2,0,1:T(4,128)(2,1)} %bitcast.127), channel_id=1, replica_groups=mesh['blk'=4,'feat'=32] {'feat'}, dimensions={1} | all-to-all | bytes 131072 | tf_op jit(solution)/shard_map/all_to_all | solution.py:261
  19.1 2.3 %collective-permute-start.1 = (bf16[256,128]{1,0:T(8,128)(2,1)S(1)}, bf16[256,128]{1,0:T(8,128)(2,1)S(1)}, u32[]{:S(2)}, u32[]{:S(2)}) collective-permute-start(bf16[256,128]{1,0:T(8,128)(2,1)S(1)} %convolution_convert_fusion.1), channel_id=1, source_target_pairs={{0,2},{1,3},{2,0},{3,1},{4,6},{5,7},{6,4},{7,5},{8,10},{9,11},{10,... | collective-permute-start | bytes 196616 | tf_op jit(solution)/shard_map/ppermute | solution.py:37
  22.5 1.5 collective-permute-done.2
  25.7 1.4 collective-permute-start.4
  27.1 1.9 collective-permute-start.3
  29.1 6.7 %collective-permute-done.4 = bf16[4,256,128]{2,1,0:T(8,128)(2,1)S(1)} collective-permute-done((bf16[4,256,128]{2,1,0:T(8,128)(2,1)S(1)}, bf16[4,256,128]{2,1,0:T(8,128)(2,1)S(1)}, u32[]{:S(2)}, u32[]{:S(2)}) %collective-permute-start.4) | collective-permute-done | bytes 262176 | tf_op jit(solution)/shard_map/ppermute | solution.py:37
  37.0 1.7 collective-permute-done.5
  38.9 3.4 %collective-permute-start.6 = (bf16[4,4,256,128]{3,2,1,0:T(8,128)(2,1)S(1)}, bf16[4,4,256,128]{3,2,1,0:T(8,128)(2,1)S(1)}, u32[]{:S(2)}, u32[]{:S(2)}) collective-permute-start(bf16[4,4,256,128]{3,2,1,0:T(8,128)(2,1)S(1)} %get-tuple-element.17), channel_id=1, source_target_pairs={{0,80},{1,81},{2,82},{3,83},{4,84},{5,85},{6,86},{7,87},{8,88},{9,... | collective-permute-start | bytes 3145736 | tf_op jit(solution)/shard_map/ppermute | solution.py:37
  42.2 12.3 %collective-permute-done.6 = bf16[4,4,256,128]{3,2,1,0:T(8,128)(2,1)S(1)} collective-permute-done((bf16[4,4,256,128]{3,2,1,0:T(8,128)(2,1)S(1)}, bf16[4,4,256,128]{3,2,1,0:T(8,128)(2,1)S(1)}, u32[]{:S(2)}, u32[]{:S(2)}) %collective-permute-start.6) | collective-permute-done | bytes 1048608 | tf_op jit(solution)/shard_map/ppermute | solution.py:37
  54.6 3.8 %collective-permute-start.9 = (bf16[4,4,128,128]{3,2,1,0:T(8,128)(2,1)S(1)}, bf16[4,4,128,128]{3,2,1,0:T(8,128)(2,1)S(1)}, u32[]{:S(2)}, u32[]{:S(2)}) collective-permute-start(bf16[4,4,128,128]{3,2,1,0:T(8,128)(2,1)S(1)} %slice.115), channel_id=1, source_target_pairs={{0,80},{1,81},{2,82},{3,83},{4,84},{5,85},{6,86},{7,87},{8,88},{9,... | collective-permute-start | bytes 1572872 | tf_op jit(solution)/shard_map/ppermute | solution.py:37
  58.5 6.6 %collective-permute-done.9 = bf16[4,4,128,128]{3,2,1,0:T(8,128)(2,1)S(1)} collective-permute-done((bf16[4,4,128,128]{3,2,1,0:T(8,128)(2,1)S(1)}, bf16[4,4,128,128]{3,2,1,0:T(8,128)(2,1)S(1)}, u32[]{:S(2)}, u32[]{:S(2)}) %collective-permute-start.9) | collective-permute-done | bytes 524320 | tf_op jit(solution)/shard_map/ppermute | solution.py:37
  65.1 3.8 %collective-permute-done.8 = bf16[4,4,128,128]{3,2,1,0:T(8,128)(2,1)S(1)} collective-permute-done((bf16[4,4,128,128]{3,2,1,0:T(8,128)(2,1)S(1)}, bf16[4,4,128,128]{3,2,1,0:T(8,128)(2,1)S(1)}, u32[]{:S(2)}, u32[]{:S(2)}) %collective-permute-start.8) | collective-permute-done | bytes 524320 | tf_op jit(solution)/shard_map/ppermute | solution.py:37
  69.0 2.3 %pad_maximum_fusion = bf16[4,4,4,256,128]{4,3,2,1,0:T(8,128)(2,1)} fusion(bf16[1,4,4,256,128]{4,3,2,1,0:T(8,128)(2,1)S(1)} %bitcast.110, bf16[1,4,4,256,128]{4,3,2,1,0:T(8,128)(2,1)S(1)} %maximum_bitcast_fusion, bf16[1,4,4,256,128]{4,3,2,1,0:T(8,128)(2,1)S(1)} %bitcast.109, bf16[1,4,4,256,128]{4,3,2,1,0:T(8,128)(2,1)S(1)} %get-tuple-element.16), kind=kLoop, calls=%fused_computation | loop fusion | flops 6291456 | bytes 8388608 | tf_op jit(solution)/shard_map/stack | solution.py:56
  71.9 7.6 %shard_map.85 = f32[2,128,128]{2,1,0:T(8,128)} custom-call(s32[1]{0:T(128)} %bitcast.core_ref, s32[256]{0:T(256)} %fusion.21.where_ref, s32[8]{0:T(128)} %count_ref.7, bf16[4,2,32,128,128]{4,3,2,1,0:T(8,128)(2,1)} %bitcast.99, bf16[128,128,128]{2,1,0:T(8,128)(2,1)} %bitcast.16.proj_ref), custom_call_target="tpu_custom_call" | custom-call | tf_op jit(solution)/shard_map/pallas_call | solution.py:161
  79.5 7.7 %shard_map.86 = f32[2,128,128]{2,1,0:T(8,128)} custom-call(s32[1]{0:T(128)} %bitcast.17.core_ref, s32[256]{0:T(256)} %fusion.21.where_ref, s32[8]{0:T(128)} %count_ref.7, bf16[4,2,32,128,128]{4,3,2,1,0:T(8,128)(2,1)} %bitcast.100, bf16[128,128,128]{2,1,0:T(8,128)(2,1)} %collective-permute-done.10.proj_ref), custom_call_target="tpu_custom_call" | custom-call | tf_op jit(solution)/shard_map/pallas_call | solution.py:161
  89.6 9.0 %shard_map.88 = bf16[128,128,128]{2,1,0:T(8,128)(2,1)} custom-call(s32[1]{0:T(128)} %bitcast.17.core_ref, s32[256]{0:T(256)} %fusion.21.where_ref, s32[8]{0:T(128)} %count_ref.7, bf16[4,2,32,128,128]{4,3,2,1,0:T(8,128)(2,1)} %bitcast.101, bf16[2,128,128]{2,1,0:T(8,128)(2,1)} %bitcast.111), custom_call_target="tpu_custom_call" | custom-call | tf_op jit(solution)/shard_map/pallas_call | solution.py:221
  98.9 10.1 %shard_map.87 = f32[128,128,128]{2,1,0:T(8,128)} custom-call(s32[1]{0:T(128)} %bitcast.core_ref, s32[256]{0:T(256)} %fusion.21.where_ref, s32[8]{0:T(128)} %count_ref.7, bf16[4,2,32,128,128]{4,3,2,1,0:T(8,128)(2,1)} %bitcast.102, bf16[2,128,128]{2,1,0:T(8,128)(2,1)} %bitcast.112), custom_call_target="tpu_custom_call" | custom-call | tf_op jit(solution)/shard_map/pallas_call | solution.py:221
  109.0 6.0 %slice_add_fusion.2 = (f32[32,128,128]{2,1,0:T(8,128)S(1)}, f32[32,128,128]{2,1,0:T(8,128)S(1)}, bf16[32,128,128]{2,1,0:T(8,128)(2,1)S(1)}, f32[32,128,128]{2,1,0:T(8,128)S(1)}) fusion(f32[128,128,128]{2,1,0:T(8,128)} %shard_map.87, bf16[128,128,128]{2,1,0:T(8,128)(2,1)} %collective-permute-done.11), kind=kLoop, calls=%fused_computation.4 | loop fusion | flops 4718592 | bytes 19922944 | tf_op jit(solution)/shard_map/add | solution.py:84
  115.2 2.0 %collective-permute-start.12 = (bf16[4,4,128,128]{3,2,1,0:T(8,128)(2,1)S(1)}, bf16[4,4,128,128]{3,2,1,0:T(8,128)(2,1)S(1)}, u32[]{:S(2)}, u32[]{:S(2)}) collective-permute-start(bf16[4,4,128,128]{3,2,1,0:T(8,128)(2,1)S(1)} %get-tuple-element.14), channel_id=1, source_target_pairs={{0,16},{1,17},{2,18},{3,19},{4,20},{5,21},{6,22},{7,23},{8,24},{9,... | collective-permute-start | bytes 1572872 | tf_op jit(solution)/shard_map/ppermute | solution.py:37
  117.4 7.0 %collective-permute-done.14 = bf16[4,4,128,128]{3,2,1,0:T(8,128)(2,1)S(1)} collective-permute-done((bf16[4,4,128,128]{3,2,1,0:T(8,128)(2,1)S(1)}, bf16[4,4,128,128]{3,2,1,0:T(8,128)(2,1)S(1)}, u32[]{:S(2)}, u32[]{:S(2)}) %collective-permute-start.14) | collective-permute-done | bytes 524320 | tf_op jit(solution)/shard_map/ppermute | solution.py:37
  124.6 1.3 collective-permute-start.15
  127.0 12.4 %collective-permute-done.15 = bf16[4,4,256,128]{3,2,1,0:T(8,128)(2,1)S(1)} collective-permute-done((bf16[4,4,256,128]{3,2,1,0:T(8,128)(2,1)S(1)}, bf16[4,4,256,128]{3,2,1,0:T(8,128)(2,1)S(1)}, u32[]{:S(2)}, u32[]{:S(2)}) %collective-permute-start.15) | collective-permute-done | bytes 1048608 | tf_op jit(solution)/shard_map/ppermute | solution.py:37
  139.4 2.8 %collective-permute-done.13 = bf16[4,4,256,128]{3,2,1,0:T(8,128)(2,1)S(1)} collective-permute-done((bf16[4,4,256,128]{3,2,1,0:T(8,128)(2,1)S(1)}, bf16[4,4,256,128]{3,2,1,0:T(8,128)(2,1)S(1)}, u32[]{:S(2)}, u32[]{:S(2)}) %collective-permute-start.13) | collective-permute-done | bytes 1048608 | tf_op jit(solution)/shard_map/ppermute | solution.py:37
  142.8 2.2 %collective-permute-start.18 = (bf16[4,256,128]{2,1,0:T(8,128)(2,1)S(1)}, bf16[4,256,128]{2,1,0:T(8,128)(2,1)S(1)}, u32[]{:S(2)}, u32[]{:S(2)}) collective-permute-start(bf16[4,256,128]{2,1,0:T(8,128)(2,1)S(1)} %get-tuple-element.12), channel_id=1, source_target_pairs={{0,8},{1,9},{2,10},{3,11},{4,12},{5,13},{6,14},{7,15},{8,0},{9,1},... | collective-permute-start | bytes 786440 | tf_op jit(solution)/shard_map/ppermute | solution.py:37
  146.0 11.0 %collective-permute-done.16 = bf16[4,256,128]{2,1,0:T(8,128)(2,1)S(1)} collective-permute-done((bf16[4,256,128]{2,1,0:T(8,128)(2,1)S(1)}, bf16[4,256,128]{2,1,0:T(8,128)(2,1)S(1)}, u32[]{:S(2)}, u32[]{:S(2)}) %collective-permute-start.16) | collective-permute-done | bytes 262176 | tf_op jit(solution)/shard_map/ppermute | solution.py:37
  157.9 1.4 collective-permute-start.21
  159.3 1.8 collective-permute-start.20
  161.1 2.9 %collective-permute-done.19 = bf16[256,128]{1,0:T(8,128)(2,1)S(1)} collective-permute-done((bf16[256,128]{1,0:T(8,128)(2,1)S(1)}, bf16[256,128]{1,0:T(8,128)(2,1)S(1)}, u32[]{:S(2)}, u32[]{:S(2)}) %collective-permute-start.19) | collective-permute-done | bytes 65568 | tf_op jit(solution)/shard_map/ppermute | solution.py:37
  165.9 5.8 %all-to-all-start.1 = ((bf16[32,4,256]{2,1,0:T(4,128)(2,1)}), bf16[32,4,256]{2,1,0:T(4,128)(2,1)S(1)}, u32[]{:S(2)}, u32[]{:S(2)}) async-start(bf16[32,4,256]{2,1,0:T(4,128)(2,1)} %all_to_all.35), calls=%async_computation.1 | async-start | bytes 131072 | tf_op jit(solution)/shard_map/all_to_all | solution.py:313
  171.9 8.2 %all-to-all-done.1 = bf16[32,4,256]{2,1,0:T(4,128)(2,1)S(1)} async-done(((bf16[32,4,256]{2,1,0:T(4,128)(2,1)}), bf16[32,4,256]{2,1,0:T(4,128)(2,1)S(1)}, u32[]{:S(2)}, u32[]{:S(2)}) %all-to-all-start.1) | async-done | bytes 65568 | tf_op jit(solution)/shard_map/all_to_all | solution.py:313
  180.8 4.6 %all-to-all-start.2 = ((f32[128,4,128]{2,1,0:T(4,128)}), f32[128,4,128]{2,1,0:T(4,128)S(1)}, u32[]{:S(2)}, u32[]{:S(2)}) async-start(f32[128,4,128]{2,1,0:T(4,128)} %bitcast.41), calls=%async_computation.2 | async-start | bytes 524288 | tf_op jit(solution)/shard_map/all_to_all | solution.py:307
  185.4 10.9 %all-to-all-done.2 = f32[128,4,128]{2,1,0:T(4,128)S(1)} async-done(((f32[128,4,128]{2,1,0:T(4,128)}), f32[128,4,128]{2,1,0:T(4,128)S(1)}, u32[]{:S(2)}, u32[]{:S(2)}) %all-to-all-start.2) | async-done | bytes 262176 | tf_op jit(solution)/shard_map/all_to_all | solution.py:307
  (62 shorter events, 16.8 us)
Async XLA Ops:
  0.6 17.6 %copy-start = (bf16[128,128]{1,0:T(8,128)(2,1)S(1)}, bf16[128,128]{1,0:T(8,128)(2,1)}, u32[]{:S(2)}) copy-start(bf16[128,128]{1,0:T(8,128)(2,1)} %param.7) | copy-start | bytes 98308
  18.5 5.5 %collective-permute-start.2 = (bf16[256,128]{1,0:T(8,128)(2,1)S(1)}, bf16[256,128]{1,0:T(8,128)(2,1)S(1)}, u32[]{:S(2)}, u32[]{:S(2)}) collective-permute-start(bf16[256,128]{1,0:T(8,128)(2,1)S(1)} %convolution_convert_fusion.1), channel_id=1, source_target_pairs={{0,1},{1,2},{2,3},{3,0},{4,5},{5,6},{6,7},{7,4},{8,9},{9,10},{10,1... | collective-permute-start | bytes 196616 | tf_op jit(solution)/shard_map/ppermute | solution.py:37
  19.1 5.8 %collective-permute-start.1 = (bf16[256,128]{1,0:T(8,128)(2,1)S(1)}, bf16[256,128]{1,0:T(8,128)(2,1)S(1)}, u32[]{:S(2)}, u32[]{:S(2)}) collective-permute-start(bf16[256,128]{1,0:T(8,128)(2,1)S(1)} %convolution_convert_fusion.1), channel_id=1, source_target_pairs={{0,2},{1,3},{2,0},{3,1},{4,6},{5,7},{6,4},{7,5},{8,10},{9,11},{10,... | collective-permute-start | bytes 196616 | tf_op jit(solution)/shard_map/ppermute | solution.py:37
  21.4 4.3 %collective-permute-start = (bf16[256,128]{1,0:T(8,128)(2,1)S(1)}, bf16[256,128]{1,0:T(8,128)(2,1)S(1)}, u32[]{:S(2)}, u32[]{:S(2)}) collective-permute-start(bf16[256,128]{1,0:T(8,128)(2,1)S(1)} %convolution_convert_fusion.1), channel_id=1, source_target_pairs={{0,3},{1,0},{2,1},{3,2},{4,7},{5,4},{6,5},{7,6},{8,11},{9,8},{10,9... | collective-permute-start | bytes 196616 | tf_op jit(solution)/shard_map/ppermute | solution.py:37
  25.7 10.1 %collective-permute-start.4 = (bf16[4,256,128]{2,1,0:T(8,128)(2,1)S(1)}, bf16[4,256,128]{2,1,0:T(8,128)(2,1)S(1)}, u32[]{:S(2)}, u32[]{:S(2)}) collective-permute-start(bf16[4,256,128]{2,1,0:T(8,128)(2,1)S(1)} %get-tuple-element.22), channel_id=1, source_target_pairs={{0,8},{1,9},{2,10},{3,11},{4,12},{5,13},{6,14},{7,15},{8,0},{9,1},... | collective-permute-start | bytes 786440 | tf_op jit(solution)/shard_map/ppermute | solution.py:37
  27.1 9.9 %collective-permute-start.3 = (bf16[4,256,128]{2,1,0:T(8,128)(2,1)S(1)}, bf16[4,256,128]{2,1,0:T(8,128)(2,1)S(1)}, u32[]{:S(2)}, u32[]{:S(2)}) collective-permute-start(bf16[4,256,128]{2,1,0:T(8,128)(2,1)S(1)} %get-tuple-element.22), channel_id=1, source_target_pairs={{0,12},{1,13},{2,14},{3,15},{4,0},{5,1},{6,2},{7,3},{8,4},{9,5},{1... | collective-permute-start | bytes 786440 | tf_op jit(solution)/shard_map/ppermute | solution.py:37
  29.0 9.7 %collective-permute-start.5 = (bf16[4,256,128]{2,1,0:T(8,128)(2,1)S(1)}, bf16[4,256,128]{2,1,0:T(8,128)(2,1)S(1)}, u32[]{:S(2)}, u32[]{:S(2)}) collective-permute-start(bf16[4,256,128]{2,1,0:T(8,128)(2,1)S(1)} %get-tuple-element.22), channel_id=1, source_target_pairs={{0,4},{1,5},{2,6},{3,7},{4,8},{5,9},{6,10},{7,11},{8,12},{9,13},{1... | collective-permute-start | bytes 786440 | tf_op jit(solution)/shard_map/ppermute | solution.py:37
  38.9 15.7 %collective-permute-start.6 = (bf16[4,4,256,128]{3,2,1,0:T(8,128)(2,1)S(1)}, bf16[4,4,256,128]{3,2,1,0:T(8,128)(2,1)S(1)}, u32[]{:S(2)}, u32[]{:S(2)}) collective-permute-start(bf16[4,4,256,128]{3,2,1,0:T(8,128)(2,1)S(1)} %get-tuple-element.17), channel_id=1, source_target_pairs={{0,80},{1,81},{2,82},{3,83},{4,84},{5,85},{6,86},{7,87},{8,88},{9,... | collective-permute-start | bytes 3145736 | tf_op jit(solution)/shard_map/ppermute | solution.py:37
  42.2 16.1 %collective-permute-start.7 = (bf16[4,4,256,128]{3,2,1,0:T(8,128)(2,1)S(1)}, bf16[4,4,256,128]{3,2,1,0:T(8,128)(2,1)S(1)}, u32[]{:S(2)}, u32[]{:S(2)}) collective-permute-start(bf16[4,4,256,128]{3,2,1,0:T(8,128)(2,1)S(1)} %get-tuple-element.17), channel_id=1, source_target_pairs={{0,16},{1,17},{2,18},{3,19},{4,20},{5,21},{6,22},{7,23},{8,24},{9,... | collective-permute-start | bytes 3145736 | tf_op jit(solution)/shard_map/ppermute | solution.py:37
  54.6 10.5 %collective-permute-start.9 = (bf16[4,4,128,128]{3,2,1,0:T(8,128)(2,1)S(1)}, bf16[4,4,128,128]{3,2,1,0:T(8,128)(2,1)S(1)}, u32[]{:S(2)}, u32[]{:S(2)}) collective-permute-start(bf16[4,4,128,128]{3,2,1,0:T(8,128)(2,1)S(1)} %slice.115), channel_id=1, source_target_pairs={{0,80},{1,81},{2,82},{3,83},{4,84},{5,85},{6,86},{7,87},{8,88},{9,... | collective-permute-start | bytes 1572872 | tf_op jit(solution)/shard_map/ppermute | solution.py:37
  58.4 10.5 %collective-permute-start.8 = (bf16[4,4,128,128]{3,2,1,0:T(8,128)(2,1)S(1)}, bf16[4,4,128,128]{3,2,1,0:T(8,128)(2,1)S(1)}, u32[]{:S(2)}, u32[]{:S(2)}) collective-permute-start(bf16[4,4,128,128]{3,2,1,0:T(8,128)(2,1)S(1)} %slice.114), channel_id=1, source_target_pairs={{0,16},{1,17},{2,18},{3,19},{4,20},{5,21},{6,22},{7,23},{8,24},{9,... | collective-permute-start | bytes 1572872 | tf_op jit(solution)/shard_map/ppermute | solution.py:37
  69.0 2.3 %copy-start.3 = (s32[256]{0:T(256)S(1)}, s32[256]{0:T(256)}, u32[]{:S(2)}) copy-start(s32[256]{0:T(256)} %param.9) | copy-start | bytes 3076
  71.3 8.2 %collective-permute-start.10 = (bf16[128,128,128]{2,1,0:T(8,128)(2,1)}, bf16[128,128,128]{2,1,0:T(8,128)(2,1)}, u32[]{:S(2)}, u32[]{:S(2)}) collective-permute-start(bf16[128,128,128]{2,1,0:T(8,128)(2,1)} %bitcast.16.proj_ref), channel_id=1, source_target_pairs={{0,32},{32,0},{64,96},{96,64},{1,33},{33,1},{65,97},{97,65},{2,34}... | collective-permute-start | bytes 12582920 | tf_op jit(solution)/shard_map/ppermute | solution.py:41
  79.5 7.7 %copy-start.1 = (f32[2,128,128]{2,1,0:T(8,128)S(1)}, f32[2,128,128]{2,1,0:T(8,128)}, u32[]{:S(2)}) copy-start(f32[2,128,128]{2,1,0:T(8,128)} %shard_map.85) | copy-start | bytes 393220
  79.5 8.7 %copy-start.2 = (bf16[256,128]{1,0:T(8,128)(2,1)S(1)}, bf16[256,128]{1,0:T(8,128)(2,1)}, u32[]{:S(2)}) copy-start(bf16[256,128]{1,0:T(8,128)(2,1)} %param.11) | copy-start | bytes 196612
  98.6 10.4 %collective-permute-start.11 = (bf16[128,128,128]{2,1,0:T(8,128)(2,1)}, bf16[128,128,128]{2,1,0:T(8,128)(2,1)}, u32[]{:S(2)}, u32[]{:S(2)}) collective-permute-start(bf16[128,128,128]{2,1,0:T(8,128)(2,1)} %shard_map.88), channel_id=1, source_target_pairs={{0,32},{32,0},{64,96},{96,64},{1,33},{33,1},{65,97},{97,65},{2,34}... | collective-permute-start | bytes 12582920 | tf_op jit(solution)/shard_map/ppermute | solution.py:41
  115.1 9.2 %collective-permute-start.14 = (bf16[4,4,128,128]{3,2,1,0:T(8,128)(2,1)S(1)}, bf16[4,4,128,128]{3,2,1,0:T(8,128)(2,1)S(1)}, u32[]{:S(2)}, u32[]{:S(2)}) collective-permute-start(bf16[4,4,128,128]{3,2,1,0:T(8,128)(2,1)S(1)} %get-tuple-element.15), channel_id=1, source_target_pairs={{0,80},{1,81},{2,82},{3,83},{4,84},{5,85},{6,86},{7,87},{8,88},{9,... | collective-permute-start | bytes 1572872 | tf_op jit(solution)/shard_map/ppermute | solution.py:37
  115.2 10.7 %collective-permute-start.12 = (bf16[4,4,128,128]{3,2,1,0:T(8,128)(2,1)S(1)}, bf16[4,4,128,128]{3,2,1,0:T(8,128)(2,1)S(1)}, u32[]{:S(2)}, u32[]{:S(2)}) collective-permute-start(bf16[4,4,128,128]{3,2,1,0:T(8,128)(2,1)S(1)} %get-tuple-element.14), channel_id=1, source_target_pairs={{0,16},{1,17},{2,18},{3,19},{4,20},{5,21},{6,22},{7,23},{8,24},{9,... | collective-permute-start | bytes 1572872 | tf_op jit(solution)/shard_map/ppermute | solution.py:37
  124.6 14.9 %collective-permute-start.15 = (bf16[4,4,256,128]{3,2,1,0:T(8,128)(2,1)S(1)}, bf16[4,4,256,128]{3,2,1,0:T(8,128)(2,1)S(1)}, u32[]{:S(2)}, u32[]{:S(2)}) collective-permute-start(bf16[4,4,256,128]{3,2,1,0:T(8,128)(2,1)S(1)} %pad_maximum_fusion.3), channel_id=1, source_target_pairs={{0,80},{1,81},{2,82},{3,83},{4,84},{5,85},{6,86},{7,87},{8,88},{9,... | collective-permute-start | bytes 3145736 | tf_op jit(solution)/shard_map/ppermute | solution.py:37
  126.1 16.1 %collective-permute-start.13 = (bf16[4,4,256,128]{3,2,1,0:T(8,128)(2,1)S(1)}, bf16[4,4,256,128]{3,2,1,0:T(8,128)(2,1)S(1)}, u32[]{:S(2)}, u32[]{:S(2)}) collective-permute-start(bf16[4,4,256,128]{3,2,1,0:T(8,128)(2,1)S(1)} %pad_maximum_fusion.2), channel_id=1, source_target_pairs={{0,16},{1,17},{2,18},{3,19},{4,20},{5,21},{6,22},{7,23},{8,24},{9,... | collective-permute-start | bytes 3145736 | tf_op jit(solution)/shard_map/ppermute | solution.py:37
  142.7 14.3 %collective-permute-start.16 = (bf16[4,256,128]{2,1,0:T(8,128)(2,1)S(1)}, bf16[4,256,128]{2,1,0:T(8,128)(2,1)S(1)}, u32[]{:S(2)}, u32[]{:S(2)}) collective-permute-start(bf16[4,256,128]{2,1,0:T(8,128)(2,1)S(1)} %get-tuple-element.11), channel_id=1, source_target_pairs={{0,4},{1,5},{2,6},{3,7},{4,8},{5,9},{6,10},{7,11},{8,12},{9,13},{1... | collective-permute-start | bytes 786440 | tf_op jit(solution)/shard_map/ppermute | solution.py:37
  142.8 14.2 %collective-permute-start.18 = (bf16[4,256,128]{2,1,0:T(8,128)(2,1)S(1)}, bf16[4,256,128]{2,1,0:T(8,128)(2,1)S(1)}, u32[]{:S(2)}, u32[]{:S(2)}) collective-permute-start(bf16[4,256,128]{2,1,0:T(8,128)(2,1)S(1)} %get-tuple-element.12), channel_id=1, source_target_pairs={{0,8},{1,9},{2,10},{3,11},{4,12},{5,13},{6,14},{7,15},{8,0},{9,1},... | collective-permute-start | bytes 786440 | tf_op jit(solution)/shard_map/ppermute | solution.py:37
  145.0 12.6 %collective-permute-start.17 = (bf16[4,256,128]{2,1,0:T(8,128)(2,1)S(1)}, bf16[4,256,128]{2,1,0:T(8,128)(2,1)S(1)}, u32[]{:S(2)}, u32[]{:S(2)}) collective-permute-start(bf16[4,256,128]{2,1,0:T(8,128)(2,1)S(1)} %get-tuple-element.13), channel_id=1, source_target_pairs={{0,12},{1,13},{2,14},{3,15},{4,0},{5,1},{6,2},{7,3},{8,4},{9,5},{1... | collective-permute-start | bytes 786440 | tf_op jit(solution)/shard_map/ppermute | solution.py:37
  157.8 6.2 %collective-permute-start.19 = (bf16[256,128]{1,0:T(8,128)(2,1)S(1)}, bf16[256,128]{1,0:T(8,128)(2,1)S(1)}, u32[]{:S(2)}, u32[]{:S(2)}) collective-permute-start(bf16[256,128]{1,0:T(8,128)(2,1)S(1)} %get-tuple-element.18), channel_id=1, source_target_pairs={{0,1},{1,2},{2,3},{3,0},{4,5},{5,6},{6,7},{7,4},{8,9},{9,10},{10,1... | collective-permute-start | bytes 196616 | tf_op jit(solution)/shard_map/ppermute | solution.py:37
  157.9 6.2 %collective-permute-start.21 = (bf16[256,128]{1,0:T(8,128)(2,1)S(1)}, bf16[256,128]{1,0:T(8,128)(2,1)S(1)}, u32[]{:S(2)}, u32[]{:S(2)}) collective-permute-start(bf16[256,128]{1,0:T(8,128)(2,1)S(1)} %get-tuple-element.19), channel_id=1, source_target_pairs={{0,2},{1,3},{2,0},{3,1},{4,6},{5,7},{6,4},{7,5},{8,10},{9,11},{10,... | collective-permute-start | bytes 196616 | tf_op jit(solution)/shard_map/ppermute | solution.py:37
  159.3 5.6 %collective-permute-start.20 = (bf16[256,128]{1,0:T(8,128)(2,1)S(1)}, bf16[256,128]{1,0:T(8,128)(2,1)S(1)}, u32[]{:S(2)}, u32[]{:S(2)}) collective-permute-start(bf16[256,128]{1,0:T(8,128)(2,1)S(1)} %get-tuple-element.20), channel_id=1, source_target_pairs={{0,3},{1,0},{2,1},{3,2},{4,7},{5,4},{6,5},{7,6},{8,11},{9,8},{10,9... | collective-permute-start | bytes 196616 | tf_op jit(solution)/shard_map/ppermute | solution.py:37
  165.9 14.2 %all-to-all-start.1 = ((bf16[32,4,256]{2,1,0:T(4,128)(2,1)}), bf16[32,4,256]{2,1,0:T(4,128)(2,1)S(1)}, u32[]{:S(2)}, u32[]{:S(2)}) async-start(bf16[32,4,256]{2,1,0:T(4,128)(2,1)} %all_to_all.35), calls=%async_computation.1 | async-start | bytes 131072 | tf_op jit(solution)/shard_map/all_to_all | solution.py:313
  180.8 15.5 %all-to-all-start.2 = ((f32[128,4,128]{2,1,0:T(4,128)}), f32[128,4,128]{2,1,0:T(4,128)S(1)}, u32[]{:S(2)}, u32[]{:S(2)}) async-start(f32[128,4,128]{2,1,0:T(4,128)} %bitcast.41), calls=%async_computation.2 | async-start | bytes 524288 | tf_op jit(solution)/shard_map/all_to_all | solution.py:307

commit v7 on v6

--- a/solution.py
+++ b/solution.py
@@ -166,9 +166,12 @@
     )(jnp.reshape(core_id, (1,)).astype(jnp.int32), spots, counts, tile_stack, buffer)
 
 
-def spread_kernel(
-    core_ref, where_ref, count_ref, tiles_ref, grad_ref, out_ref, total_ref, wide_ref, terms_ref
-):
+def spread_kernel(core_ref, where_ref, count_ref, tiles_ref, grad_ref, *rest):
+    if len(rest) == 5:
+        start_ref, out_ref, total_ref, wide_ref, terms_ref = rest
+    else:
+        start_ref = None
+        out_ref, total_ref, wide_ref, terms_ref = rest
     row = pl.program_id(0)
     half_id = pl.program_id(1)
     tile_rows = pl.num_programs(0)
@@ -179,7 +182,10 @@
 
     @pl.when((row == 0) & (half_id == 0))
     def _():
-        total_ref[...] = jnp.zeros(total_ref.shape, jnp.float32)
+        if start_ref is None:
+            total_ref[...] = jnp.zeros(total_ref.shape, jnp.float32)
+        else:
+            total_ref[...] = start_ref[...].astype(jnp.float32)
 
     for slot in range(slot_count):
         wide_ref[:, slot * tile_size:(slot + 1) * tile_size] = tiles_ref[slot]
@@ -196,7 +202,7 @@
         out_ref[...] = total_ref[...].astype(out_ref.dtype)
 
 
-def spread_pair(core_id, spots, counts, tile_stack, grad_turned, buffer_tiles, out_type):
+def spread_pair(core_id, spots, counts, tile_stack, grad_turned, buffer_tiles, out_type, start=None):
     blocks, tile_rows, slot_count, tile_size, _ = tile_stack.shape
     hidden_width = grad_turned.shape[1]
     grid_spec = pltpu.PrefetchScalarGridSpec(
@@ -208,7 +214,8 @@
                 lambda r, h, c, w, n: (h * 2 + c[0], r, 0, 0, 0),
             ),
             pl.BlockSpec((None, hidden_width, tile_size), lambda r, h, c, w, n: (r, 0, 0)),
-        ],
+        ]
+        + ([] if start is None else [pl.BlockSpec(start.shape, lambda r, h, c, w, n: (0, 0, 0))]),
         out_specs=pl.BlockSpec(
             (buffer_tiles, hidden_width, tile_size), lambda r, h, c, w, n: (0, 0, 0)
         ),
@@ -223,7 +230,14 @@
         grid_spec=grid_spec,
         out_shape=jax.ShapeDtypeStruct((buffer_tiles, hidden_width, tile_size), out_type),
         compiler_params=pltpu.CompilerParams(dimension_semantics=("arbitrary", "arbitrary")),
-    )(jnp.reshape(core_id, (1,)).astype(jnp.int32), spots, counts, tile_stack, grad_turned)
+    )(
+        jnp.reshape(core_id, (1,)).astype(jnp.int32),
+        spots,
+        counts,
+        tile_stack,
+        grad_turned,
+        *([] if start is None else [start]),
+    )
 
 
 def buffer_spots(tile_col, blk_id, feat_id, block_tiles, tiles_per_device):
@@ -286,10 +300,11 @@
     )
     arrived = sibling(outgoing)
     total = spread_pair(
-        core_id, spots, tile_count, tile_stack, grad_turned, buffer_tiles, jnp.float32
-    )
-    shape = (RING, RING, RING, rows_own, hidden_width)
-    total = reduce_phase(total.reshape(shape), 2, jnp.bfloat16, arrived.reshape(shape))
+        core_id, spots, tile_count, tile_stack, grad_turned, buffer_tiles, jnp.float32, arrived
+    )
+    total = reduce_phase(
+        total.reshape(RING, RING, RING, rows_own, hidden_width), 2, jnp.bfloat16
+    )
     total = reduce_phase_direct(total, 1, jnp.bfloat16)
     total = reduce_phase_direct(total, 0, jnp.bfloat16)
     grad_hidden = (
@@ -300,19 +315,26 @@
     )
 
     weight_term = jnp.dot(features_own, grad_hidden, preferred_element_type=jnp.float32)
-    feat_count = lax.axis_size("feat")
-    weight_rows = weight_term.reshape(1, feat_count, -1, hidden_width)
-    weight_rows = jnp.broadcast_to(weight_rows, (cycle_size,) + weight_rows.shape[1:])
-    weight_rows = weight_rows.reshape(cycle_size * feat_count, -1, hidden_width)
-    weight_got = lax.all_to_all(weight_rows, BOTH, split_axis=0, concat_axis=0, tiled=True)
-    grad_weight = jnp.sum(weight_got, axis=0) * lax.rsqrt(jnp.float32(block_rows * cycle_size))
-
     features_grad_local = lax.dot_general(
         weight, grad_hidden, (((1,), (1,)), ((), ())), preferred_element_type=jnp.float32
     ).astype(jnp.bfloat16)
-    grad_features = lax.all_to_all(
-        features_grad_local, "feat", split_axis=0, concat_axis=1, tiled=True
-    )
+    feat_count = lax.axis_size("feat")
+    shard_rows = weight_term.shape[0] // feat_count
+    outgoing = jnp.concatenate(
+        [
+            weight_term.reshape(feat_count, shard_rows, hidden_width),
+            features_grad_local.astype(jnp.float32).reshape(feat_count, shard_rows, rows_own),
+        ],
+        axis=2,
+    )
+    got = lax.all_to_all(outgoing, "feat", split_axis=0, concat_axis=0, tiled=True)
+    weight_part = jnp.sum(got[:, :, :hidden_width], axis=0)
+    grad_features = (
+        got[:, :, hidden_width:].astype(jnp.bfloat16).transpose(1, 0, 2).reshape(shard_rows, -1)
+    )
+    weight_part = weight_part + swapped(weight_part, "blk", 1)
+    weight_part = weight_part + swapped(weight_part, "blk", 2)
+    grad_weight = weight_part * lax.rsqrt(jnp.float32(block_rows * cycle_size))
     return (activations, grad_features, grad_weight)
 
 

time: 199 us -> 192 us (0.965)
  blocking collectives: 17.6 us -> 32.2 us
  waiting for transfers between devices: 92 us -> 81.3 us
  starting transfers between devices: 36.2 us -> 26.7 us
  other arithmetic: 12.7 us -> 6.6 us
  local copies, waits for them, and re-layouts: 3.32 us -> 7.02 us
    all_to_all x2 -> x0, waiting for transfers between devices: 19.1 us -> none  [the longest x1 10.9 us: body(): lax.all_to_all(weight_rows, BOTH, split_axis=0, concat_axis=0, tiled=True)]
    all_to_all x0 -> x1, blocking collectives: none -> 14.6 us  [body(): lax.all_to_all(outgoing, 'feat', split_axis=0, concat_axis=0, tiled=True)]
    all_to_all x2 -> x0, starting transfers between devices: 10.4 us -> none  [the longest x1 5.82 us: body(): lax.all_to_all(features_grad_local, 'feat', split_axis=0, concat_axis=1,...]
    ppermute x2, waiting for transfers between devices: 0.01 us -> 7.5 us  [sibling(): lax.ppermute(block, 'blk', [(i, i ^ 1) for i in range(lax.axis_size('blk'...]
    add x1, other arithmetic: 5.99 us -> 0.01 us  [body(): weight_part = weight_part + swapped(weight_part, 'blk', 1)]
    slice x0 -> x3, local copies, waits for them, and re-layouts: none -> 5.68 us  [the longest x2 5.03 us: term(): return total[k]]
    ppermute x0 -> x2, waiting for transfers between devices: none -> 4.82 us  [swapped(): return lax.ppermute(block, axis, [(i, i ^ mask) for i in range(count)])]
    ppermute x20, waiting for transfers between devices: 72.9 us -> 69 us  [ring_shift(): return lax.ppermute(block, BOTH, route)]
  transfers between devices with their start and end apart: 24 -> 24, of which waited for: 18 -> 19; matrix products, arithmetic and copies ran while one was open for 1% -> 3% of each run, Pallas kernels for 9% -> 4%
where the time goes in v7:
time: 192 us; the launch traced here: 191 us
  waiting for transfers between devices  81.3 us (42%)
  Pallas kernels  35.6 us (19%)
  blocking collectives  32.2 us (17%)
  starting transfers between devices  26.7 us (14%)
  local copies, waits for them, and re-layouts  7.02 us (4%)
  other arithmetic  6.6 us (3%)
    ppermute x20, waiting for transfers between devices, ring_shift(): return lax.ppermute(block, BOTH, route)  69 us
    ppermute x20, starting transfers between devices, ring_shift(): return lax.ppermute(block, BOTH, route)  25.9 us
    pallas_call x2, Pallas kernels, spread_pair(): pl.pallas_call(spread_kernel, grid_spec=grid_spec, out_shape=jax.ShapeDty...  20.3 us
    all_to_all x1, blocking collectives, body(): lax.all_to_all(features_t, 'feat', split_axis=1, concat_axis=0, tiled=True)  17.6 us
    pallas_call x2, Pallas kernels, aggregate_pair(): pl.pallas_call(aggregate_kernel, grid_spec=grid_spec, out_shape=jax.Shape...  15.3 us
    all_to_all x1, blocking collectives, body(): lax.all_to_all(outgoing, 'feat', split_axis=0, concat_axis=0, tiled=True)  14.6 us
    ppermute x2, waiting for transfers between devices, sibling(): lax.ppermute(block, 'blk', [(i, i ^ 1) for i in range(lax.axis_size('blk'...  7.5 us
    slice x2, local copies, waits for them, and re-layouts, term(): return total[k]  5.03 us
  transfers between devices with their start and end apart: 24, of which 19 were waited for; matrix products, arithmetic and copies ran while one was open for 3% of the time, Pallas kernels for 4%

profile of v7, /device:TPU:0, one launch (start us, length us, event | category | flops | bytes accessed | tf_op | source)
XLA Modules:
  0.0 190.9 jit_solution(9887017931866918036)
XLA Ops:
  0.6 17.6 %all_to_all.24 = bf16[4,32,256]{2,0,1:T(4,128)(2,1)S(1)} all-to-all(bf16[4,32,256]{2,0,1:T(4,128)(2,1)} %bitcast.125), channel_id=1, replica_groups=mesh['blk'=4,'feat'=32] {'feat'}, dimensions={1} | all-to-all | bytes 131072 | tf_op jit(solution)/shard_map/all_to_all | solution.py:275
  19.1 2.3 %collective-permute-start.1 = (bf16[256,128]{1,0:T(8,128)(2,1)S(1)}, bf16[256,128]{1,0:T(8,128)(2,1)S(1)}, u32[]{:S(2)}, u32[]{:S(2)}) collective-permute-start(bf16[256,128]{1,0:T(8,128)(2,1)S(1)} %convolution_convert_fusion.1), channel_id=1, source_target_pairs={{0,2},{1,3},{2,0},{3,1},{4,6},{5,7},{6,4},{7,5},{8,10},{9,11},{10,... | collective-permute-start | bytes 196616 | tf_op jit(solution)/shard_map/ppermute | solution.py:37
  22.5 1.5 collective-permute-done.2
  25.7 1.4 collective-permute-start.4
  27.1 1.9 %collective-permute-start.3 = (bf16[4,256,128]{2,1,0:T(8,128)(2,1)S(1)}, bf16[4,256,128]{2,1,0:T(8,128)(2,1)S(1)}, u32[]{:S(2)}, u32[]{:S(2)}) collective-permute-start(bf16[4,256,128]{2,1,0:T(8,128)(2,1)S(1)} %get-tuple-element.21), channel_id=1, source_target_pairs={{0,12},{1,13},{2,14},{3,15},{4,0},{5,1},{6,2},{7,3},{8,4},{9,5},{1... | collective-permute-start | bytes 786440 | tf_op jit(solution)/shard_map/ppermute | solution.py:37
  29.1 6.7 %collective-permute-done.4 = bf16[4,256,128]{2,1,0:T(8,128)(2,1)S(1)} collective-permute-done((bf16[4,256,128]{2,1,0:T(8,128)(2,1)S(1)}, bf16[4,256,128]{2,1,0:T(8,128)(2,1)S(1)}, u32[]{:S(2)}, u32[]{:S(2)}) %collective-permute-start.4) | collective-permute-done | bytes 262176 | tf_op jit(solution)/shard_map/ppermute | solution.py:37
  37.0 1.7 collective-permute-done.5
  38.9 3.4 %collective-permute-start.6 = (bf16[4,4,256,128]{3,2,1,0:T(8,128)(2,1)S(1)}, bf16[4,4,256,128]{3,2,1,0:T(8,128)(2,1)S(1)}, u32[]{:S(2)}, u32[]{:S(2)}) collective-permute-start(bf16[4,4,256,128]{3,2,1,0:T(8,128)(2,1)S(1)} %get-tuple-element.16), channel_id=1, source_target_pairs={{0,80},{1,81},{2,82},{3,83},{4,84},{5,85},{6,86},{7,87},{8,88},{9,... | collective-permute-start | bytes 3145736 | tf_op jit(solution)/shard_map/ppermute | solution.py:37
  42.2 12.3 %collective-permute-done.6 = bf16[4,4,256,128]{3,2,1,0:T(8,128)(2,1)S(1)} collective-permute-done((bf16[4,4,256,128]{3,2,1,0:T(8,128)(2,1)S(1)}, bf16[4,4,256,128]{3,2,1,0:T(8,128)(2,1)S(1)}, u32[]{:S(2)}, u32[]{:S(2)}) %collective-permute-start.6) | collective-permute-done | bytes 1048608 | tf_op jit(solution)/shard_map/ppermute | solution.py:37
  54.6 3.8 %collective-permute-start.9 = (bf16[4,4,128,128]{3,2,1,0:T(8,128)(2,1)S(1)}, bf16[4,4,128,128]{3,2,1,0:T(8,128)(2,1)S(1)}, u32[]{:S(2)}, u32[]{:S(2)}) collective-permute-start(bf16[4,4,128,128]{3,2,1,0:T(8,128)(2,1)S(1)} %slice.104), channel_id=1, source_target_pairs={{0,80},{1,81},{2,82},{3,83},{4,84},{5,85},{6,86},{7,87},{8,88},{9,... | collective-permute-start | bytes 1572872 | tf_op jit(solution)/shard_map/ppermute | solution.py:37
  58.5 6.6 %collective-permute-done.9 = bf16[4,4,128,128]{3,2,1,0:T(8,128)(2,1)S(1)} collective-permute-done((bf16[4,4,128,128]{3,2,1,0:T(8,128)(2,1)S(1)}, bf16[4,4,128,128]{3,2,1,0:T(8,128)(2,1)S(1)}, u32[]{:S(2)}, u32[]{:S(2)}) %collective-permute-start.9) | collective-permute-done | bytes 524320 | tf_op jit(solution)/shard_map/ppermute | solution.py:37
  65.1 3.8 %collective-permute-done.8 = bf16[4,4,128,128]{3,2,1,0:T(8,128)(2,1)S(1)} collective-permute-done((bf16[4,4,128,128]{3,2,1,0:T(8,128)(2,1)S(1)}, bf16[4,4,128,128]{3,2,1,0:T(8,128)(2,1)S(1)}, u32[]{:S(2)}, u32[]{:S(2)}) %collective-permute-start.8) | collective-permute-done | bytes 524320 | tf_op jit(solution)/shard_map/ppermute | solution.py:37
  69.0 2.3 %pad_maximum_fusion = bf16[4,4,4,256,128]{4,3,2,1,0:T(8,128)(2,1)} fusion(bf16[1,4,4,256,128]{4,3,2,1,0:T(8,128)(2,1)S(1)} %bitcast.109, bf16[1,4,4,256,128]{4,3,2,1,0:T(8,128)(2,1)S(1)} %maximum_bitcast_fusion, bf16[1,4,4,256,128]{4,3,2,1,0:T(8,128)(2,1)S(1)} %bitcast.108, bf16[1,4,4,256,128]{4,3,2,1,0:T(8,128)(2,1)S(1)} %get-tuple-element.15), kind=kLoop, calls=%fused_computation | loop fusion | flops 6291456 | bytes 8388608 | tf_op jit(solution)/shard_map/stack | solution.py:56
  71.9 7.6 %shard_map.85 = f32[2,128,128]{2,1,0:T(8,128)} custom-call(s32[1]{0:T(128)} %bitcast.core_ref, s32[256]{0:T(256)} %fusion.21.where_ref, s32[8]{0:T(128)} %count_ref.7, bf16[4,2,32,128,128]{4,3,2,1,0:T(8,128)(2,1)} %bitcast.98, bf16[128,128,128]{2,1,0:T(8,128)(2,1)} %bitcast.16.proj_ref), custom_call_target="tpu_custom_call" | custom-call | tf_op jit(solution)/shard_map/pallas_call | solution.py:161
  79.5 7.7 %shard_map.86 = f32[2,128,128]{2,1,0:T(8,128)} custom-call(s32[1]{0:T(128)} %bitcast.17.core_ref, s32[256]{0:T(256)} %fusion.21.where_ref, s32[8]{0:T(128)} %count_ref.7, bf16[4,2,32,128,128]{4,3,2,1,0:T(8,128)(2,1)} %bitcast.99, bf16[128,128,128]{2,1,0:T(8,128)(2,1)} %collective-permute-done.10.proj_ref), custom_call_target="tpu_custom_call" | custom-call | tf_op jit(solution)/shard_map/pallas_call | solution.py:161
  89.6 8.8 %shard_map.87 = bf16[128,128,128]{2,1,0:T(8,128)(2,1)} custom-call(s32[1]{0:T(128)} %bitcast.17.core_ref, s32[256]{0:T(256)} %fusion.21.where_ref, s32[8]{0:T(128)} %count_ref.7, bf16[4,2,32,128,128]{4,3,2,1,0:T(8,128)(2,1)} %bitcast.100, bf16[2,128,128]{2,1,0:T(8,128)(2,1)} %bitcast.110), custom_call_target="tpu_custom_call" | custom-call | tf_op jit(solution)/shard_map/pallas_call | solution.py:228
  98.4 7.5 %collective-permute-done.11.rest_0_ = bf16[128,128,128]{2,1,0:T(8,128)(2,1)} collective-permute-done((bf16[128,128,128]{2,1,0:T(8,128)(2,1)}, bf16[128,128,128]{2,1,0:T(8,128)(2,1)}, u32[]{:S(2)}, u32[]{:S(2)}) %collective-permute-start.11) | collective-permute-done | bytes 4194336 | tf_op jit(solution)/shard_map/ppermute | solution.py:41
  105.9 11.5 %shard_map.88 = f32[128,128,128]{2,1,0:T(8,128)} custom-call(s32[1]{0:T(128)} %bitcast.core_ref, s32[256]{0:T(256)} %fusion.21.where_ref, s32[8]{0:T(128)} %count_ref.7, bf16[4,2,32,128,128]{4,3,2,1,0:T(8,128)(2,1)} %bitcast.101, bf16[2,128,128]{2,1,0:T(8,128)(2,1)} %bitcast.111, bf16[128,128,128]{2,1,0:T(8,128)(2,1)} %collective-permute-done.11.rest_0_), custom_call_target="tpu_custom_call" | custom-call | tf_op jit(solution)/shard_map/pallas_call | solution.py:228
  117.4 1.7 slice.158
  119.4 2.0 %collective-permute-start.12 = (bf16[4,4,128,128]{3,2,1,0:T(8,128)(2,1)S(1)}, bf16[4,4,128,128]{3,2,1,0:T(8,128)(2,1)S(1)}, u32[]{:S(2)}, u32[]{:S(2)}) collective-permute-start(bf16[4,4,128,128]{3,2,1,0:T(8,128)(2,1)S(1)} %get-tuple-element.13), channel_id=1, source_target_pairs={{0,16},{1,17},{2,18},{3,19},{4,20},{5,21},{6,22},{7,23},{8,24},{9,... | collective-permute-start | bytes 1572872 | tf_op jit(solution)/shard_map/ppermute | solution.py:37
  121.4 3.3 %fusion.31 = (f32[32,128,128]{2,1,0:T(8,128)S(1)}, f32[32,128,128]{2,1,0:T(8,128)S(1)}, f32[32,128,128]{2,1,0:T(8,128)S(1)}) fusion(f32[128,128,128]{2,1,0:T(8,128)} %shard_map.88), kind=kLoop, calls=%fused_computation.95 | loop fusion | bytes 12582912 | tf_op jit(solution)/shard_map/slice | solution.py:83
  124.8 3.7 %collective-permute-done.14 = bf16[4,4,128,128]{3,2,1,0:T(8,128)(2,1)S(1)} collective-permute-done((bf16[4,4,128,128]{3,2,1,0:T(8,128)(2,1)S(1)}, bf16[4,4,128,128]{3,2,1,0:T(8,128)(2,1)S(1)}, u32[]{:S(2)}, u32[]{:S(2)}) %collective-permute-start.14) | collective-permute-done | bytes 524320 | tf_op jit(solution)/shard_map/ppermute | solution.py:37
  128.8 1.3 collective-permute-start.15
  131.2 12.5 %collective-permute-done.15 = bf16[4,4,256,128]{3,2,1,0:T(8,128)(2,1)S(1)} collective-permute-done((bf16[4,4,256,128]{3,2,1,0:T(8,128)(2,1)S(1)}, bf16[4,4,256,128]{3,2,1,0:T(8,128)(2,1)S(1)}, u32[]{:S(2)}, u32[]{:S(2)}) %collective-permute-start.15) | collective-permute-done | bytes 1048608 | tf_op jit(solution)/shard_map/ppermute | solution.py:37
  143.6 2.7 %collective-permute-done.13 = bf16[4,4,256,128]{3,2,1,0:T(8,128)(2,1)S(1)} collective-permute-done((bf16[4,4,256,128]{3,2,1,0:T(8,128)(2,1)S(1)}, bf16[4,4,256,128]{3,2,1,0:T(8,128)(2,1)S(1)}, u32[]{:S(2)}, u32[]{:S(2)}) %collective-permute-start.13) | collective-permute-done | bytes 1048608 | tf_op jit(solution)/shard_map/ppermute | solution.py:37
  147.4 2.3 %collective-permute-start.18 = (bf16[4,256,128]{2,1,0:T(8,128)(2,1)S(1)}, bf16[4,256,128]{2,1,0:T(8,128)(2,1)S(1)}, u32[]{:S(2)}, u32[]{:S(2)}) collective-permute-start(bf16[4,256,128]{2,1,0:T(8,128)(2,1)S(1)} %get-tuple-element.11), channel_id=1, source_target_pairs={{0,8},{1,9},{2,10},{3,11},{4,12},{5,13},{6,14},{7,15},{8,0},{9,1},... | collective-permute-start | bytes 786440 | tf_op jit(solution)/shard_map/ppermute | solution.py:37
  150.6 10.3 %collective-permute-done.16 = bf16[4,256,128]{2,1,0:T(8,128)(2,1)S(1)} collective-permute-done((bf16[4,256,128]{2,1,0:T(8,128)(2,1)S(1)}, bf16[4,256,128]{2,1,0:T(8,128)(2,1)S(1)}, u32[]{:S(2)}, u32[]{:S(2)}) %collective-permute-start.16) | collective-permute-done | bytes 262176 | tf_op jit(solution)/shard_map/ppermute | solution.py:37
  161.7 1.4 collective-permute-start.21
  163.2 1.8 collective-permute-start.20
  165.0 2.9 %collective-permute-done.19 = bf16[256,128]{1,0:T(8,128)(2,1)S(1)} collective-permute-done((bf16[256,128]{1,0:T(8,128)(2,1)S(1)}, bf16[256,128]{1,0:T(8,128)(2,1)S(1)}, u32[]{:S(2)}, u32[]{:S(2)}) %collective-permute-start.19) | collective-permute-done | bytes 65568 | tf_op jit(solution)/shard_map/ppermute | solution.py:37
  169.3 14.6 %all_to_all.25 = f32[32,4,384]{2,1,0:T(4,128)S(1)} all-to-all(f32[32,4,384]{2,1,0:T(4,128)S(1)} %pad_maximum_fusion.5), channel_id=1, replica_groups=mesh['blk'=4,'feat'=32] {'feat'}, dimensions={0} | all-to-all | bytes 393216 | tf_op jit(solution)/shard_map/all_to_all | solution.py:330
  186.6 3.7 %collective-permute-done.23 = f32[4,128]{1,0:T(4,128)S(1)} collective-permute-done((f32[4,128]{1,0:T(4,128)S(1)}, f32[4,128]{1,0:T(4,128)S(1)}, u32[]{:S(2)}, u32[]{:S(2)}) %collective-permute-start.23) | collective-permute-done | bytes 2080 | tf_op jit(solution)/shard_map/ppermute | solution.py:46
  (65 shorter events, 17.3 us)
Async XLA Ops:
  0.6 17.6 %copy-start = (bf16[128,128]{1,0:T(8,128)(2,1)S(1)}, bf16[128,128]{1,0:T(8,128)(2,1)}, u32[]{:S(2)}) copy-start(bf16[128,128]{1,0:T(8,128)(2,1)} %param.7) | copy-start | bytes 98308
  18.5 5.5 %collective-permute-start.2 = (bf16[256,128]{1,0:T(8,128)(2,1)S(1)}, bf16[256,128]{1,0:T(8,128)(2,1)S(1)}, u32[]{:S(2)}, u32[]{:S(2)}) collective-permute-start(bf16[256,128]{1,0:T(8,128)(2,1)S(1)} %convolution_convert_fusion.1), channel_id=1, source_target_pairs={{0,1},{1,2},{2,3},{3,0},{4,5},{5,6},{6,7},{7,4},{8,9},{9,10},{10,1... | collective-permute-start | bytes 196616 | tf_op jit(solution)/shard_map/ppermute | solution.py:37
  19.1 5.8 %collective-permute-start.1 = (bf16[256,128]{1,0:T(8,128)(2,1)S(1)}, bf16[256,128]{1,0:T(8,128)(2,1)S(1)}, u32[]{:S(2)}, u32[]{:S(2)}) collective-permute-start(bf16[256,128]{1,0:T(8,128)(2,1)S(1)} %convolution_convert_fusion.1), channel_id=1, source_target_pairs={{0,2},{1,3},{2,0},{3,1},{4,6},{5,7},{6,4},{7,5},{8,10},{9,11},{10,... | collective-permute-start | bytes 196616 | tf_op jit(solution)/shard_map/ppermute | solution.py:37
  21.4 4.3 %collective-permute-start = (bf16[256,128]{1,0:T(8,128)(2,1)S(1)}, bf16[256,128]{1,0:T(8,128)(2,1)S(1)}, u32[]{:S(2)}, u32[]{:S(2)}) collective-permute-start(bf16[256,128]{1,0:T(8,128)(2,1)S(1)} %convolution_convert_fusion.1), channel_id=1, source_target_pairs={{0,3},{1,0},{2,1},{3,2},{4,7},{5,4},{6,5},{7,6},{8,11},{9,8},{10,9... | collective-permute-start | bytes 196616 | tf_op jit(solution)/shard_map/ppermute | solution.py:37
  25.7 10.1 %collective-permute-start.4 = (bf16[4,256,128]{2,1,0:T(8,128)(2,1)S(1)}, bf16[4,256,128]{2,1,0:T(8,128)(2,1)S(1)}, u32[]{:S(2)}, u32[]{:S(2)}) collective-permute-start(bf16[4,256,128]{2,1,0:T(8,128)(2,1)S(1)} %get-tuple-element.21), channel_id=1, source_target_pairs={{0,8},{1,9},{2,10},{3,11},{4,12},{5,13},{6,14},{7,15},{8,0},{9,1},... | collective-permute-start | bytes 786440 | tf_op jit(solution)/shard_map/ppermute | solution.py:37
  27.1 9.9 %collective-permute-start.3 = (bf16[4,256,128]{2,1,0:T(8,128)(2,1)S(1)}, bf16[4,256,128]{2,1,0:T(8,128)(2,1)S(1)}, u32[]{:S(2)}, u32[]{:S(2)}) collective-permute-start(bf16[4,256,128]{2,1,0:T(8,128)(2,1)S(1)} %get-tuple-element.21), channel_id=1, source_target_pairs={{0,12},{1,13},{2,14},{3,15},{4,0},{5,1},{6,2},{7,3},{8,4},{9,5},{1... | collective-permute-start | bytes 786440 | tf_op jit(solution)/shard_map/ppermute | solution.py:37
  29.0 9.7 %collective-permute-start.5 = (bf16[4,256,128]{2,1,0:T(8,128)(2,1)S(1)}, bf16[4,256,128]{2,1,0:T(8,128)(2,1)S(1)}, u32[]{:S(2)}, u32[]{:S(2)}) collective-permute-start(bf16[4,256,128]{2,1,0:T(8,128)(2,1)S(1)} %get-tuple-element.21), channel_id=1, source_target_pairs={{0,4},{1,5},{2,6},{3,7},{4,8},{5,9},{6,10},{7,11},{8,12},{9,13},{1... | collective-permute-start | bytes 786440 | tf_op jit(solution)/shard_map/ppermute | solution.py:37
  38.9 15.7 %collective-permute-start.6 = (bf16[4,4,256,128]{3,2,1,0:T(8,128)(2,1)S(1)}, bf16[4,4,256,128]{3,2,1,0:T(8,128)(2,1)S(1)}, u32[]{:S(2)}, u32[]{:S(2)}) collective-permute-start(bf16[4,4,256,128]{3,2,1,0:T(8,128)(2,1)S(1)} %get-tuple-element.16), channel_id=1, source_target_pairs={{0,80},{1,81},{2,82},{3,83},{4,84},{5,85},{6,86},{7,87},{8,88},{9,... | collective-permute-start | bytes 3145736 | tf_op jit(solution)/shard_map/ppermute | solution.py:37
  42.2 16.1 %collective-permute-start.7 = (bf16[4,4,256,128]{3,2,1,0:T(8,128)(2,1)S(1)}, bf16[4,4,256,128]{3,2,1,0:T(8,128)(2,1)S(1)}, u32[]{:S(2)}, u32[]{:S(2)}) collective-permute-start(bf16[4,4,256,128]{3,2,1,0:T(8,128)(2,1)S(1)} %get-tuple-element.16), channel_id=1, source_target_pairs={{0,16},{1,17},{2,18},{3,19},{4,20},{5,21},{6,22},{7,23},{8,24},{9,... | collective-permute-start | bytes 3145736 | tf_op jit(solution)/shard_map/ppermute | solution.py:37
  54.6 10.5 %collective-permute-start.9 = (bf16[4,4,128,128]{3,2,1,0:T(8,128)(2,1)S(1)}, bf16[4,4,128,128]{3,2,1,0:T(8,128)(2,1)S(1)}, u32[]{:S(2)}, u32[]{:S(2)}) collective-permute-start(bf16[4,4,128,128]{3,2,1,0:T(8,128)(2,1)S(1)} %slice.104), channel_id=1, source_target_pairs={{0,80},{1,81},{2,82},{3,83},{4,84},{5,85},{6,86},{7,87},{8,88},{9,... | collective-permute-start | bytes 1572872 | tf_op jit(solution)/shard_map/ppermute | solution.py:37
  58.4 10.5 %collective-permute-start.8 = (bf16[4,4,128,128]{3,2,1,0:T(8,128)(2,1)S(1)}, bf16[4,4,128,128]{3,2,1,0:T(8,128)(2,1)S(1)}, u32[]{:S(2)}, u32[]{:S(2)}) collective-permute-start(bf16[4,4,128,128]{3,2,1,0:T(8,128)(2,1)S(1)} %slice.103), channel_id=1, source_target_pairs={{0,16},{1,17},{2,18},{3,19},{4,20},{5,21},{6,22},{7,23},{8,24},{9,... | collective-permute-start | bytes 1572872 | tf_op jit(solution)/shard_map/ppermute | solution.py:37
  69.0 2.3 %copy-start.3 = (s32[256]{0:T(256)S(1)}, s32[256]{0:T(256)}, u32[]{:S(2)}) copy-start(s32[256]{0:T(256)} %param.9) | copy-start | bytes 3076
  71.3 8.2 %collective-permute-start.10 = (bf16[128,128,128]{2,1,0:T(8,128)(2,1)}, bf16[128,128,128]{2,1,0:T(8,128)(2,1)}, u32[]{:S(2)}, u32[]{:S(2)}) collective-permute-start(bf16[128,128,128]{2,1,0:T(8,128)(2,1)} %bitcast.16.proj_ref), channel_id=1, source_target_pairs={{0,32},{32,0},{64,96},{96,64},{1,33},{33,1},{65,97},{97,65},{2,34}... | collective-permute-start | bytes 12582920 | tf_op jit(solution)/shard_map/ppermute | solution.py:41
  79.5 7.7 %copy-start.1 = (f32[2,128,128]{2,1,0:T(8,128)S(1)}, f32[2,128,128]{2,1,0:T(8,128)}, u32[]{:S(2)}) copy-start(f32[2,128,128]{2,1,0:T(8,128)} %shard_map.85) | copy-start | bytes 393220
  79.5 8.7 %copy-start.2 = (bf16[256,128]{1,0:T(8,128)(2,1)S(1)}, bf16[256,128]{1,0:T(8,128)(2,1)}, u32[]{:S(2)}) copy-start(bf16[256,128]{1,0:T(8,128)(2,1)} %param.11) | copy-start | bytes 196612
  98.4 7.5 %collective-permute-start.11 = (bf16[128,128,128]{2,1,0:T(8,128)(2,1)}, bf16[128,128,128]{2,1,0:T(8,128)(2,1)}, u32[]{:S(2)}, u32[]{:S(2)}) collective-permute-start(bf16[128,128,128]{2,1,0:T(8,128)(2,1)} %shard_map.87), channel_id=1, source_target_pairs={{0,32},{32,0},{64,96},{96,64},{1,33},{33,1},{65,97},{97,65},{2,34}... | collective-permute-start | bytes 12582920 | tf_op jit(solution)/shard_map/ppermute | solution.py:41
  119.3 9.2 %collective-permute-start.14 = (bf16[4,4,128,128]{3,2,1,0:T(8,128)(2,1)S(1)}, bf16[4,4,128,128]{3,2,1,0:T(8,128)(2,1)S(1)}, u32[]{:S(2)}, u32[]{:S(2)}) collective-permute-start(bf16[4,4,128,128]{3,2,1,0:T(8,128)(2,1)S(1)} %get-tuple-element.14), channel_id=1, source_target_pairs={{0,80},{1,81},{2,82},{3,83},{4,84},{5,85},{6,86},{7,87},{8,88},{9,... | collective-permute-start | bytes 1572872 | tf_op jit(solution)/shard_map/ppermute | solution.py:37
  119.4 10.7 %collective-permute-start.12 = (bf16[4,4,128,128]{3,2,1,0:T(8,128)(2,1)S(1)}, bf16[4,4,128,128]{3,2,1,0:T(8,128)(2,1)S(1)}, u32[]{:S(2)}, u32[]{:S(2)}) collective-permute-start(bf16[4,4,128,128]{3,2,1,0:T(8,128)(2,1)S(1)} %get-tuple-element.13), channel_id=1, source_target_pairs={{0,16},{1,17},{2,18},{3,19},{4,20},{5,21},{6,22},{7,23},{8,24},{9,... | collective-permute-start | bytes 1572872 | tf_op jit(solution)/shard_map/ppermute | solution.py:37
  128.8 14.9 %collective-permute-start.15 = (bf16[4,4,256,128]{3,2,1,0:T(8,128)(2,1)S(1)}, bf16[4,4,256,128]{3,2,1,0:T(8,128)(2,1)S(1)}, u32[]{:S(2)}, u32[]{:S(2)}) collective-permute-start(bf16[4,4,256,128]{3,2,1,0:T(8,128)(2,1)S(1)} %pad_maximum_fusion.3), channel_id=1, source_target_pairs={{0,80},{1,81},{2,82},{3,83},{4,84},{5,85},{6,86},{7,87},{8,88},{9,... | collective-permute-start | bytes 3145736 | tf_op jit(solution)/shard_map/ppermute | solution.py:37
  130.3 16.1 %collective-permute-start.13 = (bf16[4,4,256,128]{3,2,1,0:T(8,128)(2,1)S(1)}, bf16[4,4,256,128]{3,2,1,0:T(8,128)(2,1)S(1)}, u32[]{:S(2)}, u32[]{:S(2)}) collective-permute-start(bf16[4,4,256,128]{3,2,1,0:T(8,128)(2,1)S(1)} %pad_maximum_fusion.2), channel_id=1, source_target_pairs={{0,16},{1,17},{2,18},{3,19},{4,20},{5,21},{6,22},{7,23},{8,24},{9,... | collective-permute-start | bytes 3145736 | tf_op jit(solution)/shard_map/ppermute | solution.py:37
  146.9 14.0 %collective-permute-start.16 = (bf16[4,256,128]{2,1,0:T(8,128)(2,1)S(1)}, bf16[4,256,128]{2,1,0:T(8,128)(2,1)S(1)}, u32[]{:S(2)}, u32[]{:S(2)}) collective-permute-start(bf16[4,256,128]{2,1,0:T(8,128)(2,1)S(1)} %get-tuple-element.10), channel_id=1, source_target_pairs={{0,4},{1,5},{2,6},{3,7},{4,8},{5,9},{6,10},{7,11},{8,12},{9,13},{1... | collective-permute-start | bytes 786440 | tf_op jit(solution)/shard_map/ppermute | solution.py:37
  147.4 13.5 %collective-permute-start.18 = (bf16[4,256,128]{2,1,0:T(8,128)(2,1)S(1)}, bf16[4,256,128]{2,1,0:T(8,128)(2,1)S(1)}, u32[]{:S(2)}, u32[]{:S(2)}) collective-permute-start(bf16[4,256,128]{2,1,0:T(8,128)(2,1)S(1)} %get-tuple-element.11), channel_id=1, source_target_pairs={{0,8},{1,9},{2,10},{3,11},{4,12},{5,13},{6,14},{7,15},{8,0},{9,1},... | collective-permute-start | bytes 786440 | tf_op jit(solution)/shard_map/ppermute | solution.py:37
  149.7 11.8 %collective-permute-start.17 = (bf16[4,256,128]{2,1,0:T(8,128)(2,1)S(1)}, bf16[4,256,128]{2,1,0:T(8,128)(2,1)S(1)}, u32[]{:S(2)}, u32[]{:S(2)}) collective-permute-start(bf16[4,256,128]{2,1,0:T(8,128)(2,1)S(1)} %get-tuple-element.12), channel_id=1, source_target_pairs={{0,12},{1,13},{2,14},{3,15},{4,0},{5,1},{6,2},{7,3},{8,4},{9,5},{1... | collective-permute-start | bytes 786440 | tf_op jit(solution)/shard_map/ppermute | solution.py:37
  161.7 6.2 %collective-permute-start.19 = (bf16[256,128]{1,0:T(8,128)(2,1)S(1)}, bf16[256,128]{1,0:T(8,128)(2,1)S(1)}, u32[]{:S(2)}, u32[]{:S(2)}) collective-permute-start(bf16[256,128]{1,0:T(8,128)(2,1)S(1)} %get-tuple-element.17), channel_id=1, source_target_pairs={{0,1},{1,2},{2,3},{3,0},{4,5},{5,6},{6,7},{7,4},{8,9},{9,10},{10,1... | collective-permute-start | bytes 196616 | tf_op jit(solution)/shard_map/ppermute | solution.py:37
  161.7 6.2 %collective-permute-start.21 = (bf16[256,128]{1,0:T(8,128)(2,1)S(1)}, bf16[256,128]{1,0:T(8,128)(2,1)S(1)}, u32[]{:S(2)}, u32[]{:S(2)}) collective-permute-start(bf16[256,128]{1,0:T(8,128)(2,1)S(1)} %get-tuple-element.18), channel_id=1, source_target_pairs={{0,2},{1,3},{2,0},{3,1},{4,6},{5,7},{6,4},{7,5},{8,10},{9,11},{10,... | collective-permute-start | bytes 196616 | tf_op jit(solution)/shard_map/ppermute | solution.py:37
  163.2 5.6 %collective-permute-start.20 = (bf16[256,128]{1,0:T(8,128)(2,1)S(1)}, bf16[256,128]{1,0:T(8,128)(2,1)S(1)}, u32[]{:S(2)}, u32[]{:S(2)}) collective-permute-start(bf16[256,128]{1,0:T(8,128)(2,1)S(1)} %get-tuple-element.19), channel_id=1, source_target_pairs={{0,3},{1,0},{2,1},{3,2},{4,7},{5,4},{6,5},{7,6},{8,11},{9,8},{10,9... | collective-permute-start | bytes 196616 | tf_op jit(solution)/shard_map/ppermute | solution.py:37
  184.0 1.2 collective-permute-start.22
  185.2 5.1 %collective-permute-start.23 = (f32[4,128]{1,0:T(4,128)S(1)}, f32[4,128]{1,0:T(4,128)S(1)}, u32[]{:S(2)}, u32[]{:S(2)}) collective-permute-start(f32[4,128]{1,0:T(4,128)S(1)} %add.149), channel_id=1, source_target_pairs={{0,64},{32,96},{64,0},{96,32},{1,65},{33,97},{65,1},{97,33},{2,66}... | collective-permute-start | bytes 6152 | tf_op jit(solution)/shard_map/ppermute | solution.py:46

commit v8 on v7

--- a/solution.py
+++ b/solution.py
@@ -47,12 +47,12 @@
 
 
 def gather_phase(block, phase):
-    half = block.shape[-2] // 2
+    half = block.shape[-1] // 2
     from_minus = ring_shift(block, phase, 1)
     from_plus = ring_shift(block, phase, -1)
-    far_low = ring_shift(from_minus[..., :half, :], phase, 1)
-    far_high = ring_shift(from_plus[..., half:, :], phase, -1)
-    far = jnp.concatenate([far_low, far_high], axis=-2)
+    far_low = ring_shift(from_minus[..., :half], phase, 1)
+    far_high = ring_shift(from_plus[..., half:], phase, -1)
+    far = jnp.concatenate([far_low, far_high], axis=-1)
     return jnp.stack([block, from_plus, far, from_minus])
 
 
@@ -240,6 +240,18 @@
     )
 
 
+def chunk_sources(blk_id, feat_id):
+    own = place_of(blk_id, feat_id)
+    chunk = jnp.arange(RING ** 3, dtype=jnp.int32)
+    lead, mid, last = chunk // 16, (chunk // 4) % 4, chunk % 4
+    ry = jnp.where(own["core"] == 0, lead, last)
+    rx = jnp.where(own["core"] == 0, last, lead)
+    y = (own["y"] + ry) % RING
+    z = (own["z"] + mid) % RING
+    x = (own["x"] + rx) % RING
+    return y, (y % 2) * 16 + z * 4 + x
+
+
 def buffer_spots(tile_col, blk_id, feat_id, block_tiles, tiles_per_device):
     own = place_of(blk_id, feat_id)
     block = tile_col // block_tiles
@@ -272,19 +284,31 @@
     spots = buffer_spots(tile_col, blk_id, feat_id, block_tiles, tile_rows)
     buffer_tiles = block_tiles * 2
 
-    features_own = lax.all_to_all(features_t, "feat", split_axis=1, concat_axis=0, tiled=True)
-    projected = lax.dot_general(
-        features_own, weight, (((0,), (0,)), ((), ())), preferred_element_type=jnp.float32
-    ).astype(jnp.bfloat16)
-
-    gathered = gather_phase_direct(projected, 0)
+    gathered = gather_phase_direct(features_t, 0)
     gathered = gather_phase_direct(gathered, 1)
     gathered = gather_phase(gathered, 2)
-    own_buffer = gathered.reshape(buffer_tiles, tile_size, hidden_width)
+    part_cols = features_t.shape[0]
+    source_y, source_feat = chunk_sources(blk_id, feat_id)
+    feature_rows = (source_feat[:, None] * part_cols + jnp.arange(part_cols)[None, :]).reshape(-1)
+    weight_rows = jnp.take(weight, feature_rows, axis=0)
+    stacked = gathered.reshape(-1, block_rows)
+    halves = []
+    for half_id in range(2):
+        keep = jnp.repeat(source_y // 2 == half_id, part_cols)
+        chosen = jnp.where(keep[:, None], weight_rows, jnp.zeros((), weight.dtype))
+        halves.append(
+            lax.dot_general(
+                stacked, chosen, (((0,), (0,)), ((), ())), preferred_element_type=jnp.float32
+            ).astype(jnp.bfloat16)
+        )
+    own_buffer = jnp.stack(halves).reshape(buffer_tiles, tile_size, hidden_width)
     other_buffer = sibling(own_buffer)
-    aggregate_sum = aggregate_pair(core_id, spots, tile_count, tile_stack, own_buffer)
+    block_spots = ((tile_col // block_tiles) // 2 * block_tiles + tile_col % block_tiles).astype(
+        jnp.int32
+    )
+    aggregate_sum = aggregate_pair(core_id, block_spots, tile_count, tile_stack, own_buffer)
     aggregate_sum = aggregate_sum + aggregate_pair(
-        1 - core_id, spots, tile_count, tile_stack, other_buffer
+        1 - core_id, block_spots, tile_count, tile_stack, other_buffer
     )
 
     pre_act = aggregate_sum.reshape(rows_own, hidden_width)
@@ -314,7 +338,19 @@
         .astype(jnp.bfloat16)
     )
 
-    weight_term = jnp.dot(features_own, grad_hidden, preferred_element_type=jnp.float32)
+    own_cols = lax.dynamic_slice_in_dim(gathered, feat_id * rows_own, rows_own, gathered.ndim - 1)
+    chunk_terms = jnp.dot(
+        own_cols.reshape(-1, rows_own), grad_hidden, preferred_element_type=jnp.float32
+    )
+    own_place = place_of(blk_id, feat_id)
+    feat_all = jnp.arange(lax.axis_size("feat"), dtype=jnp.int32)
+    home = place_of(blk_id, feat_all)
+    ry = (home["y"] - own_place["y"]) % RING
+    rz = (home["z"] - own_place["z"]) % RING
+    rx = (home["x"] - own_place["x"]) % RING
+    home_chunk = jnp.where(own_place["core"] == 0, ry * 16 + rz * 4 + rx, rx * 16 + rz * 4 + ry)
+    term_rows = (home_chunk[:, None] * part_cols + jnp.arange(part_cols)[None, :]).reshape(-1)
+    weight_term = jnp.take(chunk_terms, term_rows, axis=0)
     features_grad_local = lax.dot_general(
         weight, grad_hidden, (((1,), (1,)), ((), ())), preferred_element_type=jnp.float32
     ).astype(jnp.bfloat16)

time: 192 us -> 204 us (1.062)
  blocking collectives: 32.2 us -> 14.4 us
  other arithmetic: 6.6 us -> 19.9 us
  local copies, waits for them, and re-layouts: 7.02 us -> 17.6 us
  starting transfers between devices: 26.7 us -> 32.4 us
  matrix products: 0.49 us -> 5.44 us
  waiting for transfers between devices: 81.3 us -> 77 us
    all_to_all x1 -> x0, blocking collectives: 17.6 us -> none  [body(): lax.all_to_all(features_t, 'feat', split_axis=1, concat_axis=0, tiled=True)]
    reshape x0 -> x2, local copies, waits for them, and re-layouts: none -> 6.93 us  [the longest x1 6.89 us: body(): stacked = gathered.reshape(-1, block_rows)]
    dot_general x2 -> x3, matrix products: 0.34 us -> 5.28 us  [the longest x2 5.11 us: body(): lax.dot_general(stacked, chosen, (((0,), (0,)), ((), ())), preferred_elem...]
    ppermute x20, starting transfers between devices: 25.9 us -> 30.2 us  [ring_shift(): return lax.ppermute(block, BOTH, route)]
    another operation x3, other arithmetic: 2.56 us -> 6.45 us  [gather_phase(): return jnp.stack([block, from_plus, far, from_minus])]
    another operation x4 -> x5, other arithmetic: 0.88 us -> 4.46 us  [the longest x1 2.4 us: body(): jnp.stack(halves).reshape(buffer_tiles, tile_size, hidden_width)]
    ppermute x20, waiting for transfers between devices: 69 us -> 65.5 us  [ring_shift(): return lax.ppermute(block, BOTH, route)]
    another operation x1 -> x3, other arithmetic: 0.05 us -> 3.1 us  [gather_phase_direct(): return jnp.stack([block, from_plus, far, from_minus])]
  transfers between devices with their start and end apart: 24 -> 24, of which waited for: 19 -> 16; matrix products, arithmetic and copies ran while one was open for 3% -> 6% of each run, Pallas kernels for 4% -> 4%
where the time goes in v8:
time: 204 us; the launch traced here: 203 us
  waiting for transfers between devices  77 us (38%)
  Pallas kernels  34.7 us (17%)
  starting transfers between devices  32.4 us (16%)
  other arithmetic  19.9 us (10%)
  local copies, waits for them, and re-layouts  17.6 us (9%)
  blocking collectives  14.4 us (7%)
  matrix products  5.44 us (3%)
    ppermute x20, waiting for transfers between devices, ring_shift(): return lax.ppermute(block, BOTH, route)  65.5 us
    ppermute x20, starting transfers between devices, ring_shift(): return lax.ppermute(block, BOTH, route)  30.2 us
    pallas_call x2, Pallas kernels, spread_pair(): pl.pallas_call(spread_kernel, grid_spec=grid_spec, out_shape=jax.ShapeDty...  19.4 us
    pallas_call x2, Pallas kernels, aggregate_pair(): pl.pallas_call(aggregate_kernel, grid_spec=grid_spec, out_shape=jax.Shape...  15.3 us
    all_to_all x1, blocking collectives, body(): lax.all_to_all(outgoing, 'feat', split_axis=0, concat_axis=0, tiled=True)  14.4 us
    ppermute x2, waiting for transfers between devices, sibling(): lax.ppermute(block, 'blk', [(i, i ^ 1) for i in range(lax.axis_size('blk'...  7.13 us
    reshape x1, local copies, waits for them, and re-layouts, body(): stacked = gathered.reshape(-1, block_rows)  6.89 us
    another operation x3, other arithmetic, gather_phase(): return jnp.stack([block, from_plus, far, from_minus])  6.45 us
  transfers between devices with their start and end apart: 24, of which 16 were waited for; matrix products, arithmetic and copies ran while one was open for 6% of the time, Pallas kernels for 4%

profile of v8, /device:TPU:0, one launch (start us, length us, event | category | flops | bytes accessed | tf_op | source)
XLA Modules:
  0.0 202.6 jit_solution(13091178792500866615)
XLA Ops:
  0.6 2.9 %collective-permute-start = (bf16[4,8192]{1,0:T(4,128)(2,1)}, bf16[4,8192]{1,0:T(4,128)(2,1)S(1)}, u32[]{:S(2)}, u32[]{:S(2)}) collective-permute-start(bf16[4,8192]{1,0:T(4,128)(2,1)} %param.6), channel_id=1, source_target_pairs={{0,3},{1,0},{2,1},{3,2},{4,7},{5,4},{6,5},{7,6},{8,11},{9,8},{10,9... | collective-permute-start | bytes 196616 | tf_op jit(solution)/shard_map/ppermute | solution.py:37
  3.6 2.3 %collective-permute-start.1 = (bf16[4,8192]{1,0:T(4,128)(2,1)}, bf16[4,8192]{1,0:T(4,128)(2,1)S(1)}, u32[]{:S(2)}, u32[]{:S(2)}) collective-permute-start(bf16[4,8192]{1,0:T(4,128)(2,1)} %param.6), channel_id=1, source_target_pairs={{0,2},{1,3},{2,0},{3,1},{4,6},{5,7},{6,4},{7,5},{8,10},{9,11},{10,... | collective-permute-start | bytes 196616 | tf_op jit(solution)/shard_map/ppermute | solution.py:37
  5.9 4.1 %collective-permute-done.2 = bf16[4,8192]{1,0:T(4,128)(2,1)S(1)} collective-permute-done((bf16[4,8192]{1,0:T(4,128)(2,1)}, bf16[4,8192]{1,0:T(4,128)(2,1)S(1)}, u32[]{:S(2)}, u32[]{:S(2)}) %collective-permute-start.2) | collective-permute-done | bytes 65568 | tf_op jit(solution)/shard_map/ppermute | solution.py:37
  11.0 4.0 %collective-permute-start.4 = (bf16[4,4,8192]{2,1,0:T(4,128)(2,1)S(1)}, bf16[4,4,8192]{2,1,0:T(4,128)(2,1)S(1)}, u32[]{:S(2)}, u32[]{:S(2)}) collective-permute-start(bf16[4,4,8192]{2,1,0:T(4,128)(2,1)S(1)} %pad_maximum_fusion.5), channel_id=1, source_target_pairs={{0,8},{1,9},{2,10},{3,11},{4,12},{5,13},{6,14},{7,15},{8,0},{9,1},... | collective-permute-start | bytes 786440 | tf_op jit(solution)/shard_map/ppermute | solution.py:37
  18.1 4.1 %collective-permute-done.4 = bf16[4,4,8192]{2,1,0:T(4,128)(2,1)S(1)} collective-permute-done((bf16[4,4,8192]{2,1,0:T(4,128)(2,1)S(1)}, bf16[4,4,8192]{2,1,0:T(4,128)(2,1)S(1)}, u32[]{:S(2)}, u32[]{:S(2)}) %collective-permute-start.4) | collective-permute-done | bytes 262176 | tf_op jit(solution)/shard_map/ppermute | solution.py:37
  22.2 4.6 %collective-permute-done.3 = bf16[4,4,8192]{2,1,0:T(4,128)(2,1)S(1)} collective-permute-done((bf16[4,4,8192]{2,1,0:T(4,128)(2,1)S(1)}, bf16[4,4,8192]{2,1,0:T(4,128)(2,1)S(1)}, u32[]{:S(2)}, u32[]{:S(2)}) %collective-permute-start.3) | collective-permute-done | bytes 262176 | tf_op jit(solution)/shard_map/ppermute | solution.py:37
  27.8 2.3 %collective-permute-start.6 = (bf16[4,4,4,8192]{3,2,1,0:T(4,128)(2,1)S(1)}, bf16[4,4,4,8192]{3,2,1,0:T(4,128)(2,1)S(1)}, u32[]{:S(2)}, u32[]{:S(2)}) collective-permute-start(bf16[4,4,4,8192]{3,2,1,0:T(4,128)(2,1)S(1)} %pad_maximum_fusion.2), channel_id=1, source_target_pairs={{0,80},{1,81},{2,82},{3,83},{4,84},{5,85},{6,86},{7,87},{8,88},{9,... | collective-permute-start | bytes 3145736 | tf_op jit(solution)/shard_map/ppermute | solution.py:37
  31.8 10.8 %collective-permute-done.6 = bf16[4,4,4,8192]{3,2,1,0:T(4,128)(2,1)S(1)} collective-permute-done((bf16[4,4,4,8192]{3,2,1,0:T(4,128)(2,1)S(1)}, bf16[4,4,4,8192]{3,2,1,0:T(4,128)(2,1)S(1)}, u32[]{:S(2)}, u32[]{:S(2)}) %collective-permute-start.6) | collective-permute-done | bytes 1048608 | tf_op jit(solution)/shard_map/ppermute | solution.py:37
  42.8 3.5 %collective-permute-start.9 = (bf16[4,4,4,4096]{3,2,1,0:T(4,128)(2,1)S(1)}, bf16[4,4,4,4096]{3,2,1,0:T(4,128)(2,1)S(1)}, u32[]{:S(2)}, u32[]{:S(2)}) collective-permute-start(bf16[4,4,4,4096]{3,2,1,0:T(4,128)(2,1)S(1)} %slice.108), channel_id=1, source_target_pairs={{0,80},{1,81},{2,82},{3,83},{4,84},{5,85},{6,86},{7,87},{8,88},{9,... | collective-permute-start | bytes 1572872 | tf_op jit(solution)/shard_map/ppermute | solution.py:37
  47.8 5.2 %collective-permute-done.9 = bf16[4,4,4,4096]{3,2,1,0:T(4,128)(2,1)S(1)} collective-permute-done((bf16[4,4,4,4096]{3,2,1,0:T(4,128)(2,1)S(1)}, bf16[4,4,4,4096]{3,2,1,0:T(4,128)(2,1)S(1)}, u32[]{:S(2)}, u32[]{:S(2)}) %collective-permute-start.9) | collective-permute-done | bytes 524320 | tf_op jit(solution)/shard_map/ppermute | solution.py:37
  53.1 4.2 %collective-permute-done.8 = bf16[4,4,4,4096]{3,2,1,0:T(4,128)(2,1)S(1)} collective-permute-done((bf16[4,4,4,4096]{3,2,1,0:T(4,128)(2,1)S(1)}, bf16[4,4,4,4096]{3,2,1,0:T(4,128)(2,1)S(1)}, u32[]{:S(2)}, u32[]{:S(2)}) %collective-permute-start.8) | collective-permute-done | bytes 524320 | tf_op jit(solution)/shard_map/ppermute | solution.py:37
  57.9 4.9 %pad_maximum_fusion = bf16[4,4,4,4,8192]{4,3,2,1,0:T(4,128)(2,1)} fusion(bf16[1,4,4,4,8192]{4,3,2,1,0:T(4,128)(2,1)S(1)} %bitcast.112, bf16[1,4,4,4,8192]{4,3,2,1,0:T(4,128)(2,1)S(1)} %maximum_bitcast_fusion, bf16[1,4,4,4,8192]{4,3,2,1,0:T(4,128)(2,1)S(1)} %bitcast.111, bf16[1,4,4,4,8192]{4,3,2,1,0:T(4,128)(2,1)S(1)} %fusion.73), kind=kLoop, calls=%fused_computation.6 | loop fusion | flops 6291456 | bytes 8388608 | tf_op jit(solution)/shard_map/stack | solution.py:56
  62.7 6.9 %reshape.329 = bf16[256,8192]{1,0:T(8,128)(2,1)} reshape(bf16[4,4,4,4,8192]{4,3,2,1,0:T(4,128)(2,1)} %pad_maximum_fusion) | data formatting | bytes 8388608 | tf_op jit(solution)/shard_map/reshape | solution.py:294
  69.6 3.7 %fusion.1 = bf16[1,8192,128]{2,1,0:T(8,128)(2,1)S(1)} fusion(bf16[256,8192]{1,0:T(8,128)(2,1)} %reshape.329, pred[256]{0:T(512)(128)(4,1)S(1)} %broadcast_in_dim.59, bf16[256,128]{1,0:T(8,128)(2,1)S(1)} %gather_fusion, pred[256]{0:T(512)(128)(4,1)S(1)} %compare_and_fusion.1), kind=kOutput, calls=%fused_computation.5 | convolution fusion | flops 537985024 | bytes 6357504 | tf_op jit(solution)/shard_map/dot_general | solution.py:300
  74.8 2.4 %pad_maximum_fusion.1 = bf16[2,8192,128]{2,1,0:T(8,128)(2,1)} fusion(bf16[1,8192,128]{2,1,0:T(8,128)(2,1)S(1)} %fusion.1, bf16[1,8192,128]{2,1,0:T(8,128)(2,1)S(1)} %fusion), kind=kLoop, calls=%fused_computation.7 | loop fusion | flops 2097152 | bytes 8388608 | tf_op jit(solution)/shard_map/stack | solution.py:304
  78.4 7.6 %shard_map.85 = f32[2,128,128]{2,1,0:T(8,128)} custom-call(s32[1]{0:T(128)} %bitcast.core_ref, s32[256]{0:T(256)} %multiply_add_fusion.where_ref, s32[8]{0:T(128)} %count_ref.7, bf16[4,2,32,128,128]{4,3,2,1,0:T(8,128)(2,1)} %bitcast.101, bf16[128,128,128]{2,1,0:T(8,128)(2,1)} %bitcast.17.proj_ref), custom_call_target="tpu_custom_call" | custom-call | tf_op jit(solution)/shard_map/pallas_call | solution.py:161
  85.9 7.7 %shard_map.86 = f32[2,128,128]{2,1,0:T(8,128)} custom-call(s32[1]{0:T(128)} %bitcast.18.core_ref, s32[256]{0:T(256)} %multiply_add_fusion.where_ref, s32[8]{0:T(128)} %count_ref.7, bf16[4,2,32,128,128]{4,3,2,1,0:T(8,128)(2,1)} %bitcast.102, bf16[128,128,128]{2,1,0:T(8,128)(2,1)} %collective-permute-done.10.proj_ref), custom_call_target="tpu_custom_call" | custom-call | tf_op jit(solution)/shard_map/pallas_call | solution.py:161
  96.0 8.3 %shard_map.87 = bf16[128,128,128]{2,1,0:T(8,128)(2,1)} custom-call(s32[1]{0:T(128)} %bitcast.18.core_ref, s32[256]{0:T(256)} %get-tuple-element.7.where_ref, s32[8]{0:T(128)} %count_ref.7, bf16[4,2,32,128,128]{4,3,2,1,0:T(8,128)(2,1)} %bitcast.103, bf16[2,128,128]{2,1,0:T(8,128)(2,1)} %bitcast.119), custom_call_target="tpu_custom_call" | custom-call | tf_op jit(solution)/shard_map/pallas_call | solution.py:228
  105.3 7.1 %collective-permute-done.11.rest_0_ = bf16[128,128,128]{2,1,0:T(8,128)(2,1)} collective-permute-done((bf16[128,128,128]{2,1,0:T(8,128)(2,1)}, bf16[128,128,128]{2,1,0:T(8,128)(2,1)}, u32[]{:S(2)}, u32[]{:S(2)}) %collective-permute-start.11) | collective-permute-done | bytes 4194336 | tf_op jit(solution)/shard_map/ppermute | solution.py:41
  112.4 11.1 %shard_map.88 = f32[128,128,128]{2,1,0:T(8,128)} custom-call(s32[1]{0:T(128)} %bitcast.core_ref, s32[256]{0:T(256)} %get-tuple-element.7.where_ref, s32[8]{0:T(128)} %count_ref.7, bf16[4,2,32,128,128]{4,3,2,1,0:T(8,128)(2,1)} %bitcast.104, bf16[2,128,128]{2,1,0:T(8,128)(2,1)} %bitcast.120, bf16[128,128,128]{2,1,0:T(8,128)(2,1)} %collective-permute-done.11.rest_0_), custom_call_target="tpu_custom_call" | custom-call | tf_op jit(solution)/shard_map/pallas_call | solution.py:228
  125.4 2.0 collective-permute-start.12
  127.4 3.3 %fusion.64 = (f32[32,128,128]{2,1,0:T(8,128)S(1)}, f32[32,128,128]{2,1,0:T(8,128)S(1)}, f32[32,128,128]{2,1,0:T(8,128)S(1)}) fusion(f32[128,128,128]{2,1,0:T(8,128)} %shard_map.88), kind=kLoop, calls=%fused_computation.199 | loop fusion | bytes 12582912 | tf_op jit(solution)/shard_map/slice | solution.py:83
  130.9 3.7 %collective-permute-done.14 = bf16[4,4,128,128]{3,2,1,0:T(8,128)(2,1)S(1)} collective-permute-done((bf16[4,4,128,128]{3,2,1,0:T(8,128)(2,1)S(1)}, bf16[4,4,128,128]{3,2,1,0:T(8,128)(2,1)S(1)}, u32[]{:S(2)}, u32[]{:S(2)}) %collective-permute-start.14) | collective-permute-done | bytes 524320 | tf_op jit(solution)/shard_map/ppermute | solution.py:37
  139.4 11.4 %collective-permute-done.15 = bf16[4,4,256,128]{3,2,1,0:T(8,128)(2,1)S(1)} collective-permute-done((bf16[4,4,256,128]{3,2,1,0:T(8,128)(2,1)}, bf16[4,4,256,128]{3,2,1,0:T(8,128)(2,1)S(1)}, u32[]{:S(2)}, u32[]{:S(2)}) %collective-permute-start.15) | collective-permute-done | bytes 1048608 | tf_op jit(solution)/shard_map/ppermute | solution.py:37
  150.8 3.7 %collective-permute-done.13 = bf16[4,4,256,128]{3,2,1,0:T(8,128)(2,1)} collective-permute-done((bf16[4,4,256,128]{3,2,1,0:T(8,128)(2,1)}, bf16[4,4,256,128]{3,2,1,0:T(8,128)(2,1)}, u32[]{:S(2)}, u32[]{:S(2)}) %collective-permute-start.13) | collective-permute-done | bytes 1048608 | tf_op jit(solution)/shard_map/ppermute | solution.py:37
  156.8 3.6 %collective-permute-start.18 = (bf16[4,256,128]{2,1,0:T(8,128)(2,1)S(1)}, bf16[4,256,128]{2,1,0:T(8,128)(2,1)S(1)}, u32[]{:S(2)}, u32[]{:S(2)}) collective-permute-start(bf16[4,256,128]{2,1,0:T(8,128)(2,1)S(1)} %get-tuple-element.13), channel_id=1, source_target_pairs={{0,8},{1,9},{2,10},{3,11},{4,12},{5,13},{6,14},{7,15},{8,0},{9,1},... | collective-permute-start | bytes 786440 | tf_op jit(solution)/shard_map/ppermute | solution.py:37
  161.8 4.4 %collective-permute-done.16 = bf16[4,256,128]{2,1,0:T(8,128)(2,1)S(1)} collective-permute-done((bf16[4,256,128]{2,1,0:T(8,128)(2,1)S(1)}, bf16[4,256,128]{2,1,0:T(8,128)(2,1)S(1)}, u32[]{:S(2)}, u32[]{:S(2)}) %collective-permute-start.16) | collective-permute-done | bytes 262176 | tf_op jit(solution)/shard_map/ppermute | solution.py:37
  166.2 6.5 %collective-permute-done.18 = bf16[4,256,128]{2,1,0:T(8,128)(2,1)S(1)} collective-permute-done((bf16[4,256,128]{2,1,0:T(8,128)(2,1)S(1)}, bf16[4,256,128]{2,1,0:T(8,128)(2,1)S(1)}, u32[]{:S(2)}, u32[]{:S(2)}) %collective-permute-start.18) | collective-permute-done | bytes 262176 | tf_op jit(solution)/shard_map/ppermute | solution.py:37
  174.2 1.9 collective-permute-start.20
  177.1 1.9 collective-permute-done.19
  181.3 14.4 %all_to_all.5 = f32[32,4,384]{2,1,0:T(4,128)S(1)} all-to-all(f32[32,4,384]{2,1,0:T(4,128)S(1)} %pad_maximum_fusion.6), channel_id=1, replica_groups=mesh['blk'=4,'feat'=32] {'feat'}, dimensions={0} | all-to-all | bytes 393216 | tf_op jit(solution)/shard_map/all_to_all | solution.py:366
  198.8 3.2 %collective-permute-done.23 = f32[4,128]{1,0:T(4,128)S(1)} collective-permute-done((f32[4,128]{1,0:T(4,128)S(1)}, f32[4,128]{1,0:T(4,128)S(1)}, u32[]{:S(2)}, u32[]{:S(2)}) %collective-permute-start.23) | collective-permute-done | bytes 2080 | tf_op jit(solution)/shard_map/ppermute | solution.py:46
  (108 shorter events, 33.8 us)
Async XLA Ops:
  0.6 30.3 %copy-start = (bf16[128,128]{1,0:T(8,128)(2,1)S(1)}, bf16[128,128]{1,0:T(8,128)(2,1)}, u32[]{:S(2)}) copy-start(bf16[128,128]{1,0:T(8,128)(2,1)} %param.7) | copy-start | bytes 98308
  0.6 5.2 %collective-permute-start = (bf16[4,8192]{1,0:T(4,128)(2,1)}, bf16[4,8192]{1,0:T(4,128)(2,1)S(1)}, u32[]{:S(2)}, u32[]{:S(2)}) collective-permute-start(bf16[4,8192]{1,0:T(4,128)(2,1)} %param.6), channel_id=1, source_target_pairs={{0,3},{1,0},{2,1},{3,2},{4,7},{5,4},{6,5},{7,6},{8,11},{9,8},{10,9... | collective-permute-start | bytes 196616 | tf_op jit(solution)/shard_map/ppermute | solution.py:37
  3.6 6.4 %collective-permute-start.2 = (bf16[4,8192]{1,0:T(4,128)(2,1)}, bf16[4,8192]{1,0:T(4,128)(2,1)S(1)}, u32[]{:S(2)}, u32[]{:S(2)}) collective-permute-start(bf16[4,8192]{1,0:T(4,128)(2,1)} %param.6), channel_id=1, source_target_pairs={{0,1},{1,2},{2,3},{3,0},{4,5},{5,6},{6,7},{7,4},{8,9},{9,10},{10,1... | collective-permute-start | bytes 196616 | tf_op jit(solution)/shard_map/ppermute | solution.py:37
  3.6 6.4 %collective-permute-start.1 = (bf16[4,8192]{1,0:T(4,128)(2,1)}, bf16[4,8192]{1,0:T(4,128)(2,1)S(1)}, u32[]{:S(2)}, u32[]{:S(2)}) collective-permute-start(bf16[4,8192]{1,0:T(4,128)(2,1)} %param.6), channel_id=1, source_target_pairs={{0,2},{1,3},{2,0},{3,1},{4,6},{5,7},{6,4},{7,5},{8,10},{9,11},{10,... | collective-permute-start | bytes 196616 | tf_op jit(solution)/shard_map/ppermute | solution.py:37
  11.0 11.2 %collective-permute-start.4 = (bf16[4,4,8192]{2,1,0:T(4,128)(2,1)S(1)}, bf16[4,4,8192]{2,1,0:T(4,128)(2,1)S(1)}, u32[]{:S(2)}, u32[]{:S(2)}) collective-permute-start(bf16[4,4,8192]{2,1,0:T(4,128)(2,1)S(1)} %pad_maximum_fusion.5), channel_id=1, source_target_pairs={{0,8},{1,9},{2,10},{3,11},{4,12},{5,13},{6,14},{7,15},{8,0},{9,1},... | collective-permute-start | bytes 786440 | tf_op jit(solution)/shard_map/ppermute | solution.py:37
  15.0 11.8 %collective-permute-start.3 = (bf16[4,4,8192]{2,1,0:T(4,128)(2,1)S(1)}, bf16[4,4,8192]{2,1,0:T(4,128)(2,1)S(1)}, u32[]{:S(2)}, u32[]{:S(2)}) collective-permute-start(bf16[4,4,8192]{2,1,0:T(4,128)(2,1)S(1)} %pad_maximum_fusion.5), channel_id=1, source_target_pairs={{0,12},{1,13},{2,14},{3,15},{4,0},{5,1},{6,2},{7,3},{8,4},{9,5},{1... | collective-permute-start | bytes 786440 | tf_op jit(solution)/shard_map/ppermute | solution.py:37
  15.7 11.1 %collective-permute-start.5 = (bf16[4,4,8192]{2,1,0:T(4,128)(2,1)S(1)}, bf16[4,4,8192]{2,1,0:T(4,128)(2,1)S(1)}, u32[]{:S(2)}, u32[]{:S(2)}) collective-permute-start(bf16[4,4,8192]{2,1,0:T(4,128)(2,1)S(1)} %pad_maximum_fusion.5), channel_id=1, source_target_pairs={{0,4},{1,5},{2,6},{3,7},{4,8},{5,9},{6,10},{7,11},{8,12},{9,13},{1... | collective-permute-start | bytes 786440 | tf_op jit(solution)/shard_map/ppermute | solution.py:37
  22.2 7.9 %copy-start.2 = (bf16[4,4,8192]{2,1,0:T(4,128)(2,1)}, bf16[4,4,8192]{2,1,0:T(4,128)(2,1)S(1)}, u32[]{:S(2)}) copy-start(bf16[4,4,8192]{2,1,0:T(4,128)(2,1)S(1)} %collective-permute-done.4) | copy-start | bytes 786436
  27.8 14.9 %collective-permute-start.6 = (bf16[4,4,4,8192]{3,2,1,0:T(4,128)(2,1)S(1)}, bf16[4,4,4,8192]{3,2,1,0:T(4,128)(2,1)S(1)}, u32[]{:S(2)}, u32[]{:S(2)}) collective-permute-start(bf16[4,4,4,8192]{3,2,1,0:T(4,128)(2,1)S(1)} %pad_maximum_fusion.2), channel_id=1, source_target_pairs={{0,80},{1,81},{2,82},{3,83},{4,84},{5,85},{6,86},{7,87},{8,88},{9,... | collective-permute-start | bytes 3145736 | tf_op jit(solution)/shard_map/ppermute | solution.py:37
  30.1 16.3 %collective-permute-start.7 = (bf16[4,4,4,8192]{3,2,1,0:T(4,128)(2,1)S(1)}, bf16[4,4,4,8192]{3,2,1,0:T(4,128)(2,1)S(1)}, u32[]{:S(2)}, u32[]{:S(2)}) collective-permute-start(bf16[4,4,4,8192]{3,2,1,0:T(4,128)(2,1)S(1)} %pad_maximum_fusion.2), channel_id=1, source_target_pairs={{0,16},{1,17},{2,18},{3,19},{4,20},{5,21},{6,22},{7,23},{8,24},{9,... | collective-permute-start | bytes 3145736 | tf_op jit(solution)/shard_map/ppermute | solution.py:37
  31.8 15.0 %copy-start.3 = (bf16[4,4,8192]{2,1,0:T(4,128)(2,1)S(1)}, bf16[4,4,8192]{2,1,0:T(4,128)(2,1)}, u32[]{:S(2)}) copy-start(bf16[4,4,8192]{2,1,0:T(4,128)(2,1)} %copy-done.2) | copy-start | bytes 786436
  31.8 15.0 %copy-start.5 = (bf16[4,4,8192]{2,1,0:T(4,128)(2,1)S(1)}, bf16[4,4,8192]{2,1,0:T(4,128)(2,1)}, u32[]{:S(2)}) copy-start(bf16[4,4,8192]{2,1,0:T(4,128)(2,1)} %copy-done.4) | copy-start | bytes 786436
  31.8 15.0 %copy-start.7 = (bf16[4,4,8192]{2,1,0:T(4,128)(2,1)S(1)}, bf16[4,4,8192]{2,1,0:T(4,128)(2,1)}, u32[]{:S(2)}) copy-start(bf16[4,4,8192]{2,1,0:T(4,128)(2,1)} %copy-done.6) | copy-start | bytes 786436
  42.8 10.2 %collective-permute-start.9 = (bf16[4,4,4,4096]{3,2,1,0:T(4,128)(2,1)S(1)}, bf16[4,4,4,4096]{3,2,1,0:T(4,128)(2,1)S(1)}, u32[]{:S(2)}, u32[]{:S(2)}) collective-permute-start(bf16[4,4,4,4096]{3,2,1,0:T(4,128)(2,1)S(1)} %slice.108), channel_id=1, source_target_pairs={{0,80},{1,81},{2,82},{3,83},{4,84},{5,85},{6,86},{7,87},{8,88},{9,... | collective-permute-start | bytes 1572872 | tf_op jit(solution)/shard_map/ppermute | solution.py:37
  46.6 10.6 %collective-permute-start.8 = (bf16[4,4,4,4096]{3,2,1,0:T(4,128)(2,1)S(1)}, bf16[4,4,4,4096]{3,2,1,0:T(4,128)(2,1)S(1)}, u32[]{:S(2)}, u32[]{:S(2)}) collective-permute-start(bf16[4,4,4,4096]{3,2,1,0:T(4,128)(2,1)S(1)} %slice.107), channel_id=1, source_target_pairs={{0,16},{1,17},{2,18},{3,19},{4,20},{5,21},{6,22},{7,23},{8,24},{9,... | collective-permute-start | bytes 1572872 | tf_op jit(solution)/shard_map/ppermute | solution.py:37
  69.6 3.7 %copy-start.1 = (bf16[256,8192]{1,0:T(8,128)(2,1)S(1)}, bf16[256,8192]{1,0:T(8,128)(2,1)}, u32[]{:S(2)}) copy-start(bf16[256,8192]{1,0:T(8,128)(2,1)} %reshape.329) | copy-start | bytes 12582916
  77.2 8.8 %collective-permute-start.10 = (bf16[128,128,128]{2,1,0:T(8,128)(2,1)}, bf16[128,128,128]{2,1,0:T(8,128)(2,1)}, u32[]{:S(2)}, u32[]{:S(2)}) collective-permute-start(bf16[128,128,128]{2,1,0:T(8,128)(2,1)} %bitcast.17.proj_ref), channel_id=1, source_target_pairs={{0,32},{32,0},{64,96},{96,64},{1,33},{33,1},{65,97},{97,65},{2,34}... | collective-permute-start | bytes 12582920 | tf_op jit(solution)/shard_map/ppermute | solution.py:41
  85.9 7.7 %copy-start.8 = (f32[2,128,128]{2,1,0:T(8,128)S(1)}, f32[2,128,128]{2,1,0:T(8,128)}, u32[]{:S(2)}) copy-start(f32[2,128,128]{2,1,0:T(8,128)} %shard_map.85) | copy-start | bytes 393220
  85.9 8.6 %copy-start.9 = (bf16[256,128]{1,0:T(8,128)(2,1)S(1)}, bf16[256,128]{1,0:T(8,128)(2,1)}, u32[]{:S(2)}) copy-start(bf16[256,128]{1,0:T(8,128)(2,1)} %param.11) | copy-start | bytes 196612
  104.4 8.0 %collective-permute-start.11 = (bf16[128,128,128]{2,1,0:T(8,128)(2,1)}, bf16[128,128,128]{2,1,0:T(8,128)(2,1)}, u32[]{:S(2)}, u32[]{:S(2)}) collective-permute-start(bf16[128,128,128]{2,1,0:T(8,128)(2,1)} %shard_map.87), channel_id=1, source_target_pairs={{0,32},{32,0},{64,96},{96,64},{1,33},{33,1},{65,97},{97,65},{2,34}... | collective-permute-start | bytes 12582920 | tf_op jit(solution)/shard_map/ppermute | solution.py:41
  125.3 9.2 %collective-permute-start.14 = (bf16[4,4,128,128]{3,2,1,0:T(8,128)(2,1)S(1)}, bf16[4,4,128,128]{3,2,1,0:T(8,128)(2,1)S(1)}, u32[]{:S(2)}, u32[]{:S(2)}) collective-permute-start(bf16[4,4,128,128]{3,2,1,0:T(8,128)(2,1)S(1)} %get-tuple-element.16), channel_id=1, source_target_pairs={{0,80},{1,81},{2,82},{3,83},{4,84},{5,85},{6,86},{7,87},{8,88},{9,... | collective-permute-start | bytes 1572872 | tf_op jit(solution)/shard_map/ppermute | solution.py:37
  125.4 11.6 %collective-permute-start.12 = (bf16[4,4,128,128]{3,2,1,0:T(8,128)(2,1)S(1)}, bf16[4,4,128,128]{3,2,1,0:T(8,128)(2,1)S(1)}, u32[]{:S(2)}, u32[]{:S(2)}) collective-permute-start(bf16[4,4,128,128]{3,2,1,0:T(8,128)(2,1)S(1)} %get-tuple-element.15), channel_id=1, source_target_pairs={{0,16},{1,17},{2,18},{3,19},{4,20},{5,21},{6,22},{7,23},{8,24},{9,... | collective-permute-start | bytes 1572872 | tf_op jit(solution)/shard_map/ppermute | solution.py:37
  135.8 15.0 %collective-permute-start.15 = (bf16[4,4,256,128]{3,2,1,0:T(8,128)(2,1)}, bf16[4,4,256,128]{3,2,1,0:T(8,128)(2,1)S(1)}, u32[]{:S(2)}, u32[]{:S(2)}) collective-permute-start(bf16[4,4,256,128]{3,2,1,0:T(8,128)(2,1)} %pad_maximum_fusion.4), channel_id=1, source_target_pairs={{0,80},{1,81},{2,82},{3,83},{4,84},{5,85},{6,86},{7,87},{8,88},{9,... | collective-permute-start | bytes 3145736 | tf_op jit(solution)/shard_map/ppermute | solution.py:37
  138.2 16.3 %collective-permute-start.13 = (bf16[4,4,256,128]{3,2,1,0:T(8,128)(2,1)}, bf16[4,4,256,128]{3,2,1,0:T(8,128)(2,1)}, u32[]{:S(2)}, u32[]{:S(2)}) collective-permute-start(bf16[4,4,256,128]{3,2,1,0:T(8,128)(2,1)} %pad_maximum_fusion.3), channel_id=1, source_target_pairs={{0,16},{1,17},{2,18},{3,19},{4,20},{5,21},{6,22},{7,23},{8,24},{9,... | collective-permute-start | bytes 3145736 | tf_op jit(solution)/shard_map/ppermute | solution.py:37
  156.2 9.9 %collective-permute-start.16 = (bf16[4,256,128]{2,1,0:T(8,128)(2,1)S(1)}, bf16[4,256,128]{2,1,0:T(8,128)(2,1)S(1)}, u32[]{:S(2)}, u32[]{:S(2)}) collective-permute-start(bf16[4,256,128]{2,1,0:T(8,128)(2,1)S(1)} %get-tuple-element.12), channel_id=1, source_target_pairs={{0,4},{1,5},{2,6},{3,7},{4,8},{5,9},{6,10},{7,11},{8,12},{9,13},{1... | collective-permute-start | bytes 786440 | tf_op jit(solution)/shard_map/ppermute | solution.py:37
  156.8 15.8 %collective-permute-start.18 = (bf16[4,256,128]{2,1,0:T(8,128)(2,1)S(1)}, bf16[4,256,128]{2,1,0:T(8,128)(2,1)S(1)}, u32[]{:S(2)}, u32[]{:S(2)}) collective-permute-start(bf16[4,256,128]{2,1,0:T(8,128)(2,1)S(1)} %get-tuple-element.13), channel_id=1, source_target_pairs={{0,8},{1,9},{2,10},{3,11},{4,12},{5,13},{6,14},{7,15},{8,0},{9,1},... | collective-permute-start | bytes 786440 | tf_op jit(solution)/shard_map/ppermute | solution.py:37
  160.4 12.2 %collective-permute-start.17 = (bf16[4,256,128]{2,1,0:T(8,128)(2,1)S(1)}, bf16[4,256,128]{2,1,0:T(8,128)(2,1)S(1)}, u32[]{:S(2)}, u32[]{:S(2)}) collective-permute-start(bf16[4,256,128]{2,1,0:T(8,128)(2,1)S(1)} %get-tuple-element.14), channel_id=1, source_target_pairs={{0,12},{1,13},{2,14},{3,15},{4,0},{5,1},{6,2},{7,3},{8,4},{9,5},{1... | collective-permute-start | bytes 786440 | tf_op jit(solution)/shard_map/ppermute | solution.py:37
  172.8 6.2 %collective-permute-start.19 = (bf16[256,128]{1,0:T(8,128)(2,1)S(1)}, bf16[256,128]{1,0:T(8,128)(2,1)S(1)}, u32[]{:S(2)}, u32[]{:S(2)}) collective-permute-start(bf16[256,128]{1,0:T(8,128)(2,1)S(1)} %get-tuple-element.17), channel_id=1, source_target_pairs={{0,1},{1,2},{2,3},{3,0},{4,5},{5,6},{6,7},{7,4},{8,9},{9,10},{10,1... | collective-permute-start | bytes 196616 | tf_op jit(solution)/shard_map/ppermute | solution.py:37
  172.9 6.2 %collective-permute-start.21 = (bf16[256,128]{1,0:T(8,128)(2,1)S(1)}, bf16[256,128]{1,0:T(8,128)(2,1)S(1)}, u32[]{:S(2)}, u32[]{:S(2)}) collective-permute-start(bf16[256,128]{1,0:T(8,128)(2,1)S(1)} %get-tuple-element.18), channel_id=1, source_target_pairs={{0,2},{1,3},{2,0},{3,1},{4,6},{5,7},{6,4},{7,5},{8,10},{9,11},{10,... | collective-permute-start | bytes 196616 | tf_op jit(solution)/shard_map/ppermute | solution.py:37
  174.2 5.7 %collective-permute-start.20 = (bf16[256,128]{1,0:T(8,128)(2,1)S(1)}, bf16[256,128]{1,0:T(8,128)(2,1)S(1)}, u32[]{:S(2)}, u32[]{:S(2)}) collective-permute-start(bf16[256,128]{1,0:T(8,128)(2,1)S(1)} %get-tuple-element.19), channel_id=1, source_target_pairs={{0,3},{1,0},{2,1},{3,2},{4,7},{5,4},{6,5},{7,6},{8,11},{9,8},{10,9... | collective-permute-start | bytes 196616 | tf_op jit(solution)/shard_map/ppermute | solution.py:37
  195.7 1.2 collective-permute-start.22
  196.9 5.1 %collective-permute-start.23 = (f32[4,128]{1,0:T(4,128)S(1)}, f32[4,128]{1,0:T(4,128)S(1)}, u32[]{:S(2)}, u32[]{:S(2)}) collective-permute-start(f32[4,128]{1,0:T(4,128)S(1)} %add.505), channel_id=1, source_target_pairs={{0,64},{32,96},{64,0},{96,32},{1,65},{33,97},{65,1},{97,33},{2,66}... | collective-permute-start | bytes 6152 | tf_op jit(solution)/shard_map/ppermute | solution.py:46
  (3 other events, 9.0 us)

commit v9 on v7

--- a/solution.py
+++ b/solution.py
@@ -202,8 +202,12 @@
         out_ref[...] = total_ref[...].astype(out_ref.dtype)
 
 
-def spread_pair(core_id, spots, counts, tile_stack, grad_turned, buffer_tiles, out_type, start=None):
-    blocks, tile_rows, slot_count, tile_size, _ = tile_stack.shape
+def spread_pair(
+    core_id, spots, counts, tile_stack, grad_turned, buffer_tiles, out_type, start=None,
+    block_step=2, core_step=1,
+):
+    _, tile_rows, slot_count, tile_size, _ = tile_stack.shape
+    blocks = lax.axis_size("blk")
     hidden_width = grad_turned.shape[1]
     grid_spec = pltpu.PrefetchScalarGridSpec(
         num_scalar_prefetch=3,
@@ -211,7 +215,7 @@
         in_specs=[
             pl.BlockSpec(
                 (None, None, slot_count, tile_size, tile_size),
-                lambda r, h, c, w, n: (h * 2 + c[0], r, 0, 0, 0),
+                lambda r, h, c, w, n: (h * block_step + c[0] * core_step, r, 0, 0, 0),
             ),
             pl.BlockSpec((None, hidden_width, tile_size), lambda r, h, c, w, n: (r, 0, 0)),
         ]
@@ -270,6 +274,11 @@
     core_id = blk_id % 2
     tile_stack = tile_values.reshape(cycle_size, tile_rows, slot_count, tile_size, tile_size)
     spots = buffer_spots(tile_col, blk_id, feat_id, block_tiles, tile_rows)
+    by_core = tile_stack.reshape(cycle_size // 2, 2, tile_rows, slot_count, tile_size, tile_size)
+    for_sibling = lax.dynamic_index_in_dim(by_core, 1 - core_id, 1, keepdims=False)
+    sibling_tiles = sibling(for_sibling)
+    sibling_spots = buffer_spots(sibling(tile_col), blk_id, feat_id, block_tiles, tile_rows)
+    sibling_count = sibling(tile_count)
     buffer_tiles = block_tiles * 2
 
     features_own = lax.all_to_all(features_t, "feat", split_axis=1, concat_axis=0, tiled=True)
@@ -295,12 +304,13 @@
     ).astype(jnp.bfloat16)
     grad_turned = grad_pre.reshape(tile_rows, tile_size, hidden_width).transpose(0, 2, 1)
 
-    outgoing = spread_pair(
-        1 - core_id, spots, tile_count, tile_stack, grad_turned, buffer_tiles, jnp.bfloat16
-    )
-    arrived = sibling(outgoing)
+    sibling_grad = sibling(grad_turned)
     total = spread_pair(
-        core_id, spots, tile_count, tile_stack, grad_turned, buffer_tiles, jnp.float32, arrived
+        core_id, spots, tile_count, tile_stack, grad_turned, buffer_tiles, jnp.float32
+    )
+    total = spread_pair(
+        core_id, sibling_spots, sibling_count, sibling_tiles, sibling_grad, buffer_tiles,
+        jnp.float32, total, block_step=1, core_step=0,
     )
     total = reduce_phase(
         total.reshape(RING, RING, RING, rows_own, hidden_width), 2, jnp.bfloat16

time: 192 us -> 194 us (1.010)
  waiting for transfers between devices: 81.3 us -> 73.6 us
  local copies, waits for them, and re-layouts: 7.02 us -> 12.3 us
  starting transfers between devices: 26.7 us -> 29.1 us
  Pallas kernels: 35.6 us -> 37.7 us
    ppermute x2 -> x5, waiting for transfers between devices: 7.5 us -> 0.01 us  [sibling(): lax.ppermute(block, 'blk', [(i, i ^ 1) for i in range(lax.axis_size('blk'...]
    squeeze x0 -> x1, local copies, waits for them, and re-layouts: none -> 4.82 us  [body(): lax.dynamic_index_in_dim(by_core, 1 - core_id, 1, keepdims=False)]
    pallas_call x2, Pallas kernels: 20.3 us -> 22.4 us  [spread_pair(): pl.pallas_call(spread_kernel, grid_spec=grid_spec, out_shape=jax.ShapeDty...]
  transfers between devices with their start and end apart: 24 -> 27, of which waited for: 19 -> 18; matrix products, arithmetic and copies ran while one was open for 3% -> 6% of each run, Pallas kernels for 4% -> 13%
where the time goes in v9:
time: 194 us; the launch traced here: 193 us
  waiting for transfers between devices  73.6 us (38%)
  Pallas kernels  37.7 us (19%)
  blocking collectives  32.2 us (17%)
  starting transfers between devices  29.1 us (15%)
  local copies, waits for them, and re-layouts  12.3 us (6%)
  other arithmetic  7.22 us (4%)
    ppermute x20, waiting for transfers between devices, ring_shift(): return lax.ppermute(block, BOTH, route)  68.7 us
    ppermute x20, starting transfers between devices, ring_shift(): return lax.ppermute(block, BOTH, route)  26.9 us
    pallas_call x2, Pallas kernels, spread_pair(): pl.pallas_call(spread_kernel, grid_spec=grid_spec, out_shape=jax.ShapeDty...  22.4 us
    all_to_all x1, blocking collectives, body(): lax.all_to_all(features_t, 'feat', split_axis=1, concat_axis=0, tiled=True)  17.6 us
    pallas_call x2, Pallas kernels, aggregate_pair(): pl.pallas_call(aggregate_kernel, grid_spec=grid_spec, out_shape=jax.Shape...  15.3 us
    all_to_all x1, blocking collectives, body(): lax.all_to_all(outgoing, 'feat', split_axis=0, concat_axis=0, tiled=True)  14.6 us
    slice x2, local copies, waits for them, and re-layouts, term(): return total[k]  5.03 us
    ppermute x2, waiting for transfers between devices, swapped(): return lax.ppermute(block, axis, [(i, i ^ mask) for i in range(count)])  4.83 us
  transfers between devices with their start and end apart: 27, of which 18 were waited for; matrix products, arithmetic and copies ran while one was open for 6% of the time, Pallas kernels for 13%

profile of v9, /device:TPU:0, one launch (start us, length us, event | category | flops | bytes accessed | tf_op | source)
XLA Modules:
  0.0 193.4 jit_solution(7654866163163107995)
XLA Ops:
  0.6 17.6 %all_to_all.24 = bf16[4,32,256]{2,0,1:T(4,128)(2,1)S(1)} all-to-all(bf16[4,32,256]{2,0,1:T(4,128)(2,1)} %bitcast.130), channel_id=1, replica_groups=mesh['blk'=4,'feat'=32] {'feat'}, dimensions={1} | all-to-all | bytes 131072 | tf_op jit(solution)/shard_map/all_to_all | solution.py:284
  19.1 2.3 %collective-permute-start.1 = (bf16[256,128]{1,0:T(8,128)(2,1)S(1)}, bf16[256,128]{1,0:T(8,128)(2,1)S(1)}, u32[]{:S(2)}, u32[]{:S(2)}) collective-permute-start(bf16[256,128]{1,0:T(8,128)(2,1)S(1)} %convolution_convert_fusion.1), channel_id=1, source_target_pairs={{0,2},{1,3},{2,0},{3,1},{4,6},{5,7},{6,4},{7,5},{8,10},{9,11},{10,... | collective-permute-start | bytes 196616 | tf_op jit(solution)/shard_map/ppermute | solution.py:37
  22.5 1.5 collective-permute-done.2
  25.7 1.4 collective-permute-start.4
  27.1 1.9 collective-permute-start.3
  29.1 6.7 %collective-permute-done.4 = bf16[4,256,128]{2,1,0:T(8,128)(2,1)S(1)} collective-permute-done((bf16[4,256,128]{2,1,0:T(8,128)(2,1)S(1)}, bf16[4,256,128]{2,1,0:T(8,128)(2,1)S(1)}, u32[]{:S(2)}, u32[]{:S(2)}) %collective-permute-start.4) | collective-permute-done | bytes 262176 | tf_op jit(solution)/shard_map/ppermute | solution.py:37
  37.0 1.7 collective-permute-done.5
  38.9 3.4 %collective-permute-start.6 = (bf16[4,4,256,128]{3,2,1,0:T(8,128)(2,1)S(1)}, bf16[4,4,256,128]{3,2,1,0:T(8,128)(2,1)S(1)}, u32[]{:S(2)}, u32[]{:S(2)}) collective-permute-start(bf16[4,4,256,128]{3,2,1,0:T(8,128)(2,1)S(1)} %get-tuple-element.16), channel_id=1, source_target_pairs={{0,80},{1,81},{2,82},{3,83},{4,84},{5,85},{6,86},{7,87},{8,88},{9,... | collective-permute-start | bytes 3145736 | tf_op jit(solution)/shard_map/ppermute | solution.py:37
  42.2 12.3 %collective-permute-done.6 = bf16[4,4,256,128]{3,2,1,0:T(8,128)(2,1)S(1)} collective-permute-done((bf16[4,4,256,128]{3,2,1,0:T(8,128)(2,1)S(1)}, bf16[4,4,256,128]{3,2,1,0:T(8,128)(2,1)S(1)}, u32[]{:S(2)}, u32[]{:S(2)}) %collective-permute-start.6) | collective-permute-done | bytes 1048608 | tf_op jit(solution)/shard_map/ppermute | solution.py:37
  54.6 3.8 %collective-permute-start.9 = (bf16[4,4,128,128]{3,2,1,0:T(8,128)(2,1)S(1)}, bf16[4,4,128,128]{3,2,1,0:T(8,128)(2,1)S(1)}, u32[]{:S(2)}, u32[]{:S(2)}) collective-permute-start(bf16[4,4,128,128]{3,2,1,0:T(8,128)(2,1)S(1)} %slice.104), channel_id=1, source_target_pairs={{0,80},{1,81},{2,82},{3,83},{4,84},{5,85},{6,86},{7,87},{8,88},{9,... | collective-permute-start | bytes 1572872 | tf_op jit(solution)/shard_map/ppermute | solution.py:37
  58.5 6.6 %collective-permute-done.9 = bf16[4,4,128,128]{3,2,1,0:T(8,128)(2,1)S(1)} collective-permute-done((bf16[4,4,128,128]{3,2,1,0:T(8,128)(2,1)S(1)}, bf16[4,4,128,128]{3,2,1,0:T(8,128)(2,1)S(1)}, u32[]{:S(2)}, u32[]{:S(2)}) %collective-permute-start.9) | collective-permute-done | bytes 524320 | tf_op jit(solution)/shard_map/ppermute | solution.py:37
  65.1 3.8 %collective-permute-done.8 = bf16[4,4,128,128]{3,2,1,0:T(8,128)(2,1)S(1)} collective-permute-done((bf16[4,4,128,128]{3,2,1,0:T(8,128)(2,1)S(1)}, bf16[4,4,128,128]{3,2,1,0:T(8,128)(2,1)S(1)}, u32[]{:S(2)}, u32[]{:S(2)}) %collective-permute-start.8) | collective-permute-done | bytes 524320 | tf_op jit(solution)/shard_map/ppermute | solution.py:37
  69.0 2.3 %pad_maximum_fusion = bf16[4,4,4,256,128]{4,3,2,1,0:T(8,128)(2,1)} fusion(bf16[1,4,4,256,128]{4,3,2,1,0:T(8,128)(2,1)S(1)} %bitcast.114, bf16[1,4,4,256,128]{4,3,2,1,0:T(8,128)(2,1)S(1)} %maximum_bitcast_fusion, bf16[1,4,4,256,128]{4,3,2,1,0:T(8,128)(2,1)S(1)} %bitcast.113, bf16[1,4,4,256,128]{4,3,2,1,0:T(8,128)(2,1)S(1)} %get-tuple-element.15), kind=kLoop, calls=%fused_computation | loop fusion | flops 6291456 | bytes 8388608 | tf_op jit(solution)/shard_map/stack | solution.py:56
  71.3 4.8 %dynamic-slice_bitcast_fusion = bf16[2,2,32,128,128]{4,3,2,1,0:T(8,128)(2,1)} fusion(bf16[2,2,2,32,128,128]{5,4,3,2,1,0:T(8,128)(2,1)} %bitcast.103, s32[]{:T(128)S(6)} %select_n.174), kind=kLoop, calls=%fused_computation.1 | loop fusion | bytes 8388612 | tf_op jit(solution)/shard_map/jit(dynamic_index_in_dim)/squeeze | solution.py:278
  77.7 7.6 %shard_map.85 = f32[2,128,128]{2,1,0:T(8,128)} custom-call(s32[1]{0:T(128)} %bitcast.core_ref, s32[256]{0:T(256)} %fusion.21.where_ref, s32[8]{0:T(128)} %count_ref.5, bf16[4,2,32,128,128]{4,3,2,1,0:T(8,128)(2,1)} %bitcast.104, bf16[128,128,128]{2,1,0:T(8,128)(2,1)} %bitcast.16.proj_ref), custom_call_target="tpu_custom_call" | custom-call | tf_op jit(solution)/shard_map/pallas_call | solution.py:161
  85.3 7.7 %shard_map.86 = f32[2,128,128]{2,1,0:T(8,128)} custom-call(s32[1]{0:T(128)} %bitcast.17.core_ref, s32[256]{0:T(256)} %fusion.21.where_ref, s32[8]{0:T(128)} %count_ref.5, bf16[4,2,32,128,128]{4,3,2,1,0:T(8,128)(2,1)} %bitcast.105, bf16[128,128,128]{2,1,0:T(8,128)(2,1)} %collective-permute-done.10.proj_ref), custom_call_target="tpu_custom_call" | custom-call | tf_op jit(solution)/shard_map/pallas_call | solution.py:161
  95.8 10.2 %shard_map.87.rest_0_ = f32[128,128,128]{2,1,0:T(8,128)} custom-call(s32[1]{0:T(128)} %bitcast.core_ref, s32[256]{0:T(256)} %fusion.21.where_ref, s32[8]{0:T(128)} %count_ref.5, bf16[4,2,32,128,128]{4,3,2,1,0:T(8,128)(2,1)} %bitcast.106, bf16[2,128,128]{2,1,0:T(8,128)(2,1)} %bitcast.118), custom_call_target="tpu_custom_call" | custom-call | tf_op jit(solution)/shard_map/pallas_call | solution.py:232
  107.1 12.2 %shard_map.88 = f32[128,128,128]{2,1,0:T(8,128)} custom-call(s32[1]{0:T(128)} %bitcast.core_ref, s32[256]{0:T(256)} %fusion.25.where_ref, s32[8]{0:T(128)} %copy-done.7, bf16[2,2,32,128,128]{4,3,2,1,0:T(8,128)(2,1)} %collective-permute-done.13.tiles_ref, bf16[2,128,128]{2,1,0:T(8,128)(2,1)} %copy-done.3, f32[128,128,128]{2,1,0:T(8,128)} %shard_map.87.rest_0_), custom_call_target="tpu_custom_call" | custom-call | tf_op jit(solution)/shard_map/pallas_call | solution.py:232
  119.3 1.7 slice.158
  121.2 2.0 %collective-permute-start.15 = (bf16[4,4,128,128]{3,2,1,0:T(8,128)(2,1)S(1)}, bf16[4,4,128,128]{3,2,1,0:T(8,128)(2,1)S(1)}, u32[]{:S(2)}, u32[]{:S(2)}) collective-permute-start(bf16[4,4,128,128]{3,2,1,0:T(8,128)(2,1)S(1)} %get-tuple-element.13), channel_id=1, source_target_pairs={{0,16},{1,17},{2,18},{3,19},{4,20},{5,21},{6,22},{7,23},{8,24},{9,... | collective-permute-start | bytes 1572872 | tf_op jit(solution)/shard_map/ppermute | solution.py:37
  123.2 3.3 %fusion.39 = (f32[32,128,128]{2,1,0:T(8,128)S(1)}, f32[32,128,128]{2,1,0:T(8,128)S(1)}, f32[32,128,128]{2,1,0:T(8,128)S(1)}) fusion(f32[128,128,128]{2,1,0:T(8,128)} %shard_map.88), kind=kLoop, calls=%fused_computation.140 | loop fusion | bytes 12582912 | tf_op jit(solution)/shard_map/slice | solution.py:83
  126.7 3.7 %collective-permute-done.17 = bf16[4,4,128,128]{3,2,1,0:T(8,128)(2,1)S(1)} collective-permute-done((bf16[4,4,128,128]{3,2,1,0:T(8,128)(2,1)S(1)}, bf16[4,4,128,128]{3,2,1,0:T(8,128)(2,1)S(1)}, u32[]{:S(2)}, u32[]{:S(2)}) %collective-permute-start.17) | collective-permute-done | bytes 524320 | tf_op jit(solution)/shard_map/ppermute | solution.py:37
  133.0 12.5 %collective-permute-done.18 = bf16[4,4,256,128]{3,2,1,0:T(8,128)(2,1)S(1)} collective-permute-done((bf16[4,4,256,128]{3,2,1,0:T(8,128)(2,1)S(1)}, bf16[4,4,256,128]{3,2,1,0:T(8,128)(2,1)S(1)}, u32[]{:S(2)}, u32[]{:S(2)}) %collective-permute-start.18) | collective-permute-done | bytes 1048608 | tf_op jit(solution)/shard_map/ppermute | solution.py:37
  145.5 2.7 %collective-permute-done.16 = bf16[4,4,256,128]{3,2,1,0:T(8,128)(2,1)S(1)} collective-permute-done((bf16[4,4,256,128]{3,2,1,0:T(8,128)(2,1)S(1)}, bf16[4,4,256,128]{3,2,1,0:T(8,128)(2,1)S(1)}, u32[]{:S(2)}, u32[]{:S(2)}) %collective-permute-start.16) | collective-permute-done | bytes 1048608 | tf_op jit(solution)/shard_map/ppermute | solution.py:37
  149.3 1.9 collective-permute-start.21
  151.2 2.3 %collective-permute-start.20 = (bf16[4,256,128]{2,1,0:T(8,128)(2,1)S(1)}, bf16[4,256,128]{2,1,0:T(8,128)(2,1)S(1)}, u32[]{:S(2)}, u32[]{:S(2)}) collective-permute-start(bf16[4,256,128]{2,1,0:T(8,128)(2,1)S(1)} %get-tuple-element.12), channel_id=1, source_target_pairs={{0,12},{1,13},{2,14},{3,15},{4,0},{5,1},{6,2},{7,3},{8,4},{9,5},{1... | collective-permute-start | bytes 786440 | tf_op jit(solution)/shard_map/ppermute | solution.py:37
  153.4 10.0 %collective-permute-done.19 = bf16[4,256,128]{2,1,0:T(8,128)(2,1)S(1)} collective-permute-done((bf16[4,256,128]{2,1,0:T(8,128)(2,1)S(1)}, bf16[4,256,128]{2,1,0:T(8,128)(2,1)S(1)}, u32[]{:S(2)}, u32[]{:S(2)}) %collective-permute-start.19) | collective-permute-done | bytes 262176 | tf_op jit(solution)/shard_map/ppermute | solution.py:37
  164.3 1.4 collective-permute-start.24
  165.7 1.8 collective-permute-start.23
  167.5 2.9 %collective-permute-done.22 = bf16[256,128]{1,0:T(8,128)(2,1)S(1)} collective-permute-done((bf16[256,128]{1,0:T(8,128)(2,1)S(1)}, bf16[256,128]{1,0:T(8,128)(2,1)S(1)}, u32[]{:S(2)}, u32[]{:S(2)}) %collective-permute-start.22) | collective-permute-done | bytes 65568 | tf_op jit(solution)/shard_map/ppermute | solution.py:37
  171.9 14.6 %all_to_all.25 = f32[32,4,384]{2,1,0:T(4,128)S(1)} all-to-all(f32[32,4,384]{2,1,0:T(4,128)S(1)} %pad_maximum_fusion.5), channel_id=1, replica_groups=mesh['blk'=4,'feat'=32] {'feat'}, dimensions={0} | all-to-all | bytes 393216 | tf_op jit(solution)/shard_map/all_to_all | solution.py:340
  189.2 3.7 %collective-permute-done.26 = f32[4,128]{1,0:T(4,128)S(1)} collective-permute-done((f32[4,128]{1,0:T(4,128)S(1)}, f32[4,128]{1,0:T(4,128)S(1)}, u32[]{:S(2)}, u32[]{:S(2)}) %collective-permute-start.26) | collective-permute-done | bytes 2080 | tf_op jit(solution)/shard_map/ppermute | solution.py:46
  (81 shorter events, 20.3 us)
Async XLA Ops:
  0.6 17.6 %copy-start = (bf16[128,128]{1,0:T(8,128)(2,1)S(1)}, bf16[128,128]{1,0:T(8,128)(2,1)}, u32[]{:S(2)}) copy-start(bf16[128,128]{1,0:T(8,128)(2,1)} %param.7) | copy-start | bytes 98308
  18.5 5.5 %collective-permute-start.2 = (bf16[256,128]{1,0:T(8,128)(2,1)S(1)}, bf16[256,128]{1,0:T(8,128)(2,1)S(1)}, u32[]{:S(2)}, u32[]{:S(2)}) collective-permute-start(bf16[256,128]{1,0:T(8,128)(2,1)S(1)} %convolution_convert_fusion.1), channel_id=1, source_target_pairs={{0,1},{1,2},{2,3},{3,0},{4,5},{5,6},{6,7},{7,4},{8,9},{9,10},{10,1... | collective-permute-start | bytes 196616 | tf_op jit(solution)/shard_map/ppermute | solution.py:37
  19.1 5.8 %collective-permute-start.1 = (bf16[256,128]{1,0:T(8,128)(2,1)S(1)}, bf16[256,128]{1,0:T(8,128)(2,1)S(1)}, u32[]{:S(2)}, u32[]{:S(2)}) collective-permute-start(bf16[256,128]{1,0:T(8,128)(2,1)S(1)} %convolution_convert_fusion.1), channel_id=1, source_target_pairs={{0,2},{1,3},{2,0},{3,1},{4,6},{5,7},{6,4},{7,5},{8,10},{9,11},{10,... | collective-permute-start | bytes 196616 | tf_op jit(solution)/shard_map/ppermute | solution.py:37
  21.4 4.3 %collective-permute-start = (bf16[256,128]{1,0:T(8,128)(2,1)S(1)}, bf16[256,128]{1,0:T(8,128)(2,1)S(1)}, u32[]{:S(2)}, u32[]{:S(2)}) collective-permute-start(bf16[256,128]{1,0:T(8,128)(2,1)S(1)} %convolution_convert_fusion.1), channel_id=1, source_target_pairs={{0,3},{1,0},{2,1},{3,2},{4,7},{5,4},{6,5},{7,6},{8,11},{9,8},{10,9... | collective-permute-start | bytes 196616 | tf_op jit(solution)/shard_map/ppermute | solution.py:37
  25.7 10.1 %collective-permute-start.4 = (bf16[4,256,128]{2,1,0:T(8,128)(2,1)S(1)}, bf16[4,256,128]{2,1,0:T(8,128)(2,1)S(1)}, u32[]{:S(2)}, u32[]{:S(2)}) collective-permute-start(bf16[4,256,128]{2,1,0:T(8,128)(2,1)S(1)} %get-tuple-element.21), channel_id=1, source_target_pairs={{0,8},{1,9},{2,10},{3,11},{4,12},{5,13},{6,14},{7,15},{8,0},{9,1},... | collective-permute-start | bytes 786440 | tf_op jit(solution)/shard_map/ppermute | solution.py:37
  27.1 9.9 %collective-permute-start.3 = (bf16[4,256,128]{2,1,0:T(8,128)(2,1)S(1)}, bf16[4,256,128]{2,1,0:T(8,128)(2,1)S(1)}, u32[]{:S(2)}, u32[]{:S(2)}) collective-permute-start(bf16[4,256,128]{2,1,0:T(8,128)(2,1)S(1)} %get-tuple-element.21), channel_id=1, source_target_pairs={{0,12},{1,13},{2,14},{3,15},{4,0},{5,1},{6,2},{7,3},{8,4},{9,5},{1... | collective-permute-start | bytes 786440 | tf_op jit(solution)/shard_map/ppermute | solution.py:37
  29.0 9.7 %collective-permute-start.5 = (bf16[4,256,128]{2,1,0:T(8,128)(2,1)S(1)}, bf16[4,256,128]{2,1,0:T(8,128)(2,1)S(1)}, u32[]{:S(2)}, u32[]{:S(2)}) collective-permute-start(bf16[4,256,128]{2,1,0:T(8,128)(2,1)S(1)} %get-tuple-element.21), channel_id=1, source_target_pairs={{0,4},{1,5},{2,6},{3,7},{4,8},{5,9},{6,10},{7,11},{8,12},{9,13},{1... | collective-permute-start | bytes 786440 | tf_op jit(solution)/shard_map/ppermute | solution.py:37
  38.9 15.7 %collective-permute-start.6 = (bf16[4,4,256,128]{3,2,1,0:T(8,128)(2,1)S(1)}, bf16[4,4,256,128]{3,2,1,0:T(8,128)(2,1)S(1)}, u32[]{:S(2)}, u32[]{:S(2)}) collective-permute-start(bf16[4,4,256,128]{3,2,1,0:T(8,128)(2,1)S(1)} %get-tuple-element.16), channel_id=1, source_target_pairs={{0,80},{1,81},{2,82},{3,83},{4,84},{5,85},{6,86},{7,87},{8,88},{9,... | collective-permute-start | bytes 3145736 | tf_op jit(solution)/shard_map/ppermute | solution.py:37
  42.2 16.1 %collective-permute-start.7 = (bf16[4,4,256,128]{3,2,1,0:T(8,128)(2,1)S(1)}, bf16[4,4,256,128]{3,2,1,0:T(8,128)(2,1)S(1)}, u32[]{:S(2)}, u32[]{:S(2)}) collective-permute-start(bf16[4,4,256,128]{3,2,1,0:T(8,128)(2,1)S(1)} %get-tuple-element.16), channel_id=1, source_target_pairs={{0,16},{1,17},{2,18},{3,19},{4,20},{5,21},{6,22},{7,23},{8,24},{9,... | collective-permute-start | bytes 3145736 | tf_op jit(solution)/shard_map/ppermute | solution.py:37
  54.6 10.5 %collective-permute-start.9 = (bf16[4,4,128,128]{3,2,1,0:T(8,128)(2,1)S(1)}, bf16[4,4,128,128]{3,2,1,0:T(8,128)(2,1)S(1)}, u32[]{:S(2)}, u32[]{:S(2)}) collective-permute-start(bf16[4,4,128,128]{3,2,1,0:T(8,128)(2,1)S(1)} %slice.104), channel_id=1, source_target_pairs={{0,80},{1,81},{2,82},{3,83},{4,84},{5,85},{6,86},{7,87},{8,88},{9,... | collective-permute-start | bytes 1572872 | tf_op jit(solution)/shard_map/ppermute | solution.py:37
  58.4 10.5 %collective-permute-start.8 = (bf16[4,4,128,128]{3,2,1,0:T(8,128)(2,1)S(1)}, bf16[4,4,128,128]{3,2,1,0:T(8,128)(2,1)S(1)}, u32[]{:S(2)}, u32[]{:S(2)}) collective-permute-start(bf16[4,4,128,128]{3,2,1,0:T(8,128)(2,1)S(1)} %slice.103), channel_id=1, source_target_pairs={{0,16},{1,17},{2,18},{3,19},{4,20},{5,21},{6,22},{7,23},{8,24},{9,... | collective-permute-start | bytes 1572872 | tf_op jit(solution)/shard_map/ppermute | solution.py:37
  71.3 14.0 %collective-permute-start.10 = (bf16[128,128,128]{2,1,0:T(8,128)(2,1)}, bf16[128,128,128]{2,1,0:T(8,128)(2,1)}, u32[]{:S(2)}, u32[]{:S(2)}) collective-permute-start(bf16[128,128,128]{2,1,0:T(8,128)(2,1)} %bitcast.16.proj_ref), channel_id=1, source_target_pairs={{0,32},{32,0},{64,96},{96,64},{1,33},{33,1},{65,97},{97,65},{2,34}... | collective-permute-start | bytes 12582920 | tf_op jit(solution)/shard_map/ppermute | solution.py:41
  71.3 5.3 %copy-start.5 = (s32[8]{0:T(128)S(1)}, s32[8]{0:T(128)}, u32[]{:S(2)}) copy-start(s32[8]{0:T(128)} %count_ref.5) | copy-start | bytes 100
  71.3 5.3 %copy-start.6 = (s32[256]{0:T(256)S(1)}, s32[256]{0:T(256)}, u32[]{:S(2)}) copy-start(s32[256]{0:T(256)} %param.9) | copy-start | bytes 3076
  76.1 29.9 %collective-permute-start.13 = (bf16[2,2,32,128,128]{4,3,2,1,0:T(8,128)(2,1)}, bf16[2,2,32,128,128]{4,3,2,1,0:T(8,128)(2,1)}, u32[]{:S(2)}, u32[]{:S(2)}) collective-permute-start(bf16[2,2,32,128,128]{4,3,2,1,0:T(8,128)(2,1)} %dynamic-slice_bitcast_fusion), channel_id=1, source_target_pairs={{0,32},{32,0},{64,96},{96,64},{1,33},{33,1},{65,97},{97,65},{2,34}... | collective-permute-start | bytes 12582920 | tf_op jit(solution)/shard_map/ppermute | solution.py:41
  76.6 29.4 %collective-permute-start.12 = (s32[8]{0:T(128)S(1)}, s32[8]{0:T(128)S(1)}, u32[]{:S(2)}, u32[]{:S(2)}) collective-permute-start(s32[8]{0:T(128)S(1)} %copy-done.5), channel_id=1, source_target_pairs={{0,32},{32,0},{64,96},{96,64},{1,33},{33,1},{65,97},{97,65},{2,34}... | collective-permute-start | bytes 104 | tf_op jit(solution)/shard_map/ppermute | solution.py:41
  76.6 18.5 %collective-permute-start.11 = (s32[256]{0:T(256)S(1)}, s32[256]{0:T(256)S(1)}, u32[]{:S(2)}, u32[]{:S(2)}) collective-permute-start(s32[256]{0:T(256)S(1)} %copy-done.6), channel_id=1, source_target_pairs={{0,32},{32,0},{64,96},{96,64},{1,33},{33,1},{65,97},{97,65},{2,34}... | collective-permute-start | bytes 3080 | tf_op jit(solution)/shard_map/ppermute | solution.py:41
  85.3 7.7 %copy-start.1 = (f32[2,128,128]{2,1,0:T(8,128)S(1)}, f32[2,128,128]{2,1,0:T(8,128)}, u32[]{:S(2)}) copy-start(f32[2,128,128]{2,1,0:T(8,128)} %shard_map.85) | copy-start | bytes 393220
  85.3 8.6 %copy-start.4 = (bf16[256,128]{1,0:T(8,128)(2,1)S(1)}, bf16[256,128]{1,0:T(8,128)(2,1)}, u32[]{:S(2)}) copy-start(bf16[256,128]{1,0:T(8,128)(2,1)} %param.11) | copy-start | bytes 196612
  94.8 11.2 %collective-permute-start.14 = (bf16[2,128,128]{2,1,0:T(8,128)(2,1)S(1)}, bf16[2,128,128]{2,1,0:T(8,128)(2,1)S(1)}, u32[]{:S(2)}, u32[]{:S(2)}) collective-permute-start(bf16[2,128,128]{2,1,0:T(8,128)(2,1)S(1)} %bitcast.117), channel_id=1, source_target_pairs={{0,32},{32,0},{64,96},{96,64},{1,33},{33,1},{65,97},{97,65},{2,34}... | collective-permute-start | bytes 196616 | tf_op jit(solution)/shard_map/ppermute | solution.py:41
  121.1 9.2 %collective-permute-start.17 = (bf16[4,4,128,128]{3,2,1,0:T(8,128)(2,1)S(1)}, bf16[4,4,128,128]{3,2,1,0:T(8,128)(2,1)S(1)}, u32[]{:S(2)}, u32[]{:S(2)}) collective-permute-start(bf16[4,4,128,128]{3,2,1,0:T(8,128)(2,1)S(1)} %get-tuple-element.14), channel_id=1, source_target_pairs={{0,80},{1,81},{2,82},{3,83},{4,84},{5,85},{6,86},{7,87},{8,88},{9,... | collective-permute-start | bytes 1572872 | tf_op jit(solution)/shard_map/ppermute | solution.py:37
  121.2 10.7 %collective-permute-start.15 = (bf16[4,4,128,128]{3,2,1,0:T(8,128)(2,1)S(1)}, bf16[4,4,128,128]{3,2,1,0:T(8,128)(2,1)S(1)}, u32[]{:S(2)}, u32[]{:S(2)}) collective-permute-start(bf16[4,4,128,128]{3,2,1,0:T(8,128)(2,1)S(1)} %get-tuple-element.13), channel_id=1, source_target_pairs={{0,16},{1,17},{2,18},{3,19},{4,20},{5,21},{6,22},{7,23},{8,24},{9,... | collective-permute-start | bytes 1572872 | tf_op jit(solution)/shard_map/ppermute | solution.py:37
  130.6 14.9 %collective-permute-start.18 = (bf16[4,4,256,128]{3,2,1,0:T(8,128)(2,1)S(1)}, bf16[4,4,256,128]{3,2,1,0:T(8,128)(2,1)S(1)}, u32[]{:S(2)}, u32[]{:S(2)}) collective-permute-start(bf16[4,4,256,128]{3,2,1,0:T(8,128)(2,1)S(1)} %pad_maximum_fusion.3), channel_id=1, source_target_pairs={{0,80},{1,81},{2,82},{3,83},{4,84},{5,85},{6,86},{7,87},{8,88},{9,... | collective-permute-start | bytes 3145736 | tf_op jit(solution)/shard_map/ppermute | solution.py:37
  132.1 16.1 %collective-permute-start.16 = (bf16[4,4,256,128]{3,2,1,0:T(8,128)(2,1)S(1)}, bf16[4,4,256,128]{3,2,1,0:T(8,128)(2,1)S(1)}, u32[]{:S(2)}, u32[]{:S(2)}) collective-permute-start(bf16[4,4,256,128]{3,2,1,0:T(8,128)(2,1)S(1)} %pad_maximum_fusion.2), channel_id=1, source_target_pairs={{0,16},{1,17},{2,18},{3,19},{4,20},{5,21},{6,22},{7,23},{8,24},{9,... | collective-permute-start | bytes 3145736 | tf_op jit(solution)/shard_map/ppermute | solution.py:37
  148.8 14.7 %collective-permute-start.19 = (bf16[4,256,128]{2,1,0:T(8,128)(2,1)S(1)}, bf16[4,256,128]{2,1,0:T(8,128)(2,1)S(1)}, u32[]{:S(2)}, u32[]{:S(2)}) collective-permute-start(bf16[4,256,128]{2,1,0:T(8,128)(2,1)S(1)} %get-tuple-element.10), channel_id=1, source_target_pairs={{0,4},{1,5},{2,6},{3,7},{4,8},{5,9},{6,10},{7,11},{8,12},{9,13},{1... | collective-permute-start | bytes 786440 | tf_op jit(solution)/shard_map/ppermute | solution.py:37
  149.3 14.2 %collective-permute-start.21 = (bf16[4,256,128]{2,1,0:T(8,128)(2,1)S(1)}, bf16[4,256,128]{2,1,0:T(8,128)(2,1)S(1)}, u32[]{:S(2)}, u32[]{:S(2)}) collective-permute-start(bf16[4,256,128]{2,1,0:T(8,128)(2,1)S(1)} %get-tuple-element.11), channel_id=1, source_target_pairs={{0,8},{1,9},{2,10},{3,11},{4,12},{5,13},{6,14},{7,15},{8,0},{9,1},... | collective-permute-start | bytes 786440 | tf_op jit(solution)/shard_map/ppermute | solution.py:37
  151.2 12.9 %collective-permute-start.20 = (bf16[4,256,128]{2,1,0:T(8,128)(2,1)S(1)}, bf16[4,256,128]{2,1,0:T(8,128)(2,1)S(1)}, u32[]{:S(2)}, u32[]{:S(2)}) collective-permute-start(bf16[4,256,128]{2,1,0:T(8,128)(2,1)S(1)} %get-tuple-element.12), channel_id=1, source_target_pairs={{0,12},{1,13},{2,14},{3,15},{4,0},{5,1},{6,2},{7,3},{8,4},{9,5},{1... | collective-permute-start | bytes 786440 | tf_op jit(solution)/shard_map/ppermute | solution.py:37
  164.2 6.2 %collective-permute-start.22 = (bf16[256,128]{1,0:T(8,128)(2,1)S(1)}, bf16[256,128]{1,0:T(8,128)(2,1)S(1)}, u32[]{:S(2)}, u32[]{:S(2)}) collective-permute-start(bf16[256,128]{1,0:T(8,128)(2,1)S(1)} %get-tuple-element.17), channel_id=1, source_target_pairs={{0,1},{1,2},{2,3},{3,0},{4,5},{5,6},{6,7},{7,4},{8,9},{9,10},{10,1... | collective-permute-start | bytes 196616 | tf_op jit(solution)/shard_map/ppermute | solution.py:37
  164.3 6.2 %collective-permute-start.24 = (bf16[256,128]{1,0:T(8,128)(2,1)S(1)}, bf16[256,128]{1,0:T(8,128)(2,1)S(1)}, u32[]{:S(2)}, u32[]{:S(2)}) collective-permute-start(bf16[256,128]{1,0:T(8,128)(2,1)S(1)} %get-tuple-element.18), channel_id=1, source_target_pairs={{0,2},{1,3},{2,0},{3,1},{4,6},{5,7},{6,4},{7,5},{8,10},{9,11},{10,... | collective-permute-start | bytes 196616 | tf_op jit(solution)/shard_map/ppermute | solution.py:37
  165.7 5.6 %collective-permute-start.23 = (bf16[256,128]{1,0:T(8,128)(2,1)S(1)}, bf16[256,128]{1,0:T(8,128)(2,1)S(1)}, u32[]{:S(2)}, u32[]{:S(2)}) collective-permute-start(bf16[256,128]{1,0:T(8,128)(2,1)S(1)} %get-tuple-element.19), channel_id=1, source_target_pairs={{0,3},{1,0},{2,1},{3,2},{4,7},{5,4},{6,5},{7,6},{8,11},{9,8},{10,9... | collective-permute-start | bytes 196616 | tf_op jit(solution)/shard_map/ppermute | solution.py:37
  186.5 1.2 collective-permute-start.25
  187.8 5.1 %collective-permute-start.26 = (f32[4,128]{1,0:T(4,128)S(1)}, f32[4,128]{1,0:T(4,128)S(1)}, u32[]{:S(2)}, u32[]{:S(2)}) collective-permute-start(f32[4,128]{1,0:T(4,128)S(1)} %add.227), channel_id=1, source_target_pairs={{0,64},{32,96},{64,0},{96,32},{1,65},{33,97},{65,1},{97,33},{2,66}... | collective-permute-start | bytes 6152 | tf_op jit(solution)/shard_map/ppermute | solution.py:46
  (3 other events, 2.1 us)

commit v10 on v9

--- a/solution.py
+++ b/solution.py
@@ -274,9 +274,7 @@
     core_id = blk_id % 2
     tile_stack = tile_values.reshape(cycle_size, tile_rows, slot_count, tile_size, tile_size)
     spots = buffer_spots(tile_col, blk_id, feat_id, block_tiles, tile_rows)
-    by_core = tile_stack.reshape(cycle_size // 2, 2, tile_rows, slot_count, tile_size, tile_size)
-    for_sibling = lax.dynamic_index_in_dim(by_core, 1 - core_id, 1, keepdims=False)
-    sibling_tiles = sibling(for_sibling)
+    sibling_tiles = sibling(tile_stack)
     sibling_spots = buffer_spots(sibling(tile_col), blk_id, feat_id, block_tiles, tile_rows)
     sibling_count = sibling(tile_count)
     buffer_tiles = block_tiles * 2
@@ -310,7 +308,7 @@
     )
     total = spread_pair(
         core_id, sibling_spots, sibling_count, sibling_tiles, sibling_grad, buffer_tiles,
-        jnp.float32, total, block_step=1, core_step=0,
+        jnp.float32, total,
     )
     total = reduce_phase(
         total.reshape(RING, RING, RING, rows_own, hidden_width), 2, jnp.bfloat16

time: 194 us -> 189 us (0.974)
  local copies, waits for them, and re-layouts: 12.3 us -> 7.03 us
    squeeze x1 -> x0, local copies, waits for them, and re-layouts: 4.82 us -> none  [body(): lax.dynamic_index_in_dim(by_core, 1 - core_id, 1, keepdims=False)]
where the time goes in v10:
time: 189 us; the launch traced here: 188 us
  waiting for transfers between devices  73.4 us (39%)
  Pallas kernels  37.2 us (20%)
  blocking collectives  32.2 us (17%)
  starting transfers between devices  29.5 us (16%)
  other arithmetic  7.16 us (4%)
  local copies, waits for them, and re-layouts  7.03 us (4%)
    ppermute x20, waiting for transfers between devices, ring_shift(): return lax.ppermute(block, BOTH, route)  68.6 us
    ppermute x20, starting transfers between devices, ring_shift(): return lax.ppermute(block, BOTH, route)  27.2 us
    pallas_call x2, Pallas kernels, spread_pair(): pl.pallas_call(spread_kernel, grid_spec=grid_spec, out_shape=jax.ShapeDty...  21.9 us
    all_to_all x1, blocking collectives, body(): lax.all_to_all(features_t, 'feat', split_axis=1, concat_axis=0, tiled=True)  17.6 us
    pallas_call x2, Pallas kernels, aggregate_pair(): pl.pallas_call(aggregate_kernel, grid_spec=grid_spec, out_shape=jax.Shape...  15.3 us
    all_to_all x1, blocking collectives, body(): lax.all_to_all(outgoing, 'feat', split_axis=0, concat_axis=0, tiled=True)  14.6 us
    slice x2, local copies, waits for them, and re-layouts, term(): return total[k]  5.03 us
    ppermute x2, waiting for transfers between devices, swapped(): return lax.ppermute(block, axis, [(i, i ^ mask) for i in range(count)])  4.76 us
  transfers between devices with their start and end apart: 27, of which 18 were waited for; matrix products, arithmetic and copies ran while one was open for 6% of the time, Pallas kernels for 13%

profile of v10, /device:TPU:0, one launch (start us, length us, event | category | flops | bytes accessed | tf_op | source)
XLA Modules:
  0.0 187.9 jit_solution(10233749464025758589)
XLA Ops:
  0.7 17.6 %all_to_all.24 = bf16[4,32,256]{2,0,1:T(4,128)(2,1)S(1)} all-to-all(bf16[4,32,256]{2,0,1:T(4,128)(2,1)} %bitcast.125), channel_id=1, replica_groups=mesh['blk'=4,'feat'=32] {'feat'}, dimensions={1} | all-to-all | bytes 131072 | tf_op jit(solution)/shard_map/all_to_all | solution.py:282
  19.2 2.3 %collective-permute-start.1 = (bf16[256,128]{1,0:T(8,128)(2,1)S(1)}, bf16[256,128]{1,0:T(8,128)(2,1)S(1)}, u32[]{:S(2)}, u32[]{:S(2)}) collective-permute-start(bf16[256,128]{1,0:T(8,128)(2,1)S(1)} %convolution_convert_fusion.1), channel_id=1, source_target_pairs={{0,2},{1,3},{2,0},{3,1},{4,6},{5,7},{6,4},{7,5},{8,10},{9,11},{10,... | collective-permute-start | bytes 196616 | tf_op jit(solution)/shard_map/ppermute | solution.py:37
  22.6 1.5 collective-permute-done.2
  25.8 1.4 collective-permute-start.4
  27.2 1.9 %collective-permute-start.3 = (bf16[4,256,128]{2,1,0:T(8,128)(2,1)S(1)}, bf16[4,256,128]{2,1,0:T(8,128)(2,1)S(1)}, u32[]{:S(2)}, u32[]{:S(2)}) collective-permute-start(bf16[4,256,128]{2,1,0:T(8,128)(2,1)S(1)} %get-tuple-element.21), channel_id=1, source_target_pairs={{0,12},{1,13},{2,14},{3,15},{4,0},{5,1},{6,2},{7,3},{8,4},{9,5},{1... | collective-permute-start | bytes 786440 | tf_op jit(solution)/shard_map/ppermute | solution.py:37
  29.2 7.4 %collective-permute-done.4 = bf16[4,256,128]{2,1,0:T(8,128)(2,1)S(1)} collective-permute-done((bf16[4,256,128]{2,1,0:T(8,128)(2,1)S(1)}, bf16[4,256,128]{2,1,0:T(8,128)(2,1)S(1)}, u32[]{:S(2)}, u32[]{:S(2)}) %collective-permute-start.4) | collective-permute-done | bytes 262176 | tf_op jit(solution)/shard_map/ppermute | solution.py:37
  36.6 1.4 collective-permute-done.3
  38.0 1.7 collective-permute-done.5
  39.9 3.0 %collective-permute-start.6 = (bf16[4,4,256,128]{3,2,1,0:T(8,128)(2,1)S(1)}, bf16[4,4,256,128]{3,2,1,0:T(8,128)(2,1)S(1)}, u32[]{:S(2)}, u32[]{:S(2)}) collective-permute-start(bf16[4,4,256,128]{3,2,1,0:T(8,128)(2,1)S(1)} %get-tuple-element.16), channel_id=1, source_target_pairs={{0,80},{1,81},{2,82},{3,83},{4,84},{5,85},{6,86},{7,87},{8,88},{9,... | collective-permute-start | bytes 3145736 | tf_op jit(solution)/shard_map/ppermute | solution.py:37
  42.9 12.3 %collective-permute-done.6 = bf16[4,4,256,128]{3,2,1,0:T(8,128)(2,1)S(1)} collective-permute-done((bf16[4,4,256,128]{3,2,1,0:T(8,128)(2,1)S(1)}, bf16[4,4,256,128]{3,2,1,0:T(8,128)(2,1)S(1)}, u32[]{:S(2)}, u32[]{:S(2)}) %collective-permute-start.6) | collective-permute-done | bytes 1048608 | tf_op jit(solution)/shard_map/ppermute | solution.py:37
  55.3 3.8 %collective-permute-start.9 = (bf16[4,4,128,128]{3,2,1,0:T(8,128)(2,1)S(1)}, bf16[4,4,128,128]{3,2,1,0:T(8,128)(2,1)S(1)}, u32[]{:S(2)}, u32[]{:S(2)}) collective-permute-start(bf16[4,4,128,128]{3,2,1,0:T(8,128)(2,1)S(1)} %slice.104), channel_id=1, source_target_pairs={{0,80},{1,81},{2,82},{3,83},{4,84},{5,85},{6,86},{7,87},{8,88},{9,... | collective-permute-start | bytes 1572872 | tf_op jit(solution)/shard_map/ppermute | solution.py:37
  59.2 6.6 %collective-permute-done.9 = bf16[4,4,128,128]{3,2,1,0:T(8,128)(2,1)S(1)} collective-permute-done((bf16[4,4,128,128]{3,2,1,0:T(8,128)(2,1)S(1)}, bf16[4,4,128,128]{3,2,1,0:T(8,128)(2,1)S(1)}, u32[]{:S(2)}, u32[]{:S(2)}) %collective-permute-start.9) | collective-permute-done | bytes 524320 | tf_op jit(solution)/shard_map/ppermute | solution.py:37
  65.7 3.8 %collective-permute-done.8 = bf16[4,4,128,128]{3,2,1,0:T(8,128)(2,1)S(1)} collective-permute-done((bf16[4,4,128,128]{3,2,1,0:T(8,128)(2,1)S(1)}, bf16[4,4,128,128]{3,2,1,0:T(8,128)(2,1)S(1)}, u32[]{:S(2)}, u32[]{:S(2)}) %collective-permute-start.8) | collective-permute-done | bytes 524320 | tf_op jit(solution)/shard_map/ppermute | solution.py:37
  69.6 2.3 %pad_maximum_fusion = bf16[4,4,4,256,128]{4,3,2,1,0:T(8,128)(2,1)} fusion(bf16[1,4,4,256,128]{4,3,2,1,0:T(8,128)(2,1)S(1)} %bitcast.109, bf16[1,4,4,256,128]{4,3,2,1,0:T(8,128)(2,1)S(1)} %maximum_bitcast_fusion, bf16[1,4,4,256,128]{4,3,2,1,0:T(8,128)(2,1)S(1)} %bitcast.108, bf16[1,4,4,256,128]{4,3,2,1,0:T(8,128)(2,1)S(1)} %get-tuple-element.15), kind=kLoop, calls=%fused_computation | loop fusion | flops 6291456 | bytes 8388608 | tf_op jit(solution)/shard_map/stack | solution.py:56
  73.1 7.6 %shard_map.85 = f32[2,128,128]{2,1,0:T(8,128)} custom-call(s32[1]{0:T(128)} %bitcast.core_ref, s32[256]{0:T(256)} %fusion.21.where_ref, s32[8]{0:T(128)} %count_ref.5, bf16[4,2,32,128,128]{4,3,2,1,0:T(8,128)(2,1)} %bitcast.99, bf16[128,128,128]{2,1,0:T(8,128)(2,1)} %bitcast.16.proj_ref), custom_call_target="tpu_custom_call" | custom-call | tf_op jit(solution)/shard_map/pallas_call | solution.py:161
  80.7 7.7 %shard_map.86 = f32[2,128,128]{2,1,0:T(8,128)} custom-call(s32[1]{0:T(128)} %bitcast.17.core_ref, s32[256]{0:T(256)} %fusion.21.where_ref, s32[8]{0:T(128)} %count_ref.5, bf16[4,2,32,128,128]{4,3,2,1,0:T(8,128)(2,1)} %bitcast.100, bf16[128,128,128]{2,1,0:T(8,128)(2,1)} %collective-permute-done.10.proj_ref), custom_call_target="tpu_custom_call" | custom-call | tf_op jit(solution)/shard_map/pallas_call | solution.py:161
  91.5 9.7 %shard_map.87.rest_0_ = f32[128,128,128]{2,1,0:T(8,128)} custom-call(s32[1]{0:T(128)} %bitcast.core_ref, s32[256]{0:T(256)} %fusion.21.where_ref, s32[8]{0:T(128)} %count_ref.5, bf16[4,2,32,128,128]{4,3,2,1,0:T(8,128)(2,1)} %bitcast.101, bf16[2,128,128]{2,1,0:T(8,128)(2,1)} %bitcast.113), custom_call_target="tpu_custom_call" | custom-call | tf_op jit(solution)/shard_map/pallas_call | solution.py:232
  101.9 12.2 %shard_map.88 = f32[128,128,128]{2,1,0:T(8,128)} custom-call(s32[1]{0:T(128)} %bitcast.core_ref, s32[256]{0:T(256)} %fusion.25.where_ref, s32[8]{0:T(128)} %copy-done.7, bf16[4,2,32,128,128]{4,3,2,1,0:T(8,128)(2,1)} %collective-permute-done.13.tiles_ref, bf16[2,128,128]{2,1,0:T(8,128)(2,1)} %copy-done.3, f32[128,128,128]{2,1,0:T(8,128)} %shard_map.87.rest_0_), custom_call_target="tpu_custom_call" | custom-call | tf_op jit(solution)/shard_map/pallas_call | solution.py:232
  114.1 1.7 slice.158
  116.0 2.0 %collective-permute-start.15 = (bf16[4,4,128,128]{3,2,1,0:T(8,128)(2,1)S(1)}, bf16[4,4,128,128]{3,2,1,0:T(8,128)(2,1)S(1)}, u32[]{:S(2)}, u32[]{:S(2)}) collective-permute-start(bf16[4,4,128,128]{3,2,1,0:T(8,128)(2,1)S(1)} %get-tuple-element.13), channel_id=1, source_target_pairs={{0,16},{1,17},{2,18},{3,19},{4,20},{5,21},{6,22},{7,23},{8,24},{9,... | collective-permute-start | bytes 1572872 | tf_op jit(solution)/shard_map/ppermute | solution.py:37
  118.0 3.3 %fusion.39 = (f32[32,128,128]{2,1,0:T(8,128)S(1)}, f32[32,128,128]{2,1,0:T(8,128)S(1)}, f32[32,128,128]{2,1,0:T(8,128)S(1)}) fusion(f32[128,128,128]{2,1,0:T(8,128)} %shard_map.88), kind=kLoop, calls=%fused_computation.139 | loop fusion | bytes 12582912 | tf_op jit(solution)/shard_map/slice | solution.py:83
  121.5 3.7 %collective-permute-done.17 = bf16[4,4,128,128]{3,2,1,0:T(8,128)(2,1)S(1)} collective-permute-done((bf16[4,4,128,128]{3,2,1,0:T(8,128)(2,1)S(1)}, bf16[4,4,128,128]{3,2,1,0:T(8,128)(2,1)S(1)}, u32[]{:S(2)}, u32[]{:S(2)}) %collective-permute-start.17) | collective-permute-done | bytes 524320 | tf_op jit(solution)/shard_map/ppermute | solution.py:37
  127.8 12.5 %collective-permute-done.18 = bf16[4,4,256,128]{3,2,1,0:T(8,128)(2,1)S(1)} collective-permute-done((bf16[4,4,256,128]{3,2,1,0:T(8,128)(2,1)S(1)}, bf16[4,4,256,128]{3,2,1,0:T(8,128)(2,1)S(1)}, u32[]{:S(2)}, u32[]{:S(2)}) %collective-permute-start.18) | collective-permute-done | bytes 1048608 | tf_op jit(solution)/shard_map/ppermute | solution.py:37
  140.3 2.7 %collective-permute-done.16 = bf16[4,4,256,128]{3,2,1,0:T(8,128)(2,1)S(1)} collective-permute-done((bf16[4,4,256,128]{3,2,1,0:T(8,128)(2,1)S(1)}, bf16[4,4,256,128]{3,2,1,0:T(8,128)(2,1)S(1)}, u32[]{:S(2)}, u32[]{:S(2)}) %collective-permute-start.16) | collective-permute-done | bytes 1048608 | tf_op jit(solution)/shard_map/ppermute | solution.py:37
  144.5 2.0 %collective-permute-start.21 = (bf16[4,256,128]{2,1,0:T(8,128)(2,1)S(1)}, bf16[4,256,128]{2,1,0:T(8,128)(2,1)S(1)}, u32[]{:S(2)}, u32[]{:S(2)}) collective-permute-start(bf16[4,256,128]{2,1,0:T(8,128)(2,1)S(1)} %get-tuple-element.11), channel_id=1, source_target_pairs={{0,8},{1,9},{2,10},{3,11},{4,12},{5,13},{6,14},{7,15},{8,0},{9,1},... | collective-permute-start | bytes 786440 | tf_op jit(solution)/shard_map/ppermute | solution.py:37
  146.5 2.5 %collective-permute-start.20 = (bf16[4,256,128]{2,1,0:T(8,128)(2,1)S(1)}, bf16[4,256,128]{2,1,0:T(8,128)(2,1)S(1)}, u32[]{:S(2)}, u32[]{:S(2)}) collective-permute-start(bf16[4,256,128]{2,1,0:T(8,128)(2,1)S(1)} %get-tuple-element.12), channel_id=1, source_target_pairs={{0,12},{1,13},{2,14},{3,15},{4,0},{5,1},{6,2},{7,3},{8,4},{9,5},{1... | collective-permute-start | bytes 786440 | tf_op jit(solution)/shard_map/ppermute | solution.py:37
  148.9 9.0 %collective-permute-done.19 = bf16[4,256,128]{2,1,0:T(8,128)(2,1)S(1)} collective-permute-done((bf16[4,256,128]{2,1,0:T(8,128)(2,1)S(1)}, bf16[4,256,128]{2,1,0:T(8,128)(2,1)S(1)}, u32[]{:S(2)}, u32[]{:S(2)}) %collective-permute-start.19) | collective-permute-done | bytes 262176 | tf_op jit(solution)/shard_map/ppermute | solution.py:37
  158.8 1.4 collective-permute-start.24
  160.2 1.8 collective-permute-start.23
  162.0 2.9 %collective-permute-done.22 = bf16[256,128]{1,0:T(8,128)(2,1)S(1)} collective-permute-done((bf16[256,128]{1,0:T(8,128)(2,1)S(1)}, bf16[256,128]{1,0:T(8,128)(2,1)S(1)}, u32[]{:S(2)}, u32[]{:S(2)}) %collective-permute-start.22) | collective-permute-done | bytes 65568 | tf_op jit(solution)/shard_map/ppermute | solution.py:37
  166.4 14.6 %all_to_all.25 = f32[32,4,384]{2,1,0:T(4,128)S(1)} all-to-all(f32[32,4,384]{2,1,0:T(4,128)S(1)} %pad_maximum_fusion.5), channel_id=1, replica_groups=mesh['blk'=4,'feat'=32] {'feat'}, dimensions={0} | all-to-all | bytes 393216 | tf_op jit(solution)/shard_map/all_to_all | solution.py:338
  183.7 3.6 %collective-permute-done.26 = f32[4,128]{1,0:T(4,128)S(1)} collective-permute-done((f32[4,128]{1,0:T(4,128)S(1)}, f32[4,128]{1,0:T(4,128)S(1)}, u32[]{:S(2)}, u32[]{:S(2)}) %collective-permute-start.26) | collective-permute-done | bytes 2080 | tf_op jit(solution)/shard_map/ppermute | solution.py:46
  (80 shorter events, 19.1 us)
Async XLA Ops:
  0.6 17.7 %copy-start = (bf16[128,128]{1,0:T(8,128)(2,1)S(1)}, bf16[128,128]{1,0:T(8,128)(2,1)}, u32[]{:S(2)}) copy-start(bf16[128,128]{1,0:T(8,128)(2,1)} %param.7) | copy-start | bytes 98308
  0.6 100.6 %collective-permute-start.13 = (bf16[4,2,32,128,128]{4,3,2,1,0:T(8,128)(2,1)}, bf16[4,2,32,128,128]{4,3,2,1,0:T(8,128)(2,1)}, u32[]{:S(2)}, u32[]{:S(2)}) collective-permute-start(bf16[4,2,32,128,128]{4,3,2,1,0:T(8,128)(2,1)} %bitcast.98), channel_id=1, source_target_pairs={{0,32},{32,0},{64,96},{96,64},{1,33},{33,1},{65,97},{97,65},{2,34}... | collective-permute-start | bytes 25165832 | tf_op jit(solution)/shard_map/ppermute | solution.py:41
  18.6 5.5 %collective-permute-start.2 = (bf16[256,128]{1,0:T(8,128)(2,1)S(1)}, bf16[256,128]{1,0:T(8,128)(2,1)S(1)}, u32[]{:S(2)}, u32[]{:S(2)}) collective-permute-start(bf16[256,128]{1,0:T(8,128)(2,1)S(1)} %convolution_convert_fusion.1), channel_id=1, source_target_pairs={{0,1},{1,2},{2,3},{3,0},{4,5},{5,6},{6,7},{7,4},{8,9},{9,10},{10,1... | collective-permute-start | bytes 196616 | tf_op jit(solution)/shard_map/ppermute | solution.py:37
  19.2 5.8 %collective-permute-start.1 = (bf16[256,128]{1,0:T(8,128)(2,1)S(1)}, bf16[256,128]{1,0:T(8,128)(2,1)S(1)}, u32[]{:S(2)}, u32[]{:S(2)}) collective-permute-start(bf16[256,128]{1,0:T(8,128)(2,1)S(1)} %convolution_convert_fusion.1), channel_id=1, source_target_pairs={{0,2},{1,3},{2,0},{3,1},{4,6},{5,7},{6,4},{7,5},{8,10},{9,11},{10,... | collective-permute-start | bytes 196616 | tf_op jit(solution)/shard_map/ppermute | solution.py:37
  21.5 4.3 %collective-permute-start = (bf16[256,128]{1,0:T(8,128)(2,1)S(1)}, bf16[256,128]{1,0:T(8,128)(2,1)S(1)}, u32[]{:S(2)}, u32[]{:S(2)}) collective-permute-start(bf16[256,128]{1,0:T(8,128)(2,1)S(1)} %convolution_convert_fusion.1), channel_id=1, source_target_pairs={{0,3},{1,0},{2,1},{3,2},{4,7},{5,4},{6,5},{7,6},{8,11},{9,8},{10,9... | collective-permute-start | bytes 196616 | tf_op jit(solution)/shard_map/ppermute | solution.py:37
  25.8 10.8 %collective-permute-start.4 = (bf16[4,256,128]{2,1,0:T(8,128)(2,1)S(1)}, bf16[4,256,128]{2,1,0:T(8,128)(2,1)S(1)}, u32[]{:S(2)}, u32[]{:S(2)}) collective-permute-start(bf16[4,256,128]{2,1,0:T(8,128)(2,1)S(1)} %get-tuple-element.21), channel_id=1, source_target_pairs={{0,8},{1,9},{2,10},{3,11},{4,12},{5,13},{6,14},{7,15},{8,0},{9,1},... | collective-permute-start | bytes 786440 | tf_op jit(solution)/shard_map/ppermute | solution.py:37
  27.2 10.8 %collective-permute-start.3 = (bf16[4,256,128]{2,1,0:T(8,128)(2,1)S(1)}, bf16[4,256,128]{2,1,0:T(8,128)(2,1)S(1)}, u32[]{:S(2)}, u32[]{:S(2)}) collective-permute-start(bf16[4,256,128]{2,1,0:T(8,128)(2,1)S(1)} %get-tuple-element.21), channel_id=1, source_target_pairs={{0,12},{1,13},{2,14},{3,15},{4,0},{5,1},{6,2},{7,3},{8,4},{9,5},{1... | collective-permute-start | bytes 786440 | tf_op jit(solution)/shard_map/ppermute | solution.py:37
  29.1 10.6 %collective-permute-start.5 = (bf16[4,256,128]{2,1,0:T(8,128)(2,1)S(1)}, bf16[4,256,128]{2,1,0:T(8,128)(2,1)S(1)}, u32[]{:S(2)}, u32[]{:S(2)}) collective-permute-start(bf16[4,256,128]{2,1,0:T(8,128)(2,1)S(1)} %get-tuple-element.21), channel_id=1, source_target_pairs={{0,4},{1,5},{2,6},{3,7},{4,8},{5,9},{6,10},{7,11},{8,12},{9,13},{1... | collective-permute-start | bytes 786440 | tf_op jit(solution)/shard_map/ppermute | solution.py:37
  39.9 15.3 %collective-permute-start.6 = (bf16[4,4,256,128]{3,2,1,0:T(8,128)(2,1)S(1)}, bf16[4,4,256,128]{3,2,1,0:T(8,128)(2,1)S(1)}, u32[]{:S(2)}, u32[]{:S(2)}) collective-permute-start(bf16[4,4,256,128]{3,2,1,0:T(8,128)(2,1)S(1)} %get-tuple-element.16), channel_id=1, source_target_pairs={{0,80},{1,81},{2,82},{3,83},{4,84},{5,85},{6,86},{7,87},{8,88},{9,... | collective-permute-start | bytes 3145736 | tf_op jit(solution)/shard_map/ppermute | solution.py:37
  42.9 16.1 %collective-permute-start.7 = (bf16[4,4,256,128]{3,2,1,0:T(8,128)(2,1)S(1)}, bf16[4,4,256,128]{3,2,1,0:T(8,128)(2,1)S(1)}, u32[]{:S(2)}, u32[]{:S(2)}) collective-permute-start(bf16[4,4,256,128]{3,2,1,0:T(8,128)(2,1)S(1)} %get-tuple-element.16), channel_id=1, source_target_pairs={{0,16},{1,17},{2,18},{3,19},{4,20},{5,21},{6,22},{7,23},{8,24},{9,... | collective-permute-start | bytes 3145736 | tf_op jit(solution)/shard_map/ppermute | solution.py:37
  55.3 10.5 %collective-permute-start.9 = (bf16[4,4,128,128]{3,2,1,0:T(8,128)(2,1)S(1)}, bf16[4,4,128,128]{3,2,1,0:T(8,128)(2,1)S(1)}, u32[]{:S(2)}, u32[]{:S(2)}) collective-permute-start(bf16[4,4,128,128]{3,2,1,0:T(8,128)(2,1)S(1)} %slice.104), channel_id=1, source_target_pairs={{0,80},{1,81},{2,82},{3,83},{4,84},{5,85},{6,86},{7,87},{8,88},{9,... | collective-permute-start | bytes 1572872 | tf_op jit(solution)/shard_map/ppermute | solution.py:37
  59.1 10.5 %collective-permute-start.8 = (bf16[4,4,128,128]{3,2,1,0:T(8,128)(2,1)S(1)}, bf16[4,4,128,128]{3,2,1,0:T(8,128)(2,1)S(1)}, u32[]{:S(2)}, u32[]{:S(2)}) collective-permute-start(bf16[4,4,128,128]{3,2,1,0:T(8,128)(2,1)S(1)} %slice.103), channel_id=1, source_target_pairs={{0,16},{1,17},{2,18},{3,19},{4,20},{5,21},{6,22},{7,23},{8,24},{9,... | collective-permute-start | bytes 1572872 | tf_op jit(solution)/shard_map/ppermute | solution.py:37
  69.6 2.3 %copy-start.5 = (s32[8]{0:T(128)S(1)}, s32[8]{0:T(128)}, u32[]{:S(2)}) copy-start(s32[8]{0:T(128)} %count_ref.5) | copy-start | bytes 100
  69.6 2.8 %copy-start.6 = (s32[256]{0:T(256)S(1)}, s32[256]{0:T(256)}, u32[]{:S(2)}) copy-start(s32[256]{0:T(256)} %param.9) | copy-start | bytes 3076
  71.9 8.8 %collective-permute-start.10 = (bf16[128,128,128]{2,1,0:T(8,128)(2,1)}, bf16[128,128,128]{2,1,0:T(8,128)(2,1)}, u32[]{:S(2)}, u32[]{:S(2)}) collective-permute-start(bf16[128,128,128]{2,1,0:T(8,128)(2,1)} %bitcast.16.proj_ref), channel_id=1, source_target_pairs={{0,32},{32,0},{64,96},{96,64},{1,33},{33,1},{65,97},{97,65},{2,34}... | collective-permute-start | bytes 12582920 | tf_op jit(solution)/shard_map/ppermute | solution.py:41
  71.9 29.3 %collective-permute-start.12 = (s32[8]{0:T(128)S(1)}, s32[8]{0:T(128)S(1)}, u32[]{:S(2)}, u32[]{:S(2)}) collective-permute-start(s32[8]{0:T(128)S(1)} %copy-done.5), channel_id=1, source_target_pairs={{0,32},{32,0},{64,96},{96,64},{1,33},{33,1},{65,97},{97,65},{2,34}... | collective-permute-start | bytes 104 | tf_op jit(solution)/shard_map/ppermute | solution.py:41
  72.4 18.4 %collective-permute-start.11 = (s32[256]{0:T(256)S(1)}, s32[256]{0:T(256)S(1)}, u32[]{:S(2)}, u32[]{:S(2)}) collective-permute-start(s32[256]{0:T(256)S(1)} %copy-done.6), channel_id=1, source_target_pairs={{0,32},{32,0},{64,96},{96,64},{1,33},{33,1},{65,97},{97,65},{2,34}... | collective-permute-start | bytes 3080 | tf_op jit(solution)/shard_map/ppermute | solution.py:41
  80.7 7.7 %copy-start.1 = (f32[2,128,128]{2,1,0:T(8,128)S(1)}, f32[2,128,128]{2,1,0:T(8,128)}, u32[]{:S(2)}) copy-start(f32[2,128,128]{2,1,0:T(8,128)} %shard_map.85) | copy-start | bytes 393220
  80.7 8.6 %copy-start.4 = (bf16[256,128]{1,0:T(8,128)(2,1)S(1)}, bf16[256,128]{1,0:T(8,128)(2,1)}, u32[]{:S(2)}) copy-start(bf16[256,128]{1,0:T(8,128)(2,1)} %param.11) | copy-start | bytes 196612
  90.2 11.0 %collective-permute-start.14 = (bf16[2,128,128]{2,1,0:T(8,128)(2,1)S(1)}, bf16[2,128,128]{2,1,0:T(8,128)(2,1)S(1)}, u32[]{:S(2)}, u32[]{:S(2)}) collective-permute-start(bf16[2,128,128]{2,1,0:T(8,128)(2,1)S(1)} %bitcast.112), channel_id=1, source_target_pairs={{0,32},{32,0},{64,96},{96,64},{1,33},{33,1},{65,97},{97,65},{2,34}... | collective-permute-start | bytes 196616 | tf_op jit(solution)/shard_map/ppermute | solution.py:41
  115.9 9.2 %collective-permute-start.17 = (bf16[4,4,128,128]{3,2,1,0:T(8,128)(2,1)S(1)}, bf16[4,4,128,128]{3,2,1,0:T(8,128)(2,1)S(1)}, u32[]{:S(2)}, u32[]{:S(2)}) collective-permute-start(bf16[4,4,128,128]{3,2,1,0:T(8,128)(2,1)S(1)} %get-tuple-element.14), channel_id=1, source_target_pairs={{0,80},{1,81},{2,82},{3,83},{4,84},{5,85},{6,86},{7,87},{8,88},{9,... | collective-permute-start | bytes 1572872 | tf_op jit(solution)/shard_map/ppermute | solution.py:37
  116.0 10.7 %collective-permute-start.15 = (bf16[4,4,128,128]{3,2,1,0:T(8,128)(2,1)S(1)}, bf16[4,4,128,128]{3,2,1,0:T(8,128)(2,1)S(1)}, u32[]{:S(2)}, u32[]{:S(2)}) collective-permute-start(bf16[4,4,128,128]{3,2,1,0:T(8,128)(2,1)S(1)} %get-tuple-element.13), channel_id=1, source_target_pairs={{0,16},{1,17},{2,18},{3,19},{4,20},{5,21},{6,22},{7,23},{8,24},{9,... | collective-permute-start | bytes 1572872 | tf_op jit(solution)/shard_map/ppermute | solution.py:37
  125.4 14.9 %collective-permute-start.18 = (bf16[4,4,256,128]{3,2,1,0:T(8,128)(2,1)S(1)}, bf16[4,4,256,128]{3,2,1,0:T(8,128)(2,1)S(1)}, u32[]{:S(2)}, u32[]{:S(2)}) collective-permute-start(bf16[4,4,256,128]{3,2,1,0:T(8,128)(2,1)S(1)} %pad_maximum_fusion.3), channel_id=1, source_target_pairs={{0,80},{1,81},{2,82},{3,83},{4,84},{5,85},{6,86},{7,87},{8,88},{9,... | collective-permute-start | bytes 3145736 | tf_op jit(solution)/shard_map/ppermute | solution.py:37
  126.9 16.1 %collective-permute-start.16 = (bf16[4,4,256,128]{3,2,1,0:T(8,128)(2,1)S(1)}, bf16[4,4,256,128]{3,2,1,0:T(8,128)(2,1)S(1)}, u32[]{:S(2)}, u32[]{:S(2)}) collective-permute-start(bf16[4,4,256,128]{3,2,1,0:T(8,128)(2,1)S(1)} %pad_maximum_fusion.2), channel_id=1, source_target_pairs={{0,16},{1,17},{2,18},{3,19},{4,20},{5,21},{6,22},{7,23},{8,24},{9,... | collective-permute-start | bytes 3145736 | tf_op jit(solution)/shard_map/ppermute | solution.py:37
  143.5 14.4 %collective-permute-start.19 = (bf16[4,256,128]{2,1,0:T(8,128)(2,1)S(1)}, bf16[4,256,128]{2,1,0:T(8,128)(2,1)S(1)}, u32[]{:S(2)}, u32[]{:S(2)}) collective-permute-start(bf16[4,256,128]{2,1,0:T(8,128)(2,1)S(1)} %get-tuple-element.10), channel_id=1, source_target_pairs={{0,4},{1,5},{2,6},{3,7},{4,8},{5,9},{6,10},{7,11},{8,12},{9,13},{1... | collective-permute-start | bytes 786440 | tf_op jit(solution)/shard_map/ppermute | solution.py:37
  144.5 13.4 %collective-permute-start.21 = (bf16[4,256,128]{2,1,0:T(8,128)(2,1)S(1)}, bf16[4,256,128]{2,1,0:T(8,128)(2,1)S(1)}, u32[]{:S(2)}, u32[]{:S(2)}) collective-permute-start(bf16[4,256,128]{2,1,0:T(8,128)(2,1)S(1)} %get-tuple-element.11), channel_id=1, source_target_pairs={{0,8},{1,9},{2,10},{3,11},{4,12},{5,13},{6,14},{7,15},{8,0},{9,1},... | collective-permute-start | bytes 786440 | tf_op jit(solution)/shard_map/ppermute | solution.py:37
  146.5 12.1 %collective-permute-start.20 = (bf16[4,256,128]{2,1,0:T(8,128)(2,1)S(1)}, bf16[4,256,128]{2,1,0:T(8,128)(2,1)S(1)}, u32[]{:S(2)}, u32[]{:S(2)}) collective-permute-start(bf16[4,256,128]{2,1,0:T(8,128)(2,1)S(1)} %get-tuple-element.12), channel_id=1, source_target_pairs={{0,12},{1,13},{2,14},{3,15},{4,0},{5,1},{6,2},{7,3},{8,4},{9,5},{1... | collective-permute-start | bytes 786440 | tf_op jit(solution)/shard_map/ppermute | solution.py:37
  158.7 6.2 %collective-permute-start.22 = (bf16[256,128]{1,0:T(8,128)(2,1)S(1)}, bf16[256,128]{1,0:T(8,128)(2,1)S(1)}, u32[]{:S(2)}, u32[]{:S(2)}) collective-permute-start(bf16[256,128]{1,0:T(8,128)(2,1)S(1)} %get-tuple-element.17), channel_id=1, source_target_pairs={{0,1},{1,2},{2,3},{3,0},{4,5},{5,6},{6,7},{7,4},{8,9},{9,10},{10,1... | collective-permute-start | bytes 196616 | tf_op jit(solution)/shard_map/ppermute | solution.py:37
  158.8 6.2 %collective-permute-start.24 = (bf16[256,128]{1,0:T(8,128)(2,1)S(1)}, bf16[256,128]{1,0:T(8,128)(2,1)S(1)}, u32[]{:S(2)}, u32[]{:S(2)}) collective-permute-start(bf16[256,128]{1,0:T(8,128)(2,1)S(1)} %get-tuple-element.18), channel_id=1, source_target_pairs={{0,2},{1,3},{2,0},{3,1},{4,6},{5,7},{6,4},{7,5},{8,10},{9,11},{10,... | collective-permute-start | bytes 196616 | tf_op jit(solution)/shard_map/ppermute | solution.py:37
  160.2 5.6 %collective-permute-start.23 = (bf16[256,128]{1,0:T(8,128)(2,1)S(1)}, bf16[256,128]{1,0:T(8,128)(2,1)S(1)}, u32[]{:S(2)}, u32[]{:S(2)}) collective-permute-start(bf16[256,128]{1,0:T(8,128)(2,1)S(1)} %get-tuple-element.19), channel_id=1, source_target_pairs={{0,3},{1,0},{2,1},{3,2},{4,7},{5,4},{6,5},{7,6},{8,11},{9,8},{10,9... | collective-permute-start | bytes 196616 | tf_op jit(solution)/shard_map/ppermute | solution.py:37
  181.0 1.2 collective-permute-start.25
  182.2 5.1 %collective-permute-start.26 = (f32[4,128]{1,0:T(4,128)S(1)}, f32[4,128]{1,0:T(4,128)S(1)}, u32[]{:S(2)}, u32[]{:S(2)}) collective-permute-start(f32[4,128]{1,0:T(4,128)S(1)} %add.221), channel_id=1, source_target_pairs={{0,64},{32,96},{64,0},{96,32},{1,65},{33,97},{65,1},{97,33},{2,66}... | collective-permute-start | bytes 6152 | tf_op jit(solution)/shard_map/ppermute | solution.py:46
  (3 other events, 2.5 us)

commit v11 on v10

--- a/solution.py
+++ b/solution.py
@@ -166,62 +166,65 @@
     )(jnp.reshape(core_id, (1,)).astype(jnp.int32), spots, counts, tile_stack, buffer)
 
 
-def spread_kernel(core_ref, where_ref, count_ref, tiles_ref, grad_ref, *rest):
-    if len(rest) == 5:
-        start_ref, out_ref, total_ref, wide_ref, terms_ref = rest
-    else:
-        start_ref = None
-        out_ref, total_ref, wide_ref, terms_ref = rest
-    row = pl.program_id(0)
-    half_id = pl.program_id(1)
-    tile_rows = pl.num_programs(0)
-    halves = pl.num_programs(1)
-    slot_count, tile_size, _ = tiles_ref.shape
-    base = (half_id * 2 + core_ref[0]) * tile_rows + row
-    live = count_ref[base]
-
-    @pl.when((row == 0) & (half_id == 0))
-    def _():
-        if start_ref is None:
+def spread_pair(core_id, spots, counts, tile_stack, sibling_tiles, grads, buffer_tiles):
+    blocks, tile_rows, slot_count, tile_size, _ = tile_stack.shape
+    hidden_width = grads.shape[2]
+    halves = blocks // 2
+    last = halves - 1
+
+    def own_map(s, r, h, c, w, n):
+        return (
+            jnp.where(s == 0, h * 2 + c[0], last * 2 + c[0]),
+            jnp.where(s == 0, r, tile_rows - 1),
+            0, 0, 0,
+        )
+
+    def sibling_map(s, r, h, c, w, n):
+        return (jnp.where(s == 1, h * 2 + c[0], c[0]), jnp.where(s == 1, r, 0), 0, 0, 0)
+
+    def kernel(core_ref, where_ref, count_ref, own_ref, other_ref, grad_ref, out_ref, total_ref,
+               wide_ref, terms_ref):
+        source = pl.program_id(0)
+        row = pl.program_id(1)
+        half_id = pl.program_id(2)
+        base = (half_id * 2 + core_ref[0]) * tile_rows + row
+        live = count_ref[source * blocks * tile_rows + base]
+
+        @pl.when((source == 0) & (row == 0) & (half_id == 0))
+        def _():
             total_ref[...] = jnp.zeros(total_ref.shape, jnp.float32)
-        else:
-            total_ref[...] = start_ref[...].astype(jnp.float32)
-
-    for slot in range(slot_count):
-        wide_ref[:, slot * tile_size:(slot + 1) * tile_size] = tiles_ref[slot]
-    terms_ref[...] = jnp.dot(grad_ref[...], wide_ref[...], preferred_element_type=jnp.float32)
-    for slot in range(slot_count):
-        spot = where_ref[base * slot_count + slot]
-
-        @pl.when(slot < live)
+
+        def fill(tiles_ref):
+            for slot in range(slot_count):
+                wide_ref[:, slot * tile_size:(slot + 1) * tile_size] = tiles_ref[slot]
+
+        pl.when(source == 0)(lambda: fill(own_ref))
+        pl.when(source == 1)(lambda: fill(other_ref))
+        terms_ref[...] = jnp.dot(grad_ref[...], wide_ref[...], preferred_element_type=jnp.float32)
+        for slot in range(slot_count):
+            spot = where_ref[(source * blocks * tile_rows + base) * slot_count + slot]
+
+            @pl.when(slot < live)
+            def _():
+                total_ref[spot] += terms_ref[:, slot * tile_size:(slot + 1) * tile_size]
+
+        @pl.when((source == 1) & (row == tile_rows - 1) & (half_id == halves - 1))
         def _():
-            total_ref[spot] += terms_ref[:, slot * tile_size:(slot + 1) * tile_size]
-
-    @pl.when((row == tile_rows - 1) & (half_id == halves - 1))
-    def _():
-        out_ref[...] = total_ref[...].astype(out_ref.dtype)
-
-
-def spread_pair(
-    core_id, spots, counts, tile_stack, grad_turned, buffer_tiles, out_type, start=None,
-    block_step=2, core_step=1,
-):
-    _, tile_rows, slot_count, tile_size, _ = tile_stack.shape
-    blocks = lax.axis_size("blk")
-    hidden_width = grad_turned.shape[1]
+            out_ref[...] = total_ref[...]
+
+    tile_spec = (None, None, slot_count, tile_size, tile_size)
     grid_spec = pltpu.PrefetchScalarGridSpec(
         num_scalar_prefetch=3,
-        grid=(tile_rows, blocks // 2),
+        grid=(2, tile_rows, halves),
         in_specs=[
+            pl.BlockSpec(tile_spec, own_map),
+            pl.BlockSpec(tile_spec, sibling_map),
             pl.BlockSpec(
-                (None, None, slot_count, tile_size, tile_size),
-                lambda r, h, c, w, n: (h * block_step + c[0] * core_step, r, 0, 0, 0),
+                (None, None, hidden_width, tile_size), lambda s, r, h, c, w, n: (s, r, 0, 0)
             ),
-            pl.BlockSpec((None, hidden_width, tile_size), lambda r, h, c, w, n: (r, 0, 0)),
-        ]
-        + ([] if start is None else [pl.BlockSpec(start.shape, lambda r, h, c, w, n: (0, 0, 0))]),
+        ],
         out_specs=pl.BlockSpec(
-            (buffer_tiles, hidden_width, tile_size), lambda r, h, c, w, n: (0, 0, 0)
+            (buffer_tiles, hidden_width, tile_size), lambda s, r, h, c, w, n: (0, 0, 0)
         ),
         scratch_shapes=[
             pltpu.VMEM((buffer_tiles, hidden_width, tile_size), jnp.float32),
@@ -230,17 +233,19 @@
         ],
     )
     return pl.pallas_call(
-        spread_kernel,
+        kernel,
         grid_spec=grid_spec,
-        out_shape=jax.ShapeDtypeStruct((buffer_tiles, hidden_width, tile_size), out_type),
-        compiler_params=pltpu.CompilerParams(dimension_semantics=("arbitrary", "arbitrary")),
+        out_shape=jax.ShapeDtypeStruct((buffer_tiles, hidden_width, tile_size), jnp.float32),
+        compiler_params=pltpu.CompilerParams(
+            dimension_semantics=("arbitrary", "arbitrary", "arbitrary")
+        ),
     )(
         jnp.reshape(core_id, (1,)).astype(jnp.int32),
         spots,
         counts,
         tile_stack,
-        grad_turned,
-        *([] if start is None else [start]),
+        sibling_tiles,
+        grads,
     )
 
 
@@ -304,11 +309,13 @@
 
     sibling_grad = sibling(grad_turned)
     total = spread_pair(
-        core_id, spots, tile_count, tile_stack, grad_turned, buffer_tiles, jnp.float32
-    )
-    total = spread_pair(
-        core_id, sibling_spots, sibling_count, sibling_tiles, sibling_grad, buffer_tiles,
-        jnp.float32, total,
+        core_id,
+        jnp.concatenate([spots, sibling_spots]),
+        jnp.concatenate([tile_count, sibling_count]),
+        tile_stack,
+        sibling_tiles,
+        jnp.stack([grad_turned, sibling_grad]),
+        buffer_tiles,
     )
     total = reduce_phase(
         total.reshape(RING, RING, RING, rows_own, hidden_width), 2, jnp.bfloat16

time: 189 us -> 187 us (0.989)
  Pallas kernels: 37.2 us -> 30.5 us
  waiting for transfers between devices: 73.4 us -> 79.8 us
    pallas_call x2 -> x1, Pallas kernels: 21.9 us -> 15.2 us  [spread_pair(): pl.pallas_call(kernel, grid_spec=grid_spec, out_shape=jax.ShapeDtypeStruc...]
    ppermute x5, waiting for transfers between devices: 0.01 us -> 5.35 us  [sibling(): lax.ppermute(block, 'blk', [(i, i ^ 1) for i in range(lax.axis_size('blk'...]
  transfers between devices with their start and end apart: 27 -> 27, of which waited for: 18 -> 21; matrix products, arithmetic and copies ran while one was open for 6% -> 6% of each run, Pallas kernels for 13% -> 8%
where the time goes in v11:
time: 187 us
  waiting for transfers between devices  79.8 us (43%)
  blocking collectives  32.2 us (17%)
  Pallas kernels  30.5 us (16%)
  starting transfers between devices  28.1 us (15%)
  other arithmetic  8.37 us (4%)
  local copies, waits for them, and re-layouts  6.41 us (3%)
    ppermute x20, waiting for transfers between devices, ring_shift(): return lax.ppermute(block, BOTH, route)  69.6 us
    ppermute x20, starting transfers between devices, ring_shift(): return lax.ppermute(block, BOTH, route)  26.2 us
    all_to_all x1, blocking collectives, body(): lax.all_to_all(features_t, 'feat', split_axis=1, concat_axis=0, tiled=True)  17.6 us
    pallas_call x2, Pallas kernels, aggregate_pair(): pl.pallas_call(aggregate_kernel, grid_spec=grid_spec, out_shape=jax.Shape...  15.3 us
    pallas_call x1, Pallas kernels, spread_pair(): pl.pallas_call(kernel, grid_spec=grid_spec, out_shape=jax.ShapeDtypeStruc...  15.2 us
    all_to_all x1, blocking collectives, body(): lax.all_to_all(outgoing, 'feat', split_axis=0, concat_axis=0, tiled=True)  14.6 us
    ppermute x5, waiting for transfers between devices, sibling(): lax.ppermute(block, 'blk', [(i, i ^ 1) for i in range(lax.axis_size('blk'...  5.35 us
    slice x2, local copies, waits for them, and re-layouts, term(): return total[k]  5.03 us
  transfers between devices with their start and end apart: 27, of which 21 were waited for; matrix products, arithmetic and copies ran while one was open for 6% of the time, Pallas kernels for 8%

profile of v11, /device:TPU:0, one launch (start us, length us, event | category | flops | bytes accessed | tf_op | source)
XLA Modules:
  0.0 186.8 jit_solution(12377215066501897875)
XLA Ops:
  0.7 17.6 %all_to_all.24 = bf16[4,32,256]{2,0,1:T(4,128)(2,1)S(1)} all-to-all(bf16[4,32,256]{2,0,1:T(4,128)(2,1)} %bitcast.128), channel_id=1, replica_groups=mesh['blk'=4,'feat'=32] {'feat'}, dimensions={1} | all-to-all | bytes 131072 | tf_op jit(solution)/shard_map/all_to_all | solution.py:287
  19.2 2.3 %collective-permute-start.1 = (bf16[256,128]{1,0:T(8,128)(2,1)S(1)}, bf16[256,128]{1,0:T(8,128)(2,1)S(1)}, u32[]{:S(2)}, u32[]{:S(2)}) collective-permute-start(bf16[256,128]{1,0:T(8,128)(2,1)S(1)} %convolution_convert_fusion.1), channel_id=1, source_target_pairs={{0,2},{1,3},{2,0},{3,1},{4,6},{5,7},{6,4},{7,5},{8,10},{9,11},{10,... | collective-permute-start | bytes 196616 | tf_op jit(solution)/shard_map/ppermute | solution.py:37
  22.6 1.5 collective-permute-done.2
  25.8 1.4 collective-permute-start.4
  27.2 1.9 %collective-permute-start.3 = (bf16[4,256,128]{2,1,0:T(8,128)(2,1)S(1)}, bf16[4,256,128]{2,1,0:T(8,128)(2,1)S(1)}, u32[]{:S(2)}, u32[]{:S(2)}) collective-permute-start(bf16[4,256,128]{2,1,0:T(8,128)(2,1)S(1)} %get-tuple-element.21), channel_id=1, source_target_pairs={{0,12},{1,13},{2,14},{3,15},{4,0},{5,1},{6,2},{7,3},{8,4},{9,5},{1... | collective-permute-start | bytes 786440 | tf_op jit(solution)/shard_map/ppermute | solution.py:37
  29.2 7.4 %collective-permute-done.4 = bf16[4,256,128]{2,1,0:T(8,128)(2,1)S(1)} collective-permute-done((bf16[4,256,128]{2,1,0:T(8,128)(2,1)S(1)}, bf16[4,256,128]{2,1,0:T(8,128)(2,1)S(1)}, u32[]{:S(2)}, u32[]{:S(2)}) %collective-permute-start.4) | collective-permute-done | bytes 262176 | tf_op jit(solution)/shard_map/ppermute | solution.py:37
  36.6 1.4 collective-permute-done.3
  38.0 1.7 collective-permute-done.5
  39.9 3.0 %collective-permute-start.6 = (bf16[4,4,256,128]{3,2,1,0:T(8,128)(2,1)S(1)}, bf16[4,4,256,128]{3,2,1,0:T(8,128)(2,1)S(1)}, u32[]{:S(2)}, u32[]{:S(2)}) collective-permute-start(bf16[4,4,256,128]{3,2,1,0:T(8,128)(2,1)S(1)} %get-tuple-element.16), channel_id=1, source_target_pairs={{0,80},{1,81},{2,82},{3,83},{4,84},{5,85},{6,86},{7,87},{8,88},{9,... | collective-permute-start | bytes 3145736 | tf_op jit(solution)/shard_map/ppermute | solution.py:37
  42.9 12.3 %collective-permute-done.6 = bf16[4,4,256,128]{3,2,1,0:T(8,128)(2,1)S(1)} collective-permute-done((bf16[4,4,256,128]{3,2,1,0:T(8,128)(2,1)S(1)}, bf16[4,4,256,128]{3,2,1,0:T(8,128)(2,1)S(1)}, u32[]{:S(2)}, u32[]{:S(2)}) %collective-permute-start.6) | collective-permute-done | bytes 1048608 | tf_op jit(solution)/shard_map/ppermute | solution.py:37
  55.3 3.8 %collective-permute-start.9 = (bf16[4,4,128,128]{3,2,1,0:T(8,128)(2,1)S(1)}, bf16[4,4,128,128]{3,2,1,0:T(8,128)(2,1)S(1)}, u32[]{:S(2)}, u32[]{:S(2)}) collective-permute-start(bf16[4,4,128,128]{3,2,1,0:T(8,128)(2,1)S(1)} %slice.104), channel_id=1, source_target_pairs={{0,80},{1,81},{2,82},{3,83},{4,84},{5,85},{6,86},{7,87},{8,88},{9,... | collective-permute-start | bytes 1572872 | tf_op jit(solution)/shard_map/ppermute | solution.py:37
  59.2 6.6 %collective-permute-done.9 = bf16[4,4,128,128]{3,2,1,0:T(8,128)(2,1)S(1)} collective-permute-done((bf16[4,4,128,128]{3,2,1,0:T(8,128)(2,1)S(1)}, bf16[4,4,128,128]{3,2,1,0:T(8,128)(2,1)S(1)}, u32[]{:S(2)}, u32[]{:S(2)}) %collective-permute-start.9) | collective-permute-done | bytes 524320 | tf_op jit(solution)/shard_map/ppermute | solution.py:37
  65.7 3.8 %collective-permute-done.8 = bf16[4,4,128,128]{3,2,1,0:T(8,128)(2,1)S(1)} collective-permute-done((bf16[4,4,128,128]{3,2,1,0:T(8,128)(2,1)S(1)}, bf16[4,4,128,128]{3,2,1,0:T(8,128)(2,1)S(1)}, u32[]{:S(2)}, u32[]{:S(2)}) %collective-permute-start.8) | collective-permute-done | bytes 524320 | tf_op jit(solution)/shard_map/ppermute | solution.py:37
  69.6 2.2 %pad_maximum_fusion = bf16[4,4,4,256,128]{4,3,2,1,0:T(8,128)(2,1)} fusion(bf16[1,4,4,256,128]{4,3,2,1,0:T(8,128)(2,1)S(1)} %bitcast.112, bf16[1,4,4,256,128]{4,3,2,1,0:T(8,128)(2,1)S(1)} %maximum_bitcast_fusion, bf16[1,4,4,256,128]{4,3,2,1,0:T(8,128)(2,1)S(1)} %bitcast.111, bf16[1,4,4,256,128]{4,3,2,1,0:T(8,128)(2,1)S(1)} %get-tuple-element.15), kind=kLoop, calls=%fused_computation | loop fusion | flops 6291456 | bytes 8388608 | tf_op jit(solution)/shard_map/stack | solution.py:56
  73.1 4.7 %collective-permute-done.12 = s32[8]{0:T(128)S(1)} collective-permute-done((s32[8]{0:T(128)S(1)}, s32[8]{0:T(128)S(1)}, u32[]{:S(2)}, u32[]{:S(2)}) %collective-permute-start.12) | collective-permute-done | bytes 64 | tf_op jit(solution)/shard_map/ppermute | solution.py:41
  78.7 7.6 %shard_map.85 = f32[2,128,128]{2,1,0:T(8,128)} custom-call(s32[1]{0:T(128)} %bitcast.core_ref, s32[256]{0:T(256)} %fusion.21.where_ref, s32[8]{0:T(128)} %count_ref.3, bf16[4,2,32,128,128]{4,3,2,1,0:T(8,128)(2,1)} %bitcast.102, bf16[128,128,128]{2,1,0:T(8,128)(2,1)} %bitcast.16.proj_ref), custom_call_target="tpu_custom_call" | custom-call | tf_op jit(solution)/shard_map/pallas_call | solution.py:161
  86.3 7.7 %shard_map.86 = f32[2,128,128]{2,1,0:T(8,128)} custom-call(s32[1]{0:T(128)} %bitcast.17.core_ref, s32[256]{0:T(256)} %fusion.21.where_ref, s32[8]{0:T(128)} %count_ref.3, bf16[4,2,32,128,128]{4,3,2,1,0:T(8,128)(2,1)} %bitcast.103, bf16[128,128,128]{2,1,0:T(8,128)(2,1)} %collective-permute-done.10.proj_ref), custom_call_target="tpu_custom_call" | custom-call | tf_op jit(solution)/shard_map/pallas_call | solution.py:161
  97.8 15.2 %shard_map.87 = f32[128,128,128]{2,1,0:T(8,128)} custom-call(s32[1]{0:T(128)} %bitcast.core_ref, s32[512]{0:T(512)} %pad_add_fusion.where_ref, s32[16]{0:T(128)} %pad_add_fusion.1.count_ref, bf16[4,2,32,128,128]{4,3,2,1,0:T(8,128)(2,1)} %bitcast.104, bf16[4,2,32,128,128]{4,3,2,1,0:T(8,128)(2,1)} %collective-permute-done.13.other_ref, ...), custom_call_target="tpu_custom_call" | custom-call | tf_op jit(solution)/shard_map/pallas_call | solution.py:235
  113.0 1.7 slice.158
  114.9 2.0 %collective-permute-start.15 = (bf16[4,4,128,128]{3,2,1,0:T(8,128)(2,1)S(1)}, bf16[4,4,128,128]{3,2,1,0:T(8,128)(2,1)S(1)}, u32[]{:S(2)}, u32[]{:S(2)}) collective-permute-start(bf16[4,4,128,128]{3,2,1,0:T(8,128)(2,1)S(1)} %get-tuple-element.13), channel_id=1, source_target_pairs={{0,16},{1,17},{2,18},{3,19},{4,20},{5,21},{6,22},{7,23},{8,24},{9,... | collective-permute-start | bytes 1572872 | tf_op jit(solution)/shard_map/ppermute | solution.py:37
  116.9 3.3 %fusion.39 = (f32[32,128,128]{2,1,0:T(8,128)S(1)}, f32[32,128,128]{2,1,0:T(8,128)S(1)}, f32[32,128,128]{2,1,0:T(8,128)S(1)}) fusion(f32[128,128,128]{2,1,0:T(8,128)} %shard_map.87), kind=kLoop, calls=%fused_computation.142 | loop fusion | bytes 12582912 | tf_op jit(solution)/shard_map/slice | solution.py:83
  120.4 3.7 %collective-permute-done.17 = bf16[4,4,128,128]{3,2,1,0:T(8,128)(2,1)S(1)} collective-permute-done((bf16[4,4,128,128]{3,2,1,0:T(8,128)(2,1)S(1)}, bf16[4,4,128,128]{3,2,1,0:T(8,128)(2,1)S(1)}, u32[]{:S(2)}, u32[]{:S(2)}) %collective-permute-start.17) | collective-permute-done | bytes 524320 | tf_op jit(solution)/shard_map/ppermute | solution.py:37
  126.7 12.5 %collective-permute-done.18 = bf16[4,4,256,128]{3,2,1,0:T(8,128)(2,1)S(1)} collective-permute-done((bf16[4,4,256,128]{3,2,1,0:T(8,128)(2,1)S(1)}, bf16[4,4,256,128]{3,2,1,0:T(8,128)(2,1)S(1)}, u32[]{:S(2)}, u32[]{:S(2)}) %collective-permute-start.18) | collective-permute-done | bytes 1048608 | tf_op jit(solution)/shard_map/ppermute | solution.py:37
  139.2 2.7 %collective-permute-done.16 = bf16[4,4,256,128]{3,2,1,0:T(8,128)(2,1)S(1)} collective-permute-done((bf16[4,4,256,128]{3,2,1,0:T(8,128)(2,1)S(1)}, bf16[4,4,256,128]{3,2,1,0:T(8,128)(2,1)S(1)}, u32[]{:S(2)}, u32[]{:S(2)}) %collective-permute-start.16) | collective-permute-done | bytes 1048608 | tf_op jit(solution)/shard_map/ppermute | solution.py:37
  142.7 2.4 %collective-permute-start.21 = (bf16[4,256,128]{2,1,0:T(8,128)(2,1)S(1)}, bf16[4,256,128]{2,1,0:T(8,128)(2,1)S(1)}, u32[]{:S(2)}, u32[]{:S(2)}) collective-permute-start(bf16[4,256,128]{2,1,0:T(8,128)(2,1)S(1)} %get-tuple-element.11), channel_id=1, source_target_pairs={{0,8},{1,9},{2,10},{3,11},{4,12},{5,13},{6,14},{7,15},{8,0},{9,1},... | collective-permute-start | bytes 786440 | tf_op jit(solution)/shard_map/ppermute | solution.py:37
  145.1 1.7 collective-permute-start.20
  146.8 10.0 %collective-permute-done.19 = bf16[4,256,128]{2,1,0:T(8,128)(2,1)S(1)} collective-permute-done((bf16[4,256,128]{2,1,0:T(8,128)(2,1)S(1)}, bf16[4,256,128]{2,1,0:T(8,128)(2,1)S(1)}, u32[]{:S(2)}, u32[]{:S(2)}) %collective-permute-start.19) | collective-permute-done | bytes 262176 | tf_op jit(solution)/shard_map/ppermute | solution.py:37
  157.6 1.4 collective-permute-start.24
  159.1 1.8 collective-permute-start.23
  160.9 2.9 %collective-permute-done.22 = bf16[256,128]{1,0:T(8,128)(2,1)S(1)} collective-permute-done((bf16[256,128]{1,0:T(8,128)(2,1)S(1)}, bf16[256,128]{1,0:T(8,128)(2,1)S(1)}, u32[]{:S(2)}, u32[]{:S(2)}) %collective-permute-start.22) | collective-permute-done | bytes 65568 | tf_op jit(solution)/shard_map/ppermute | solution.py:37
  165.3 14.6 %all_to_all.25 = f32[32,4,384]{2,1,0:T(4,128)S(1)} all-to-all(f32[32,4,384]{2,1,0:T(4,128)S(1)} %pad_maximum_fusion.5), channel_id=1, replica_groups=mesh['blk'=4,'feat'=32] {'feat'}, dimensions={0} | all-to-all | bytes 393216 | tf_op jit(solution)/shard_map/all_to_all | solution.py:345
  182.5 3.7 %collective-permute-done.26 = f32[4,128]{1,0:T(4,128)S(1)} collective-permute-done((f32[4,128]{1,0:T(4,128)S(1)}, f32[4,128]{1,0:T(4,128)S(1)}, u32[]{:S(2)}, u32[]{:S(2)}) %collective-permute-start.26) | collective-permute-done | bytes 2080 | tf_op jit(solution)/shard_map/ppermute | solution.py:46
  (78 shorter events, 19.4 us)
Async XLA Ops:
  0.6 17.7 %copy-start = (bf16[128,128]{1,0:T(8,128)(2,1)S(1)}, bf16[128,128]{1,0:T(8,128)(2,1)}, u32[]{:S(2)}) copy-start(bf16[128,128]{1,0:T(8,128)(2,1)} %param.7) | copy-start | bytes 98308
  0.6 97.1 %collective-permute-start.13 = (bf16[4,2,32,128,128]{4,3,2,1,0:T(8,128)(2,1)}, bf16[4,2,32,128,128]{4,3,2,1,0:T(8,128)(2,1)}, u32[]{:S(2)}, u32[]{:S(2)}) collective-permute-start(bf16[4,2,32,128,128]{4,3,2,1,0:T(8,128)(2,1)} %bitcast.101), channel_id=1, source_target_pairs={{0,32},{32,0},{64,96},{96,64},{1,33},{33,1},{65,97},{97,65},{2,34}... | collective-permute-start | bytes 25165832 | tf_op jit(solution)/shard_map/ppermute | solution.py:41
  18.6 5.5 %collective-permute-start.2 = (bf16[256,128]{1,0:T(8,128)(2,1)S(1)}, bf16[256,128]{1,0:T(8,128)(2,1)S(1)}, u32[]{:S(2)}, u32[]{:S(2)}) collective-permute-start(bf16[256,128]{1,0:T(8,128)(2,1)S(1)} %convolution_convert_fusion.1), channel_id=1, source_target_pairs={{0,1},{1,2},{2,3},{3,0},{4,5},{5,6},{6,7},{7,4},{8,9},{9,10},{10,1... | collective-permute-start | bytes 196616 | tf_op jit(solution)/shard_map/ppermute | solution.py:37
  19.2 5.8 %collective-permute-start.1 = (bf16[256,128]{1,0:T(8,128)(2,1)S(1)}, bf16[256,128]{1,0:T(8,128)(2,1)S(1)}, u32[]{:S(2)}, u32[]{:S(2)}) collective-permute-start(bf16[256,128]{1,0:T(8,128)(2,1)S(1)} %convolution_convert_fusion.1), channel_id=1, source_target_pairs={{0,2},{1,3},{2,0},{3,1},{4,6},{5,7},{6,4},{7,5},{8,10},{9,11},{10,... | collective-permute-start | bytes 196616 | tf_op jit(solution)/shard_map/ppermute | solution.py:37
  21.5 4.3 %collective-permute-start = (bf16[256,128]{1,0:T(8,128)(2,1)S(1)}, bf16[256,128]{1,0:T(8,128)(2,1)S(1)}, u32[]{:S(2)}, u32[]{:S(2)}) collective-permute-start(bf16[256,128]{1,0:T(8,128)(2,1)S(1)} %convolution_convert_fusion.1), channel_id=1, source_target_pairs={{0,3},{1,0},{2,1},{3,2},{4,7},{5,4},{6,5},{7,6},{8,11},{9,8},{10,9... | collective-permute-start | bytes 196616 | tf_op jit(solution)/shard_map/ppermute | solution.py:37
  25.8 10.8 %collective-permute-start.4 = (bf16[4,256,128]{2,1,0:T(8,128)(2,1)S(1)}, bf16[4,256,128]{2,1,0:T(8,128)(2,1)S(1)}, u32[]{:S(2)}, u32[]{:S(2)}) collective-permute-start(bf16[4,256,128]{2,1,0:T(8,128)(2,1)S(1)} %get-tuple-element.21), channel_id=1, source_target_pairs={{0,8},{1,9},{2,10},{3,11},{4,12},{5,13},{6,14},{7,15},{8,0},{9,1},... | collective-permute-start | bytes 786440 | tf_op jit(solution)/shard_map/ppermute | solution.py:37
  27.2 10.8 %collective-permute-start.3 = (bf16[4,256,128]{2,1,0:T(8,128)(2,1)S(1)}, bf16[4,256,128]{2,1,0:T(8,128)(2,1)S(1)}, u32[]{:S(2)}, u32[]{:S(2)}) collective-permute-start(bf16[4,256,128]{2,1,0:T(8,128)(2,1)S(1)} %get-tuple-element.21), channel_id=1, source_target_pairs={{0,12},{1,13},{2,14},{3,15},{4,0},{5,1},{6,2},{7,3},{8,4},{9,5},{1... | collective-permute-start | bytes 786440 | tf_op jit(solution)/shard_map/ppermute | solution.py:37
  29.1 10.6 %collective-permute-start.5 = (bf16[4,256,128]{2,1,0:T(8,128)(2,1)S(1)}, bf16[4,256,128]{2,1,0:T(8,128)(2,1)S(1)}, u32[]{:S(2)}, u32[]{:S(2)}) collective-permute-start(bf16[4,256,128]{2,1,0:T(8,128)(2,1)S(1)} %get-tuple-element.21), channel_id=1, source_target_pairs={{0,4},{1,5},{2,6},{3,7},{4,8},{5,9},{6,10},{7,11},{8,12},{9,13},{1... | collective-permute-start | bytes 786440 | tf_op jit(solution)/shard_map/ppermute | solution.py:37
  39.9 15.3 %collective-permute-start.6 = (bf16[4,4,256,128]{3,2,1,0:T(8,128)(2,1)S(1)}, bf16[4,4,256,128]{3,2,1,0:T(8,128)(2,1)S(1)}, u32[]{:S(2)}, u32[]{:S(2)}) collective-permute-start(bf16[4,4,256,128]{3,2,1,0:T(8,128)(2,1)S(1)} %get-tuple-element.16), channel_id=1, source_target_pairs={{0,80},{1,81},{2,82},{3,83},{4,84},{5,85},{6,86},{7,87},{8,88},{9,... | collective-permute-start | bytes 3145736 | tf_op jit(solution)/shard_map/ppermute | solution.py:37
  42.9 16.1 %collective-permute-start.7 = (bf16[4,4,256,128]{3,2,1,0:T(8,128)(2,1)S(1)}, bf16[4,4,256,128]{3,2,1,0:T(8,128)(2,1)S(1)}, u32[]{:S(2)}, u32[]{:S(2)}) collective-permute-start(bf16[4,4,256,128]{3,2,1,0:T(8,128)(2,1)S(1)} %get-tuple-element.16), channel_id=1, source_target_pairs={{0,16},{1,17},{2,18},{3,19},{4,20},{5,21},{6,22},{7,23},{8,24},{9,... | collective-permute-start | bytes 3145736 | tf_op jit(solution)/shard_map/ppermute | solution.py:37
  55.3 10.5 %collective-permute-start.9 = (bf16[4,4,128,128]{3,2,1,0:T(8,128)(2,1)S(1)}, bf16[4,4,128,128]{3,2,1,0:T(8,128)(2,1)S(1)}, u32[]{:S(2)}, u32[]{:S(2)}) collective-permute-start(bf16[4,4,128,128]{3,2,1,0:T(8,128)(2,1)S(1)} %slice.104), channel_id=1, source_target_pairs={{0,80},{1,81},{2,82},{3,83},{4,84},{5,85},{6,86},{7,87},{8,88},{9,... | collective-permute-start | bytes 1572872 | tf_op jit(solution)/shard_map/ppermute | solution.py:37
  59.1 10.5 %collective-permute-start.8 = (bf16[4,4,128,128]{3,2,1,0:T(8,128)(2,1)S(1)}, bf16[4,4,128,128]{3,2,1,0:T(8,128)(2,1)S(1)}, u32[]{:S(2)}, u32[]{:S(2)}) collective-permute-start(bf16[4,4,128,128]{3,2,1,0:T(8,128)(2,1)S(1)} %slice.103), channel_id=1, source_target_pairs={{0,16},{1,17},{2,18},{3,19},{4,20},{5,21},{6,22},{7,23},{8,24},{9,... | collective-permute-start | bytes 1572872 | tf_op jit(solution)/shard_map/ppermute | solution.py:37
  69.6 2.8 %copy-start.5 = (s32[256]{0:T(256)S(1)}, s32[256]{0:T(256)}, u32[]{:S(2)}) copy-start(s32[256]{0:T(256)} %param.9) | copy-start | bytes 3076
  71.9 14.4 %collective-permute-start.10 = (bf16[128,128,128]{2,1,0:T(8,128)(2,1)}, bf16[128,128,128]{2,1,0:T(8,128)(2,1)}, u32[]{:S(2)}, u32[]{:S(2)}) collective-permute-start(bf16[128,128,128]{2,1,0:T(8,128)(2,1)} %bitcast.16.proj_ref), channel_id=1, source_target_pairs={{0,32},{32,0},{64,96},{96,64},{1,33},{33,1},{65,97},{97,65},{2,34}... | collective-permute-start | bytes 12582920 | tf_op jit(solution)/shard_map/ppermute | solution.py:41
  71.9 5.9 %collective-permute-start.12 = (s32[8]{0:T(128)S(1)}, s32[8]{0:T(128)S(1)}, u32[]{:S(2)}, u32[]{:S(2)}) collective-permute-start(s32[8]{0:T(128)S(1)} %copy-done.4), channel_id=1, source_target_pairs={{0,32},{32,0},{64,96},{96,64},{1,33},{33,1},{65,97},{97,65},{2,34}... | collective-permute-start | bytes 104 | tf_op jit(solution)/shard_map/ppermute | solution.py:41
  72.4 6.3 %collective-permute-start.11 = (s32[256]{0:T(256)S(1)}, s32[256]{0:T(256)S(1)}, u32[]{:S(2)}, u32[]{:S(2)}) collective-permute-start(s32[256]{0:T(256)S(1)} %copy-done.5), channel_id=1, source_target_pairs={{0,32},{32,0},{64,96},{96,64},{1,33},{33,1},{65,97},{97,65},{2,34}... | collective-permute-start | bytes 3080 | tf_op jit(solution)/shard_map/ppermute | solution.py:41
  86.3 7.7 %copy-start.1 = (f32[2,128,128]{2,1,0:T(8,128)S(1)}, f32[2,128,128]{2,1,0:T(8,128)}, u32[]{:S(2)}) copy-start(f32[2,128,128]{2,1,0:T(8,128)} %shard_map.85) | copy-start | bytes 393220
  86.3 8.7 %copy-start.2 = (bf16[256,128]{1,0:T(8,128)(2,1)S(1)}, bf16[256,128]{1,0:T(8,128)(2,1)}, u32[]{:S(2)}) copy-start(bf16[256,128]{1,0:T(8,128)(2,1)} %param.11) | copy-start | bytes 196612
  86.3 9.9 %copy-start.3 = (s32[256]{0:T(256)S(1)}, s32[256]{0:T(256)}, u32[]{:S(2)}) copy-start(s32[256]{0:T(256)} %fusion.21.where_ref) | copy-start | bytes 3076
  95.8 1.3 collective-permute-start.14
  114.8 9.2 %collective-permute-start.17 = (bf16[4,4,128,128]{3,2,1,0:T(8,128)(2,1)S(1)}, bf16[4,4,128,128]{3,2,1,0:T(8,128)(2,1)S(1)}, u32[]{:S(2)}, u32[]{:S(2)}) collective-permute-start(bf16[4,4,128,128]{3,2,1,0:T(8,128)(2,1)S(1)} %get-tuple-element.14), channel_id=1, source_target_pairs={{0,80},{1,81},{2,82},{3,83},{4,84},{5,85},{6,86},{7,87},{8,88},{9,... | collective-permute-start | bytes 1572872 | tf_op jit(solution)/shard_map/ppermute | solution.py:37
  114.9 10.7 %collective-permute-start.15 = (bf16[4,4,128,128]{3,2,1,0:T(8,128)(2,1)S(1)}, bf16[4,4,128,128]{3,2,1,0:T(8,128)(2,1)S(1)}, u32[]{:S(2)}, u32[]{:S(2)}) collective-permute-start(bf16[4,4,128,128]{3,2,1,0:T(8,128)(2,1)S(1)} %get-tuple-element.13), channel_id=1, source_target_pairs={{0,16},{1,17},{2,18},{3,19},{4,20},{5,21},{6,22},{7,23},{8,24},{9,... | collective-permute-start | bytes 1572872 | tf_op jit(solution)/shard_map/ppermute | solution.py:37
  124.3 14.9 %collective-permute-start.18 = (bf16[4,4,256,128]{3,2,1,0:T(8,128)(2,1)S(1)}, bf16[4,4,256,128]{3,2,1,0:T(8,128)(2,1)S(1)}, u32[]{:S(2)}, u32[]{:S(2)}) collective-permute-start(bf16[4,4,256,128]{3,2,1,0:T(8,128)(2,1)S(1)} %pad_maximum_fusion.3), channel_id=1, source_target_pairs={{0,80},{1,81},{2,82},{3,83},{4,84},{5,85},{6,86},{7,87},{8,88},{9,... | collective-permute-start | bytes 3145736 | tf_op jit(solution)/shard_map/ppermute | solution.py:37
  125.8 16.1 %collective-permute-start.16 = (bf16[4,4,256,128]{3,2,1,0:T(8,128)(2,1)S(1)}, bf16[4,4,256,128]{3,2,1,0:T(8,128)(2,1)S(1)}, u32[]{:S(2)}, u32[]{:S(2)}) collective-permute-start(bf16[4,4,256,128]{3,2,1,0:T(8,128)(2,1)S(1)} %pad_maximum_fusion.2), channel_id=1, source_target_pairs={{0,16},{1,17},{2,18},{3,19},{4,20},{5,21},{6,22},{7,23},{8,24},{9,... | collective-permute-start | bytes 3145736 | tf_op jit(solution)/shard_map/ppermute | solution.py:37
  142.4 14.3 %collective-permute-start.19 = (bf16[4,256,128]{2,1,0:T(8,128)(2,1)S(1)}, bf16[4,256,128]{2,1,0:T(8,128)(2,1)S(1)}, u32[]{:S(2)}, u32[]{:S(2)}) collective-permute-start(bf16[4,256,128]{2,1,0:T(8,128)(2,1)S(1)} %get-tuple-element.10), channel_id=1, source_target_pairs={{0,4},{1,5},{2,6},{3,7},{4,8},{5,9},{6,10},{7,11},{8,12},{9,13},{1... | collective-permute-start | bytes 786440 | tf_op jit(solution)/shard_map/ppermute | solution.py:37
  142.7 14.0 %collective-permute-start.21 = (bf16[4,256,128]{2,1,0:T(8,128)(2,1)S(1)}, bf16[4,256,128]{2,1,0:T(8,128)(2,1)S(1)}, u32[]{:S(2)}, u32[]{:S(2)}) collective-permute-start(bf16[4,256,128]{2,1,0:T(8,128)(2,1)S(1)} %get-tuple-element.11), channel_id=1, source_target_pairs={{0,8},{1,9},{2,10},{3,11},{4,12},{5,13},{6,14},{7,15},{8,0},{9,1},... | collective-permute-start | bytes 786440 | tf_op jit(solution)/shard_map/ppermute | solution.py:37
  145.1 12.3 %collective-permute-start.20 = (bf16[4,256,128]{2,1,0:T(8,128)(2,1)S(1)}, bf16[4,256,128]{2,1,0:T(8,128)(2,1)S(1)}, u32[]{:S(2)}, u32[]{:S(2)}) collective-permute-start(bf16[4,256,128]{2,1,0:T(8,128)(2,1)S(1)} %get-tuple-element.12), channel_id=1, source_target_pairs={{0,12},{1,13},{2,14},{3,15},{4,0},{5,1},{6,2},{7,3},{8,4},{9,5},{1... | collective-permute-start | bytes 786440 | tf_op jit(solution)/shard_map/ppermute | solution.py:37
  157.6 6.2 %collective-permute-start.22 = (bf16[256,128]{1,0:T(8,128)(2,1)S(1)}, bf16[256,128]{1,0:T(8,128)(2,1)S(1)}, u32[]{:S(2)}, u32[]{:S(2)}) collective-permute-start(bf16[256,128]{1,0:T(8,128)(2,1)S(1)} %get-tuple-element.17), channel_id=1, source_target_pairs={{0,1},{1,2},{2,3},{3,0},{4,5},{5,6},{6,7},{7,4},{8,9},{9,10},{10,1... | collective-permute-start | bytes 196616 | tf_op jit(solution)/shard_map/ppermute | solution.py:37
  157.6 6.2 %collective-permute-start.24 = (bf16[256,128]{1,0:T(8,128)(2,1)S(1)}, bf16[256,128]{1,0:T(8,128)(2,1)S(1)}, u32[]{:S(2)}, u32[]{:S(2)}) collective-permute-start(bf16[256,128]{1,0:T(8,128)(2,1)S(1)} %get-tuple-element.18), channel_id=1, source_target_pairs={{0,2},{1,3},{2,0},{3,1},{4,6},{5,7},{6,4},{7,5},{8,10},{9,11},{10,... | collective-permute-start | bytes 196616 | tf_op jit(solution)/shard_map/ppermute | solution.py:37
  159.1 5.6 %collective-permute-start.23 = (bf16[256,128]{1,0:T(8,128)(2,1)S(1)}, bf16[256,128]{1,0:T(8,128)(2,1)S(1)}, u32[]{:S(2)}, u32[]{:S(2)}) collective-permute-start(bf16[256,128]{1,0:T(8,128)(2,1)S(1)} %get-tuple-element.19), channel_id=1, source_target_pairs={{0,3},{1,0},{2,1},{3,2},{4,7},{5,4},{6,5},{7,6},{8,11},{9,8},{10,9... | collective-permute-start | bytes 196616 | tf_op jit(solution)/shard_map/ppermute | solution.py:37
  179.9 1.2 collective-permute-start.25
  181.1 5.1 %collective-permute-start.26 = (f32[4,128]{1,0:T(4,128)S(1)}, f32[4,128]{1,0:T(4,128)S(1)}, u32[]{:S(2)}, u32[]{:S(2)}) collective-permute-start(f32[4,128]{1,0:T(4,128)S(1)} %add.221), channel_id=1, source_target_pairs={{0,64},{32,96},{64,0},{96,32},{1,65},{33,97},{65,1},{97,33},{2,66}... | collective-permute-start | bytes 6152 | tf_op jit(solution)/shard_map/ppermute | solution.py:46
  (1 other events, 2.3 us)

commit v12 on v11

--- a/solution.py
+++ b/solution.py
@@ -280,7 +280,7 @@
     tile_stack = tile_values.reshape(cycle_size, tile_rows, slot_count, tile_size, tile_size)
     spots = buffer_spots(tile_col, blk_id, feat_id, block_tiles, tile_rows)
     sibling_tiles = sibling(tile_stack)
-    sibling_spots = buffer_spots(sibling(tile_col), blk_id, feat_id, block_tiles, tile_rows)
+    sibling_col = sibling(tile_col)
     sibling_count = sibling(tile_count)
     buffer_tiles = block_tiles * 2
 
@@ -289,6 +289,10 @@
         features_own, weight, (((0,), (0,)), ((), ())), preferred_element_type=jnp.float32
     ).astype(jnp.bfloat16)
 
+    sibling_col, sibling_count, projected = lax.optimization_barrier(
+        (sibling_col, sibling_count, projected)
+    )
+    sibling_spots = buffer_spots(sibling_col, blk_id, feat_id, block_tiles, tile_rows)
     gathered = gather_phase_direct(projected, 0)
     gathered = gather_phase_direct(gathered, 1)
     gathered = gather_phase(gathered, 2)

time: 187 us -> 182 us (0.973)
  blocking collectives: 32.2 us -> 14.6 us
  starting transfers between devices: 28.1 us -> 37.7 us
  waiting for transfers between devices: 79.8 us -> 82.4 us
    all_to_all x1 -> x0, blocking collectives: 17.6 us -> none  [body(): lax.all_to_all(features_t, 'feat', split_axis=1, concat_axis=0, tiled=True)]
    all_to_all x0 -> x1, starting transfers between devices: none -> 9.27 us  [body(): lax.all_to_all(features_t, 'feat', split_axis=1, concat_axis=0, tiled=True)]
    all_to_all x0 -> x1, waiting for transfers between devices: none -> 7.74 us  [body(): lax.all_to_all(features_t, 'feat', split_axis=1, concat_axis=0, tiled=True)]
    ppermute x5, waiting for transfers between devices: 5.35 us -> 0.33 us  [sibling(): lax.ppermute(block, 'blk', [(i, i ^ 1) for i in range(lax.axis_size('blk'...]
  transfers between devices with their start and end apart: 27 -> 28, of which waited for: 21 -> 21; matrix products, arithmetic and copies ran while one was open for 6% -> 6% of each run, Pallas kernels for 8% -> 8%
where the time goes in v12:
time: 182 us; the launch traced here: 181 us
  waiting for transfers between devices  82.4 us (45%)
  starting transfers between devices  37.7 us (21%)
  Pallas kernels  30.5 us (17%)
  blocking collectives  14.6 us (8%)
  other arithmetic  7.84 us (4%)
  local copies, waits for them, and re-layouts  6.44 us (4%)
    ppermute x20, waiting for transfers between devices, ring_shift(): return lax.ppermute(block, BOTH, route)  69.9 us
    ppermute x20, starting transfers between devices, ring_shift(): return lax.ppermute(block, BOTH, route)  25.9 us
    pallas_call x2, Pallas kernels, aggregate_pair(): pl.pallas_call(aggregate_kernel, grid_spec=grid_spec, out_shape=jax.Shape...  15.3 us
    pallas_call x1, Pallas kernels, spread_pair(): pl.pallas_call(kernel, grid_spec=grid_spec, out_shape=jax.ShapeDtypeStruc...  15.2 us
    all_to_all x1, blocking collectives, body(): lax.all_to_all(outgoing, 'feat', split_axis=0, concat_axis=0, tiled=True)  14.6 us
    all_to_all x1, starting transfers between devices, body(): lax.all_to_all(features_t, 'feat', split_axis=1, concat_axis=0, tiled=True)  9.27 us
    all_to_all x1, waiting for transfers between devices, body(): lax.all_to_all(features_t, 'feat', split_axis=1, concat_axis=0, tiled=True)  7.74 us
    slice x2, local copies, waits for them, and re-layouts, term(): return total[k]  5.03 us
  transfers between devices with their start and end apart: 28, of which 21 were waited for; matrix products, arithmetic and copies ran while one was open for 6% of the time, Pallas kernels for 8%

profile of v12, /device:TPU:0, one launch (start us, length us, event | category | flops | bytes accessed | tf_op | source)
XLA Modules:
  0.0 180.9 jit_solution(12332234230101078296)
XLA Ops:
  0.7 9.3 %all-to-all-start = ((bf16[4,32,256]{2,0,1:T(4,128)(2,1)}), bf16[4,32,256]{2,0,1:T(4,128)(2,1)S(1)}, u32[]{:S(2)}, u32[]{:S(2)}) async-start(bf16[4,32,256]{2,0,1:T(4,128)(2,1)} %bitcast.128), calls=%async_computation | async-start | bytes 131072 | tf_op jit(solution)/shard_map/all_to_all | solution.py:287
  10.6 7.7 %all-to-all-done = bf16[4,32,256]{2,0,1:T(4,128)(2,1)S(1)} async-done(((bf16[4,32,256]{2,0,1:T(4,128)(2,1)}), bf16[4,32,256]{2,0,1:T(4,128)(2,1)S(1)}, u32[]{:S(2)}, u32[]{:S(2)}) %all-to-all-start) | async-done | bytes 65568 | tf_op jit(solution)/shard_map/all_to_all | solution.py:287
  19.2 2.3 %collective-permute-start.3 = (bf16[256,128]{1,0:T(8,128)(2,1)S(1)}, bf16[256,128]{1,0:T(8,128)(2,1)S(1)}, u32[]{:S(2)}, u32[]{:S(2)}) collective-permute-start(bf16[256,128]{1,0:T(8,128)(2,1)S(1)} %convolution_convert_fusion.1), channel_id=1, source_target_pairs={{0,2},{1,3},{2,0},{3,1},{4,6},{5,7},{6,4},{7,5},{8,10},{9,11},{10,... | collective-permute-start | bytes 196616 | tf_op jit(solution)/shard_map/ppermute | solution.py:37
  22.6 1.5 collective-permute-done.4
  25.8 1.4 collective-permute-start.6
  27.2 1.9 %collective-permute-start.5 = (bf16[4,256,128]{2,1,0:T(8,128)(2,1)S(1)}, bf16[4,256,128]{2,1,0:T(8,128)(2,1)S(1)}, u32[]{:S(2)}, u32[]{:S(2)}) collective-permute-start(bf16[4,256,128]{2,1,0:T(8,128)(2,1)S(1)} %get-tuple-element.27), channel_id=1, source_target_pairs={{0,12},{1,13},{2,14},{3,15},{4,0},{5,1},{6,2},{7,3},{8,4},{9,5},{1... | collective-permute-start | bytes 786440 | tf_op jit(solution)/shard_map/ppermute | solution.py:37
  29.3 7.4 %collective-permute-done.6 = bf16[4,256,128]{2,1,0:T(8,128)(2,1)S(1)} collective-permute-done((bf16[4,256,128]{2,1,0:T(8,128)(2,1)S(1)}, bf16[4,256,128]{2,1,0:T(8,128)(2,1)S(1)}, u32[]{:S(2)}, u32[]{:S(2)}) %collective-permute-start.6) | collective-permute-done | bytes 262176 | tf_op jit(solution)/shard_map/ppermute | solution.py:37
  36.6 1.9 %collective-permute-done.5 = bf16[4,256,128]{2,1,0:T(8,128)(2,1)S(1)} collective-permute-done((bf16[4,256,128]{2,1,0:T(8,128)(2,1)S(1)}, bf16[4,256,128]{2,1,0:T(8,128)(2,1)S(1)}, u32[]{:S(2)}, u32[]{:S(2)}) %collective-permute-start.5) | collective-permute-done | bytes 262176 | tf_op jit(solution)/shard_map/ppermute | solution.py:37
  39.9 3.0 %collective-permute-start.8 = (bf16[4,4,256,128]{3,2,1,0:T(8,128)(2,1)S(1)}, bf16[4,4,256,128]{3,2,1,0:T(8,128)(2,1)S(1)}, u32[]{:S(2)}, u32[]{:S(2)}) collective-permute-start(bf16[4,4,256,128]{3,2,1,0:T(8,128)(2,1)S(1)} %get-tuple-element.22), channel_id=1, source_target_pairs={{0,80},{1,81},{2,82},{3,83},{4,84},{5,85},{6,86},{7,87},{8,88},{9,... | collective-permute-start | bytes 3145736 | tf_op jit(solution)/shard_map/ppermute | solution.py:37
  42.9 12.3 %collective-permute-done.8 = bf16[4,4,256,128]{3,2,1,0:T(8,128)(2,1)S(1)} collective-permute-done((bf16[4,4,256,128]{3,2,1,0:T(8,128)(2,1)S(1)}, bf16[4,4,256,128]{3,2,1,0:T(8,128)(2,1)S(1)}, u32[]{:S(2)}, u32[]{:S(2)}) %collective-permute-start.8) | collective-permute-done | bytes 1048608 | tf_op jit(solution)/shard_map/ppermute | solution.py:37
  55.3 3.8 %collective-permute-start.11 = (bf16[4,4,128,128]{3,2,1,0:T(8,128)(2,1)S(1)}, bf16[4,4,128,128]{3,2,1,0:T(8,128)(2,1)S(1)}, u32[]{:S(2)}, u32[]{:S(2)}) collective-permute-start(bf16[4,4,128,128]{3,2,1,0:T(8,128)(2,1)S(1)} %slice.104), channel_id=1, source_target_pairs={{0,80},{1,81},{2,82},{3,83},{4,84},{5,85},{6,86},{7,87},{8,88},{9,... | collective-permute-start | bytes 1572872 | tf_op jit(solution)/shard_map/ppermute | solution.py:37
  59.2 6.6 %collective-permute-done.11 = bf16[4,4,128,128]{3,2,1,0:T(8,128)(2,1)S(1)} collective-permute-done((bf16[4,4,128,128]{3,2,1,0:T(8,128)(2,1)S(1)}, bf16[4,4,128,128]{3,2,1,0:T(8,128)(2,1)S(1)}, u32[]{:S(2)}, u32[]{:S(2)}) %collective-permute-start.11) | collective-permute-done | bytes 524320 | tf_op jit(solution)/shard_map/ppermute | solution.py:37
  65.7 3.8 %collective-permute-done.10 = bf16[4,4,128,128]{3,2,1,0:T(8,128)(2,1)S(1)} collective-permute-done((bf16[4,4,128,128]{3,2,1,0:T(8,128)(2,1)S(1)}, bf16[4,4,128,128]{3,2,1,0:T(8,128)(2,1)S(1)}, u32[]{:S(2)}, u32[]{:S(2)}) %collective-permute-start.10) | collective-permute-done | bytes 524320 | tf_op jit(solution)/shard_map/ppermute | solution.py:37
  69.6 2.3 %pad_maximum_fusion = bf16[4,4,4,256,128]{4,3,2,1,0:T(8,128)(2,1)} fusion(bf16[1,4,4,256,128]{4,3,2,1,0:T(8,128)(2,1)S(1)} %bitcast.112, bf16[1,4,4,256,128]{4,3,2,1,0:T(8,128)(2,1)S(1)} %maximum_bitcast_fusion, bf16[1,4,4,256,128]{4,3,2,1,0:T(8,128)(2,1)S(1)} %bitcast.111, bf16[1,4,4,256,128]{4,3,2,1,0:T(8,128)(2,1)S(1)} %get-tuple-element.21), kind=kLoop, calls=%fused_computation | loop fusion | flops 6291456 | bytes 8388608 | tf_op jit(solution)/shard_map/stack | solution.py:56
  72.6 7.6 %shard_map.85 = f32[2,128,128]{2,1,0:T(8,128)} custom-call(s32[1]{0:T(128)} %bitcast.core_ref, s32[256]{0:T(256)} %copy-done.3, s32[8]{0:T(128)} %count_ref.3, bf16[4,2,32,128,128]{4,3,2,1,0:T(8,128)(2,1)} %bitcast.102, bf16[128,128,128]{2,1,0:T(8,128)(2,1)} %bitcast.16.proj_ref), custom_call_target="tpu_custom_call" | custom-call | tf_op jit(solution)/shard_map/pallas_call | solution.py:161
  80.2 7.7 %shard_map.86 = f32[2,128,128]{2,1,0:T(8,128)} custom-call(s32[1]{0:T(128)} %bitcast.17.core_ref, s32[256]{0:T(256)} %copy-done.3, s32[8]{0:T(128)} %count_ref.3, bf16[4,2,32,128,128]{4,3,2,1,0:T(8,128)(2,1)} %bitcast.103, bf16[128,128,128]{2,1,0:T(8,128)(2,1)} %collective-permute-done.12.proj_ref), custom_call_target="tpu_custom_call" | custom-call | tf_op jit(solution)/shard_map/pallas_call | solution.py:161
  91.8 15.2 %shard_map.87 = f32[128,128,128]{2,1,0:T(8,128)} custom-call(s32[1]{0:T(128)} %bitcast.core_ref, s32[512]{0:T(512)} %pad_add_fusion.where_ref, s32[16]{0:T(128)} %pad_add_fusion.1.count_ref, bf16[4,2,32,128,128]{4,3,2,1,0:T(8,128)(2,1)} %bitcast.104, bf16[4,2,32,128,128]{4,3,2,1,0:T(8,128)(2,1)} %collective-permute-done.13.other_ref, ...), custom_call_target="tpu_custom_call" | custom-call | tf_op jit(solution)/shard_map/pallas_call | solution.py:235
  107.0 1.7 slice.158
  109.1 1.9 %collective-permute-start.15 = (bf16[4,4,128,128]{3,2,1,0:T(8,128)(2,1)S(1)}, bf16[4,4,128,128]{3,2,1,0:T(8,128)(2,1)S(1)}, u32[]{:S(2)}, u32[]{:S(2)}) collective-permute-start(bf16[4,4,128,128]{3,2,1,0:T(8,128)(2,1)S(1)} %get-tuple-element.19), channel_id=1, source_target_pairs={{0,16},{1,17},{2,18},{3,19},{4,20},{5,21},{6,22},{7,23},{8,24},{9,... | collective-permute-start | bytes 1572872 | tf_op jit(solution)/shard_map/ppermute | solution.py:37
  111.0 3.3 %fusion.39 = (f32[32,128,128]{2,1,0:T(8,128)S(1)}, f32[32,128,128]{2,1,0:T(8,128)S(1)}, f32[32,128,128]{2,1,0:T(8,128)S(1)}) fusion(f32[128,128,128]{2,1,0:T(8,128)} %shard_map.87), kind=kLoop, calls=%fused_computation.142 | loop fusion | bytes 12582912 | tf_op jit(solution)/shard_map/slice | solution.py:83
  114.5 3.7 %collective-permute-done.17 = bf16[4,4,128,128]{3,2,1,0:T(8,128)(2,1)S(1)} collective-permute-done((bf16[4,4,128,128]{3,2,1,0:T(8,128)(2,1)S(1)}, bf16[4,4,128,128]{3,2,1,0:T(8,128)(2,1)S(1)}, u32[]{:S(2)}, u32[]{:S(2)}) %collective-permute-start.17) | collective-permute-done | bytes 524320 | tf_op jit(solution)/shard_map/ppermute | solution.py:37
  118.4 1.4 collective-permute-start.18
  120.8 12.5 %collective-permute-done.18 = bf16[4,4,256,128]{3,2,1,0:T(8,128)(2,1)S(1)} collective-permute-done((bf16[4,4,256,128]{3,2,1,0:T(8,128)(2,1)S(1)}, bf16[4,4,256,128]{3,2,1,0:T(8,128)(2,1)S(1)}, u32[]{:S(2)}, u32[]{:S(2)}) %collective-permute-start.18) | collective-permute-done | bytes 1048608 | tf_op jit(solution)/shard_map/ppermute | solution.py:37
  133.2 2.8 %collective-permute-done.16 = bf16[4,4,256,128]{3,2,1,0:T(8,128)(2,1)S(1)} collective-permute-done((bf16[4,4,256,128]{3,2,1,0:T(8,128)(2,1)S(1)}, bf16[4,4,256,128]{3,2,1,0:T(8,128)(2,1)S(1)}, u32[]{:S(2)}, u32[]{:S(2)}) %collective-permute-start.16) | collective-permute-done | bytes 1048608 | tf_op jit(solution)/shard_map/ppermute | solution.py:37
  137.0 2.4 %collective-permute-start.21 = (bf16[4,256,128]{2,1,0:T(8,128)(2,1)S(1)}, bf16[4,256,128]{2,1,0:T(8,128)(2,1)S(1)}, u32[]{:S(2)}, u32[]{:S(2)}) collective-permute-start(bf16[4,256,128]{2,1,0:T(8,128)(2,1)S(1)} %get-tuple-element.17), channel_id=1, source_target_pairs={{0,8},{1,9},{2,10},{3,11},{4,12},{5,13},{6,14},{7,15},{8,0},{9,1},... | collective-permute-start | bytes 786440 | tf_op jit(solution)/shard_map/ppermute | solution.py:37
  140.7 4.7 %collective-permute-done.19 = bf16[4,256,128]{2,1,0:T(8,128)(2,1)S(1)} collective-permute-done((bf16[4,256,128]{2,1,0:T(8,128)(2,1)S(1)}, bf16[4,256,128]{2,1,0:T(8,128)(2,1)S(1)}, u32[]{:S(2)}, u32[]{:S(2)}) %collective-permute-start.19) | collective-permute-done | bytes 262176 | tf_op jit(solution)/shard_map/ppermute | solution.py:37
  145.4 6.0 %collective-permute-done.21 = bf16[4,256,128]{2,1,0:T(8,128)(2,1)S(1)} collective-permute-done((bf16[4,256,128]{2,1,0:T(8,128)(2,1)S(1)}, bf16[4,256,128]{2,1,0:T(8,128)(2,1)S(1)}, u32[]{:S(2)}, u32[]{:S(2)}) %collective-permute-start.21) | collective-permute-done | bytes 262176 | tf_op jit(solution)/shard_map/ppermute | solution.py:37
  151.8 1.6 collective-permute-start.24
  153.4 1.6 collective-permute-start.23
  155.0 2.9 %collective-permute-done.22 = bf16[256,128]{1,0:T(8,128)(2,1)S(1)} collective-permute-done((bf16[256,128]{1,0:T(8,128)(2,1)S(1)}, bf16[256,128]{1,0:T(8,128)(2,1)S(1)}, u32[]{:S(2)}, u32[]{:S(2)}) %collective-permute-start.22) | collective-permute-done | bytes 65568 | tf_op jit(solution)/shard_map/ppermute | solution.py:37
  159.4 14.6 %all_to_all.24 = f32[32,4,384]{2,1,0:T(4,128)S(1)} all-to-all(f32[32,4,384]{2,1,0:T(4,128)S(1)} %pad_maximum_fusion.5), channel_id=1, replica_groups=mesh['blk'=4,'feat'=32] {'feat'}, dimensions={0} | all-to-all | bytes 393216 | tf_op jit(solution)/shard_map/all_to_all | solution.py:349
  177.1 3.3 %collective-permute-done.26 = f32[4,128]{1,0:T(4,128)S(1)} collective-permute-done((f32[4,128]{1,0:T(4,128)S(1)}, f32[4,128]{1,0:T(4,128)S(1)}, u32[]{:S(2)}, u32[]{:S(2)}) %collective-permute-start.26) | collective-permute-done | bytes 2080 | tf_op jit(solution)/shard_map/ppermute | solution.py:46
  (79 shorter events, 20.0 us)
Async XLA Ops:
  0.6 17.7 %copy-start = (bf16[128,128]{1,0:T(8,128)(2,1)S(1)}, bf16[128,128]{1,0:T(8,128)(2,1)}, u32[]{:S(2)}) copy-start(bf16[128,128]{1,0:T(8,128)(2,1)} %param.7) | copy-start | bytes 98308
  0.6 91.2 %collective-permute-start.13 = (bf16[4,2,32,128,128]{4,3,2,1,0:T(8,128)(2,1)}, bf16[4,2,32,128,128]{4,3,2,1,0:T(8,128)(2,1)}, u32[]{:S(2)}, u32[]{:S(2)}) collective-permute-start(bf16[4,2,32,128,128]{4,3,2,1,0:T(8,128)(2,1)} %bitcast.101), channel_id=1, source_target_pairs={{0,32},{32,0},{64,96},{96,64},{1,33},{33,1},{65,97},{97,65},{2,34}... | collective-permute-start | bytes 25165832 | tf_op jit(solution)/shard_map/ppermute | solution.py:41
  0.7 17.6 %all-to-all-start = ((bf16[4,32,256]{2,0,1:T(4,128)(2,1)}), bf16[4,32,256]{2,0,1:T(4,128)(2,1)S(1)}, u32[]{:S(2)}, u32[]{:S(2)}) async-start(bf16[4,32,256]{2,0,1:T(4,128)(2,1)} %bitcast.128), calls=%async_computation | async-start | bytes 131072 | tf_op jit(solution)/shard_map/all_to_all | solution.py:287
  10.0 8.6 %collective-permute-start.1 = (s32[8]{0:T(128)}, s32[8]{0:T(128)S(1)}, u32[]{:S(2)}, u32[]{:S(2)}) collective-permute-start(s32[8]{0:T(128)} %count_ref.3), channel_id=1, source_target_pairs={{0,32},{32,0},{64,96},{96,64},{1,33},{33,1},{65,97},{97,65},{2,34}... | collective-permute-start | bytes 104 | tf_op jit(solution)/shard_map/ppermute | solution.py:41
  10.3 8.3 %collective-permute-start = (s32[256]{0:T(256)}, s32[256]{0:T(256)S(1)}, u32[]{:S(2)}, u32[]{:S(2)}) collective-permute-start(s32[256]{0:T(256)} %param.9), channel_id=1, source_target_pairs={{0,32},{32,0},{64,96},{96,64},{1,33},{33,1},{65,97},{97,65},{2,34}... | collective-permute-start | bytes 3080 | tf_op jit(solution)/shard_map/ppermute | solution.py:41
  18.6 5.5 %collective-permute-start.4 = (bf16[256,128]{1,0:T(8,128)(2,1)S(1)}, bf16[256,128]{1,0:T(8,128)(2,1)S(1)}, u32[]{:S(2)}, u32[]{:S(2)}) collective-permute-start(bf16[256,128]{1,0:T(8,128)(2,1)S(1)} %convolution_convert_fusion.1), channel_id=1, source_target_pairs={{0,1},{1,2},{2,3},{3,0},{4,5},{5,6},{6,7},{7,4},{8,9},{9,10},{10,1... | collective-permute-start | bytes 196616 | tf_op jit(solution)/shard_map/ppermute | solution.py:37
  19.2 5.8 %collective-permute-start.3 = (bf16[256,128]{1,0:T(8,128)(2,1)S(1)}, bf16[256,128]{1,0:T(8,128)(2,1)S(1)}, u32[]{:S(2)}, u32[]{:S(2)}) collective-permute-start(bf16[256,128]{1,0:T(8,128)(2,1)S(1)} %convolution_convert_fusion.1), channel_id=1, source_target_pairs={{0,2},{1,3},{2,0},{3,1},{4,6},{5,7},{6,4},{7,5},{8,10},{9,11},{10,... | collective-permute-start | bytes 196616 | tf_op jit(solution)/shard_map/ppermute | solution.py:37
  21.5 4.3 %collective-permute-start.2 = (bf16[256,128]{1,0:T(8,128)(2,1)S(1)}, bf16[256,128]{1,0:T(8,128)(2,1)S(1)}, u32[]{:S(2)}, u32[]{:S(2)}) collective-permute-start(bf16[256,128]{1,0:T(8,128)(2,1)S(1)} %convolution_convert_fusion.1), channel_id=1, source_target_pairs={{0,3},{1,0},{2,1},{3,2},{4,7},{5,4},{6,5},{7,6},{8,11},{9,8},{10,9... | collective-permute-start | bytes 196616 | tf_op jit(solution)/shard_map/ppermute | solution.py:37
  25.8 10.8 %collective-permute-start.6 = (bf16[4,256,128]{2,1,0:T(8,128)(2,1)S(1)}, bf16[4,256,128]{2,1,0:T(8,128)(2,1)S(1)}, u32[]{:S(2)}, u32[]{:S(2)}) collective-permute-start(bf16[4,256,128]{2,1,0:T(8,128)(2,1)S(1)} %get-tuple-element.27), channel_id=1, source_target_pairs={{0,8},{1,9},{2,10},{3,11},{4,12},{5,13},{6,14},{7,15},{8,0},{9,1},... | collective-permute-start | bytes 786440 | tf_op jit(solution)/shard_map/ppermute | solution.py:37
  27.2 11.3 %collective-permute-start.5 = (bf16[4,256,128]{2,1,0:T(8,128)(2,1)S(1)}, bf16[4,256,128]{2,1,0:T(8,128)(2,1)S(1)}, u32[]{:S(2)}, u32[]{:S(2)}) collective-permute-start(bf16[4,256,128]{2,1,0:T(8,128)(2,1)S(1)} %get-tuple-element.27), channel_id=1, source_target_pairs={{0,12},{1,13},{2,14},{3,15},{4,0},{5,1},{6,2},{7,3},{8,4},{9,5},{1... | collective-permute-start | bytes 786440 | tf_op jit(solution)/shard_map/ppermute | solution.py:37
  29.1 10.6 %collective-permute-start.7 = (bf16[4,256,128]{2,1,0:T(8,128)(2,1)S(1)}, bf16[4,256,128]{2,1,0:T(8,128)(2,1)S(1)}, u32[]{:S(2)}, u32[]{:S(2)}) collective-permute-start(bf16[4,256,128]{2,1,0:T(8,128)(2,1)S(1)} %get-tuple-element.27), channel_id=1, source_target_pairs={{0,4},{1,5},{2,6},{3,7},{4,8},{5,9},{6,10},{7,11},{8,12},{9,13},{1... | collective-permute-start | bytes 786440 | tf_op jit(solution)/shard_map/ppermute | solution.py:37
  39.9 15.3 %collective-permute-start.8 = (bf16[4,4,256,128]{3,2,1,0:T(8,128)(2,1)S(1)}, bf16[4,4,256,128]{3,2,1,0:T(8,128)(2,1)S(1)}, u32[]{:S(2)}, u32[]{:S(2)}) collective-permute-start(bf16[4,4,256,128]{3,2,1,0:T(8,128)(2,1)S(1)} %get-tuple-element.22), channel_id=1, source_target_pairs={{0,80},{1,81},{2,82},{3,83},{4,84},{5,85},{6,86},{7,87},{8,88},{9,... | collective-permute-start | bytes 3145736 | tf_op jit(solution)/shard_map/ppermute | solution.py:37
  42.9 16.1 %collective-permute-start.9 = (bf16[4,4,256,128]{3,2,1,0:T(8,128)(2,1)S(1)}, bf16[4,4,256,128]{3,2,1,0:T(8,128)(2,1)S(1)}, u32[]{:S(2)}, u32[]{:S(2)}) collective-permute-start(bf16[4,4,256,128]{3,2,1,0:T(8,128)(2,1)S(1)} %get-tuple-element.22), channel_id=1, source_target_pairs={{0,16},{1,17},{2,18},{3,19},{4,20},{5,21},{6,22},{7,23},{8,24},{9,... | collective-permute-start | bytes 3145736 | tf_op jit(solution)/shard_map/ppermute | solution.py:37
  55.3 10.5 %collective-permute-start.11 = (bf16[4,4,128,128]{3,2,1,0:T(8,128)(2,1)S(1)}, bf16[4,4,128,128]{3,2,1,0:T(8,128)(2,1)S(1)}, u32[]{:S(2)}, u32[]{:S(2)}) collective-permute-start(bf16[4,4,128,128]{3,2,1,0:T(8,128)(2,1)S(1)} %slice.104), channel_id=1, source_target_pairs={{0,80},{1,81},{2,82},{3,83},{4,84},{5,85},{6,86},{7,87},{8,88},{9,... | collective-permute-start | bytes 1572872 | tf_op jit(solution)/shard_map/ppermute | solution.py:37
  59.1 10.5 %collective-permute-start.10 = (bf16[4,4,128,128]{3,2,1,0:T(8,128)(2,1)S(1)}, bf16[4,4,128,128]{3,2,1,0:T(8,128)(2,1)S(1)}, u32[]{:S(2)}, u32[]{:S(2)}) collective-permute-start(bf16[4,4,128,128]{3,2,1,0:T(8,128)(2,1)S(1)} %slice.103), channel_id=1, source_target_pairs={{0,16},{1,17},{2,18},{3,19},{4,20},{5,21},{6,22},{7,23},{8,24},{9,... | collective-permute-start | bytes 1572872 | tf_op jit(solution)/shard_map/ppermute | solution.py:37
  71.9 8.3 %collective-permute-start.12 = (bf16[128,128,128]{2,1,0:T(8,128)(2,1)}, bf16[128,128,128]{2,1,0:T(8,128)(2,1)}, u32[]{:S(2)}, u32[]{:S(2)}) collective-permute-start(bf16[128,128,128]{2,1,0:T(8,128)(2,1)} %bitcast.16.proj_ref), channel_id=1, source_target_pairs={{0,32},{32,0},{64,96},{96,64},{1,33},{33,1},{65,97},{97,65},{2,34}... | collective-permute-start | bytes 12582920 | tf_op jit(solution)/shard_map/ppermute | solution.py:41
  80.2 7.7 %copy-start.1 = (f32[2,128,128]{2,1,0:T(8,128)S(1)}, f32[2,128,128]{2,1,0:T(8,128)}, u32[]{:S(2)}) copy-start(f32[2,128,128]{2,1,0:T(8,128)} %shard_map.85) | copy-start | bytes 393220
  80.2 8.7 %copy-start.2 = (bf16[256,128]{1,0:T(8,128)(2,1)S(1)}, bf16[256,128]{1,0:T(8,128)(2,1)}, u32[]{:S(2)}) copy-start(bf16[256,128]{1,0:T(8,128)(2,1)} %param.11) | copy-start | bytes 196612
  80.2 10.1 %copy-start.4 = (s32[8]{0:T(128)S(1)}, s32[8]{0:T(128)}, u32[]{:S(2)}) copy-start(s32[8]{0:T(128)} %count_ref.3) | copy-start | bytes 100
  89.7 1.5 collective-permute-start.14
  108.9 9.2 %collective-permute-start.17 = (bf16[4,4,128,128]{3,2,1,0:T(8,128)(2,1)S(1)}, bf16[4,4,128,128]{3,2,1,0:T(8,128)(2,1)S(1)}, u32[]{:S(2)}, u32[]{:S(2)}) collective-permute-start(bf16[4,4,128,128]{3,2,1,0:T(8,128)(2,1)S(1)} %get-tuple-element.20), channel_id=1, source_target_pairs={{0,80},{1,81},{2,82},{3,83},{4,84},{5,85},{6,86},{7,87},{8,88},{9,... | collective-permute-start | bytes 1572872 | tf_op jit(solution)/shard_map/ppermute | solution.py:37
  109.1 10.7 %collective-permute-start.15 = (bf16[4,4,128,128]{3,2,1,0:T(8,128)(2,1)S(1)}, bf16[4,4,128,128]{3,2,1,0:T(8,128)(2,1)S(1)}, u32[]{:S(2)}, u32[]{:S(2)}) collective-permute-start(bf16[4,4,128,128]{3,2,1,0:T(8,128)(2,1)S(1)} %get-tuple-element.19), channel_id=1, source_target_pairs={{0,16},{1,17},{2,18},{3,19},{4,20},{5,21},{6,22},{7,23},{8,24},{9,... | collective-permute-start | bytes 1572872 | tf_op jit(solution)/shard_map/ppermute | solution.py:37
  118.4 14.9 %collective-permute-start.18 = (bf16[4,4,256,128]{3,2,1,0:T(8,128)(2,1)S(1)}, bf16[4,4,256,128]{3,2,1,0:T(8,128)(2,1)S(1)}, u32[]{:S(2)}, u32[]{:S(2)}) collective-permute-start(bf16[4,4,256,128]{3,2,1,0:T(8,128)(2,1)S(1)} %pad_maximum_fusion.3), channel_id=1, source_target_pairs={{0,80},{1,81},{2,82},{3,83},{4,84},{5,85},{6,86},{7,87},{8,88},{9,... | collective-permute-start | bytes 3145736 | tf_op jit(solution)/shard_map/ppermute | solution.py:37
  120.0 16.1 %collective-permute-start.16 = (bf16[4,4,256,128]{3,2,1,0:T(8,128)(2,1)S(1)}, bf16[4,4,256,128]{3,2,1,0:T(8,128)(2,1)S(1)}, u32[]{:S(2)}, u32[]{:S(2)}) collective-permute-start(bf16[4,4,256,128]{3,2,1,0:T(8,128)(2,1)S(1)} %pad_maximum_fusion.2), channel_id=1, source_target_pairs={{0,16},{1,17},{2,18},{3,19},{4,20},{5,21},{6,22},{7,23},{8,24},{9,... | collective-permute-start | bytes 3145736 | tf_op jit(solution)/shard_map/ppermute | solution.py:37
  136.6 8.8 %collective-permute-start.19 = (bf16[4,256,128]{2,1,0:T(8,128)(2,1)S(1)}, bf16[4,256,128]{2,1,0:T(8,128)(2,1)S(1)}, u32[]{:S(2)}, u32[]{:S(2)}) collective-permute-start(bf16[4,256,128]{2,1,0:T(8,128)(2,1)S(1)} %get-tuple-element.16), channel_id=1, source_target_pairs={{0,4},{1,5},{2,6},{3,7},{4,8},{5,9},{6,10},{7,11},{8,12},{9,13},{1... | collective-permute-start | bytes 786440 | tf_op jit(solution)/shard_map/ppermute | solution.py:37
  137.0 14.4 %collective-permute-start.21 = (bf16[4,256,128]{2,1,0:T(8,128)(2,1)S(1)}, bf16[4,256,128]{2,1,0:T(8,128)(2,1)S(1)}, u32[]{:S(2)}, u32[]{:S(2)}) collective-permute-start(bf16[4,256,128]{2,1,0:T(8,128)(2,1)S(1)} %get-tuple-element.17), channel_id=1, source_target_pairs={{0,8},{1,9},{2,10},{3,11},{4,12},{5,13},{6,14},{7,15},{8,0},{9,1},... | collective-permute-start | bytes 786440 | tf_op jit(solution)/shard_map/ppermute | solution.py:37
  139.4 12.1 %collective-permute-start.20 = (bf16[4,256,128]{2,1,0:T(8,128)(2,1)S(1)}, bf16[4,256,128]{2,1,0:T(8,128)(2,1)S(1)}, u32[]{:S(2)}, u32[]{:S(2)}) collective-permute-start(bf16[4,256,128]{2,1,0:T(8,128)(2,1)S(1)} %get-tuple-element.18), channel_id=1, source_target_pairs={{0,12},{1,13},{2,14},{3,15},{4,0},{5,1},{6,2},{7,3},{8,4},{9,5},{1... | collective-permute-start | bytes 786440 | tf_op jit(solution)/shard_map/ppermute | solution.py:37
  151.7 6.2 %collective-permute-start.22 = (bf16[256,128]{1,0:T(8,128)(2,1)S(1)}, bf16[256,128]{1,0:T(8,128)(2,1)S(1)}, u32[]{:S(2)}, u32[]{:S(2)}) collective-permute-start(bf16[256,128]{1,0:T(8,128)(2,1)S(1)} %get-tuple-element.23), channel_id=1, source_target_pairs={{0,1},{1,2},{2,3},{3,0},{4,5},{5,6},{6,7},{7,4},{8,9},{9,10},{10,1... | collective-permute-start | bytes 196616 | tf_op jit(solution)/shard_map/ppermute | solution.py:37
  151.8 6.2 %collective-permute-start.24 = (bf16[256,128]{1,0:T(8,128)(2,1)S(1)}, bf16[256,128]{1,0:T(8,128)(2,1)S(1)}, u32[]{:S(2)}, u32[]{:S(2)}) collective-permute-start(bf16[256,128]{1,0:T(8,128)(2,1)S(1)} %get-tuple-element.24), channel_id=1, source_target_pairs={{0,2},{1,3},{2,0},{3,1},{4,6},{5,7},{6,4},{7,5},{8,10},{9,11},{10,... | collective-permute-start | bytes 196616 | tf_op jit(solution)/shard_map/ppermute | solution.py:37
  153.4 5.4 %collective-permute-start.23 = (bf16[256,128]{1,0:T(8,128)(2,1)S(1)}, bf16[256,128]{1,0:T(8,128)(2,1)S(1)}, u32[]{:S(2)}, u32[]{:S(2)}) collective-permute-start(bf16[256,128]{1,0:T(8,128)(2,1)S(1)} %get-tuple-element.25), channel_id=1, source_target_pairs={{0,3},{1,0},{2,1},{3,2},{4,7},{5,4},{6,5},{7,6},{8,11},{9,8},{10,9... | collective-permute-start | bytes 196616 | tf_op jit(solution)/shard_map/ppermute | solution.py:37
  174.0 1.2 collective-permute-start.25
  175.3 5.1 %collective-permute-start.26 = (f32[4,128]{1,0:T(4,128)S(1)}, f32[4,128]{1,0:T(4,128)S(1)}, u32[]{:S(2)}, u32[]{:S(2)}) collective-permute-start(f32[4,128]{1,0:T(4,128)S(1)} %add.221), channel_id=1, source_target_pairs={{0,64},{32,96},{64,0},{96,32},{1,65},{33,97},{65,1},{97,33},{2,66}... | collective-permute-start | bytes 6152 | tf_op jit(solution)/shard_map/ppermute | solution.py:46
  (2 other events, 2.9 us)

commit v13 on v12

--- a/solution.py
+++ b/solution.py
@@ -351,8 +351,11 @@
     grad_features = (
         got[:, :, hidden_width:].astype(jnp.bfloat16).transpose(1, 0, 2).reshape(shard_rows, -1)
     )
-    weight_part = weight_part + swapped(weight_part, "blk", 1)
-    weight_part = weight_part + swapped(weight_part, "blk", 2)
+    parts = [weight_part] + [swapped(weight_part, "blk", mask) for mask in range(1, cycle_size)]
+    by_blk = jnp.stack(parts)[jnp.bitwise_xor(jnp.arange(cycle_size), blk_id)]
+    weight_part = by_blk[0]
+    for index in range(1, cycle_size):
+        weight_part = weight_part + by_blk[index]
     grad_weight = weight_part * lax.rsqrt(jnp.float32(block_rows * cycle_size))
     return (activations, grad_features, grad_weight)
 

time: 182 us -> 182 us (level)
  blocking collectives: 14.6 us -> 0 us
  waiting for transfers between devices: 82.4 us -> 89.8 us
  starting transfers between devices: 37.7 us -> 43.2 us
    all_to_all x1 -> x0, blocking collectives: 14.6 us -> none  [body(): lax.all_to_all(outgoing, 'feat', split_axis=0, concat_axis=0, tiled=True)]
    all_to_all x0 -> x1, waiting for transfers between devices: none -> 8.67 us  [body(): lax.all_to_all(outgoing, 'feat', split_axis=0, concat_axis=0, tiled=True)]
    all_to_all x0 -> x1, starting transfers between devices: none -> 4.25 us  [body(): lax.all_to_all(outgoing, 'feat', split_axis=0, concat_axis=0, tiled=True)]
    ppermute x2 -> x3, waiting for transfers between devices: 4.41 us -> 1.16 us  [swapped(): return lax.ppermute(block, axis, [(i, i ^ mask) for i in range(count)])]
    ppermute x2 -> x3, starting transfers between devices: 1.25 us -> 3.43 us  [swapped(): return lax.ppermute(block, axis, [(i, i ^ mask) for i in range(count)])]
    ppermute x20, waiting for transfers between devices: 69.9 us -> 71.9 us  [ring_shift(): return lax.ppermute(block, BOTH, route)]
  transfers between devices with their start and end apart: 28 -> 30, of which waited for: 21 -> 21; matrix products, arithmetic and copies ran while one was open for 6% -> 6% of each run, Pallas kernels for 8% -> 8%
where the time goes in v13:
time: 182 us; the launch traced here: 180 us
  waiting for transfers between devices  89.8 us (49%)
  starting transfers between devices  43.2 us (24%)
  Pallas kernels  30.2 us (17%)
  other arithmetic  8.54 us (5%)
  local copies, waits for them, and re-layouts  7.01 us (4%)
    ppermute x20, waiting for transfers between devices, ring_shift(): return lax.ppermute(block, BOTH, route)  71.9 us
    ppermute x20, starting transfers between devices, ring_shift(): return lax.ppermute(block, BOTH, route)  25 us
    pallas_call x2, Pallas kernels, aggregate_pair(): pl.pallas_call(aggregate_kernel, grid_spec=grid_spec, out_shape=jax.Shape...  15.3 us
    pallas_call x1, Pallas kernels, spread_pair(): pl.pallas_call(kernel, grid_spec=grid_spec, out_shape=jax.ShapeDtypeStruc...  14.9 us
    all_to_all x1, starting transfers between devices, body(): lax.all_to_all(features_t, 'feat', split_axis=1, concat_axis=0, tiled=True)  9.27 us
    all_to_all x1, waiting for transfers between devices, body(): lax.all_to_all(outgoing, 'feat', split_axis=0, concat_axis=0, tiled=True)  8.67 us
    all_to_all x1, waiting for transfers between devices, body(): lax.all_to_all(features_t, 'feat', split_axis=1, concat_axis=0, tiled=True)  7.74 us
    slice x2, local copies, waits for them, and re-layouts, term(): return total[k]  5.03 us
  transfers between devices with their start and end apart: 30, of which 21 were waited for; matrix products, arithmetic and copies ran while one was open for 6% of the time, Pallas kernels for 8%

profile of v13, /device:TPU:0, one launch (start us, length us, event | category | flops | bytes accessed | tf_op | source)
XLA Modules:
  0.0 180.2 jit_solution(12180604258055495135)
XLA Ops:
  0.7 9.3 %all-to-all-start = ((bf16[4,32,256]{2,0,1:T(4,128)(2,1)}), bf16[4,32,256]{2,0,1:T(4,128)(2,1)S(1)}, u32[]{:S(2)}, u32[]{:S(2)}) async-start(bf16[4,32,256]{2,0,1:T(4,128)(2,1)} %bitcast.136), calls=%async_computation | async-start | bytes 131072 | tf_op jit(solution)/shard_map/all_to_all | solution.py:287
  10.6 7.7 %all-to-all-done = bf16[4,32,256]{2,0,1:T(4,128)(2,1)S(1)} async-done(((bf16[4,32,256]{2,0,1:T(4,128)(2,1)}), bf16[4,32,256]{2,0,1:T(4,128)(2,1)S(1)}, u32[]{:S(2)}, u32[]{:S(2)}) %all-to-all-start) | async-done | bytes 65568 | tf_op jit(solution)/shard_map/all_to_all | solution.py:287
  19.2 2.3 %collective-permute-start.3 = (bf16[256,128]{1,0:T(8,128)(2,1)S(1)}, bf16[256,128]{1,0:T(8,128)(2,1)S(1)}, u32[]{:S(2)}, u32[]{:S(2)}) collective-permute-start(bf16[256,128]{1,0:T(8,128)(2,1)S(1)} %convolution_convert_fusion.1), channel_id=1, source_target_pairs={{0,2},{1,3},{2,0},{3,1},{4,6},{5,7},{6,4},{7,5},{8,10},{9,11},{10,... | collective-permute-start | bytes 196616 | tf_op jit(solution)/shard_map/ppermute | solution.py:37
  22.6 1.5 collective-permute-done.4
  26.5 2.1 %collective-permute-start.6 = (bf16[4,256,128]{2,1,0:T(8,128)(2,1)S(1)}, bf16[4,256,128]{2,1,0:T(8,128)(2,1)S(1)}, u32[]{:S(2)}, u32[]{:S(2)}) collective-permute-start(bf16[4,256,128]{2,1,0:T(8,128)(2,1)S(1)} %get-tuple-element.27), channel_id=1, source_target_pairs={{0,8},{1,9},{2,10},{3,11},{4,12},{5,13},{6,14},{7,15},{8,0},{9,1},... | collective-permute-start | bytes 786440 | tf_op jit(solution)/shard_map/ppermute | solution.py:37
  29.8 9.6 %collective-permute-done.7 = bf16[4,256,128]{2,1,0:T(8,128)(2,1)S(1)} collective-permute-done((bf16[4,256,128]{2,1,0:T(8,128)(2,1)S(1)}, bf16[4,256,128]{2,1,0:T(8,128)(2,1)S(1)}, u32[]{:S(2)}, u32[]{:S(2)}) %collective-permute-start.7) | collective-permute-done | bytes 262176 | tf_op jit(solution)/shard_map/ppermute | solution.py:37
  40.3 3.0 %collective-permute-start.8 = (bf16[4,4,256,128]{3,2,1,0:T(8,128)(2,1)S(1)}, bf16[4,4,256,128]{3,2,1,0:T(8,128)(2,1)S(1)}, u32[]{:S(2)}, u32[]{:S(2)}) collective-permute-start(bf16[4,4,256,128]{3,2,1,0:T(8,128)(2,1)S(1)} %get-tuple-element.22), channel_id=1, source_target_pairs={{0,80},{1,81},{2,82},{3,83},{4,84},{5,85},{6,86},{7,87},{8,88},{9,... | collective-permute-start | bytes 3145736 | tf_op jit(solution)/shard_map/ppermute | solution.py:37
  43.2 12.3 %collective-permute-done.8 = bf16[4,4,256,128]{3,2,1,0:T(8,128)(2,1)S(1)} collective-permute-done((bf16[4,4,256,128]{3,2,1,0:T(8,128)(2,1)S(1)}, bf16[4,4,256,128]{3,2,1,0:T(8,128)(2,1)S(1)}, u32[]{:S(2)}, u32[]{:S(2)}) %collective-permute-start.8) | collective-permute-done | bytes 1048608 | tf_op jit(solution)/shard_map/ppermute | solution.py:37
  55.6 3.8 %collective-permute-start.11 = (bf16[4,4,128,128]{3,2,1,0:T(8,128)(2,1)S(1)}, bf16[4,4,128,128]{3,2,1,0:T(8,128)(2,1)S(1)}, u32[]{:S(2)}, u32[]{:S(2)}) collective-permute-start(bf16[4,4,128,128]{3,2,1,0:T(8,128)(2,1)S(1)} %slice.122), channel_id=1, source_target_pairs={{0,80},{1,81},{2,82},{3,83},{4,84},{5,85},{6,86},{7,87},{8,88},{9,... | collective-permute-start | bytes 1572872 | tf_op jit(solution)/shard_map/ppermute | solution.py:37
  59.5 6.6 %collective-permute-done.11 = bf16[4,4,128,128]{3,2,1,0:T(8,128)(2,1)S(1)} collective-permute-done((bf16[4,4,128,128]{3,2,1,0:T(8,128)(2,1)S(1)}, bf16[4,4,128,128]{3,2,1,0:T(8,128)(2,1)S(1)}, u32[]{:S(2)}, u32[]{:S(2)}) %collective-permute-start.11) | collective-permute-done | bytes 524320 | tf_op jit(solution)/shard_map/ppermute | solution.py:37
  66.1 3.8 %collective-permute-done.10 = bf16[4,4,128,128]{3,2,1,0:T(8,128)(2,1)S(1)} collective-permute-done((bf16[4,4,128,128]{3,2,1,0:T(8,128)(2,1)S(1)}, bf16[4,4,128,128]{3,2,1,0:T(8,128)(2,1)S(1)}, u32[]{:S(2)}, u32[]{:S(2)}) %collective-permute-start.10) | collective-permute-done | bytes 524320 | tf_op jit(solution)/shard_map/ppermute | solution.py:37
  70.0 2.3 %pad_maximum_fusion = bf16[4,4,4,256,128]{4,3,2,1,0:T(8,128)(2,1)} fusion(bf16[1,4,4,256,128]{4,3,2,1,0:T(8,128)(2,1)S(1)} %bitcast.120, bf16[1,4,4,256,128]{4,3,2,1,0:T(8,128)(2,1)S(1)} %maximum_bitcast_fusion, bf16[1,4,4,256,128]{4,3,2,1,0:T(8,128)(2,1)S(1)} %bitcast.119, bf16[1,4,4,256,128]{4,3,2,1,0:T(8,128)(2,1)S(1)} %get-tuple-element.21), kind=kLoop, calls=%fused_computation.1 | loop fusion | flops 6291456 | bytes 8388608 | tf_op jit(solution)/shard_map/stack | solution.py:56
  72.9 7.6 %shard_map.85 = f32[2,128,128]{2,1,0:T(8,128)} custom-call(s32[1]{0:T(128)} %bitcast.core_ref, s32[256]{0:T(256)} %copy-done.3, s32[8]{0:T(128)} %count_ref.3, bf16[4,2,32,128,128]{4,3,2,1,0:T(8,128)(2,1)} %bitcast.110, bf16[128,128,128]{2,1,0:T(8,128)(2,1)} %bitcast.16.proj_ref), custom_call_target="tpu_custom_call" | custom-call | tf_op jit(solution)/shard_map/pallas_call | solution.py:161
  80.5 7.7 %shard_map.86 = f32[2,128,128]{2,1,0:T(8,128)} custom-call(s32[1]{0:T(128)} %bitcast.17.core_ref, s32[256]{0:T(256)} %copy-done.3, s32[8]{0:T(128)} %count_ref.3, bf16[4,2,32,128,128]{4,3,2,1,0:T(8,128)(2,1)} %bitcast.111, bf16[128,128,128]{2,1,0:T(8,128)(2,1)} %collective-permute-done.12.proj_ref), custom_call_target="tpu_custom_call" | custom-call | tf_op jit(solution)/shard_map/pallas_call | solution.py:161
  92.2 14.9 %shard_map.87 = f32[128,128,128]{2,1,0:T(8,128)} custom-call(s32[1]{0:T(128)} %bitcast.core_ref, s32[512]{0:T(512)} %pad_add_fusion.where_ref, s32[16]{0:T(128)} %pad_add_fusion.1.count_ref, bf16[4,2,32,128,128]{4,3,2,1,0:T(8,128)(2,1)} %bitcast.112, bf16[4,2,32,128,128]{4,3,2,1,0:T(8,128)(2,1)} %collective-permute-done.13.other_ref, ...), custom_call_target="tpu_custom_call" | custom-call | tf_op jit(solution)/shard_map/pallas_call | solution.py:235
  107.0 1.7 slice.192
  109.4 1.6 collective-permute-start.15
  111.0 3.3 %fusion.42 = (f32[32,128,128]{2,1,0:T(8,128)S(1)}, f32[32,128,128]{2,1,0:T(8,128)S(1)}, f32[32,128,128]{2,1,0:T(8,128)S(1)}) fusion(f32[128,128,128]{2,1,0:T(8,128)} %shard_map.87), kind=kLoop, calls=%fused_computation.151 | loop fusion | bytes 12582912 | tf_op jit(solution)/shard_map/slice | solution.py:83
  114.5 3.7 %collective-permute-done.17 = bf16[4,4,128,128]{3,2,1,0:T(8,128)(2,1)S(1)} collective-permute-done((bf16[4,4,128,128]{3,2,1,0:T(8,128)(2,1)S(1)}, bf16[4,4,128,128]{3,2,1,0:T(8,128)(2,1)S(1)}, u32[]{:S(2)}, u32[]{:S(2)}) %collective-permute-start.17) | collective-permute-done | bytes 524320 | tf_op jit(solution)/shard_map/ppermute | solution.py:37
  118.4 1.7 collective-permute-start.18
  120.8 12.5 %collective-permute-done.18 = bf16[4,4,256,128]{3,2,1,0:T(8,128)(2,1)S(1)} collective-permute-done((bf16[4,4,256,128]{3,2,1,0:T(8,128)(2,1)S(1)}, bf16[4,4,256,128]{3,2,1,0:T(8,128)(2,1)S(1)}, u32[]{:S(2)}, u32[]{:S(2)}) %collective-permute-start.18) | collective-permute-done | bytes 1048608 | tf_op jit(solution)/shard_map/ppermute | solution.py:37
  133.3 3.1 %collective-permute-done.16 = bf16[4,4,256,128]{3,2,1,0:T(8,128)(2,1)S(1)} collective-permute-done((bf16[4,4,256,128]{3,2,1,0:T(8,128)(2,1)S(1)}, bf16[4,4,256,128]{3,2,1,0:T(8,128)(2,1)S(1)}, u32[]{:S(2)}, u32[]{:S(2)}) %collective-permute-start.16) | collective-permute-done | bytes 1048608 | tf_op jit(solution)/shard_map/ppermute | solution.py:37
  136.9 1.6 collective-permute-start.21
  138.5 2.1 %collective-permute-start.20 = (bf16[4,256,128]{2,1,0:T(8,128)(2,1)S(1)}, bf16[4,256,128]{2,1,0:T(8,128)(2,1)S(1)}, u32[]{:S(2)}, u32[]{:S(2)}) collective-permute-start(bf16[4,256,128]{2,1,0:T(8,128)(2,1)S(1)} %get-tuple-element.18), channel_id=1, source_target_pairs={{0,12},{1,13},{2,14},{3,15},{4,0},{5,1},{6,2},{7,3},{8,4},{9,5},{1... | collective-permute-start | bytes 786440 | tf_op jit(solution)/shard_map/ppermute | solution.py:37
  140.6 7.1 %collective-permute-done.21 = bf16[4,256,128]{2,1,0:T(8,128)(2,1)S(1)} collective-permute-done((bf16[4,256,128]{2,1,0:T(8,128)(2,1)S(1)}, bf16[4,256,128]{2,1,0:T(8,128)(2,1)S(1)}, u32[]{:S(2)}, u32[]{:S(2)}) %collective-permute-start.21) | collective-permute-done | bytes 262176 | tf_op jit(solution)/shard_map/ppermute | solution.py:37
  147.7 3.7 %collective-permute-done.20 = bf16[4,256,128]{2,1,0:T(8,128)(2,1)S(1)} collective-permute-done((bf16[4,256,128]{2,1,0:T(8,128)(2,1)S(1)}, bf16[4,256,128]{2,1,0:T(8,128)(2,1)S(1)}, u32[]{:S(2)}, u32[]{:S(2)}) %collective-permute-start.20) | collective-permute-done | bytes 262176 | tf_op jit(solution)/shard_map/ppermute | solution.py:37
  152.3 1.7 collective-permute-start.23
  154.4 3.7 %collective-permute-done.24 = bf16[256,128]{1,0:T(8,128)(2,1)S(1)} collective-permute-done((bf16[256,128]{1,0:T(8,128)(2,1)S(1)}, bf16[256,128]{1,0:T(8,128)(2,1)S(1)}, u32[]{:S(2)}, u32[]{:S(2)}) %collective-permute-start.24) | collective-permute-done | bytes 65568 | tf_op jit(solution)/shard_map/ppermute | solution.py:37
  158.1 1.5 collective-permute-done.22
  160.8 4.3 %all-to-all-start.1 = ((f32[32,4,384]{2,1,0:T(4,128)}), f32[32,4,384]{2,1,0:T(4,128)S(1)}, u32[]{:S(2)}, u32[]{:S(2)}) async-start(f32[32,4,384]{2,1,0:T(4,128)} %pad_maximum_fusion.5), calls=%async_computation.1 | async-start | bytes 393216 | tf_op jit(solution)/shard_map/all_to_all | solution.py:349
  165.1 8.7 %all-to-all-done.1 = f32[32,4,384]{2,1,0:T(4,128)S(1)} async-done(((f32[32,4,384]{2,1,0:T(4,128)}), f32[32,4,384]{2,1,0:T(4,128)S(1)}, u32[]{:S(2)}, u32[]{:S(2)}) %all-to-all-start.1) | async-done | bytes 196640 | tf_op jit(solution)/shard_map/all_to_all | solution.py:349
  175.1 2.1 %collective-permute-start.25 = (f32[4,128]{1,0:T(4,128)S(1)}, f32[4,128]{1,0:T(4,128)S(1)}, u32[]{:S(2)}, u32[]{:S(2)}) collective-permute-start(f32[4,128]{1,0:T(4,128)S(1)} %slice_reduce_fusion), channel_id=1, source_target_pairs={{0,32},{32,0},{64,96},{96,64},{1,33},{33,1},{65,97},{97,65},{2,34}... | collective-permute-start | bytes 6152 | tf_op jit(solution)/shard_map/ppermute | solution.py:46
  (85 shorter events, 20.8 us)
Async XLA Ops:
  0.6 17.7 %copy-start = (bf16[128,128]{1,0:T(8,128)(2,1)S(1)}, bf16[128,128]{1,0:T(8,128)(2,1)}, u32[]{:S(2)}) copy-start(bf16[128,128]{1,0:T(8,128)(2,1)} %param.7) | copy-start | bytes 98308
  0.6 91.5 %collective-permute-start.13 = (bf16[4,2,32,128,128]{4,3,2,1,0:T(8,128)(2,1)}, bf16[4,2,32,128,128]{4,3,2,1,0:T(8,128)(2,1)}, u32[]{:S(2)}, u32[]{:S(2)}) collective-permute-start(bf16[4,2,32,128,128]{4,3,2,1,0:T(8,128)(2,1)} %bitcast.109), channel_id=1, source_target_pairs={{0,32},{32,0},{64,96},{96,64},{1,33},{33,1},{65,97},{97,65},{2,34}... | collective-permute-start | bytes 25165832 | tf_op jit(solution)/shard_map/ppermute | solution.py:41
  0.7 17.6 %all-to-all-start = ((bf16[4,32,256]{2,0,1:T(4,128)(2,1)}), bf16[4,32,256]{2,0,1:T(4,128)(2,1)S(1)}, u32[]{:S(2)}, u32[]{:S(2)}) async-start(bf16[4,32,256]{2,0,1:T(4,128)(2,1)} %bitcast.136), calls=%async_computation | async-start | bytes 131072 | tf_op jit(solution)/shard_map/all_to_all | solution.py:287
  10.0 8.6 %collective-permute-start = (s32[256]{0:T(256)}, s32[256]{0:T(256)S(1)}, u32[]{:S(2)}, u32[]{:S(2)}) collective-permute-start(s32[256]{0:T(256)} %param.9), channel_id=1, source_target_pairs={{0,32},{32,0},{64,96},{96,64},{1,33},{33,1},{65,97},{97,65},{2,34}... | collective-permute-start | bytes 3080 | tf_op jit(solution)/shard_map/ppermute | solution.py:41
  10.3 8.3 %collective-permute-start.1 = (s32[8]{0:T(128)}, s32[8]{0:T(128)S(1)}, u32[]{:S(2)}, u32[]{:S(2)}) collective-permute-start(s32[8]{0:T(128)} %count_ref.3), channel_id=1, source_target_pairs={{0,32},{32,0},{64,96},{96,64},{1,33},{33,1},{65,97},{97,65},{2,34}... | collective-permute-start | bytes 104 | tf_op jit(solution)/shard_map/ppermute | solution.py:41
  18.6 5.5 %collective-permute-start.4 = (bf16[256,128]{1,0:T(8,128)(2,1)S(1)}, bf16[256,128]{1,0:T(8,128)(2,1)S(1)}, u32[]{:S(2)}, u32[]{:S(2)}) collective-permute-start(bf16[256,128]{1,0:T(8,128)(2,1)S(1)} %convolution_convert_fusion.1), channel_id=1, source_target_pairs={{0,1},{1,2},{2,3},{3,0},{4,5},{5,6},{6,7},{7,4},{8,9},{9,10},{10,1... | collective-permute-start | bytes 196616 | tf_op jit(solution)/shard_map/ppermute | solution.py:37
  19.2 5.8 %collective-permute-start.3 = (bf16[256,128]{1,0:T(8,128)(2,1)S(1)}, bf16[256,128]{1,0:T(8,128)(2,1)S(1)}, u32[]{:S(2)}, u32[]{:S(2)}) collective-permute-start(bf16[256,128]{1,0:T(8,128)(2,1)S(1)} %convolution_convert_fusion.1), channel_id=1, source_target_pairs={{0,2},{1,3},{2,0},{3,1},{4,6},{5,7},{6,4},{7,5},{8,10},{9,11},{10,... | collective-permute-start | bytes 196616 | tf_op jit(solution)/shard_map/ppermute | solution.py:37
  21.5 4.3 %collective-permute-start.2 = (bf16[256,128]{1,0:T(8,128)(2,1)S(1)}, bf16[256,128]{1,0:T(8,128)(2,1)S(1)}, u32[]{:S(2)}, u32[]{:S(2)}) collective-permute-start(bf16[256,128]{1,0:T(8,128)(2,1)S(1)} %convolution_convert_fusion.1), channel_id=1, source_target_pairs={{0,3},{1,0},{2,1},{3,2},{4,7},{5,4},{6,5},{7,6},{8,11},{9,8},{10,9... | collective-permute-start | bytes 196616 | tf_op jit(solution)/shard_map/ppermute | solution.py:37
  25.8 13.7 %collective-permute-start.7 = (bf16[4,256,128]{2,1,0:T(8,128)(2,1)S(1)}, bf16[4,256,128]{2,1,0:T(8,128)(2,1)S(1)}, u32[]{:S(2)}, u32[]{:S(2)}) collective-permute-start(bf16[4,256,128]{2,1,0:T(8,128)(2,1)S(1)} %get-tuple-element.27), channel_id=1, source_target_pairs={{0,4},{1,5},{2,6},{3,7},{4,8},{5,9},{6,10},{7,11},{8,12},{9,13},{1... | collective-permute-start | bytes 786440 | tf_op jit(solution)/shard_map/ppermute | solution.py:37
  26.5 13.0 %collective-permute-start.6 = (bf16[4,256,128]{2,1,0:T(8,128)(2,1)S(1)}, bf16[4,256,128]{2,1,0:T(8,128)(2,1)S(1)}, u32[]{:S(2)}, u32[]{:S(2)}) collective-permute-start(bf16[4,256,128]{2,1,0:T(8,128)(2,1)S(1)} %get-tuple-element.27), channel_id=1, source_target_pairs={{0,8},{1,9},{2,10},{3,11},{4,12},{5,13},{6,14},{7,15},{8,0},{9,1},... | collective-permute-start | bytes 786440 | tf_op jit(solution)/shard_map/ppermute | solution.py:37
  28.6 11.5 %collective-permute-start.5 = (bf16[4,256,128]{2,1,0:T(8,128)(2,1)S(1)}, bf16[4,256,128]{2,1,0:T(8,128)(2,1)S(1)}, u32[]{:S(2)}, u32[]{:S(2)}) collective-permute-start(bf16[4,256,128]{2,1,0:T(8,128)(2,1)S(1)} %get-tuple-element.27), channel_id=1, source_target_pairs={{0,12},{1,13},{2,14},{3,15},{4,0},{5,1},{6,2},{7,3},{8,4},{9,5},{1... | collective-permute-start | bytes 786440 | tf_op jit(solution)/shard_map/ppermute | solution.py:37
  40.3 15.3 %collective-permute-start.8 = (bf16[4,4,256,128]{3,2,1,0:T(8,128)(2,1)S(1)}, bf16[4,4,256,128]{3,2,1,0:T(8,128)(2,1)S(1)}, u32[]{:S(2)}, u32[]{:S(2)}) collective-permute-start(bf16[4,4,256,128]{3,2,1,0:T(8,128)(2,1)S(1)} %get-tuple-element.22), channel_id=1, source_target_pairs={{0,80},{1,81},{2,82},{3,83},{4,84},{5,85},{6,86},{7,87},{8,88},{9,... | collective-permute-start | bytes 3145736 | tf_op jit(solution)/shard_map/ppermute | solution.py:37
  43.2 16.1 %collective-permute-start.9 = (bf16[4,4,256,128]{3,2,1,0:T(8,128)(2,1)S(1)}, bf16[4,4,256,128]{3,2,1,0:T(8,128)(2,1)S(1)}, u32[]{:S(2)}, u32[]{:S(2)}) collective-permute-start(bf16[4,4,256,128]{3,2,1,0:T(8,128)(2,1)S(1)} %get-tuple-element.22), channel_id=1, source_target_pairs={{0,16},{1,17},{2,18},{3,19},{4,20},{5,21},{6,22},{7,23},{8,24},{9,... | collective-permute-start | bytes 3145736 | tf_op jit(solution)/shard_map/ppermute | solution.py:37
  55.6 10.5 %collective-permute-start.11 = (bf16[4,4,128,128]{3,2,1,0:T(8,128)(2,1)S(1)}, bf16[4,4,128,128]{3,2,1,0:T(8,128)(2,1)S(1)}, u32[]{:S(2)}, u32[]{:S(2)}) collective-permute-start(bf16[4,4,128,128]{3,2,1,0:T(8,128)(2,1)S(1)} %slice.122), channel_id=1, source_target_pairs={{0,80},{1,81},{2,82},{3,83},{4,84},{5,85},{6,86},{7,87},{8,88},{9,... | collective-permute-start | bytes 1572872 | tf_op jit(solution)/shard_map/ppermute | solution.py:37
  59.4 10.5 %collective-permute-start.10 = (bf16[4,4,128,128]{3,2,1,0:T(8,128)(2,1)S(1)}, bf16[4,4,128,128]{3,2,1,0:T(8,128)(2,1)S(1)}, u32[]{:S(2)}, u32[]{:S(2)}) collective-permute-start(bf16[4,4,128,128]{3,2,1,0:T(8,128)(2,1)S(1)} %slice.121), channel_id=1, source_target_pairs={{0,16},{1,17},{2,18},{3,19},{4,20},{5,21},{6,22},{7,23},{8,24},{9,... | collective-permute-start | bytes 1572872 | tf_op jit(solution)/shard_map/ppermute | solution.py:37
  72.2 8.3 %collective-permute-start.12 = (bf16[128,128,128]{2,1,0:T(8,128)(2,1)}, bf16[128,128,128]{2,1,0:T(8,128)(2,1)}, u32[]{:S(2)}, u32[]{:S(2)}) collective-permute-start(bf16[128,128,128]{2,1,0:T(8,128)(2,1)} %bitcast.16.proj_ref), channel_id=1, source_target_pairs={{0,32},{32,0},{64,96},{96,64},{1,33},{33,1},{65,97},{97,65},{2,34}... | collective-permute-start | bytes 12582920 | tf_op jit(solution)/shard_map/ppermute | solution.py:41
  80.5 10.1 %copy-start.4 = (s32[8]{0:T(128)S(1)}, s32[8]{0:T(128)}, u32[]{:S(2)}) copy-start(s32[8]{0:T(128)} %count_ref.3) | copy-start | bytes 100
  90.0 1.5 collective-permute-start.14
  108.9 9.2 %collective-permute-start.17 = (bf16[4,4,128,128]{3,2,1,0:T(8,128)(2,1)S(1)}, bf16[4,4,128,128]{3,2,1,0:T(8,128)(2,1)S(1)}, u32[]{:S(2)}, u32[]{:S(2)}) collective-permute-start(bf16[4,4,128,128]{3,2,1,0:T(8,128)(2,1)S(1)} %get-tuple-element.20), channel_id=1, source_target_pairs={{0,80},{1,81},{2,82},{3,83},{4,84},{5,85},{6,86},{7,87},{8,88},{9,... | collective-permute-start | bytes 1572872 | tf_op jit(solution)/shard_map/ppermute | solution.py:37
  109.4 10.7 %collective-permute-start.15 = (bf16[4,4,128,128]{3,2,1,0:T(8,128)(2,1)S(1)}, bf16[4,4,128,128]{3,2,1,0:T(8,128)(2,1)S(1)}, u32[]{:S(2)}, u32[]{:S(2)}) collective-permute-start(bf16[4,4,128,128]{3,2,1,0:T(8,128)(2,1)S(1)} %get-tuple-element.19), channel_id=1, source_target_pairs={{0,16},{1,17},{2,18},{3,19},{4,20},{5,21},{6,22},{7,23},{8,24},{9,... | collective-permute-start | bytes 1572872 | tf_op jit(solution)/shard_map/ppermute | solution.py:37
  118.4 14.9 %collective-permute-start.18 = (bf16[4,4,256,128]{3,2,1,0:T(8,128)(2,1)S(1)}, bf16[4,4,256,128]{3,2,1,0:T(8,128)(2,1)S(1)}, u32[]{:S(2)}, u32[]{:S(2)}) collective-permute-start(bf16[4,4,256,128]{3,2,1,0:T(8,128)(2,1)S(1)} %pad_maximum_fusion.3), channel_id=1, source_target_pairs={{0,80},{1,81},{2,82},{3,83},{4,84},{5,85},{6,86},{7,87},{8,88},{9,... | collective-permute-start | bytes 3145736 | tf_op jit(solution)/shard_map/ppermute | solution.py:37
  120.3 16.1 %collective-permute-start.16 = (bf16[4,4,256,128]{3,2,1,0:T(8,128)(2,1)S(1)}, bf16[4,4,256,128]{3,2,1,0:T(8,128)(2,1)S(1)}, u32[]{:S(2)}, u32[]{:S(2)}) collective-permute-start(bf16[4,4,256,128]{3,2,1,0:T(8,128)(2,1)S(1)} %pad_maximum_fusion.2), channel_id=1, source_target_pairs={{0,16},{1,17},{2,18},{3,19},{4,20},{5,21},{6,22},{7,23},{8,24},{9,... | collective-permute-start | bytes 3145736 | tf_op jit(solution)/shard_map/ppermute | solution.py:37
  136.9 10.8 %collective-permute-start.21 = (bf16[4,256,128]{2,1,0:T(8,128)(2,1)S(1)}, bf16[4,256,128]{2,1,0:T(8,128)(2,1)S(1)}, u32[]{:S(2)}, u32[]{:S(2)}) collective-permute-start(bf16[4,256,128]{2,1,0:T(8,128)(2,1)S(1)} %get-tuple-element.17), channel_id=1, source_target_pairs={{0,8},{1,9},{2,10},{3,11},{4,12},{5,13},{6,14},{7,15},{8,0},{9,1},... | collective-permute-start | bytes 786440 | tf_op jit(solution)/shard_map/ppermute | solution.py:37
  138.5 13.0 %collective-permute-start.20 = (bf16[4,256,128]{2,1,0:T(8,128)(2,1)S(1)}, bf16[4,256,128]{2,1,0:T(8,128)(2,1)S(1)}, u32[]{:S(2)}, u32[]{:S(2)}) collective-permute-start(bf16[4,256,128]{2,1,0:T(8,128)(2,1)S(1)} %get-tuple-element.18), channel_id=1, source_target_pairs={{0,12},{1,13},{2,14},{3,15},{4,0},{5,1},{6,2},{7,3},{8,4},{9,5},{1... | collective-permute-start | bytes 786440 | tf_op jit(solution)/shard_map/ppermute | solution.py:37
  140.6 11.5 %collective-permute-start.19 = (bf16[4,256,128]{2,1,0:T(8,128)(2,1)S(1)}, bf16[4,256,128]{2,1,0:T(8,128)(2,1)S(1)}, u32[]{:S(2)}, u32[]{:S(2)}) collective-permute-start(bf16[4,256,128]{2,1,0:T(8,128)(2,1)S(1)} %get-tuple-element.16), channel_id=1, source_target_pairs={{0,4},{1,5},{2,6},{3,7},{4,8},{5,9},{6,10},{7,11},{8,12},{9,13},{1... | collective-permute-start | bytes 786440 | tf_op jit(solution)/shard_map/ppermute | solution.py:37
  152.2 5.8 %collective-permute-start.24 = (bf16[256,128]{1,0:T(8,128)(2,1)S(1)}, bf16[256,128]{1,0:T(8,128)(2,1)S(1)}, u32[]{:S(2)}, u32[]{:S(2)}) collective-permute-start(bf16[256,128]{1,0:T(8,128)(2,1)S(1)} %get-tuple-element.24), channel_id=1, source_target_pairs={{0,2},{1,3},{2,0},{3,1},{4,6},{5,7},{6,4},{7,5},{8,10},{9,11},{10,... | collective-permute-start | bytes 196616 | tf_op jit(solution)/shard_map/ppermute | solution.py:37
  152.3 5.8 %collective-permute-start.23 = (bf16[256,128]{1,0:T(8,128)(2,1)S(1)}, bf16[256,128]{1,0:T(8,128)(2,1)S(1)}, u32[]{:S(2)}, u32[]{:S(2)}) collective-permute-start(bf16[256,128]{1,0:T(8,128)(2,1)S(1)} %get-tuple-element.25), channel_id=1, source_target_pairs={{0,3},{1,0},{2,1},{3,2},{4,7},{5,4},{6,5},{7,6},{8,11},{9,8},{10,9... | collective-permute-start | bytes 196616 | tf_op jit(solution)/shard_map/ppermute | solution.py:37
  154.1 5.5 %collective-permute-start.22 = (bf16[256,128]{1,0:T(8,128)(2,1)S(1)}, bf16[256,128]{1,0:T(8,128)(2,1)S(1)}, u32[]{:S(2)}, u32[]{:S(2)}) collective-permute-start(bf16[256,128]{1,0:T(8,128)(2,1)S(1)} %get-tuple-element.23), channel_id=1, source_target_pairs={{0,1},{1,2},{2,3},{3,0},{4,5},{5,6},{6,7},{7,4},{8,9},{9,10},{10,1... | collective-permute-start | bytes 196616 | tf_op jit(solution)/shard_map/ppermute | solution.py:37
  160.8 12.9 %all-to-all-start.1 = ((f32[32,4,384]{2,1,0:T(4,128)}), f32[32,4,384]{2,1,0:T(4,128)S(1)}, u32[]{:S(2)}, u32[]{:S(2)}) async-start(f32[32,4,384]{2,1,0:T(4,128)} %pad_maximum_fusion.5), calls=%async_computation.1 | async-start | bytes 393216 | tf_op jit(solution)/shard_map/all_to_all | solution.py:349
  173.8 4.6 %collective-permute-start.27 = (f32[4,128]{1,0:T(4,128)S(1)}, f32[4,128]{1,0:T(4,128)S(1)}, u32[]{:S(2)}, u32[]{:S(2)}) collective-permute-start(f32[4,128]{1,0:T(4,128)S(1)} %slice_reduce_fusion), channel_id=1, source_target_pairs={{0,96},{32,64},{64,32},{96,0},{1,97},{33,65},{65,33},{97,1},{2,98}... | collective-permute-start | bytes 6152 | tf_op jit(solution)/shard_map/ppermute | solution.py:46
  173.9 5.2 %collective-permute-start.26 = (f32[4,128]{1,0:T(4,128)S(1)}, f32[4,128]{1,0:T(4,128)S(1)}, u32[]{:S(2)}, u32[]{:S(2)}) collective-permute-start(f32[4,128]{1,0:T(4,128)S(1)} %slice_reduce_fusion), channel_id=1, source_target_pairs={{0,64},{32,96},{64,0},{96,32},{1,65},{33,97},{65,1},{97,33},{2,66}... | collective-permute-start | bytes 6152 | tf_op jit(solution)/shard_map/ppermute | solution.py:46
  175.1 3.9 %collective-permute-start.25 = (f32[4,128]{1,0:T(4,128)S(1)}, f32[4,128]{1,0:T(4,128)S(1)}, u32[]{:S(2)}, u32[]{:S(2)}) collective-permute-start(f32[4,128]{1,0:T(4,128)S(1)} %slice_reduce_fusion), channel_id=1, source_target_pairs={{0,32},{32,0},{64,96},{96,64},{1,33},{33,1},{65,97},{97,65},{2,34}... | collective-permute-start | bytes 6152 | tf_op jit(solution)/shard_map/ppermute | solution.py:46
  (4 other events, 19.4 us)

commit v14 on v13

--- a/solution.py
+++ b/solution.py
@@ -47,12 +47,12 @@
 
 
 def gather_phase(block, phase):
-    half = block.shape[-2] // 2
+    half = block.shape[0] // 2
     from_minus = ring_shift(block, phase, 1)
     from_plus = ring_shift(block, phase, -1)
-    far_low = ring_shift(from_minus[..., :half, :], phase, 1)
-    far_high = ring_shift(from_plus[..., half:, :], phase, -1)
-    far = jnp.concatenate([far_low, far_high], axis=-2)
+    far_low = ring_shift(from_minus[:half], phase, 1)
+    far_high = ring_shift(from_plus[half:], phase, -1)
+    far = jnp.concatenate([far_low, far_high], axis=0)
     return jnp.stack([block, from_plus, far, from_minus])
 
 
@@ -76,7 +76,7 @@
 
 
 def reduce_phase(total, phase, wire_type, extra=None):
-    half = total.shape[-2] // 2
+    half = total.shape[1] // 2
 
     def term(k):
         if extra is None:
@@ -84,16 +84,12 @@
         return total[k] + extra[k].astype(jnp.float32)
 
     far = term(2)
-    got_minus = ring_shift(far[..., :half, :].astype(wire_type), phase, 1)
-    got_plus = ring_shift(far[..., half:, :].astype(wire_type), phase, -1)
+    got_minus = ring_shift(far[:half].astype(wire_type), phase, 1)
+    got_plus = ring_shift(far[half:].astype(wire_type), phase, -1)
     ahead = term(1)
-    ahead = jnp.concatenate(
-        [ahead[..., :half, :] + got_minus.astype(jnp.float32), ahead[..., half:, :]], axis=-2
-    )
+    ahead = jnp.concatenate([ahead[:half] + got_minus.astype(jnp.float32), ahead[half:]], axis=0)
     behind = term(3)
-    behind = jnp.concatenate(
-        [behind[..., :half, :], behind[..., half:, :] + got_plus.astype(jnp.float32)], axis=-2
-    )
+    behind = jnp.concatenate([behind[:half], behind[half:] + got_plus.astype(jnp.float32)], axis=0)
     from_minus = ring_shift(ahead.astype(wire_type), phase, 1)
     from_plus = ring_shift(behind.astype(wire_type), phase, -1)
     return term(0) + from_minus.astype(jnp.float32) + from_plus.astype(jnp.float32)

time: 182 us -> 184 us (1.011)
  local copies, waits for them, and re-layouts: 7.01 us -> 2.12 us
  other arithmetic: 8.54 us -> 13.1 us
  waiting for transfers between devices: 89.8 us -> 92.8 us
    slice x2, local copies, waits for them, and re-layouts: 5.03 us -> 0.01 us  [term(): return total[k]]
    another operation x4 -> x5, other arithmetic: 0.87 us -> 5.37 us
    ppermute x20, waiting for transfers between devices: 71.9 us -> 74.8 us  [ring_shift(): return lax.ppermute(block, BOTH, route)]
  transfers between devices with their start and end apart: 30 -> 30, of which waited for: 21 -> 20; matrix products, arithmetic and copies ran while one was open for 6% -> 4% of each run, Pallas kernels for 8% -> 8%
where the time goes in v14:
time: 184 us
  waiting for transfers between devices  92.8 us (50%)
  starting transfers between devices  44 us (24%)
  Pallas kernels  30.2 us (16%)
  other arithmetic  13.1 us (7%)
  local copies, waits for them, and re-layouts  2.12 us (1%)
    ppermute x20, waiting for transfers between devices, ring_shift(): return lax.ppermute(block, BOTH, route)  74.8 us
    ppermute x20, starting transfers between devices, ring_shift(): return lax.ppermute(block, BOTH, route)  25.4 us
    pallas_call x2, Pallas kernels, aggregate_pair(): pl.pallas_call(aggregate_kernel, grid_spec=grid_spec, out_shape=jax.Shape...  15.3 us
    pallas_call x1, Pallas kernels, spread_pair(): pl.pallas_call(kernel, grid_spec=grid_spec, out_shape=jax.ShapeDtypeStruc...  14.9 us
    all_to_all x1, starting transfers between devices, body(): lax.all_to_all(features_t, 'feat', split_axis=1, concat_axis=0, tiled=True)  9.27 us
    all_to_all x1, waiting for transfers between devices, body(): lax.all_to_all(outgoing, 'feat', split_axis=0, concat_axis=0, tiled=True)  8.67 us
    all_to_all x1, waiting for transfers between devices, body(): lax.all_to_all(features_t, 'feat', split_axis=1, concat_axis=0, tiled=True)  7.74 us
    another operation x5, other arithmetic  5.37 us
  transfers between devices with their start and end apart: 30, of which 20 were waited for; matrix products, arithmetic and copies ran while one was open for 4% of the time, Pallas kernels for 8%

profile of v14, /device:TPU:0, one launch (start us, length us, event | category | flops | bytes accessed | tf_op | source)
XLA Modules:
  0.0 183.6 jit_solution(9138363938017821702)
XLA Ops:
  0.7 9.3 %all-to-all-start = ((bf16[4,32,256]{2,0,1:T(4,128)(2,1)}), bf16[4,32,256]{2,0,1:T(4,128)(2,1)S(1)}, u32[]{:S(2)}, u32[]{:S(2)}) async-start(bf16[4,32,256]{2,0,1:T(4,128)(2,1)} %bitcast.140), calls=%async_computation | async-start | bytes 131072 | tf_op jit(solution)/shard_map/all_to_all | solution.py:283
  10.6 7.7 %all-to-all-done = bf16[4,32,256]{2,0,1:T(4,128)(2,1)S(1)} async-done(((bf16[4,32,256]{2,0,1:T(4,128)(2,1)}), bf16[4,32,256]{2,0,1:T(4,128)(2,1)S(1)}, u32[]{:S(2)}, u32[]{:S(2)}) %all-to-all-start) | async-done | bytes 65568 | tf_op jit(solution)/shard_map/all_to_all | solution.py:283
  19.2 2.3 %collective-permute-start.3 = (bf16[256,128]{1,0:T(8,128)(2,1)S(1)}, bf16[256,128]{1,0:T(8,128)(2,1)S(1)}, u32[]{:S(2)}, u32[]{:S(2)}) collective-permute-start(bf16[256,128]{1,0:T(8,128)(2,1)S(1)} %convolution_convert_fusion.1), channel_id=1, source_target_pairs={{0,2},{1,3},{2,0},{3,1},{4,6},{5,7},{6,4},{7,5},{8,10},{9,11},{10,... | collective-permute-start | bytes 196616 | tf_op jit(solution)/shard_map/ppermute | solution.py:37
  22.6 1.5 collective-permute-done.4
  26.5 2.1 %collective-permute-start.6 = (bf16[4,256,128]{2,1,0:T(8,128)(2,1)S(1)}, bf16[4,256,128]{2,1,0:T(8,128)(2,1)S(1)}, u32[]{:S(2)}, u32[]{:S(2)}) collective-permute-start(bf16[4,256,128]{2,1,0:T(8,128)(2,1)S(1)} %get-tuple-element.28), channel_id=1, source_target_pairs={{0,8},{1,9},{2,10},{3,11},{4,12},{5,13},{6,14},{7,15},{8,0},{9,1},... | collective-permute-start | bytes 786440 | tf_op jit(solution)/shard_map/ppermute | solution.py:37
  28.6 1.3 collective-permute-start.5
  29.8 9.6 %collective-permute-done.7 = bf16[4,256,128]{2,1,0:T(8,128)(2,1)S(1)} collective-permute-done((bf16[4,256,128]{2,1,0:T(8,128)(2,1)S(1)}, bf16[4,256,128]{2,1,0:T(8,128)(2,1)S(1)}, u32[]{:S(2)}, u32[]{:S(2)}) %collective-permute-start.7) | collective-permute-done | bytes 262176 | tf_op jit(solution)/shard_map/ppermute | solution.py:37
  40.3 3.0 %collective-permute-start.8 = (bf16[4,4,256,128]{3,2,1,0:T(8,128)(2,1)S(1)}, bf16[4,4,256,128]{3,2,1,0:T(8,128)(2,1)S(1)}, u32[]{:S(2)}, u32[]{:S(2)}) collective-permute-start(bf16[4,4,256,128]{3,2,1,0:T(8,128)(2,1)S(1)} %get-tuple-element.23), channel_id=1, source_target_pairs={{0,80},{1,81},{2,82},{3,83},{4,84},{5,85},{6,86},{7,87},{8,88},{9,... | collective-permute-start | bytes 3145736 | tf_op jit(solution)/shard_map/ppermute | solution.py:37
  43.2 12.3 %collective-permute-done.8 = bf16[4,4,256,128]{3,2,1,0:T(8,128)(2,1)S(1)} collective-permute-done((bf16[4,4,256,128]{3,2,1,0:T(8,128)(2,1)S(1)}, bf16[4,4,256,128]{3,2,1,0:T(8,128)(2,1)S(1)}, u32[]{:S(2)}, u32[]{:S(2)}) %collective-permute-start.8) | collective-permute-done | bytes 1048608 | tf_op jit(solution)/shard_map/ppermute | solution.py:37
  55.6 3.8 %collective-permute-start.11 = (bf16[2,4,256,128]{3,2,1,0:T(8,128)(2,1)S(1)}, bf16[2,4,256,128]{3,2,1,0:T(8,128)(2,1)S(1)}, u32[]{:S(2)}, u32[]{:S(2)}) collective-permute-start(bf16[2,4,256,128]{3,2,1,0:T(8,128)(2,1)S(1)} %slice.137), channel_id=1, source_target_pairs={{0,80},{1,81},{2,82},{3,83},{4,84},{5,85},{6,86},{7,87},{8,88},{9,... | collective-permute-start | bytes 1572872 | tf_op jit(solution)/shard_map/ppermute | solution.py:37
  59.5 6.6 %collective-permute-done.11 = bf16[2,4,256,128]{3,2,1,0:T(8,128)(2,1)S(1)} collective-permute-done((bf16[2,4,256,128]{3,2,1,0:T(8,128)(2,1)S(1)}, bf16[2,4,256,128]{3,2,1,0:T(8,128)(2,1)S(1)}, u32[]{:S(2)}, u32[]{:S(2)}) %collective-permute-start.11) | collective-permute-done | bytes 524320 | tf_op jit(solution)/shard_map/ppermute | solution.py:37
  66.1 3.8 %collective-permute-done.10 = bf16[2,4,256,128]{3,2,1,0:T(8,128)(2,1)S(1)} collective-permute-done((bf16[2,4,256,128]{3,2,1,0:T(8,128)(2,1)S(1)}, bf16[2,4,256,128]{3,2,1,0:T(8,128)(2,1)S(1)}, u32[]{:S(2)}, u32[]{:S(2)}) %collective-permute-start.10) | collective-permute-done | bytes 524320 | tf_op jit(solution)/shard_map/ppermute | solution.py:37
  70.0 2.3 %pad_maximum_fusion = bf16[4,4,4,256,128]{4,3,2,1,0:T(8,128)(2,1)} fusion(bf16[1,4,4,256,128]{4,3,2,1,0:T(8,128)(2,1)S(1)} %bitcast.120, bf16[1,4,4,256,128]{4,3,2,1,0:T(8,128)(2,1)S(1)} %maximum_bitcast_fusion, bf16[1,4,4,256,128]{4,3,2,1,0:T(8,128)(2,1)S(1)} %bitcast.119, bf16[1,4,4,256,128]{4,3,2,1,0:T(8,128)(2,1)S(1)} %get-tuple-element.22), kind=kLoop, calls=%fused_computation.1 | loop fusion | flops 6291456 | bytes 8388608 | tf_op jit(solution)/shard_map/stack | solution.py:56
  72.9 7.6 %shard_map.85 = f32[2,128,128]{2,1,0:T(8,128)} custom-call(s32[1]{0:T(128)} %bitcast.core_ref, s32[256]{0:T(256)} %copy-done.4, s32[8]{0:T(128)} %count_ref.3, bf16[4,2,32,128,128]{4,3,2,1,0:T(8,128)(2,1)} %bitcast.113, bf16[128,128,128]{2,1,0:T(8,128)(2,1)} %bitcast.16.proj_ref), custom_call_target="tpu_custom_call" | custom-call | tf_op jit(solution)/shard_map/pallas_call | solution.py:157
  80.5 7.7 %shard_map.86 = f32[2,128,128]{2,1,0:T(8,128)} custom-call(s32[1]{0:T(128)} %bitcast.17.core_ref, s32[256]{0:T(256)} %copy-done.4, s32[8]{0:T(128)} %count_ref.3, bf16[4,2,32,128,128]{4,3,2,1,0:T(8,128)(2,1)} %bitcast.114, bf16[128,128,128]{2,1,0:T(8,128)(2,1)} %collective-permute-done.12.proj_ref), custom_call_target="tpu_custom_call" | custom-call | tf_op jit(solution)/shard_map/pallas_call | solution.py:157
  92.2 14.9 %shard_map.87 = f32[128,128,128]{2,1,0:T(8,128)} custom-call(s32[1]{0:T(128)} %bitcast.core_ref, s32[512]{0:T(512)} %pad_add_fusion.where_ref, s32[16]{0:T(128)} %pad_add_fusion.1.count_ref, bf16[4,2,32,128,128]{4,3,2,1,0:T(8,128)(2,1)} %bitcast.115, bf16[4,2,32,128,128]{4,3,2,1,0:T(8,128)(2,1)} %collective-permute-done.13.other_ref, ...), custom_call_target="tpu_custom_call" | custom-call | tf_op jit(solution)/shard_map/pallas_call | solution.py:231
  107.1 4.5 %convert.31 = bf16[128,128,128]{2,1,0:T(8,128)(2,1)S(1)} convert(f32[128,128,128]{2,1,0:T(8,128)} %shard_map.87) | non-fusion elementwise | flops 2097152 | bytes 12582912 | tf_op jit(solution)/shard_map/convert.18
  112.2 1.7 collective-permute-start.15
  114.2 6.9 %collective-permute-done.17 = bf16[2,4,256,128]{3,2,1,0:T(8,128)(2,1)S(1)} collective-permute-done((bf16[2,4,256,128]{3,2,1,0:T(8,128)(2,1)S(1)}, bf16[2,4,256,128]{3,2,1,0:T(8,128)(2,1)S(1)}, u32[]{:S(2)}, u32[]{:S(2)}) %collective-permute-start.17) | collective-permute-done | bytes 524320 | tf_op jit(solution)/shard_map/ppermute | solution.py:37
  121.3 1.6 collective-permute-start.18
  123.7 12.5 %collective-permute-done.18 = bf16[4,4,256,128]{3,2,1,0:T(8,128)(2,1)S(1)} collective-permute-done((bf16[4,4,256,128]{3,2,1,0:T(8,128)(2,1)S(1)}, bf16[4,4,256,128]{3,2,1,0:T(8,128)(2,1)S(1)}, u32[]{:S(2)}, u32[]{:S(2)}) %collective-permute-start.18) | collective-permute-done | bytes 1048608 | tf_op jit(solution)/shard_map/ppermute | solution.py:37
  136.2 3.0 %collective-permute-done.16 = bf16[4,4,256,128]{3,2,1,0:T(8,128)(2,1)S(1)} collective-permute-done((bf16[4,4,256,128]{3,2,1,0:T(8,128)(2,1)S(1)}, bf16[4,4,256,128]{3,2,1,0:T(8,128)(2,1)S(1)}, u32[]{:S(2)}, u32[]{:S(2)}) %collective-permute-start.16) | collective-permute-done | bytes 1048608 | tf_op jit(solution)/shard_map/ppermute | solution.py:37
  139.7 1.4 collective-permute-start.21
  141.2 1.9 %collective-permute-start.20 = (bf16[4,256,128]{2,1,0:T(8,128)(2,1)S(1)}, bf16[4,256,128]{2,1,0:T(8,128)(2,1)S(1)}, u32[]{:S(2)}, u32[]{:S(2)}) collective-permute-start(bf16[4,256,128]{2,1,0:T(8,128)(2,1)S(1)} %get-tuple-element.21), channel_id=1, source_target_pairs={{0,12},{1,13},{2,14},{3,15},{4,0},{5,1},{6,2},{7,3},{8,4},{9,5},{1... | collective-permute-start | bytes 786440 | tf_op jit(solution)/shard_map/ppermute | solution.py:37
  143.8 6.7 %collective-permute-done.21 = bf16[4,256,128]{2,1,0:T(8,128)(2,1)S(1)} collective-permute-done((bf16[4,256,128]{2,1,0:T(8,128)(2,1)S(1)}, bf16[4,256,128]{2,1,0:T(8,128)(2,1)S(1)}, u32[]{:S(2)}, u32[]{:S(2)}) %collective-permute-start.21) | collective-permute-done | bytes 262176 | tf_op jit(solution)/shard_map/ppermute | solution.py:37
  150.6 4.2 %collective-permute-done.20 = bf16[4,256,128]{2,1,0:T(8,128)(2,1)S(1)} collective-permute-done((bf16[4,256,128]{2,1,0:T(8,128)(2,1)S(1)}, bf16[4,256,128]{2,1,0:T(8,128)(2,1)S(1)}, u32[]{:S(2)}, u32[]{:S(2)}) %collective-permute-start.20) | collective-permute-done | bytes 262176 | tf_op jit(solution)/shard_map/ppermute | solution.py:37
  155.1 2.0 %collective-permute-start.23 = (bf16[256,128]{1,0:T(8,128)(2,1)S(1)}, bf16[256,128]{1,0:T(8,128)(2,1)S(1)}, u32[]{:S(2)}, u32[]{:S(2)}) collective-permute-start(bf16[256,128]{1,0:T(8,128)(2,1)S(1)} %get-tuple-element.26), channel_id=1, source_target_pairs={{0,3},{1,0},{2,1},{3,2},{4,7},{5,4},{6,5},{7,6},{8,11},{9,8},{10,9... | collective-permute-start | bytes 196616 | tf_op jit(solution)/shard_map/ppermute | solution.py:37
  157.2 3.7 %collective-permute-done.24 = bf16[256,128]{1,0:T(8,128)(2,1)S(1)} collective-permute-done((bf16[256,128]{1,0:T(8,128)(2,1)S(1)}, bf16[256,128]{1,0:T(8,128)(2,1)S(1)}, u32[]{:S(2)}, u32[]{:S(2)}) %collective-permute-start.24) | collective-permute-done | bytes 65568 | tf_op jit(solution)/shard_map/ppermute | solution.py:37
  160.8 1.7 collective-permute-done.22
  163.8 4.6 %all-to-all-start.1 = ((f32[32,4,384]{2,1,0:T(4,128)}), f32[32,4,384]{2,1,0:T(4,128)S(1)}, u32[]{:S(2)}, u32[]{:S(2)}) async-start(f32[32,4,384]{2,1,0:T(4,128)} %pad_maximum_fusion.5), calls=%async_computation.1 | async-start | bytes 393216 | tf_op jit(solution)/shard_map/all_to_all | solution.py:345
  168.4 8.7 %all-to-all-done.1 = f32[32,4,384]{2,1,0:T(4,128)S(1)} async-done(((f32[32,4,384]{2,1,0:T(4,128)}), f32[32,4,384]{2,1,0:T(4,128)S(1)}, u32[]{:S(2)}, u32[]{:S(2)}) %all-to-all-start.1) | async-done | bytes 196640 | tf_op jit(solution)/shard_map/all_to_all | solution.py:345
  177.7 2.9 %collective-permute-start.25 = (f32[4,128]{1,0:T(4,128)S(1)}, f32[4,128]{1,0:T(4,128)S(1)}, u32[]{:S(2)}, u32[]{:S(2)}) collective-permute-start(f32[4,128]{1,0:T(4,128)S(1)} %slice_reduce_fusion), channel_id=1, source_target_pairs={{0,32},{32,0},{64,96},{96,64},{1,33},{33,1},{65,97},{97,65},{2,34}... | collective-permute-start | bytes 6152 | tf_op jit(solution)/shard_map/ppermute | solution.py:46
  (87 shorter events, 18.8 us)
Async XLA Ops:
  0.6 17.7 %copy-start = (bf16[128,128]{1,0:T(8,128)(2,1)S(1)}, bf16[128,128]{1,0:T(8,128)(2,1)}, u32[]{:S(2)}) copy-start(bf16[128,128]{1,0:T(8,128)(2,1)} %param.7) | copy-start | bytes 98308
  0.6 91.5 %collective-permute-start.13 = (bf16[4,2,32,128,128]{4,3,2,1,0:T(8,128)(2,1)}, bf16[4,2,32,128,128]{4,3,2,1,0:T(8,128)(2,1)}, u32[]{:S(2)}, u32[]{:S(2)}) collective-permute-start(bf16[4,2,32,128,128]{4,3,2,1,0:T(8,128)(2,1)} %bitcast.112), channel_id=1, source_target_pairs={{0,32},{32,0},{64,96},{96,64},{1,33},{33,1},{65,97},{97,65},{2,34}... | collective-permute-start | bytes 25165832 | tf_op jit(solution)/shard_map/ppermute | solution.py:41
  0.7 17.6 %all-to-all-start = ((bf16[4,32,256]{2,0,1:T(4,128)(2,1)}), bf16[4,32,256]{2,0,1:T(4,128)(2,1)S(1)}, u32[]{:S(2)}, u32[]{:S(2)}) async-start(bf16[4,32,256]{2,0,1:T(4,128)(2,1)} %bitcast.140), calls=%async_computation | async-start | bytes 131072 | tf_op jit(solution)/shard_map/all_to_all | solution.py:283
  10.0 8.6 %collective-permute-start = (s32[256]{0:T(256)}, s32[256]{0:T(256)S(1)}, u32[]{:S(2)}, u32[]{:S(2)}) collective-permute-start(s32[256]{0:T(256)} %param.9), channel_id=1, source_target_pairs={{0,32},{32,0},{64,96},{96,64},{1,33},{33,1},{65,97},{97,65},{2,34}... | collective-permute-start | bytes 3080 | tf_op jit(solution)/shard_map/ppermute | solution.py:41
  10.3 8.3 %collective-permute-start.1 = (s32[8]{0:T(128)}, s32[8]{0:T(128)S(1)}, u32[]{:S(2)}, u32[]{:S(2)}) collective-permute-start(s32[8]{0:T(128)} %count_ref.3), channel_id=1, source_target_pairs={{0,32},{32,0},{64,96},{96,64},{1,33},{33,1},{65,97},{97,65},{2,34}... | collective-permute-start | bytes 104 | tf_op jit(solution)/shard_map/ppermute | solution.py:41
  18.6 5.5 %collective-permute-start.4 = (bf16[256,128]{1,0:T(8,128)(2,1)S(1)}, bf16[256,128]{1,0:T(8,128)(2,1)S(1)}, u32[]{:S(2)}, u32[]{:S(2)}) collective-permute-start(bf16[256,128]{1,0:T(8,128)(2,1)S(1)} %convolution_convert_fusion.1), channel_id=1, source_target_pairs={{0,1},{1,2},{2,3},{3,0},{4,5},{5,6},{6,7},{7,4},{8,9},{9,10},{10,1... | collective-permute-start | bytes 196616 | tf_op jit(solution)/shard_map/ppermute | solution.py:37
  19.2 5.8 %collective-permute-start.3 = (bf16[256,128]{1,0:T(8,128)(2,1)S(1)}, bf16[256,128]{1,0:T(8,128)(2,1)S(1)}, u32[]{:S(2)}, u32[]{:S(2)}) collective-permute-start(bf16[256,128]{1,0:T(8,128)(2,1)S(1)} %convolution_convert_fusion.1), channel_id=1, source_target_pairs={{0,2},{1,3},{2,0},{3,1},{4,6},{5,7},{6,4},{7,5},{8,10},{9,11},{10,... | collective-permute-start | bytes 196616 | tf_op jit(solution)/shard_map/ppermute | solution.py:37
  21.5 4.3 %collective-permute-start.2 = (bf16[256,128]{1,0:T(8,128)(2,1)S(1)}, bf16[256,128]{1,0:T(8,128)(2,1)S(1)}, u32[]{:S(2)}, u32[]{:S(2)}) collective-permute-start(bf16[256,128]{1,0:T(8,128)(2,1)S(1)} %convolution_convert_fusion.1), channel_id=1, source_target_pairs={{0,3},{1,0},{2,1},{3,2},{4,7},{5,4},{6,5},{7,6},{8,11},{9,8},{10,9... | collective-permute-start | bytes 196616 | tf_op jit(solution)/shard_map/ppermute | solution.py:37
  25.8 13.7 %collective-permute-start.7 = (bf16[4,256,128]{2,1,0:T(8,128)(2,1)S(1)}, bf16[4,256,128]{2,1,0:T(8,128)(2,1)S(1)}, u32[]{:S(2)}, u32[]{:S(2)}) collective-permute-start(bf16[4,256,128]{2,1,0:T(8,128)(2,1)S(1)} %get-tuple-element.28), channel_id=1, source_target_pairs={{0,4},{1,5},{2,6},{3,7},{4,8},{5,9},{6,10},{7,11},{8,12},{9,13},{1... | collective-permute-start | bytes 786440 | tf_op jit(solution)/shard_map/ppermute | solution.py:37
  26.5 13.0 %collective-permute-start.6 = (bf16[4,256,128]{2,1,0:T(8,128)(2,1)S(1)}, bf16[4,256,128]{2,1,0:T(8,128)(2,1)S(1)}, u32[]{:S(2)}, u32[]{:S(2)}) collective-permute-start(bf16[4,256,128]{2,1,0:T(8,128)(2,1)S(1)} %get-tuple-element.28), channel_id=1, source_target_pairs={{0,8},{1,9},{2,10},{3,11},{4,12},{5,13},{6,14},{7,15},{8,0},{9,1},... | collective-permute-start | bytes 786440 | tf_op jit(solution)/shard_map/ppermute | solution.py:37
  28.6 11.5 %collective-permute-start.5 = (bf16[4,256,128]{2,1,0:T(8,128)(2,1)S(1)}, bf16[4,256,128]{2,1,0:T(8,128)(2,1)S(1)}, u32[]{:S(2)}, u32[]{:S(2)}) collective-permute-start(bf16[4,256,128]{2,1,0:T(8,128)(2,1)S(1)} %get-tuple-element.28), channel_id=1, source_target_pairs={{0,12},{1,13},{2,14},{3,15},{4,0},{5,1},{6,2},{7,3},{8,4},{9,5},{1... | collective-permute-start | bytes 786440 | tf_op jit(solution)/shard_map/ppermute | solution.py:37
  40.3 15.3 %collective-permute-start.8 = (bf16[4,4,256,128]{3,2,1,0:T(8,128)(2,1)S(1)}, bf16[4,4,256,128]{3,2,1,0:T(8,128)(2,1)S(1)}, u32[]{:S(2)}, u32[]{:S(2)}) collective-permute-start(bf16[4,4,256,128]{3,2,1,0:T(8,128)(2,1)S(1)} %get-tuple-element.23), channel_id=1, source_target_pairs={{0,80},{1,81},{2,82},{3,83},{4,84},{5,85},{6,86},{7,87},{8,88},{9,... | collective-permute-start | bytes 3145736 | tf_op jit(solution)/shard_map/ppermute | solution.py:37
  43.2 16.1 %collective-permute-start.9 = (bf16[4,4,256,128]{3,2,1,0:T(8,128)(2,1)S(1)}, bf16[4,4,256,128]{3,2,1,0:T(8,128)(2,1)S(1)}, u32[]{:S(2)}, u32[]{:S(2)}) collective-permute-start(bf16[4,4,256,128]{3,2,1,0:T(8,128)(2,1)S(1)} %get-tuple-element.23), channel_id=1, source_target_pairs={{0,16},{1,17},{2,18},{3,19},{4,20},{5,21},{6,22},{7,23},{8,24},{9,... | collective-permute-start | bytes 3145736 | tf_op jit(solution)/shard_map/ppermute | solution.py:37
  55.6 10.5 %collective-permute-start.11 = (bf16[2,4,256,128]{3,2,1,0:T(8,128)(2,1)S(1)}, bf16[2,4,256,128]{3,2,1,0:T(8,128)(2,1)S(1)}, u32[]{:S(2)}, u32[]{:S(2)}) collective-permute-start(bf16[2,4,256,128]{3,2,1,0:T(8,128)(2,1)S(1)} %slice.137), channel_id=1, source_target_pairs={{0,80},{1,81},{2,82},{3,83},{4,84},{5,85},{6,86},{7,87},{8,88},{9,... | collective-permute-start | bytes 1572872 | tf_op jit(solution)/shard_map/ppermute | solution.py:37
  59.4 10.5 %collective-permute-start.10 = (bf16[2,4,256,128]{3,2,1,0:T(8,128)(2,1)S(1)}, bf16[2,4,256,128]{3,2,1,0:T(8,128)(2,1)S(1)}, u32[]{:S(2)}, u32[]{:S(2)}) collective-permute-start(bf16[2,4,256,128]{3,2,1,0:T(8,128)(2,1)S(1)} %slice.136), channel_id=1, source_target_pairs={{0,16},{1,17},{2,18},{3,19},{4,20},{5,21},{6,22},{7,23},{8,24},{9,... | collective-permute-start | bytes 1572872 | tf_op jit(solution)/shard_map/ppermute | solution.py:37
  72.2 8.3 %collective-permute-start.12 = (bf16[128,128,128]{2,1,0:T(8,128)(2,1)}, bf16[128,128,128]{2,1,0:T(8,128)(2,1)}, u32[]{:S(2)}, u32[]{:S(2)}) collective-permute-start(bf16[128,128,128]{2,1,0:T(8,128)(2,1)} %bitcast.16.proj_ref), channel_id=1, source_target_pairs={{0,32},{32,0},{64,96},{96,64},{1,33},{33,1},{65,97},{97,65},{2,34}... | collective-permute-start | bytes 12582920 | tf_op jit(solution)/shard_map/ppermute | solution.py:41
  90.0 1.5 collective-permute-start.14
  111.9 9.2 %collective-permute-start.17 = (bf16[2,4,256,128]{3,2,1,0:T(8,128)(2,1)S(1)}, bf16[2,4,256,128]{3,2,1,0:T(8,128)(2,1)S(1)}, u32[]{:S(2)}, u32[]{:S(2)}) collective-permute-start(bf16[2,4,256,128]{3,2,1,0:T(8,128)(2,1)S(1)} %bitcast.126), channel_id=1, source_target_pairs={{0,80},{1,81},{2,82},{3,83},{4,84},{5,85},{6,86},{7,87},{8,88},{9,... | collective-permute-start | bytes 1572872 | tf_op jit(solution)/shard_map/ppermute | solution.py:37
  112.2 10.7 %collective-permute-start.15 = (bf16[2,4,256,128]{3,2,1,0:T(8,128)(2,1)S(1)}, bf16[2,4,256,128]{3,2,1,0:T(8,128)(2,1)S(1)}, u32[]{:S(2)}, u32[]{:S(2)}) collective-permute-start(bf16[2,4,256,128]{3,2,1,0:T(8,128)(2,1)S(1)} %bitcast.125), channel_id=1, source_target_pairs={{0,16},{1,17},{2,18},{3,19},{4,20},{5,21},{6,22},{7,23},{8,24},{9,... | collective-permute-start | bytes 1572872 | tf_op jit(solution)/shard_map/ppermute | solution.py:37
  121.3 14.9 %collective-permute-start.18 = (bf16[4,4,256,128]{3,2,1,0:T(8,128)(2,1)S(1)}, bf16[4,4,256,128]{3,2,1,0:T(8,128)(2,1)S(1)}, u32[]{:S(2)}, u32[]{:S(2)}) collective-permute-start(bf16[4,4,256,128]{3,2,1,0:T(8,128)(2,1)S(1)} %pad_maximum_fusion.3), channel_id=1, source_target_pairs={{0,80},{1,81},{2,82},{3,83},{4,84},{5,85},{6,86},{7,87},{8,88},{9,... | collective-permute-start | bytes 3145736 | tf_op jit(solution)/shard_map/ppermute | solution.py:37
  122.9 16.3 %slice-start = ((f32[128,128,128]{2,1,0:T(8,128)}), f32[32,128,128]{2,1,0:T(8,128)S(1)}, s32[]{:S(2)}) async-start(f32[128,128,128]{2,1,0:T(8,128)} %shard_map.87), calls=%async_computation.2 | async-start | bytes 4194304 | tf_op jit(solution)/shard_map/slice | solution.py:83
  123.1 16.1 %collective-permute-start.16 = (bf16[4,4,256,128]{3,2,1,0:T(8,128)(2,1)S(1)}, bf16[4,4,256,128]{3,2,1,0:T(8,128)(2,1)S(1)}, u32[]{:S(2)}, u32[]{:S(2)}) collective-permute-start(bf16[4,4,256,128]{3,2,1,0:T(8,128)(2,1)S(1)} %pad_maximum_fusion.2), channel_id=1, source_target_pairs={{0,16},{1,17},{2,18},{3,19},{4,20},{5,21},{6,22},{7,23},{8,24},{9,... | collective-permute-start | bytes 3145736 | tf_op jit(solution)/shard_map/ppermute | solution.py:37
  139.7 10.8 %collective-permute-start.21 = (bf16[4,256,128]{2,1,0:T(8,128)(2,1)S(1)}, bf16[4,256,128]{2,1,0:T(8,128)(2,1)S(1)}, u32[]{:S(2)}, u32[]{:S(2)}) collective-permute-start(bf16[4,256,128]{2,1,0:T(8,128)(2,1)S(1)} %get-tuple-element.20), channel_id=1, source_target_pairs={{0,8},{1,9},{2,10},{3,11},{4,12},{5,13},{6,14},{7,15},{8,0},{9,1},... | collective-permute-start | bytes 786440 | tf_op jit(solution)/shard_map/ppermute | solution.py:37
  141.2 13.6 %collective-permute-start.20 = (bf16[4,256,128]{2,1,0:T(8,128)(2,1)S(1)}, bf16[4,256,128]{2,1,0:T(8,128)(2,1)S(1)}, u32[]{:S(2)}, u32[]{:S(2)}) collective-permute-start(bf16[4,256,128]{2,1,0:T(8,128)(2,1)S(1)} %get-tuple-element.21), channel_id=1, source_target_pairs={{0,12},{1,13},{2,14},{3,15},{4,0},{5,1},{6,2},{7,3},{8,4},{9,5},{1... | collective-permute-start | bytes 786440 | tf_op jit(solution)/shard_map/ppermute | solution.py:37
  143.1 11.7 %collective-permute-start.19 = (bf16[4,256,128]{2,1,0:T(8,128)(2,1)S(1)}, bf16[4,256,128]{2,1,0:T(8,128)(2,1)S(1)}, u32[]{:S(2)}, u32[]{:S(2)}) collective-permute-start(bf16[4,256,128]{2,1,0:T(8,128)(2,1)S(1)} %get-tuple-element.19), channel_id=1, source_target_pairs={{0,4},{1,5},{2,6},{3,7},{4,8},{5,9},{6,10},{7,11},{8,12},{9,13},{1... | collective-permute-start | bytes 786440 | tf_op jit(solution)/shard_map/ppermute | solution.py:37
  155.0 5.8 %collective-permute-start.24 = (bf16[256,128]{1,0:T(8,128)(2,1)S(1)}, bf16[256,128]{1,0:T(8,128)(2,1)S(1)}, u32[]{:S(2)}, u32[]{:S(2)}) collective-permute-start(bf16[256,128]{1,0:T(8,128)(2,1)S(1)} %get-tuple-element.25), channel_id=1, source_target_pairs={{0,2},{1,3},{2,0},{3,1},{4,6},{5,7},{6,4},{7,5},{8,10},{9,11},{10,... | collective-permute-start | bytes 196616 | tf_op jit(solution)/shard_map/ppermute | solution.py:37
  155.1 5.8 %collective-permute-start.23 = (bf16[256,128]{1,0:T(8,128)(2,1)S(1)}, bf16[256,128]{1,0:T(8,128)(2,1)S(1)}, u32[]{:S(2)}, u32[]{:S(2)}) collective-permute-start(bf16[256,128]{1,0:T(8,128)(2,1)S(1)} %get-tuple-element.26), channel_id=1, source_target_pairs={{0,3},{1,0},{2,1},{3,2},{4,7},{5,4},{6,5},{7,6},{8,11},{9,8},{10,9... | collective-permute-start | bytes 196616 | tf_op jit(solution)/shard_map/ppermute | solution.py:37
  157.1 5.5 %collective-permute-start.22 = (bf16[256,128]{1,0:T(8,128)(2,1)S(1)}, bf16[256,128]{1,0:T(8,128)(2,1)S(1)}, u32[]{:S(2)}, u32[]{:S(2)}) collective-permute-start(bf16[256,128]{1,0:T(8,128)(2,1)S(1)} %get-tuple-element.24), channel_id=1, source_target_pairs={{0,1},{1,2},{2,3},{3,0},{4,5},{5,6},{6,7},{7,4},{8,9},{9,10},{10,1... | collective-permute-start | bytes 196616 | tf_op jit(solution)/shard_map/ppermute | solution.py:37
  163.8 13.3 %all-to-all-start.1 = ((f32[32,4,384]{2,1,0:T(4,128)}), f32[32,4,384]{2,1,0:T(4,128)S(1)}, u32[]{:S(2)}, u32[]{:S(2)}) async-start(f32[32,4,384]{2,1,0:T(4,128)} %pad_maximum_fusion.5), calls=%async_computation.1 | async-start | bytes 393216 | tf_op jit(solution)/shard_map/all_to_all | solution.py:345
  177.1 4.6 %collective-permute-start.27 = (f32[4,128]{1,0:T(4,128)S(1)}, f32[4,128]{1,0:T(4,128)S(1)}, u32[]{:S(2)}, u32[]{:S(2)}) collective-permute-start(f32[4,128]{1,0:T(4,128)S(1)} %slice_reduce_fusion), channel_id=1, source_target_pairs={{0,96},{32,64},{64,32},{96,0},{1,97},{33,65},{65,33},{97,1},{2,98}... | collective-permute-start | bytes 6152 | tf_op jit(solution)/shard_map/ppermute | solution.py:46
  177.2 5.2 %collective-permute-start.26 = (f32[4,128]{1,0:T(4,128)S(1)}, f32[4,128]{1,0:T(4,128)S(1)}, u32[]{:S(2)}, u32[]{:S(2)}) collective-permute-start(f32[4,128]{1,0:T(4,128)S(1)} %slice_reduce_fusion), channel_id=1, source_target_pairs={{0,64},{32,96},{64,0},{96,32},{1,65},{33,97},{65,1},{97,33},{2,66}... | collective-permute-start | bytes 6152 | tf_op jit(solution)/shard_map/ppermute | solution.py:46
  177.7 4.8 %collective-permute-start.25 = (f32[4,128]{1,0:T(4,128)S(1)}, f32[4,128]{1,0:T(4,128)S(1)}, u32[]{:S(2)}, u32[]{:S(2)}) collective-permute-start(f32[4,128]{1,0:T(4,128)S(1)} %slice_reduce_fusion), channel_id=1, source_target_pairs={{0,32},{32,0},{64,96},{96,64},{1,33},{33,1},{65,97},{97,65},{2,34}... | collective-permute-start | bytes 6152 | tf_op jit(solution)/shard_map/ppermute | solution.py:46
  (6 other events, 36.3 us)

commit v15 on v12

--- a/solution.py
+++ b/solution.py
@@ -294,7 +294,7 @@
     )
     sibling_spots = buffer_spots(sibling_col, blk_id, feat_id, block_tiles, tile_rows)
     gathered = gather_phase_direct(projected, 0)
-    gathered = gather_phase_direct(gathered, 1)
+    gathered = gather_phase(gathered, 1)
     gathered = gather_phase(gathered, 2)
     own_buffer = gathered.reshape(buffer_tiles, tile_size, hidden_width)
     other_buffer = sibling(own_buffer)
@@ -324,7 +324,7 @@
     total = reduce_phase(
         total.reshape(RING, RING, RING, rows_own, hidden_width), 2, jnp.bfloat16
     )
-    total = reduce_phase_direct(total, 1, jnp.bfloat16)
+    total = reduce_phase(total, 1, jnp.bfloat16)
     total = reduce_phase_direct(total, 0, jnp.bfloat16)
     grad_hidden = (
         total.reshape(tile_rows, hidden_width, tile_size)

time: 182 us -> 183 us (level)
  blocking collectives: 14.6 us -> 12.7 us
    all_to_all x1, blocking collectives: 14.6 us -> 12.7 us  [body(): lax.all_to_all(outgoing, 'feat', split_axis=0, concat_axis=0, tiled=True)]
    ppermute x20 -> x22, starting transfers between devices: 25.9 us -> 27.7 us  [ring_shift(): return lax.ppermute(block, BOTH, route)]
    ppermute x20 -> x22, waiting for transfers between devices: 69.9 us -> 71.3 us  [ring_shift(): return lax.ppermute(block, BOTH, route)]
  transfers between devices with their start and end apart: 28 -> 30, of which waited for: 21 -> 21; matrix products, arithmetic and copies ran while one was open for 6% -> 6% of each run, Pallas kernels for 8% -> 8%
where the time goes in v15:
time: 183 us; the launch traced here: 182 us
  waiting for transfers between devices  84 us (46%)
  starting transfers between devices  39.3 us (21%)
  Pallas kernels  30.2 us (17%)
  blocking collectives  12.7 us (7%)
  other arithmetic  7.78 us (4%)
  local copies, waits for them, and re-layouts  6.56 us (4%)
    ppermute x22, waiting for transfers between devices, ring_shift(): return lax.ppermute(block, BOTH, route)  71.3 us
    ppermute x22, starting transfers between devices, ring_shift(): return lax.ppermute(block, BOTH, route)  27.7 us
    pallas_call x2, Pallas kernels, aggregate_pair(): pl.pallas_call(aggregate_kernel, grid_spec=grid_spec, out_shape=jax.Shape...  15.3 us
    pallas_call x1, Pallas kernels, spread_pair(): pl.pallas_call(kernel, grid_spec=grid_spec, out_shape=jax.ShapeDtypeStruc...  14.9 us
    all_to_all x1, blocking collectives, body(): lax.all_to_all(outgoing, 'feat', split_axis=0, concat_axis=0, tiled=True)  12.7 us
    all_to_all x1, starting transfers between devices, body(): lax.all_to_all(features_t, 'feat', split_axis=1, concat_axis=0, tiled=True)  9.27 us
    all_to_all x1, waiting for transfers between devices, body(): lax.all_to_all(features_t, 'feat', split_axis=1, concat_axis=0, tiled=True)  7.74 us
    slice x2, local copies, waits for them, and re-layouts, term(): return total[k]  5.03 us
  transfers between devices with their start and end apart: 30, of which 21 were waited for; matrix products, arithmetic and copies ran while one was open for 6% of the time, Pallas kernels for 8%

profile of v15, /device:TPU:0, one launch (start us, length us, event | category | flops | bytes accessed | tf_op | source)
XLA Modules:
  0.0 182.1 jit_solution(3533838814372591781)
XLA Ops:
  0.7 9.3 %all-to-all-start = ((bf16[4,32,256]{2,0,1:T(4,128)(2,1)}), bf16[4,32,256]{2,0,1:T(4,128)(2,1)S(1)}, u32[]{:S(2)}, u32[]{:S(2)}) async-start(bf16[4,32,256]{2,0,1:T(4,128)(2,1)} %bitcast.126), calls=%async_computation | async-start | bytes 131072 | tf_op jit(solution)/shard_map/all_to_all | solution.py:287
  10.6 7.7 %all-to-all-done = bf16[4,32,256]{2,0,1:T(4,128)(2,1)S(1)} async-done(((bf16[4,32,256]{2,0,1:T(4,128)(2,1)}), bf16[4,32,256]{2,0,1:T(4,128)(2,1)S(1)}, u32[]{:S(2)}, u32[]{:S(2)}) %all-to-all-start) | async-done | bytes 65568 | tf_op jit(solution)/shard_map/all_to_all | solution.py:287
  19.2 2.3 %collective-permute-start.3 = (bf16[256,128]{1,0:T(8,128)(2,1)S(1)}, bf16[256,128]{1,0:T(8,128)(2,1)S(1)}, u32[]{:S(2)}, u32[]{:S(2)}) collective-permute-start(bf16[256,128]{1,0:T(8,128)(2,1)S(1)} %convolution_convert_fusion.1), channel_id=1, source_target_pairs={{0,2},{1,3},{2,0},{3,1},{4,6},{5,7},{6,4},{7,5},{8,10},{9,11},{10,... | collective-permute-start | bytes 196616 | tf_op jit(solution)/shard_map/ppermute | solution.py:37
  27.9 4.7 %collective-permute-done.5 = bf16[4,256,128]{2,1,0:T(8,128)(2,1)S(1)} collective-permute-done((bf16[4,256,128]{2,1,0:T(8,128)(2,1)S(1)}, bf16[4,256,128]{2,1,0:T(8,128)(2,1)S(1)}, u32[]{:S(2)}, u32[]{:S(2)}) %collective-permute-start.5) | collective-permute-done | bytes 262176 | tf_op jit(solution)/shard_map/ppermute | solution.py:37
  32.6 2.7 %collective-permute-start.8 = (bf16[4,128,128]{2,1,0:T(8,128)(2,1)S(1)}, bf16[4,128,128]{2,1,0:T(8,128)(2,1)S(1)}, u32[]{:S(2)}, u32[]{:S(2)}) collective-permute-start(bf16[4,128,128]{2,1,0:T(8,128)(2,1)S(1)} %slice.137), channel_id=1, source_target_pairs={{0,12},{1,13},{2,14},{3,15},{4,0},{5,1},{6,2},{7,3},{8,4},{9,5},{1... | collective-permute-start | bytes 393224 | tf_op jit(solution)/shard_map/ppermute | solution.py:37
  35.4 2.4 %collective-permute-done.8 = bf16[4,128,128]{2,1,0:T(8,128)(2,1)S(1)} collective-permute-done((bf16[4,128,128]{2,1,0:T(8,128)(2,1)S(1)}, bf16[4,128,128]{2,1,0:T(8,128)(2,1)S(1)}, u32[]{:S(2)}, u32[]{:S(2)}) %collective-permute-start.8) | collective-permute-done | bytes 131104 | tf_op jit(solution)/shard_map/ppermute | solution.py:37
  37.8 3.7 %collective-permute-done.7 = bf16[4,128,128]{2,1,0:T(8,128)(2,1)S(1)} collective-permute-done((bf16[4,128,128]{2,1,0:T(8,128)(2,1)S(1)}, bf16[4,128,128]{2,1,0:T(8,128)(2,1)S(1)}, u32[]{:S(2)}, u32[]{:S(2)}) %collective-permute-start.7) | collective-permute-done | bytes 131104 | tf_op jit(solution)/shard_map/ppermute | solution.py:37
  41.8 3.0 %collective-permute-start.9 = (bf16[4,4,256,128]{3,2,1,0:T(8,128)(2,1)S(1)}, bf16[4,4,256,128]{3,2,1,0:T(8,128)(2,1)S(1)}, u32[]{:S(2)}, u32[]{:S(2)}) collective-permute-start(bf16[4,4,256,128]{3,2,1,0:T(8,128)(2,1)S(1)} %get-tuple-element.19), channel_id=1, source_target_pairs={{0,80},{1,81},{2,82},{3,83},{4,84},{5,85},{6,86},{7,87},{8,88},{9,... | collective-permute-start | bytes 3145736 | tf_op jit(solution)/shard_map/ppermute | solution.py:37
  44.7 12.3 %collective-permute-done.9 = bf16[4,4,256,128]{3,2,1,0:T(8,128)(2,1)S(1)} collective-permute-done((bf16[4,4,256,128]{3,2,1,0:T(8,128)(2,1)S(1)}, bf16[4,4,256,128]{3,2,1,0:T(8,128)(2,1)S(1)}, u32[]{:S(2)}, u32[]{:S(2)}) %collective-permute-start.9) | collective-permute-done | bytes 1048608 | tf_op jit(solution)/shard_map/ppermute | solution.py:37
  57.1 3.8 %collective-permute-start.12 = (bf16[4,4,128,128]{3,2,1,0:T(8,128)(2,1)S(1)}, bf16[4,4,128,128]{3,2,1,0:T(8,128)(2,1)S(1)}, u32[]{:S(2)}, u32[]{:S(2)}) collective-permute-start(bf16[4,4,128,128]{3,2,1,0:T(8,128)(2,1)S(1)} %slice.139), channel_id=1, source_target_pairs={{0,80},{1,81},{2,82},{3,83},{4,84},{5,85},{6,86},{7,87},{8,88},{9,... | collective-permute-start | bytes 1572872 | tf_op jit(solution)/shard_map/ppermute | solution.py:37
  61.0 6.6 %collective-permute-done.12 = bf16[4,4,128,128]{3,2,1,0:T(8,128)(2,1)S(1)} collective-permute-done((bf16[4,4,128,128]{3,2,1,0:T(8,128)(2,1)S(1)}, bf16[4,4,128,128]{3,2,1,0:T(8,128)(2,1)S(1)}, u32[]{:S(2)}, u32[]{:S(2)}) %collective-permute-start.12) | collective-permute-done | bytes 524320 | tf_op jit(solution)/shard_map/ppermute | solution.py:37
  67.6 3.8 %collective-permute-done.11 = bf16[4,4,128,128]{3,2,1,0:T(8,128)(2,1)S(1)} collective-permute-done((bf16[4,4,128,128]{3,2,1,0:T(8,128)(2,1)S(1)}, bf16[4,4,128,128]{3,2,1,0:T(8,128)(2,1)S(1)}, u32[]{:S(2)}, u32[]{:S(2)}) %collective-permute-start.11) | collective-permute-done | bytes 524320 | tf_op jit(solution)/shard_map/ppermute | solution.py:37
  71.5 2.3 %pad_maximum_fusion = bf16[4,4,4,256,128]{4,3,2,1,0:T(8,128)(2,1)} fusion(bf16[1,4,4,256,128]{4,3,2,1,0:T(8,128)(2,1)S(1)} %bitcast.111, bf16[1,4,4,256,128]{4,3,2,1,0:T(8,128)(2,1)S(1)} %maximum_bitcast_fusion, bf16[1,4,4,256,128]{4,3,2,1,0:T(8,128)(2,1)S(1)} %bitcast.110, bf16[1,4,4,256,128]{4,3,2,1,0:T(8,128)(2,1)S(1)} %get-tuple-element.18), kind=kLoop, calls=%fused_computation | loop fusion | flops 6291456 | bytes 8388608 | tf_op jit(solution)/shard_map/stack | solution.py:56
  74.4 7.6 %shard_map.85 = f32[2,128,128]{2,1,0:T(8,128)} custom-call(s32[1]{0:T(128)} %bitcast.core_ref, s32[256]{0:T(256)} %copy-done.3, s32[8]{0:T(128)} %count_ref.3, bf16[4,2,32,128,128]{4,3,2,1,0:T(8,128)(2,1)} %bitcast.101, bf16[128,128,128]{2,1,0:T(8,128)(2,1)} %bitcast.16.proj_ref), custom_call_target="tpu_custom_call" | custom-call | tf_op jit(solution)/shard_map/pallas_call | solution.py:161
  82.0 7.7 %shard_map.86 = f32[2,128,128]{2,1,0:T(8,128)} custom-call(s32[1]{0:T(128)} %bitcast.17.core_ref, s32[256]{0:T(256)} %copy-done.3, s32[8]{0:T(128)} %count_ref.3, bf16[4,2,32,128,128]{4,3,2,1,0:T(8,128)(2,1)} %bitcast.102, bf16[128,128,128]{2,1,0:T(8,128)(2,1)} %collective-permute-done.13.proj_ref), custom_call_target="tpu_custom_call" | custom-call | tf_op jit(solution)/shard_map/pallas_call | solution.py:161
  93.6 14.9 %shard_map.87 = f32[128,128,128]{2,1,0:T(8,128)} custom-call(s32[1]{0:T(128)} %bitcast.core_ref, s32[512]{0:T(512)} %pad_add_fusion.where_ref, s32[16]{0:T(128)} %pad_add_fusion.1.count_ref, bf16[4,2,32,128,128]{4,3,2,1,0:T(8,128)(2,1)} %bitcast.103, bf16[4,2,32,128,128]{4,3,2,1,0:T(8,128)(2,1)} %collective-permute-done.14.other_ref, ...), custom_call_target="tpu_custom_call" | custom-call | tf_op jit(solution)/shard_map/pallas_call | solution.py:235
  108.6 1.7 slice.207
  110.5 2.0 %collective-permute-start.16 = (bf16[4,4,128,128]{3,2,1,0:T(8,128)(2,1)S(1)}, bf16[4,4,128,128]{3,2,1,0:T(8,128)(2,1)S(1)}, u32[]{:S(2)}, u32[]{:S(2)}) collective-permute-start(bf16[4,4,128,128]{3,2,1,0:T(8,128)(2,1)S(1)} %get-tuple-element.16), channel_id=1, source_target_pairs={{0,16},{1,17},{2,18},{3,19},{4,20},{5,21},{6,22},{7,23},{8,24},{9,... | collective-permute-start | bytes 1572872 | tf_op jit(solution)/shard_map/ppermute | solution.py:37
  112.5 3.3 %fusion.40 = (f32[32,128,128]{2,1,0:T(8,128)S(1)}, f32[32,128,128]{2,1,0:T(8,128)S(1)}, f32[32,128,128]{2,1,0:T(8,128)S(1)}) fusion(f32[128,128,128]{2,1,0:T(8,128)} %shard_map.87), kind=kLoop, calls=%fused_computation.150 | loop fusion | bytes 12582912 | tf_op jit(solution)/shard_map/slice | solution.py:83
  116.0 3.7 %collective-permute-done.18 = bf16[4,4,128,128]{3,2,1,0:T(8,128)(2,1)S(1)} collective-permute-done((bf16[4,4,128,128]{3,2,1,0:T(8,128)(2,1)S(1)}, bf16[4,4,128,128]{3,2,1,0:T(8,128)(2,1)S(1)}, u32[]{:S(2)}, u32[]{:S(2)}) %collective-permute-start.18) | collective-permute-done | bytes 524320 | tf_op jit(solution)/shard_map/ppermute | solution.py:37
  122.3 12.5 %collective-permute-done.19 = bf16[4,4,256,128]{3,2,1,0:T(8,128)(2,1)S(1)} collective-permute-done((bf16[4,4,256,128]{3,2,1,0:T(8,128)(2,1)S(1)}, bf16[4,4,256,128]{3,2,1,0:T(8,128)(2,1)S(1)}, u32[]{:S(2)}, u32[]{:S(2)}) %collective-permute-start.19) | collective-permute-done | bytes 1048608 | tf_op jit(solution)/shard_map/ppermute | solution.py:37
  134.8 2.7 %collective-permute-done.17 = bf16[4,4,256,128]{3,2,1,0:T(8,128)(2,1)S(1)} collective-permute-done((bf16[4,4,256,128]{3,2,1,0:T(8,128)(2,1)S(1)}, bf16[4,4,256,128]{3,2,1,0:T(8,128)(2,1)S(1)}, u32[]{:S(2)}, u32[]{:S(2)}) %collective-permute-start.17) | collective-permute-done | bytes 1048608 | tf_op jit(solution)/shard_map/ppermute | solution.py:37
  138.1 2.1 %collective-permute-start.20 = (bf16[4,128,128]{2,1,0:T(8,128)(2,1)S(1)}, bf16[4,128,128]{2,1,0:T(8,128)(2,1)S(1)}, u32[]{:S(2)}, u32[]{:S(2)}) collective-permute-start(bf16[4,128,128]{2,1,0:T(8,128)(2,1)S(1)} %get-tuple-element.23), channel_id=1, source_target_pairs={{0,4},{1,5},{2,6},{3,7},{4,8},{5,9},{6,10},{7,11},{8,12},{9,13},{1... | collective-permute-start | bytes 393224 | tf_op jit(solution)/shard_map/ppermute | solution.py:37
  140.2 3.6 %collective-permute-done.22 = bf16[4,128,128]{2,1,0:T(8,128)(2,1)S(1)} collective-permute-done((bf16[4,128,128]{2,1,0:T(8,128)(2,1)S(1)}, bf16[4,128,128]{2,1,0:T(8,128)(2,1)S(1)}, u32[]{:S(2)}, u32[]{:S(2)}) %collective-permute-start.22) | collective-permute-done | bytes 131104 | tf_op jit(solution)/shard_map/ppermute | solution.py:37
  143.9 1.6 collective-permute-start.23
  146.1 5.7 %collective-permute-done.23 = bf16[4,256,128]{2,1,0:T(8,128)(2,1)S(1)} collective-permute-done((bf16[4,256,128]{2,1,0:T(8,128)(2,1)S(1)}, bf16[4,256,128]{2,1,0:T(8,128)(2,1)S(1)}, u32[]{:S(2)}, u32[]{:S(2)}) %collective-permute-start.23) | collective-permute-done | bytes 262176 | tf_op jit(solution)/shard_map/ppermute | solution.py:37
  151.9 2.8 %collective-permute-done.21 = bf16[4,256,128]{2,1,0:T(8,128)(2,1)S(1)} collective-permute-done((bf16[4,256,128]{2,1,0:T(8,128)(2,1)S(1)}, bf16[4,256,128]{2,1,0:T(8,128)(2,1)S(1)}, u32[]{:S(2)}, u32[]{:S(2)}) %collective-permute-start.21) | collective-permute-done | bytes 262176 | tf_op jit(solution)/shard_map/ppermute | solution.py:37
  154.8 1.8 collective-permute-start.26
  156.6 1.6 collective-permute-start.25
  158.3 2.7 %collective-permute-done.24 = bf16[256,128]{1,0:T(8,128)(2,1)S(1)} collective-permute-done((bf16[256,128]{1,0:T(8,128)(2,1)S(1)}, bf16[256,128]{1,0:T(8,128)(2,1)S(1)}, u32[]{:S(2)}, u32[]{:S(2)}) %collective-permute-start.24) | collective-permute-done | bytes 65568 | tf_op jit(solution)/shard_map/ppermute | solution.py:37
  162.4 12.7 %all_to_all.24 = f32[32,4,384]{2,1,0:T(4,128)S(1)} all-to-all(f32[32,4,384]{2,1,0:T(4,128)S(1)} %pad_maximum_fusion.7), channel_id=1, replica_groups=mesh['blk'=4,'feat'=32] {'feat'}, dimensions={0} | all-to-all | bytes 393216 | tf_op jit(solution)/shard_map/all_to_all | solution.py:349
  178.0 3.5 %collective-permute-done.28 = f32[4,128]{1,0:T(4,128)S(1)} collective-permute-done((f32[4,128]{1,0:T(4,128)S(1)}, f32[4,128]{1,0:T(4,128)S(1)}, u32[]{:S(2)}, u32[]{:S(2)}) %collective-permute-start.28) | collective-permute-done | bytes 2080 | tf_op jit(solution)/shard_map/ppermute | solution.py:46
  (94 shorter events, 22.3 us)
Async XLA Ops:
  0.6 17.7 %copy-start = (bf16[128,128]{1,0:T(8,128)(2,1)S(1)}, bf16[128,128]{1,0:T(8,128)(2,1)}, u32[]{:S(2)}) copy-start(bf16[128,128]{1,0:T(8,128)(2,1)} %param.7) | copy-start | bytes 98308
  0.6 93.0 %collective-permute-start.14 = (bf16[4,2,32,128,128]{4,3,2,1,0:T(8,128)(2,1)}, bf16[4,2,32,128,128]{4,3,2,1,0:T(8,128)(2,1)}, u32[]{:S(2)}, u32[]{:S(2)}) collective-permute-start(bf16[4,2,32,128,128]{4,3,2,1,0:T(8,128)(2,1)} %bitcast.100), channel_id=1, source_target_pairs={{0,32},{32,0},{64,96},{96,64},{1,33},{33,1},{65,97},{97,65},{2,34}... | collective-permute-start | bytes 25165832 | tf_op jit(solution)/shard_map/ppermute | solution.py:41
  0.7 17.6 %all-to-all-start = ((bf16[4,32,256]{2,0,1:T(4,128)(2,1)}), bf16[4,32,256]{2,0,1:T(4,128)(2,1)S(1)}, u32[]{:S(2)}, u32[]{:S(2)}) async-start(bf16[4,32,256]{2,0,1:T(4,128)(2,1)} %bitcast.126), calls=%async_computation | async-start | bytes 131072 | tf_op jit(solution)/shard_map/all_to_all | solution.py:287
  10.0 8.6 %collective-permute-start.1 = (s32[8]{0:T(128)}, s32[8]{0:T(128)S(1)}, u32[]{:S(2)}, u32[]{:S(2)}) collective-permute-start(s32[8]{0:T(128)} %count_ref.3), channel_id=1, source_target_pairs={{0,32},{32,0},{64,96},{96,64},{1,33},{33,1},{65,97},{97,65},{2,34}... | collective-permute-start | bytes 104 | tf_op jit(solution)/shard_map/ppermute | solution.py:41
  10.3 8.3 %collective-permute-start = (s32[256]{0:T(256)}, s32[256]{0:T(256)S(1)}, u32[]{:S(2)}, u32[]{:S(2)}) collective-permute-start(s32[256]{0:T(256)} %param.9), channel_id=1, source_target_pairs={{0,32},{32,0},{64,96},{96,64},{1,33},{33,1},{65,97},{97,65},{2,34}... | collective-permute-start | bytes 3080 | tf_op jit(solution)/shard_map/ppermute | solution.py:41
  18.6 5.5 %collective-permute-start.4 = (bf16[256,128]{1,0:T(8,128)(2,1)S(1)}, bf16[256,128]{1,0:T(8,128)(2,1)S(1)}, u32[]{:S(2)}, u32[]{:S(2)}) collective-permute-start(bf16[256,128]{1,0:T(8,128)(2,1)S(1)} %convolution_convert_fusion.1), channel_id=1, source_target_pairs={{0,1},{1,2},{2,3},{3,0},{4,5},{5,6},{6,7},{7,4},{8,9},{9,10},{10,1... | collective-permute-start | bytes 196616 | tf_op jit(solution)/shard_map/ppermute | solution.py:37
  19.2 5.8 %collective-permute-start.3 = (bf16[256,128]{1,0:T(8,128)(2,1)S(1)}, bf16[256,128]{1,0:T(8,128)(2,1)S(1)}, u32[]{:S(2)}, u32[]{:S(2)}) collective-permute-start(bf16[256,128]{1,0:T(8,128)(2,1)S(1)} %convolution_convert_fusion.1), channel_id=1, source_target_pairs={{0,2},{1,3},{2,0},{3,1},{4,6},{5,7},{6,4},{7,5},{8,10},{9,11},{10,... | collective-permute-start | bytes 196616 | tf_op jit(solution)/shard_map/ppermute | solution.py:37
  21.5 4.3 %collective-permute-start.2 = (bf16[256,128]{1,0:T(8,128)(2,1)S(1)}, bf16[256,128]{1,0:T(8,128)(2,1)S(1)}, u32[]{:S(2)}, u32[]{:S(2)}) collective-permute-start(bf16[256,128]{1,0:T(8,128)(2,1)S(1)} %convolution_convert_fusion.1), channel_id=1, source_target_pairs={{0,3},{1,0},{2,1},{3,2},{4,7},{5,4},{6,5},{7,6},{8,11},{9,8},{10,9... | collective-permute-start | bytes 196616 | tf_op jit(solution)/shard_map/ppermute | solution.py:37
  25.8 6.8 %collective-permute-start.5 = (bf16[4,256,128]{2,1,0:T(8,128)(2,1)S(1)}, bf16[4,256,128]{2,1,0:T(8,128)(2,1)S(1)}, u32[]{:S(2)}, u32[]{:S(2)}) collective-permute-start(bf16[4,256,128]{2,1,0:T(8,128)(2,1)S(1)} %get-tuple-element.26), channel_id=1, source_target_pairs={{0,12},{1,13},{2,14},{3,15},{4,0},{5,1},{6,2},{7,3},{8,4},{9,5},{1... | collective-permute-start | bytes 786440 | tf_op jit(solution)/shard_map/ppermute | solution.py:37
  27.1 8.2 %collective-permute-start.6 = (bf16[4,256,128]{2,1,0:T(8,128)(2,1)S(1)}, bf16[4,256,128]{2,1,0:T(8,128)(2,1)S(1)}, u32[]{:S(2)}, u32[]{:S(2)}) collective-permute-start(bf16[4,256,128]{2,1,0:T(8,128)(2,1)S(1)} %get-tuple-element.26), channel_id=1, source_target_pairs={{0,4},{1,5},{2,6},{3,7},{4,8},{5,9},{6,10},{7,11},{8,12},{9,13},{1... | collective-permute-start | bytes 786440 | tf_op jit(solution)/shard_map/ppermute | solution.py:37
  32.6 5.2 %collective-permute-start.8 = (bf16[4,128,128]{2,1,0:T(8,128)(2,1)S(1)}, bf16[4,128,128]{2,1,0:T(8,128)(2,1)S(1)}, u32[]{:S(2)}, u32[]{:S(2)}) collective-permute-start(bf16[4,128,128]{2,1,0:T(8,128)(2,1)S(1)} %slice.137), channel_id=1, source_target_pairs={{0,12},{1,13},{2,14},{3,15},{4,0},{5,1},{6,2},{7,3},{8,4},{9,5},{1... | collective-permute-start | bytes 393224 | tf_op jit(solution)/shard_map/ppermute | solution.py:37
  35.3 6.2 %collective-permute-start.7 = (bf16[4,128,128]{2,1,0:T(8,128)(2,1)S(1)}, bf16[4,128,128]{2,1,0:T(8,128)(2,1)S(1)}, u32[]{:S(2)}, u32[]{:S(2)}) collective-permute-start(bf16[4,128,128]{2,1,0:T(8,128)(2,1)S(1)} %slice.136), channel_id=1, source_target_pairs={{0,4},{1,5},{2,6},{3,7},{4,8},{5,9},{6,10},{7,11},{8,12},{9,13},{1... | collective-permute-start | bytes 393224 | tf_op jit(solution)/shard_map/ppermute | solution.py:37
  41.8 15.3 %collective-permute-start.9 = (bf16[4,4,256,128]{3,2,1,0:T(8,128)(2,1)S(1)}, bf16[4,4,256,128]{3,2,1,0:T(8,128)(2,1)S(1)}, u32[]{:S(2)}, u32[]{:S(2)}) collective-permute-start(bf16[4,4,256,128]{3,2,1,0:T(8,128)(2,1)S(1)} %get-tuple-element.19), channel_id=1, source_target_pairs={{0,80},{1,81},{2,82},{3,83},{4,84},{5,85},{6,86},{7,87},{8,88},{9,... | collective-permute-start | bytes 3145736 | tf_op jit(solution)/shard_map/ppermute | solution.py:37
  44.7 16.1 %collective-permute-start.10 = (bf16[4,4,256,128]{3,2,1,0:T(8,128)(2,1)S(1)}, bf16[4,4,256,128]{3,2,1,0:T(8,128)(2,1)S(1)}, u32[]{:S(2)}, u32[]{:S(2)}) collective-permute-start(bf16[4,4,256,128]{3,2,1,0:T(8,128)(2,1)S(1)} %get-tuple-element.19), channel_id=1, source_target_pairs={{0,16},{1,17},{2,18},{3,19},{4,20},{5,21},{6,22},{7,23},{8,24},{9,... | collective-permute-start | bytes 3145736 | tf_op jit(solution)/shard_map/ppermute | solution.py:37
  57.1 10.5 %collective-permute-start.12 = (bf16[4,4,128,128]{3,2,1,0:T(8,128)(2,1)S(1)}, bf16[4,4,128,128]{3,2,1,0:T(8,128)(2,1)S(1)}, u32[]{:S(2)}, u32[]{:S(2)}) collective-permute-start(bf16[4,4,128,128]{3,2,1,0:T(8,128)(2,1)S(1)} %slice.139), channel_id=1, source_target_pairs={{0,80},{1,81},{2,82},{3,83},{4,84},{5,85},{6,86},{7,87},{8,88},{9,... | collective-permute-start | bytes 1572872 | tf_op jit(solution)/shard_map/ppermute | solution.py:37
  60.9 10.5 %collective-permute-start.11 = (bf16[4,4,128,128]{3,2,1,0:T(8,128)(2,1)S(1)}, bf16[4,4,128,128]{3,2,1,0:T(8,128)(2,1)S(1)}, u32[]{:S(2)}, u32[]{:S(2)}) collective-permute-start(bf16[4,4,128,128]{3,2,1,0:T(8,128)(2,1)S(1)} %slice.138), channel_id=1, source_target_pairs={{0,16},{1,17},{2,18},{3,19},{4,20},{5,21},{6,22},{7,23},{8,24},{9,... | collective-permute-start | bytes 1572872 | tf_op jit(solution)/shard_map/ppermute | solution.py:37
  73.7 8.3 %collective-permute-start.13 = (bf16[128,128,128]{2,1,0:T(8,128)(2,1)}, bf16[128,128,128]{2,1,0:T(8,128)(2,1)}, u32[]{:S(2)}, u32[]{:S(2)}) collective-permute-start(bf16[128,128,128]{2,1,0:T(8,128)(2,1)} %bitcast.16.proj_ref), channel_id=1, source_target_pairs={{0,32},{32,0},{64,96},{96,64},{1,33},{33,1},{65,97},{97,65},{2,34}... | collective-permute-start | bytes 12582920 | tf_op jit(solution)/shard_map/ppermute | solution.py:41
  82.0 10.1 %copy-start.4 = (s32[8]{0:T(128)S(1)}, s32[8]{0:T(128)}, u32[]{:S(2)}) copy-start(s32[8]{0:T(128)} %count_ref.3) | copy-start | bytes 100
  91.5 1.5 collective-permute-start.15
  110.4 9.2 %collective-permute-start.18 = (bf16[4,4,128,128]{3,2,1,0:T(8,128)(2,1)S(1)}, bf16[4,4,128,128]{3,2,1,0:T(8,128)(2,1)S(1)}, u32[]{:S(2)}, u32[]{:S(2)}) collective-permute-start(bf16[4,4,128,128]{3,2,1,0:T(8,128)(2,1)S(1)} %get-tuple-element.17), channel_id=1, source_target_pairs={{0,80},{1,81},{2,82},{3,83},{4,84},{5,85},{6,86},{7,87},{8,88},{9,... | collective-permute-start | bytes 1572872 | tf_op jit(solution)/shard_map/ppermute | solution.py:37
  110.5 10.7 %collective-permute-start.16 = (bf16[4,4,128,128]{3,2,1,0:T(8,128)(2,1)S(1)}, bf16[4,4,128,128]{3,2,1,0:T(8,128)(2,1)S(1)}, u32[]{:S(2)}, u32[]{:S(2)}) collective-permute-start(bf16[4,4,128,128]{3,2,1,0:T(8,128)(2,1)S(1)} %get-tuple-element.16), channel_id=1, source_target_pairs={{0,16},{1,17},{2,18},{3,19},{4,20},{5,21},{6,22},{7,23},{8,24},{9,... | collective-permute-start | bytes 1572872 | tf_op jit(solution)/shard_map/ppermute | solution.py:37
  119.9 14.9 %collective-permute-start.19 = (bf16[4,4,256,128]{3,2,1,0:T(8,128)(2,1)S(1)}, bf16[4,4,256,128]{3,2,1,0:T(8,128)(2,1)S(1)}, u32[]{:S(2)}, u32[]{:S(2)}) collective-permute-start(bf16[4,4,256,128]{3,2,1,0:T(8,128)(2,1)S(1)} %pad_maximum_fusion.3), channel_id=1, source_target_pairs={{0,80},{1,81},{2,82},{3,83},{4,84},{5,85},{6,86},{7,87},{8,88},{9,... | collective-permute-start | bytes 3145736 | tf_op jit(solution)/shard_map/ppermute | solution.py:37
  121.5 16.1 %collective-permute-start.17 = (bf16[4,4,256,128]{3,2,1,0:T(8,128)(2,1)S(1)}, bf16[4,4,256,128]{3,2,1,0:T(8,128)(2,1)S(1)}, u32[]{:S(2)}, u32[]{:S(2)}) collective-permute-start(bf16[4,4,256,128]{3,2,1,0:T(8,128)(2,1)S(1)} %pad_maximum_fusion.2), channel_id=1, source_target_pairs={{0,16},{1,17},{2,18},{3,19},{4,20},{5,21},{6,22},{7,23},{8,24},{9,... | collective-permute-start | bytes 3145736 | tf_op jit(solution)/shard_map/ppermute | solution.py:37
  137.9 5.9 %collective-permute-start.22 = (bf16[4,128,128]{2,1,0:T(8,128)(2,1)S(1)}, bf16[4,128,128]{2,1,0:T(8,128)(2,1)S(1)}, u32[]{:S(2)}, u32[]{:S(2)}) collective-permute-start(bf16[4,128,128]{2,1,0:T(8,128)(2,1)S(1)} %get-tuple-element.24), channel_id=1, source_target_pairs={{0,12},{1,13},{2,14},{3,15},{4,0},{5,1},{6,2},{7,3},{8,4},{9,5},{1... | collective-permute-start | bytes 393224 | tf_op jit(solution)/shard_map/ppermute | solution.py:37
  138.1 7.4 %collective-permute-start.20 = (bf16[4,128,128]{2,1,0:T(8,128)(2,1)S(1)}, bf16[4,128,128]{2,1,0:T(8,128)(2,1)S(1)}, u32[]{:S(2)}, u32[]{:S(2)}) collective-permute-start(bf16[4,128,128]{2,1,0:T(8,128)(2,1)S(1)} %get-tuple-element.23), channel_id=1, source_target_pairs={{0,4},{1,5},{2,6},{3,7},{4,8},{5,9},{6,10},{7,11},{8,12},{9,13},{1... | collective-permute-start | bytes 393224 | tf_op jit(solution)/shard_map/ppermute | solution.py:37
  143.9 7.9 %collective-permute-start.23 = (bf16[4,256,128]{2,1,0:T(8,128)(2,1)S(1)}, bf16[4,256,128]{2,1,0:T(8,128)(2,1)S(1)}, u32[]{:S(2)}, u32[]{:S(2)}) collective-permute-start(bf16[4,256,128]{2,1,0:T(8,128)(2,1)S(1)} %pad_maximum_fusion.6), channel_id=1, source_target_pairs={{0,12},{1,13},{2,14},{3,15},{4,0},{5,1},{6,2},{7,3},{8,4},{9,5},{1... | collective-permute-start | bytes 786440 | tf_op jit(solution)/shard_map/ppermute | solution.py:37
  145.5 9.1 %collective-permute-start.21 = (bf16[4,256,128]{2,1,0:T(8,128)(2,1)S(1)}, bf16[4,256,128]{2,1,0:T(8,128)(2,1)S(1)}, u32[]{:S(2)}, u32[]{:S(2)}) collective-permute-start(bf16[4,256,128]{2,1,0:T(8,128)(2,1)S(1)} %pad_maximum_fusion.5), channel_id=1, source_target_pairs={{0,4},{1,5},{2,6},{3,7},{4,8},{5,9},{6,10},{7,11},{8,12},{9,13},{1... | collective-permute-start | bytes 786440 | tf_op jit(solution)/shard_map/ppermute | solution.py:37
  154.8 6.2 %collective-permute-start.24 = (bf16[256,128]{1,0:T(8,128)(2,1)S(1)}, bf16[256,128]{1,0:T(8,128)(2,1)S(1)}, u32[]{:S(2)}, u32[]{:S(2)}) collective-permute-start(bf16[256,128]{1,0:T(8,128)(2,1)S(1)} %get-tuple-element.20), channel_id=1, source_target_pairs={{0,1},{1,2},{2,3},{3,0},{4,5},{5,6},{6,7},{7,4},{8,9},{9,10},{10,1... | collective-permute-start | bytes 196616 | tf_op jit(solution)/shard_map/ppermute | solution.py:37
  154.8 6.2 %collective-permute-start.26 = (bf16[256,128]{1,0:T(8,128)(2,1)S(1)}, bf16[256,128]{1,0:T(8,128)(2,1)S(1)}, u32[]{:S(2)}, u32[]{:S(2)}) collective-permute-start(bf16[256,128]{1,0:T(8,128)(2,1)S(1)} %get-tuple-element.21), channel_id=1, source_target_pairs={{0,2},{1,3},{2,0},{3,1},{4,6},{5,7},{6,4},{7,5},{8,10},{9,11},{10,... | collective-permute-start | bytes 196616 | tf_op jit(solution)/shard_map/ppermute | solution.py:37
  156.6 5.3 %collective-permute-start.25 = (bf16[256,128]{1,0:T(8,128)(2,1)S(1)}, bf16[256,128]{1,0:T(8,128)(2,1)S(1)}, u32[]{:S(2)}, u32[]{:S(2)}) collective-permute-start(bf16[256,128]{1,0:T(8,128)(2,1)S(1)} %get-tuple-element.22), channel_id=1, source_target_pairs={{0,3},{1,0},{2,1},{3,2},{4,7},{5,4},{6,5},{7,6},{8,11},{9,8},{10,9... | collective-permute-start | bytes 196616 | tf_op jit(solution)/shard_map/ppermute | solution.py:37
  175.2 1.2 collective-permute-start.27
  176.4 5.1 %collective-permute-start.28 = (f32[4,128]{1,0:T(4,128)S(1)}, f32[4,128]{1,0:T(4,128)S(1)}, u32[]{:S(2)}, u32[]{:S(2)}) collective-permute-start(f32[4,128]{1,0:T(4,128)S(1)} %add.225), channel_id=1, source_target_pairs={{0,64},{32,96},{64,0},{96,32},{1,65},{33,97},{65,1},{97,33},{2,66}... | collective-permute-start | bytes 6152 | tf_op jit(solution)/shard_map/ppermute | solution.py:46
  (4 other events, 19.3 us)

commit v16 on v12

--- a/solution.py
+++ b/solution.py
@@ -115,20 +115,18 @@
     return total
 
 
-def aggregate_kernel(core_ref, where_ref, count_ref, tiles_ref, proj_ref, out_ref, wide_ref, picked_ref):
+def aggregate_kernel(core_ref, where_ref, count_ref, tiles_ref, proj_ref, out_ref):
     row = pl.program_id(0)
     half_id = pl.program_id(1)
     tile_rows = pl.num_programs(0)
     slot_count, tile_size, _ = tiles_ref.shape
     base = (half_id * 2 + core_ref[0]) * tile_rows + row
     live = count_ref[base]
+    part = jnp.zeros(out_ref.shape, jnp.float32)
     for slot in range(slot_count):
-        wide_ref[:, slot * tile_size:(slot + 1) * tile_size] = tiles_ref[slot]
         piece = proj_ref[where_ref[base * slot_count + slot]]
-        picked_ref[slot * tile_size:(slot + 1) * tile_size, :] = jnp.where(
-            slot < live, piece, jnp.zeros_like(piece)
-        )
-    part = jnp.dot(wide_ref[...], picked_ref[...], preferred_element_type=jnp.float32)
+        piece = jnp.where(slot < live, piece, jnp.zeros_like(piece))
+        part = part + jnp.dot(tiles_ref[slot], piece, preferred_element_type=jnp.float32)
 
     @pl.when(half_id == 0)
     def _():
@@ -153,10 +151,6 @@
             pl.BlockSpec(buffer.shape, lambda r, h, c, w, n: (0, 0, 0)),
         ],
         out_specs=pl.BlockSpec((None, tile_size, hidden_width), lambda r, h, c, w, n: (r, 0, 0)),
-        scratch_shapes=[
-            pltpu.VMEM((tile_size, slot_count * tile_size), tile_stack.dtype),
-            pltpu.VMEM((slot_count * tile_size, hidden_width), buffer.dtype),
-        ],
     )
     return pl.pallas_call(
         aggregate_kernel,

time: 182 us -> 180 us (0.989)
  Pallas kernels: 30.5 us -> 28.5 us
    pallas_call x2, Pallas kernels: 15.3 us -> 13.2 us  [aggregate_pair(): pl.pallas_call(aggregate_kernel, grid_spec=grid_spec, out_shape=jax.Shape...]
  transfers between devices with their start and end apart: 28 -> 28, of which waited for: 21 -> 21; matrix products, arithmetic and copies ran while one was open for 6% -> 6% of each run, Pallas kernels for 8% -> 7%
where the time goes in v16:
time: 180 us; the launch traced here: 179 us
  waiting for transfers between devices  82.4 us (46%)
  starting transfers between devices  38.2 us (21%)
  Pallas kernels  28.5 us (16%)
  blocking collectives  14.5 us (8%)
  other arithmetic  7.84 us (4%)
  local copies, waits for them, and re-layouts  6.43 us (4%)
    ppermute x20, waiting for transfers between devices, ring_shift(): return lax.ppermute(block, BOTH, route)  69.6 us
    ppermute x20, starting transfers between devices, ring_shift(): return lax.ppermute(block, BOTH, route)  26.6 us
    pallas_call x1, Pallas kernels, spread_pair(): pl.pallas_call(kernel, grid_spec=grid_spec, out_shape=jax.ShapeDtypeStruc...  15.3 us
    all_to_all x1, blocking collectives, body(): lax.all_to_all(outgoing, 'feat', split_axis=0, concat_axis=0, tiled=True)  14.5 us
    pallas_call x2, Pallas kernels, aggregate_pair(): pl.pallas_call(aggregate_kernel, grid_spec=grid_spec, out_shape=jax.Shape...  13.2 us
    all_to_all x1, starting transfers between devices, body(): lax.all_to_all(features_t, 'feat', split_axis=1, concat_axis=0, tiled=True)  9.27 us
    all_to_all x1, waiting for transfers between devices, body(): lax.all_to_all(features_t, 'feat', split_axis=1, concat_axis=0, tiled=True)  7.74 us
    slice x2, local copies, waits for them, and re-layouts, term(): return total[k]  5.03 us
  transfers between devices with their start and end apart: 28, of which 21 were waited for; matrix products, arithmetic and copies ran while one was open for 6% of the time, Pallas kernels for 7%

profile of v16, /device:TPU:0, one launch (start us, length us, event | category | flops | bytes accessed | tf_op | source)
XLA Modules:
  0.0 179.4 jit_solution(17636044880941560962)
XLA Ops:
  0.7 9.3 %all-to-all-start = ((bf16[4,32,256]{2,0,1:T(4,128)(2,1)}), bf16[4,32,256]{2,0,1:T(4,128)(2,1)S(1)}, u32[]{:S(2)}, u32[]{:S(2)}) async-start(bf16[4,32,256]{2,0,1:T(4,128)(2,1)} %bitcast.128), calls=%async_computation | async-start | bytes 131072 | tf_op jit(solution)/shard_map/all_to_all | solution.py:281
  10.6 7.7 %all-to-all-done = bf16[4,32,256]{2,0,1:T(4,128)(2,1)S(1)} async-done(((bf16[4,32,256]{2,0,1:T(4,128)(2,1)}), bf16[4,32,256]{2,0,1:T(4,128)(2,1)S(1)}, u32[]{:S(2)}, u32[]{:S(2)}) %all-to-all-start) | async-done | bytes 65568 | tf_op jit(solution)/shard_map/all_to_all | solution.py:281
  19.2 2.3 %collective-permute-start.3 = (bf16[256,128]{1,0:T(8,128)(2,1)S(1)}, bf16[256,128]{1,0:T(8,128)(2,1)S(1)}, u32[]{:S(2)}, u32[]{:S(2)}) collective-permute-start(bf16[256,128]{1,0:T(8,128)(2,1)S(1)} %convolution_convert_fusion.1), channel_id=1, source_target_pairs={{0,2},{1,3},{2,0},{3,1},{4,6},{5,7},{6,4},{7,5},{8,10},{9,11},{10,... | collective-permute-start | bytes 196616 | tf_op jit(solution)/shard_map/ppermute | solution.py:37
  22.6 1.5 collective-permute-done.4
  27.2 1.9 %collective-permute-start.5 = (bf16[4,256,128]{2,1,0:T(8,128)(2,1)S(1)}, bf16[4,256,128]{2,1,0:T(8,128)(2,1)S(1)}, u32[]{:S(2)}, u32[]{:S(2)}) collective-permute-start(bf16[4,256,128]{2,1,0:T(8,128)(2,1)S(1)} %get-tuple-element.27), channel_id=1, source_target_pairs={{0,12},{1,13},{2,14},{3,15},{4,0},{5,1},{6,2},{7,3},{8,4},{9,5},{1... | collective-permute-start | bytes 786440 | tf_op jit(solution)/shard_map/ppermute | solution.py:37
  29.3 7.4 %collective-permute-done.6 = bf16[4,256,128]{2,1,0:T(8,128)(2,1)S(1)} collective-permute-done((bf16[4,256,128]{2,1,0:T(8,128)(2,1)S(1)}, bf16[4,256,128]{2,1,0:T(8,128)(2,1)S(1)}, u32[]{:S(2)}, u32[]{:S(2)}) %collective-permute-start.6) | collective-permute-done | bytes 262176 | tf_op jit(solution)/shard_map/ppermute | solution.py:37
  36.6 1.9 %collective-permute-done.5 = bf16[4,256,128]{2,1,0:T(8,128)(2,1)S(1)} collective-permute-done((bf16[4,256,128]{2,1,0:T(8,128)(2,1)S(1)}, bf16[4,256,128]{2,1,0:T(8,128)(2,1)S(1)}, u32[]{:S(2)}, u32[]{:S(2)}) %collective-permute-start.5) | collective-permute-done | bytes 262176 | tf_op jit(solution)/shard_map/ppermute | solution.py:37
  39.9 3.0 %collective-permute-start.8 = (bf16[4,4,256,128]{3,2,1,0:T(8,128)(2,1)S(1)}, bf16[4,4,256,128]{3,2,1,0:T(8,128)(2,1)S(1)}, u32[]{:S(2)}, u32[]{:S(2)}) collective-permute-start(bf16[4,4,256,128]{3,2,1,0:T(8,128)(2,1)S(1)} %get-tuple-element.22), channel_id=1, source_target_pairs={{0,80},{1,81},{2,82},{3,83},{4,84},{5,85},{6,86},{7,87},{8,88},{9,... | collective-permute-start | bytes 3145736 | tf_op jit(solution)/shard_map/ppermute | solution.py:37
  42.9 12.3 %collective-permute-done.8 = bf16[4,4,256,128]{3,2,1,0:T(8,128)(2,1)S(1)} collective-permute-done((bf16[4,4,256,128]{3,2,1,0:T(8,128)(2,1)S(1)}, bf16[4,4,256,128]{3,2,1,0:T(8,128)(2,1)S(1)}, u32[]{:S(2)}, u32[]{:S(2)}) %collective-permute-start.8) | collective-permute-done | bytes 1048608 | tf_op jit(solution)/shard_map/ppermute | solution.py:37
  55.3 3.8 %collective-permute-start.11 = (bf16[4,4,128,128]{3,2,1,0:T(8,128)(2,1)S(1)}, bf16[4,4,128,128]{3,2,1,0:T(8,128)(2,1)S(1)}, u32[]{:S(2)}, u32[]{:S(2)}) collective-permute-start(bf16[4,4,128,128]{3,2,1,0:T(8,128)(2,1)S(1)} %slice.104), channel_id=1, source_target_pairs={{0,80},{1,81},{2,82},{3,83},{4,84},{5,85},{6,86},{7,87},{8,88},{9,... | collective-permute-start | bytes 1572872 | tf_op jit(solution)/shard_map/ppermute | solution.py:37
  59.2 6.6 %collective-permute-done.11 = bf16[4,4,128,128]{3,2,1,0:T(8,128)(2,1)S(1)} collective-permute-done((bf16[4,4,128,128]{3,2,1,0:T(8,128)(2,1)S(1)}, bf16[4,4,128,128]{3,2,1,0:T(8,128)(2,1)S(1)}, u32[]{:S(2)}, u32[]{:S(2)}) %collective-permute-start.11) | collective-permute-done | bytes 524320 | tf_op jit(solution)/shard_map/ppermute | solution.py:37
  65.7 3.8 %collective-permute-done.10 = bf16[4,4,128,128]{3,2,1,0:T(8,128)(2,1)S(1)} collective-permute-done((bf16[4,4,128,128]{3,2,1,0:T(8,128)(2,1)S(1)}, bf16[4,4,128,128]{3,2,1,0:T(8,128)(2,1)S(1)}, u32[]{:S(2)}, u32[]{:S(2)}) %collective-permute-start.10) | collective-permute-done | bytes 524320 | tf_op jit(solution)/shard_map/ppermute | solution.py:37
  69.6 2.3 %pad_maximum_fusion = bf16[4,4,4,256,128]{4,3,2,1,0:T(8,128)(2,1)} fusion(bf16[1,4,4,256,128]{4,3,2,1,0:T(8,128)(2,1)S(1)} %bitcast.112, bf16[1,4,4,256,128]{4,3,2,1,0:T(8,128)(2,1)S(1)} %maximum_bitcast_fusion, bf16[1,4,4,256,128]{4,3,2,1,0:T(8,128)(2,1)S(1)} %bitcast.111, bf16[1,4,4,256,128]{4,3,2,1,0:T(8,128)(2,1)S(1)} %get-tuple-element.21), kind=kLoop, calls=%fused_computation | loop fusion | flops 6291456 | bytes 8388608 | tf_op jit(solution)/shard_map/stack | solution.py:56
  72.6 6.5 %shard_map.85 = f32[2,128,128]{2,1,0:T(8,128)} custom-call(s32[1]{0:T(128)} %bitcast.core_ref, s32[256]{0:T(256)} %copy-done.3, s32[8]{0:T(128)} %count_ref.3, bf16[4,2,32,128,128]{4,3,2,1,0:T(8,128)(2,1)} %bitcast.102, bf16[128,128,128]{2,1,0:T(8,128)(2,1)} %bitcast.16.proj_ref), custom_call_target="tpu_custom_call" | custom-call | tf_op jit(solution)/shard_map/pallas_call | solution.py:155
  79.4 6.7 %shard_map.86 = f32[2,128,128]{2,1,0:T(8,128)} custom-call(s32[1]{0:T(128)} %bitcast.17.core_ref, s32[256]{0:T(256)} %copy-done.3, s32[8]{0:T(128)} %count_ref.3, bf16[4,2,32,128,128]{4,3,2,1,0:T(8,128)(2,1)} %bitcast.103, bf16[128,128,128]{2,1,0:T(8,128)(2,1)} %collective-permute-done.12.proj_ref), custom_call_target="tpu_custom_call" | custom-call | tf_op jit(solution)/shard_map/pallas_call | solution.py:155
  89.9 15.3 %shard_map.87 = f32[128,128,128]{2,1,0:T(8,128)} custom-call(s32[1]{0:T(128)} %bitcast.core_ref, s32[512]{0:T(512)} %pad_add_fusion.where_ref, s32[16]{0:T(128)} %pad_add_fusion.1.count_ref, bf16[4,2,32,128,128]{4,3,2,1,0:T(8,128)(2,1)} %bitcast.104, bf16[4,2,32,128,128]{4,3,2,1,0:T(8,128)(2,1)} %collective-permute-done.13.other_ref, ...), custom_call_target="tpu_custom_call" | custom-call | tf_op jit(solution)/shard_map/pallas_call | solution.py:229
  105.1 1.7 slice.158
  107.1 2.0 %collective-permute-start.15 = (bf16[4,4,128,128]{3,2,1,0:T(8,128)(2,1)S(1)}, bf16[4,4,128,128]{3,2,1,0:T(8,128)(2,1)S(1)}, u32[]{:S(2)}, u32[]{:S(2)}) collective-permute-start(bf16[4,4,128,128]{3,2,1,0:T(8,128)(2,1)S(1)} %get-tuple-element.19), channel_id=1, source_target_pairs={{0,16},{1,17},{2,18},{3,19},{4,20},{5,21},{6,22},{7,23},{8,24},{9,... | collective-permute-start | bytes 1572872 | tf_op jit(solution)/shard_map/ppermute | solution.py:37
  109.1 3.3 %fusion.39 = (f32[32,128,128]{2,1,0:T(8,128)S(1)}, f32[32,128,128]{2,1,0:T(8,128)S(1)}, f32[32,128,128]{2,1,0:T(8,128)S(1)}) fusion(f32[128,128,128]{2,1,0:T(8,128)} %shard_map.87), kind=kLoop, calls=%fused_computation.142 | loop fusion | bytes 12582912 | tf_op jit(solution)/shard_map/slice | solution.py:83
  112.6 3.7 %collective-permute-done.17 = bf16[4,4,128,128]{3,2,1,0:T(8,128)(2,1)S(1)} collective-permute-done((bf16[4,4,128,128]{3,2,1,0:T(8,128)(2,1)S(1)}, bf16[4,4,128,128]{3,2,1,0:T(8,128)(2,1)S(1)}, u32[]{:S(2)}, u32[]{:S(2)}) %collective-permute-start.17) | collective-permute-done | bytes 524320 | tf_op jit(solution)/shard_map/ppermute | solution.py:37
  116.5 1.5 collective-permute-start.18
  119.0 12.5 %collective-permute-done.18 = bf16[4,4,256,128]{3,2,1,0:T(8,128)(2,1)S(1)} collective-permute-done((bf16[4,4,256,128]{3,2,1,0:T(8,128)(2,1)S(1)}, bf16[4,4,256,128]{3,2,1,0:T(8,128)(2,1)S(1)}, u32[]{:S(2)}, u32[]{:S(2)}) %collective-permute-start.18) | collective-permute-done | bytes 1048608 | tf_op jit(solution)/shard_map/ppermute | solution.py:37
  131.5 2.7 %collective-permute-done.16 = bf16[4,4,256,128]{3,2,1,0:T(8,128)(2,1)S(1)} collective-permute-done((bf16[4,4,256,128]{3,2,1,0:T(8,128)(2,1)S(1)}, bf16[4,4,256,128]{3,2,1,0:T(8,128)(2,1)S(1)}, u32[]{:S(2)}, u32[]{:S(2)}) %collective-permute-start.16) | collective-permute-done | bytes 1048608 | tf_op jit(solution)/shard_map/ppermute | solution.py:37
  134.9 2.5 %collective-permute-start.21 = (bf16[4,256,128]{2,1,0:T(8,128)(2,1)S(1)}, bf16[4,256,128]{2,1,0:T(8,128)(2,1)S(1)}, u32[]{:S(2)}, u32[]{:S(2)}) collective-permute-start(bf16[4,256,128]{2,1,0:T(8,128)(2,1)S(1)} %get-tuple-element.17), channel_id=1, source_target_pairs={{0,8},{1,9},{2,10},{3,11},{4,12},{5,13},{6,14},{7,15},{8,0},{9,1},... | collective-permute-start | bytes 786440 | tf_op jit(solution)/shard_map/ppermute | solution.py:37
  137.4 2.0 %collective-permute-start.20 = (bf16[4,256,128]{2,1,0:T(8,128)(2,1)S(1)}, bf16[4,256,128]{2,1,0:T(8,128)(2,1)S(1)}, u32[]{:S(2)}, u32[]{:S(2)}) collective-permute-start(bf16[4,256,128]{2,1,0:T(8,128)(2,1)S(1)} %get-tuple-element.18), channel_id=1, source_target_pairs={{0,12},{1,13},{2,14},{3,15},{4,0},{5,1},{6,2},{7,3},{8,4},{9,5},{1... | collective-permute-start | bytes 786440 | tf_op jit(solution)/shard_map/ppermute | solution.py:37
  139.4 3.9 %collective-permute-done.19 = bf16[4,256,128]{2,1,0:T(8,128)(2,1)S(1)} collective-permute-done((bf16[4,256,128]{2,1,0:T(8,128)(2,1)S(1)}, bf16[4,256,128]{2,1,0:T(8,128)(2,1)S(1)}, u32[]{:S(2)}, u32[]{:S(2)}) %collective-permute-start.19) | collective-permute-done | bytes 262176 | tf_op jit(solution)/shard_map/ppermute | solution.py:37
  143.3 6.7 %collective-permute-done.21 = bf16[4,256,128]{2,1,0:T(8,128)(2,1)S(1)} collective-permute-done((bf16[4,256,128]{2,1,0:T(8,128)(2,1)S(1)}, bf16[4,256,128]{2,1,0:T(8,128)(2,1)S(1)}, u32[]{:S(2)}, u32[]{:S(2)}) %collective-permute-start.21) | collective-permute-done | bytes 262176 | tf_op jit(solution)/shard_map/ppermute | solution.py:37
  150.3 1.7 collective-permute-start.24
  152.0 1.5 collective-permute-start.23
  153.5 2.9 %collective-permute-done.22 = bf16[256,128]{1,0:T(8,128)(2,1)S(1)} collective-permute-done((bf16[256,128]{1,0:T(8,128)(2,1)S(1)}, bf16[256,128]{1,0:T(8,128)(2,1)S(1)}, u32[]{:S(2)}, u32[]{:S(2)}) %collective-permute-start.22) | collective-permute-done | bytes 65568 | tf_op jit(solution)/shard_map/ppermute | solution.py:37
  157.9 14.5 %all_to_all.24 = f32[32,4,384]{2,1,0:T(4,128)S(1)} all-to-all(f32[32,4,384]{2,1,0:T(4,128)S(1)} %pad_maximum_fusion.5), channel_id=1, replica_groups=mesh['blk'=4,'feat'=32] {'feat'}, dimensions={0} | all-to-all | bytes 393216 | tf_op jit(solution)/shard_map/all_to_all | solution.py:343
  175.5 3.2 %collective-permute-done.26 = f32[4,128]{1,0:T(4,128)S(1)} collective-permute-done((f32[4,128]{1,0:T(4,128)S(1)}, f32[4,128]{1,0:T(4,128)S(1)}, u32[]{:S(2)}, u32[]{:S(2)}) %collective-permute-start.26) | collective-permute-done | bytes 2080 | tf_op jit(solution)/shard_map/ppermute | solution.py:46
  (79 shorter events, 19.8 us)
Async XLA Ops:
  0.6 17.7 %copy-start = (bf16[128,128]{1,0:T(8,128)(2,1)S(1)}, bf16[128,128]{1,0:T(8,128)(2,1)}, u32[]{:S(2)}) copy-start(bf16[128,128]{1,0:T(8,128)(2,1)} %param.7) | copy-start | bytes 98308
  0.6 89.2 %collective-permute-start.13 = (bf16[4,2,32,128,128]{4,3,2,1,0:T(8,128)(2,1)}, bf16[4,2,32,128,128]{4,3,2,1,0:T(8,128)(2,1)}, u32[]{:S(2)}, u32[]{:S(2)}) collective-permute-start(bf16[4,2,32,128,128]{4,3,2,1,0:T(8,128)(2,1)} %bitcast.101), channel_id=1, source_target_pairs={{0,32},{32,0},{64,96},{96,64},{1,33},{33,1},{65,97},{97,65},{2,34}... | collective-permute-start | bytes 25165832 | tf_op jit(solution)/shard_map/ppermute | solution.py:41
  0.7 17.6 %all-to-all-start = ((bf16[4,32,256]{2,0,1:T(4,128)(2,1)}), bf16[4,32,256]{2,0,1:T(4,128)(2,1)S(1)}, u32[]{:S(2)}, u32[]{:S(2)}) async-start(bf16[4,32,256]{2,0,1:T(4,128)(2,1)} %bitcast.128), calls=%async_computation | async-start | bytes 131072 | tf_op jit(solution)/shard_map/all_to_all | solution.py:281
  10.0 8.6 %collective-permute-start.1 = (s32[8]{0:T(128)}, s32[8]{0:T(128)S(1)}, u32[]{:S(2)}, u32[]{:S(2)}) collective-permute-start(s32[8]{0:T(128)} %count_ref.3), channel_id=1, source_target_pairs={{0,32},{32,0},{64,96},{96,64},{1,33},{33,1},{65,97},{97,65},{2,34}... | collective-permute-start | bytes 104 | tf_op jit(solution)/shard_map/ppermute | solution.py:41
  10.3 8.3 %collective-permute-start = (s32[256]{0:T(256)}, s32[256]{0:T(256)S(1)}, u32[]{:S(2)}, u32[]{:S(2)}) collective-permute-start(s32[256]{0:T(256)} %param.9), channel_id=1, source_target_pairs={{0,32},{32,0},{64,96},{96,64},{1,33},{33,1},{65,97},{97,65},{2,34}... | collective-permute-start | bytes 3080 | tf_op jit(solution)/shard_map/ppermute | solution.py:41
  18.6 5.5 %collective-permute-start.4 = (bf16[256,128]{1,0:T(8,128)(2,1)S(1)}, bf16[256,128]{1,0:T(8,128)(2,1)S(1)}, u32[]{:S(2)}, u32[]{:S(2)}) collective-permute-start(bf16[256,128]{1,0:T(8,128)(2,1)S(1)} %convolution_convert_fusion.1), channel_id=1, source_target_pairs={{0,1},{1,2},{2,3},{3,0},{4,5},{5,6},{6,7},{7,4},{8,9},{9,10},{10,1... | collective-permute-start | bytes 196616 | tf_op jit(solution)/shard_map/ppermute | solution.py:37
  19.2 5.8 %collective-permute-start.3 = (bf16[256,128]{1,0:T(8,128)(2,1)S(1)}, bf16[256,128]{1,0:T(8,128)(2,1)S(1)}, u32[]{:S(2)}, u32[]{:S(2)}) collective-permute-start(bf16[256,128]{1,0:T(8,128)(2,1)S(1)} %convolution_convert_fusion.1), channel_id=1, source_target_pairs={{0,2},{1,3},{2,0},{3,1},{4,6},{5,7},{6,4},{7,5},{8,10},{9,11},{10,... | collective-permute-start | bytes 196616 | tf_op jit(solution)/shard_map/ppermute | solution.py:37
  21.5 4.3 %collective-permute-start.2 = (bf16[256,128]{1,0:T(8,128)(2,1)S(1)}, bf16[256,128]{1,0:T(8,128)(2,1)S(1)}, u32[]{:S(2)}, u32[]{:S(2)}) collective-permute-start(bf16[256,128]{1,0:T(8,128)(2,1)S(1)} %convolution_convert_fusion.1), channel_id=1, source_target_pairs={{0,3},{1,0},{2,1},{3,2},{4,7},{5,4},{6,5},{7,6},{8,11},{9,8},{10,9... | collective-permute-start | bytes 196616 | tf_op jit(solution)/shard_map/ppermute | solution.py:37
  25.8 10.8 %collective-permute-start.6 = (bf16[4,256,128]{2,1,0:T(8,128)(2,1)S(1)}, bf16[4,256,128]{2,1,0:T(8,128)(2,1)S(1)}, u32[]{:S(2)}, u32[]{:S(2)}) collective-permute-start(bf16[4,256,128]{2,1,0:T(8,128)(2,1)S(1)} %get-tuple-element.27), channel_id=1, source_target_pairs={{0,8},{1,9},{2,10},{3,11},{4,12},{5,13},{6,14},{7,15},{8,0},{9,1},... | collective-permute-start | bytes 786440 | tf_op jit(solution)/shard_map/ppermute | solution.py:37
  27.2 11.3 %collective-permute-start.5 = (bf16[4,256,128]{2,1,0:T(8,128)(2,1)S(1)}, bf16[4,256,128]{2,1,0:T(8,128)(2,1)S(1)}, u32[]{:S(2)}, u32[]{:S(2)}) collective-permute-start(bf16[4,256,128]{2,1,0:T(8,128)(2,1)S(1)} %get-tuple-element.27), channel_id=1, source_target_pairs={{0,12},{1,13},{2,14},{3,15},{4,0},{5,1},{6,2},{7,3},{8,4},{9,5},{1... | collective-permute-start | bytes 786440 | tf_op jit(solution)/shard_map/ppermute | solution.py:37
  29.1 10.6 %collective-permute-start.7 = (bf16[4,256,128]{2,1,0:T(8,128)(2,1)S(1)}, bf16[4,256,128]{2,1,0:T(8,128)(2,1)S(1)}, u32[]{:S(2)}, u32[]{:S(2)}) collective-permute-start(bf16[4,256,128]{2,1,0:T(8,128)(2,1)S(1)} %get-tuple-element.27), channel_id=1, source_target_pairs={{0,4},{1,5},{2,6},{3,7},{4,8},{5,9},{6,10},{7,11},{8,12},{9,13},{1... | collective-permute-start | bytes 786440 | tf_op jit(solution)/shard_map/ppermute | solution.py:37
  39.9 15.3 %collective-permute-start.8 = (bf16[4,4,256,128]{3,2,1,0:T(8,128)(2,1)S(1)}, bf16[4,4,256,128]{3,2,1,0:T(8,128)(2,1)S(1)}, u32[]{:S(2)}, u32[]{:S(2)}) collective-permute-start(bf16[4,4,256,128]{3,2,1,0:T(8,128)(2,1)S(1)} %get-tuple-element.22), channel_id=1, source_target_pairs={{0,80},{1,81},{2,82},{3,83},{4,84},{5,85},{6,86},{7,87},{8,88},{9,... | collective-permute-start | bytes 3145736 | tf_op jit(solution)/shard_map/ppermute | solution.py:37
  42.9 16.1 %collective-permute-start.9 = (bf16[4,4,256,128]{3,2,1,0:T(8,128)(2,1)S(1)}, bf16[4,4,256,128]{3,2,1,0:T(8,128)(2,1)S(1)}, u32[]{:S(2)}, u32[]{:S(2)}) collective-permute-start(bf16[4,4,256,128]{3,2,1,0:T(8,128)(2,1)S(1)} %get-tuple-element.22), channel_id=1, source_target_pairs={{0,16},{1,17},{2,18},{3,19},{4,20},{5,21},{6,22},{7,23},{8,24},{9,... | collective-permute-start | bytes 3145736 | tf_op jit(solution)/shard_map/ppermute | solution.py:37
  55.3 10.5 %collective-permute-start.11 = (bf16[4,4,128,128]{3,2,1,0:T(8,128)(2,1)S(1)}, bf16[4,4,128,128]{3,2,1,0:T(8,128)(2,1)S(1)}, u32[]{:S(2)}, u32[]{:S(2)}) collective-permute-start(bf16[4,4,128,128]{3,2,1,0:T(8,128)(2,1)S(1)} %slice.104), channel_id=1, source_target_pairs={{0,80},{1,81},{2,82},{3,83},{4,84},{5,85},{6,86},{7,87},{8,88},{9,... | collective-permute-start | bytes 1572872 | tf_op jit(solution)/shard_map/ppermute | solution.py:37
  59.1 10.5 %collective-permute-start.10 = (bf16[4,4,128,128]{3,2,1,0:T(8,128)(2,1)S(1)}, bf16[4,4,128,128]{3,2,1,0:T(8,128)(2,1)S(1)}, u32[]{:S(2)}, u32[]{:S(2)}) collective-permute-start(bf16[4,4,128,128]{3,2,1,0:T(8,128)(2,1)S(1)} %slice.103), channel_id=1, source_target_pairs={{0,16},{1,17},{2,18},{3,19},{4,20},{5,21},{6,22},{7,23},{8,24},{9,... | collective-permute-start | bytes 1572872 | tf_op jit(solution)/shard_map/ppermute | solution.py:37
  71.9 7.5 %collective-permute-start.12 = (bf16[128,128,128]{2,1,0:T(8,128)(2,1)}, bf16[128,128,128]{2,1,0:T(8,128)(2,1)}, u32[]{:S(2)}, u32[]{:S(2)}) collective-permute-start(bf16[128,128,128]{2,1,0:T(8,128)(2,1)} %bitcast.16.proj_ref), channel_id=1, source_target_pairs={{0,32},{32,0},{64,96},{96,64},{1,33},{33,1},{65,97},{97,65},{2,34}... | collective-permute-start | bytes 12582920 | tf_op jit(solution)/shard_map/ppermute | solution.py:41
  79.4 6.7 %copy-start.1 = (f32[2,128,128]{2,1,0:T(8,128)S(1)}, f32[2,128,128]{2,1,0:T(8,128)}, u32[]{:S(2)}) copy-start(f32[2,128,128]{2,1,0:T(8,128)} %shard_map.85) | copy-start | bytes 393220
  79.4 7.6 %copy-start.2 = (bf16[256,128]{1,0:T(8,128)(2,1)S(1)}, bf16[256,128]{1,0:T(8,128)(2,1)}, u32[]{:S(2)}) copy-start(bf16[256,128]{1,0:T(8,128)(2,1)} %param.11) | copy-start | bytes 196612
  79.4 8.8 %copy-start.4 = (s32[8]{0:T(128)S(1)}, s32[8]{0:T(128)}, u32[]{:S(2)}) copy-start(s32[8]{0:T(128)} %count_ref.3) | copy-start | bytes 100
  87.9 1.3 collective-permute-start.14
  107.0 9.2 %collective-permute-start.17 = (bf16[4,4,128,128]{3,2,1,0:T(8,128)(2,1)S(1)}, bf16[4,4,128,128]{3,2,1,0:T(8,128)(2,1)S(1)}, u32[]{:S(2)}, u32[]{:S(2)}) collective-permute-start(bf16[4,4,128,128]{3,2,1,0:T(8,128)(2,1)S(1)} %get-tuple-element.20), channel_id=1, source_target_pairs={{0,80},{1,81},{2,82},{3,83},{4,84},{5,85},{6,86},{7,87},{8,88},{9,... | collective-permute-start | bytes 1572872 | tf_op jit(solution)/shard_map/ppermute | solution.py:37
  107.1 10.9 %collective-permute-start.15 = (bf16[4,4,128,128]{3,2,1,0:T(8,128)(2,1)S(1)}, bf16[4,4,128,128]{3,2,1,0:T(8,128)(2,1)S(1)}, u32[]{:S(2)}, u32[]{:S(2)}) collective-permute-start(bf16[4,4,128,128]{3,2,1,0:T(8,128)(2,1)S(1)} %get-tuple-element.19), channel_id=1, source_target_pairs={{0,16},{1,17},{2,18},{3,19},{4,20},{5,21},{6,22},{7,23},{8,24},{9,... | collective-permute-start | bytes 1572872 | tf_op jit(solution)/shard_map/ppermute | solution.py:37
  116.5 15.0 %collective-permute-start.18 = (bf16[4,4,256,128]{3,2,1,0:T(8,128)(2,1)S(1)}, bf16[4,4,256,128]{3,2,1,0:T(8,128)(2,1)S(1)}, u32[]{:S(2)}, u32[]{:S(2)}) collective-permute-start(bf16[4,4,256,128]{3,2,1,0:T(8,128)(2,1)S(1)} %pad_maximum_fusion.3), channel_id=1, source_target_pairs={{0,80},{1,81},{2,82},{3,83},{4,84},{5,85},{6,86},{7,87},{8,88},{9,... | collective-permute-start | bytes 3145736 | tf_op jit(solution)/shard_map/ppermute | solution.py:37
  118.2 16.1 %collective-permute-start.16 = (bf16[4,4,256,128]{3,2,1,0:T(8,128)(2,1)S(1)}, bf16[4,4,256,128]{3,2,1,0:T(8,128)(2,1)S(1)}, u32[]{:S(2)}, u32[]{:S(2)}) collective-permute-start(bf16[4,4,256,128]{3,2,1,0:T(8,128)(2,1)S(1)} %pad_maximum_fusion.2), channel_id=1, source_target_pairs={{0,16},{1,17},{2,18},{3,19},{4,20},{5,21},{6,22},{7,23},{8,24},{9,... | collective-permute-start | bytes 3145736 | tf_op jit(solution)/shard_map/ppermute | solution.py:37
  134.8 8.5 %collective-permute-start.19 = (bf16[4,256,128]{2,1,0:T(8,128)(2,1)S(1)}, bf16[4,256,128]{2,1,0:T(8,128)(2,1)S(1)}, u32[]{:S(2)}, u32[]{:S(2)}) collective-permute-start(bf16[4,256,128]{2,1,0:T(8,128)(2,1)S(1)} %get-tuple-element.16), channel_id=1, source_target_pairs={{0,4},{1,5},{2,6},{3,7},{4,8},{5,9},{6,10},{7,11},{8,12},{9,13},{1... | collective-permute-start | bytes 786440 | tf_op jit(solution)/shard_map/ppermute | solution.py:37
  134.9 15.1 %collective-permute-start.21 = (bf16[4,256,128]{2,1,0:T(8,128)(2,1)S(1)}, bf16[4,256,128]{2,1,0:T(8,128)(2,1)S(1)}, u32[]{:S(2)}, u32[]{:S(2)}) collective-permute-start(bf16[4,256,128]{2,1,0:T(8,128)(2,1)S(1)} %get-tuple-element.17), channel_id=1, source_target_pairs={{0,8},{1,9},{2,10},{3,11},{4,12},{5,13},{6,14},{7,15},{8,0},{9,1},... | collective-permute-start | bytes 786440 | tf_op jit(solution)/shard_map/ppermute | solution.py:37
  137.4 12.6 %collective-permute-start.20 = (bf16[4,256,128]{2,1,0:T(8,128)(2,1)S(1)}, bf16[4,256,128]{2,1,0:T(8,128)(2,1)S(1)}, u32[]{:S(2)}, u32[]{:S(2)}) collective-permute-start(bf16[4,256,128]{2,1,0:T(8,128)(2,1)S(1)} %get-tuple-element.18), channel_id=1, source_target_pairs={{0,12},{1,13},{2,14},{3,15},{4,0},{5,1},{6,2},{7,3},{8,4},{9,5},{1... | collective-permute-start | bytes 786440 | tf_op jit(solution)/shard_map/ppermute | solution.py:37
  150.2 6.2 %collective-permute-start.22 = (bf16[256,128]{1,0:T(8,128)(2,1)S(1)}, bf16[256,128]{1,0:T(8,128)(2,1)S(1)}, u32[]{:S(2)}, u32[]{:S(2)}) collective-permute-start(bf16[256,128]{1,0:T(8,128)(2,1)S(1)} %get-tuple-element.23), channel_id=1, source_target_pairs={{0,1},{1,2},{2,3},{3,0},{4,5},{5,6},{6,7},{7,4},{8,9},{9,10},{10,1... | collective-permute-start | bytes 196616 | tf_op jit(solution)/shard_map/ppermute | solution.py:37
  150.3 6.2 %collective-permute-start.24 = (bf16[256,128]{1,0:T(8,128)(2,1)S(1)}, bf16[256,128]{1,0:T(8,128)(2,1)S(1)}, u32[]{:S(2)}, u32[]{:S(2)}) collective-permute-start(bf16[256,128]{1,0:T(8,128)(2,1)S(1)} %get-tuple-element.24), channel_id=1, source_target_pairs={{0,2},{1,3},{2,0},{3,1},{4,6},{5,7},{6,4},{7,5},{8,10},{9,11},{10,... | collective-permute-start | bytes 196616 | tf_op jit(solution)/shard_map/ppermute | solution.py:37
  152.0 5.3 %collective-permute-start.23 = (bf16[256,128]{1,0:T(8,128)(2,1)S(1)}, bf16[256,128]{1,0:T(8,128)(2,1)S(1)}, u32[]{:S(2)}, u32[]{:S(2)}) collective-permute-start(bf16[256,128]{1,0:T(8,128)(2,1)S(1)} %get-tuple-element.25), channel_id=1, source_target_pairs={{0,3},{1,0},{2,1},{3,2},{4,7},{5,4},{6,5},{7,6},{8,11},{9,8},{10,9... | collective-permute-start | bytes 196616 | tf_op jit(solution)/shard_map/ppermute | solution.py:37
  172.4 1.2 collective-permute-start.25
  173.7 5.1 %collective-permute-start.26 = (f32[4,128]{1,0:T(4,128)S(1)}, f32[4,128]{1,0:T(4,128)S(1)}, u32[]{:S(2)}, u32[]{:S(2)}) collective-permute-start(f32[4,128]{1,0:T(4,128)S(1)} %add.221), channel_id=1, source_target_pairs={{0,64},{32,96},{64,0},{96,32},{1,65},{33,97},{65,1},{97,33},{2,66}... | collective-permute-start | bytes 6152 | tf_op jit(solution)/shard_map/ppermute | solution.py:46
  (2 other events, 2.9 us)

commit v17 on v16

--- a/solution.py
+++ b/solution.py
@@ -176,8 +176,7 @@
     def sibling_map(s, r, h, c, w, n):
         return (jnp.where(s == 1, h * 2 + c[0], c[0]), jnp.where(s == 1, r, 0), 0, 0, 0)
 
-    def kernel(core_ref, where_ref, count_ref, own_ref, other_ref, grad_ref, out_ref, total_ref,
-               wide_ref, terms_ref):
+    def kernel(core_ref, where_ref, count_ref, own_ref, other_ref, grad_ref, out_ref, total_ref):
         source = pl.program_id(0)
         row = pl.program_id(1)
         half_id = pl.program_id(2)
@@ -188,19 +187,18 @@
         def _():
             total_ref[...] = jnp.zeros(total_ref.shape, jnp.float32)
 
-        def fill(tiles_ref):
+        def spread(tiles_ref):
+            grad_rows = grad_ref[...]
             for slot in range(slot_count):
-                wide_ref[:, slot * tile_size:(slot + 1) * tile_size] = tiles_ref[slot]
-
-        pl.when(source == 0)(lambda: fill(own_ref))
-        pl.when(source == 1)(lambda: fill(other_ref))
-        terms_ref[...] = jnp.dot(grad_ref[...], wide_ref[...], preferred_element_type=jnp.float32)
-        for slot in range(slot_count):
-            spot = where_ref[(source * blocks * tile_rows + base) * slot_count + slot]
-
-            @pl.when(slot < live)
-            def _():
-                total_ref[spot] += terms_ref[:, slot * tile_size:(slot + 1) * tile_size]
+                spot = where_ref[(source * blocks * tile_rows + base) * slot_count + slot]
+                term = jnp.dot(grad_rows, tiles_ref[slot], preferred_element_type=jnp.float32)
+
+                @pl.when(slot < live)
+                def _():
+                    total_ref[spot] += term
+
+        pl.when(source == 0)(lambda: spread(own_ref))
+        pl.when(source == 1)(lambda: spread(other_ref))
 
         @pl.when((source == 1) & (row == tile_rows - 1) & (half_id == halves - 1))
         def _():
@@ -222,8 +220,6 @@
         ),
         scratch_shapes=[
             pltpu.VMEM((buffer_tiles, hidden_width, tile_size), jnp.float32),
-            pltpu.VMEM((tile_size, slot_count * tile_size), tile_stack.dtype),
-            pltpu.VMEM((hidden_width, slot_count * tile_size), jnp.float32),
         ],
     )
     return pl.pallas_call(

time: 180 us -> 208 us (1.16)
  Pallas kernels: 28.5 us -> 57 us
    pallas_call x1, Pallas kernels: 15.3 us -> 43.8 us  [spread_pair(): pl.pallas_call(kernel, grid_spec=grid_spec, out_shape=jax.ShapeDtypeStruc...]
  transfers between devices with their start and end apart: 28 -> 28, of which waited for: 21 -> 21; matrix products, arithmetic and copies ran while one was open for 6% -> 5% of each run, Pallas kernels for 7% -> 6%
where the time goes in v17:
time: 208 us
  waiting for transfers between devices  83 us (40%)
  Pallas kernels  57 us (27%)
  starting transfers between devices  37.4 us (18%)
  blocking collectives  14.6 us (7%)
  other arithmetic  7.84 us (4%)
  local copies, waits for them, and re-layouts  6.43 us (3%)
    ppermute x20, waiting for transfers between devices, ring_shift(): return lax.ppermute(block, BOTH, route)  69.9 us
    pallas_call x1, Pallas kernels, spread_pair(): pl.pallas_call(kernel, grid_spec=grid_spec, out_shape=jax.ShapeDtypeStruc...  43.8 us
    ppermute x20, starting transfers between devices, ring_shift(): return lax.ppermute(block, BOTH, route)  26.1 us
    all_to_all x1, blocking collectives, body(): lax.all_to_all(outgoing, 'feat', split_axis=0, concat_axis=0, tiled=True)  14.6 us
    pallas_call x2, Pallas kernels, aggregate_pair(): pl.pallas_call(aggregate_kernel, grid_spec=grid_spec, out_shape=jax.Shape...  13.2 us
    all_to_all x1, starting transfers between devices, body(): lax.all_to_all(features_t, 'feat', split_axis=1, concat_axis=0, tiled=True)  9.27 us
    all_to_all x1, waiting for transfers between devices, body(): lax.all_to_all(features_t, 'feat', split_axis=1, concat_axis=0, tiled=True)  7.74 us
    slice x2, local copies, waits for them, and re-layouts, term(): return total[k]  5.03 us
  transfers between devices with their start and end apart: 28, of which 21 were waited for; matrix products, arithmetic and copies ran while one was open for 5% of the time, Pallas kernels for 6%

profile of v17, /device:TPU:0, one launch (start us, length us, event | category | flops | bytes accessed | tf_op | source)
XLA Modules:
  0.0 207.7 jit_solution(10789308926029014193)
XLA Ops:
  0.7 9.3 %all-to-all-start = ((bf16[4,32,256]{2,0,1:T(4,128)(2,1)}), bf16[4,32,256]{2,0,1:T(4,128)(2,1)S(1)}, u32[]{:S(2)}, u32[]{:S(2)}) async-start(bf16[4,32,256]{2,0,1:T(4,128)(2,1)} %bitcast.128), calls=%async_computation | async-start | bytes 131072 | tf_op jit(solution)/shard_map/all_to_all | solution.py:277
  10.6 7.7 %all-to-all-done = bf16[4,32,256]{2,0,1:T(4,128)(2,1)S(1)} async-done(((bf16[4,32,256]{2,0,1:T(4,128)(2,1)}), bf16[4,32,256]{2,0,1:T(4,128)(2,1)S(1)}, u32[]{:S(2)}, u32[]{:S(2)}) %all-to-all-start) | async-done | bytes 65568 | tf_op jit(solution)/shard_map/all_to_all | solution.py:277
  19.2 2.3 %collective-permute-start.3 = (bf16[256,128]{1,0:T(8,128)(2,1)S(1)}, bf16[256,128]{1,0:T(8,128)(2,1)S(1)}, u32[]{:S(2)}, u32[]{:S(2)}) collective-permute-start(bf16[256,128]{1,0:T(8,128)(2,1)S(1)} %convolution_convert_fusion.1), channel_id=1, source_target_pairs={{0,2},{1,3},{2,0},{3,1},{4,6},{5,7},{6,4},{7,5},{8,10},{9,11},{10,... | collective-permute-start | bytes 196616 | tf_op jit(solution)/shard_map/ppermute | solution.py:37
  22.6 1.5 collective-permute-done.4
  25.8 1.4 collective-permute-start.6
  27.2 1.9 collective-permute-start.5
  29.3 7.4 %collective-permute-done.6 = bf16[4,256,128]{2,1,0:T(8,128)(2,1)S(1)} collective-permute-done((bf16[4,256,128]{2,1,0:T(8,128)(2,1)S(1)}, bf16[4,256,128]{2,1,0:T(8,128)(2,1)S(1)}, u32[]{:S(2)}, u32[]{:S(2)}) %collective-permute-start.6) | collective-permute-done | bytes 262176 | tf_op jit(solution)/shard_map/ppermute | solution.py:37
  36.6 1.9 collective-permute-done.5
  39.9 3.0 %collective-permute-start.8 = (bf16[4,4,256,128]{3,2,1,0:T(8,128)(2,1)S(1)}, bf16[4,4,256,128]{3,2,1,0:T(8,128)(2,1)S(1)}, u32[]{:S(2)}, u32[]{:S(2)}) collective-permute-start(bf16[4,4,256,128]{3,2,1,0:T(8,128)(2,1)S(1)} %get-tuple-element.22), channel_id=1, source_target_pairs={{0,80},{1,81},{2,82},{3,83},{4,84},{5,85},{6,86},{7,87},{8,88},{9,... | collective-permute-start | bytes 3145736 | tf_op jit(solution)/shard_map/ppermute | solution.py:37
  42.9 12.3 %collective-permute-done.8 = bf16[4,4,256,128]{3,2,1,0:T(8,128)(2,1)S(1)} collective-permute-done((bf16[4,4,256,128]{3,2,1,0:T(8,128)(2,1)S(1)}, bf16[4,4,256,128]{3,2,1,0:T(8,128)(2,1)S(1)}, u32[]{:S(2)}, u32[]{:S(2)}) %collective-permute-start.8) | collective-permute-done | bytes 1048608 | tf_op jit(solution)/shard_map/ppermute | solution.py:37
  55.3 3.8 %collective-permute-start.11 = (bf16[4,4,128,128]{3,2,1,0:T(8,128)(2,1)S(1)}, bf16[4,4,128,128]{3,2,1,0:T(8,128)(2,1)S(1)}, u32[]{:S(2)}, u32[]{:S(2)}) collective-permute-start(bf16[4,4,128,128]{3,2,1,0:T(8,128)(2,1)S(1)} %slice.104), channel_id=1, source_target_pairs={{0,80},{1,81},{2,82},{3,83},{4,84},{5,85},{6,86},{7,87},{8,88},{9,... | collective-permute-start | bytes 1572872 | tf_op jit(solution)/shard_map/ppermute | solution.py:37
  59.2 6.6 %collective-permute-done.11 = bf16[4,4,128,128]{3,2,1,0:T(8,128)(2,1)S(1)} collective-permute-done((bf16[4,4,128,128]{3,2,1,0:T(8,128)(2,1)S(1)}, bf16[4,4,128,128]{3,2,1,0:T(8,128)(2,1)S(1)}, u32[]{:S(2)}, u32[]{:S(2)}) %collective-permute-start.11) | collective-permute-done | bytes 524320 | tf_op jit(solution)/shard_map/ppermute | solution.py:37
  65.7 3.8 %collective-permute-done.10 = bf16[4,4,128,128]{3,2,1,0:T(8,128)(2,1)S(1)} collective-permute-done((bf16[4,4,128,128]{3,2,1,0:T(8,128)(2,1)S(1)}, bf16[4,4,128,128]{3,2,1,0:T(8,128)(2,1)S(1)}, u32[]{:S(2)}, u32[]{:S(2)}) %collective-permute-start.10) | collective-permute-done | bytes 524320 | tf_op jit(solution)/shard_map/ppermute | solution.py:37
  69.6 2.3 %pad_maximum_fusion = bf16[4,4,4,256,128]{4,3,2,1,0:T(8,128)(2,1)} fusion(bf16[1,4,4,256,128]{4,3,2,1,0:T(8,128)(2,1)S(1)} %bitcast.112, bf16[1,4,4,256,128]{4,3,2,1,0:T(8,128)(2,1)S(1)} %maximum_bitcast_fusion, bf16[1,4,4,256,128]{4,3,2,1,0:T(8,128)(2,1)S(1)} %bitcast.111, bf16[1,4,4,256,128]{4,3,2,1,0:T(8,128)(2,1)S(1)} %get-tuple-element.21), kind=kLoop, calls=%fused_computation | loop fusion | flops 6291456 | bytes 8388608 | tf_op jit(solution)/shard_map/stack | solution.py:56
  72.6 6.5 %shard_map.85 = f32[2,128,128]{2,1,0:T(8,128)} custom-call(s32[1]{0:T(128)} %bitcast.core_ref, s32[256]{0:T(256)} %copy-done.3, s32[8]{0:T(128)} %count_ref.3, bf16[4,2,32,128,128]{4,3,2,1,0:T(8,128)(2,1)} %bitcast.102, bf16[128,128,128]{2,1,0:T(8,128)(2,1)} %bitcast.16.proj_ref), custom_call_target="tpu_custom_call" | custom-call | tf_op jit(solution)/shard_map/pallas_call | solution.py:155
  79.4 6.7 %shard_map.86 = f32[2,128,128]{2,1,0:T(8,128)} custom-call(s32[1]{0:T(128)} %bitcast.17.core_ref, s32[256]{0:T(256)} %copy-done.3, s32[8]{0:T(128)} %count_ref.3, bf16[4,2,32,128,128]{4,3,2,1,0:T(8,128)(2,1)} %bitcast.103, bf16[128,128,128]{2,1,0:T(8,128)(2,1)} %collective-permute-done.12.proj_ref), custom_call_target="tpu_custom_call" | custom-call | tf_op jit(solution)/shard_map/pallas_call | solution.py:155
  89.9 43.8 %shard_map.87 = f32[128,128,128]{2,1,0:T(8,128)} custom-call(s32[1]{0:T(128)} %bitcast.core_ref, s32[512]{0:T(512)} %pad_add_fusion.where_ref, s32[16]{0:T(128)} %pad_add_fusion.1.count_ref, bf16[4,2,32,128,128]{4,3,2,1,0:T(8,128)(2,1)} %bitcast.104, bf16[4,2,32,128,128]{4,3,2,1,0:T(8,128)(2,1)} %collective-permute-done.13.other_ref, ...), custom_call_target="tpu_custom_call" | custom-call | tf_op jit(solution)/shard_map/pallas_call | solution.py:225
  133.6 1.7 slice.158
  135.6 2.0 collective-permute-start.15
  137.6 3.3 %fusion.39 = (f32[32,128,128]{2,1,0:T(8,128)S(1)}, f32[32,128,128]{2,1,0:T(8,128)S(1)}, f32[32,128,128]{2,1,0:T(8,128)S(1)}) fusion(f32[128,128,128]{2,1,0:T(8,128)} %shard_map.87), kind=kLoop, calls=%fused_computation.142 | loop fusion | bytes 12582912 | tf_op jit(solution)/shard_map/slice | solution.py:83
  141.1 3.7 %collective-permute-done.17 = bf16[4,4,128,128]{3,2,1,0:T(8,128)(2,1)S(1)} collective-permute-done((bf16[4,4,128,128]{3,2,1,0:T(8,128)(2,1)S(1)}, bf16[4,4,128,128]{3,2,1,0:T(8,128)(2,1)S(1)}, u32[]{:S(2)}, u32[]{:S(2)}) %collective-permute-start.17) | collective-permute-done | bytes 524320 | tf_op jit(solution)/shard_map/ppermute | solution.py:37
  147.4 12.5 %collective-permute-done.18 = bf16[4,4,256,128]{3,2,1,0:T(8,128)(2,1)S(1)} collective-permute-done((bf16[4,4,256,128]{3,2,1,0:T(8,128)(2,1)S(1)}, bf16[4,4,256,128]{3,2,1,0:T(8,128)(2,1)S(1)}, u32[]{:S(2)}, u32[]{:S(2)}) %collective-permute-start.18) | collective-permute-done | bytes 1048608 | tf_op jit(solution)/shard_map/ppermute | solution.py:37
  159.9 2.7 %collective-permute-done.16 = bf16[4,4,256,128]{3,2,1,0:T(8,128)(2,1)S(1)} collective-permute-done((bf16[4,4,256,128]{3,2,1,0:T(8,128)(2,1)S(1)}, bf16[4,4,256,128]{3,2,1,0:T(8,128)(2,1)S(1)}, u32[]{:S(2)}, u32[]{:S(2)}) %collective-permute-start.16) | collective-permute-done | bytes 1048608 | tf_op jit(solution)/shard_map/ppermute | solution.py:37
  163.7 2.3 %collective-permute-start.21 = (bf16[4,256,128]{2,1,0:T(8,128)(2,1)S(1)}, bf16[4,256,128]{2,1,0:T(8,128)(2,1)S(1)}, u32[]{:S(2)}, u32[]{:S(2)}) collective-permute-start(bf16[4,256,128]{2,1,0:T(8,128)(2,1)S(1)} %get-tuple-element.17), channel_id=1, source_target_pairs={{0,8},{1,9},{2,10},{3,11},{4,12},{5,13},{6,14},{7,15},{8,0},{9,1},... | collective-permute-start | bytes 786440 | tf_op jit(solution)/shard_map/ppermute | solution.py:37
  166.0 1.4 collective-permute-start.20
  167.4 4.6 %collective-permute-done.19 = bf16[4,256,128]{2,1,0:T(8,128)(2,1)S(1)} collective-permute-done((bf16[4,256,128]{2,1,0:T(8,128)(2,1)S(1)}, bf16[4,256,128]{2,1,0:T(8,128)(2,1)S(1)}, u32[]{:S(2)}, u32[]{:S(2)}) %collective-permute-start.19) | collective-permute-done | bytes 262176 | tf_op jit(solution)/shard_map/ppermute | solution.py:37
  172.0 6.2 %collective-permute-done.21 = bf16[4,256,128]{2,1,0:T(8,128)(2,1)S(1)} collective-permute-done((bf16[4,256,128]{2,1,0:T(8,128)(2,1)S(1)}, bf16[4,256,128]{2,1,0:T(8,128)(2,1)S(1)}, u32[]{:S(2)}, u32[]{:S(2)}) %collective-permute-start.21) | collective-permute-done | bytes 262176 | tf_op jit(solution)/shard_map/ppermute | solution.py:37
  178.5 1.7 collective-permute-start.24
  180.3 1.5 collective-permute-start.23
  181.8 2.9 %collective-permute-done.22 = bf16[256,128]{1,0:T(8,128)(2,1)S(1)} collective-permute-done((bf16[256,128]{1,0:T(8,128)(2,1)S(1)}, bf16[256,128]{1,0:T(8,128)(2,1)S(1)}, u32[]{:S(2)}, u32[]{:S(2)}) %collective-permute-start.22) | collective-permute-done | bytes 65568 | tf_op jit(solution)/shard_map/ppermute | solution.py:37
  186.1 14.6 %all_to_all.24 = f32[32,4,384]{2,1,0:T(4,128)S(1)} all-to-all(f32[32,4,384]{2,1,0:T(4,128)S(1)} %pad_maximum_fusion.5), channel_id=1, replica_groups=mesh['blk'=4,'feat'=32] {'feat'}, dimensions={0} | all-to-all | bytes 393216 | tf_op jit(solution)/shard_map/all_to_all | solution.py:339
  203.6 3.5 %collective-permute-done.26 = f32[4,128]{1,0:T(4,128)S(1)} collective-permute-done((f32[4,128]{1,0:T(4,128)S(1)}, f32[4,128]{1,0:T(4,128)S(1)}, u32[]{:S(2)}, u32[]{:S(2)}) %collective-permute-start.26) | collective-permute-done | bytes 2080 | tf_op jit(solution)/shard_map/ppermute | solution.py:46
  (79 shorter events, 19.9 us)
Async XLA Ops:
  0.6 17.7 %copy-start = (bf16[128,128]{1,0:T(8,128)(2,1)S(1)}, bf16[128,128]{1,0:T(8,128)(2,1)}, u32[]{:S(2)}) copy-start(bf16[128,128]{1,0:T(8,128)(2,1)} %param.7) | copy-start | bytes 98308
  0.6 89.2 %collective-permute-start.13 = (bf16[4,2,32,128,128]{4,3,2,1,0:T(8,128)(2,1)}, bf16[4,2,32,128,128]{4,3,2,1,0:T(8,128)(2,1)}, u32[]{:S(2)}, u32[]{:S(2)}) collective-permute-start(bf16[4,2,32,128,128]{4,3,2,1,0:T(8,128)(2,1)} %bitcast.101), channel_id=1, source_target_pairs={{0,32},{32,0},{64,96},{96,64},{1,33},{33,1},{65,97},{97,65},{2,34}... | collective-permute-start | bytes 25165832 | tf_op jit(solution)/shard_map/ppermute | solution.py:41
  0.7 17.6 %all-to-all-start = ((bf16[4,32,256]{2,0,1:T(4,128)(2,1)}), bf16[4,32,256]{2,0,1:T(4,128)(2,1)S(1)}, u32[]{:S(2)}, u32[]{:S(2)}) async-start(bf16[4,32,256]{2,0,1:T(4,128)(2,1)} %bitcast.128), calls=%async_computation | async-start | bytes 131072 | tf_op jit(solution)/shard_map/all_to_all | solution.py:277
  10.0 8.6 %collective-permute-start.1 = (s32[8]{0:T(128)}, s32[8]{0:T(128)S(1)}, u32[]{:S(2)}, u32[]{:S(2)}) collective-permute-start(s32[8]{0:T(128)} %count_ref.3), channel_id=1, source_target_pairs={{0,32},{32,0},{64,96},{96,64},{1,33},{33,1},{65,97},{97,65},{2,34}... | collective-permute-start | bytes 104 | tf_op jit(solution)/shard_map/ppermute | solution.py:41
  10.3 8.3 %collective-permute-start = (s32[256]{0:T(256)}, s32[256]{0:T(256)S(1)}, u32[]{:S(2)}, u32[]{:S(2)}) collective-permute-start(s32[256]{0:T(256)} %param.9), channel_id=1, source_target_pairs={{0,32},{32,0},{64,96},{96,64},{1,33},{33,1},{65,97},{97,65},{2,34}... | collective-permute-start | bytes 3080 | tf_op jit(solution)/shard_map/ppermute | solution.py:41
  18.6 5.5 %collective-permute-start.4 = (bf16[256,128]{1,0:T(8,128)(2,1)S(1)}, bf16[256,128]{1,0:T(8,128)(2,1)S(1)}, u32[]{:S(2)}, u32[]{:S(2)}) collective-permute-start(bf16[256,128]{1,0:T(8,128)(2,1)S(1)} %convolution_convert_fusion.1), channel_id=1, source_target_pairs={{0,1},{1,2},{2,3},{3,0},{4,5},{5,6},{6,7},{7,4},{8,9},{9,10},{10,1... | collective-permute-start | bytes 196616 | tf_op jit(solution)/shard_map/ppermute | solution.py:37
  19.2 5.8 %collective-permute-start.3 = (bf16[256,128]{1,0:T(8,128)(2,1)S(1)}, bf16[256,128]{1,0:T(8,128)(2,1)S(1)}, u32[]{:S(2)}, u32[]{:S(2)}) collective-permute-start(bf16[256,128]{1,0:T(8,128)(2,1)S(1)} %convolution_convert_fusion.1), channel_id=1, source_target_pairs={{0,2},{1,3},{2,0},{3,1},{4,6},{5,7},{6,4},{7,5},{8,10},{9,11},{10,... | collective-permute-start | bytes 196616 | tf_op jit(solution)/shard_map/ppermute | solution.py:37
  21.5 4.3 %collective-permute-start.2 = (bf16[256,128]{1,0:T(8,128)(2,1)S(1)}, bf16[256,128]{1,0:T(8,128)(2,1)S(1)}, u32[]{:S(2)}, u32[]{:S(2)}) collective-permute-start(bf16[256,128]{1,0:T(8,128)(2,1)S(1)} %convolution_convert_fusion.1), channel_id=1, source_target_pairs={{0,3},{1,0},{2,1},{3,2},{4,7},{5,4},{6,5},{7,6},{8,11},{9,8},{10,9... | collective-permute-start | bytes 196616 | tf_op jit(solution)/shard_map/ppermute | solution.py:37
  25.8 10.8 %collective-permute-start.6 = (bf16[4,256,128]{2,1,0:T(8,128)(2,1)S(1)}, bf16[4,256,128]{2,1,0:T(8,128)(2,1)S(1)}, u32[]{:S(2)}, u32[]{:S(2)}) collective-permute-start(bf16[4,256,128]{2,1,0:T(8,128)(2,1)S(1)} %get-tuple-element.27), channel_id=1, source_target_pairs={{0,8},{1,9},{2,10},{3,11},{4,12},{5,13},{6,14},{7,15},{8,0},{9,1},... | collective-permute-start | bytes 786440 | tf_op jit(solution)/shard_map/ppermute | solution.py:37
  27.2 11.3 %collective-permute-start.5 = (bf16[4,256,128]{2,1,0:T(8,128)(2,1)S(1)}, bf16[4,256,128]{2,1,0:T(8,128)(2,1)S(1)}, u32[]{:S(2)}, u32[]{:S(2)}) collective-permute-start(bf16[4,256,128]{2,1,0:T(8,128)(2,1)S(1)} %get-tuple-element.27), channel_id=1, source_target_pairs={{0,12},{1,13},{2,14},{3,15},{4,0},{5,1},{6,2},{7,3},{8,4},{9,5},{1... | collective-permute-start | bytes 786440 | tf_op jit(solution)/shard_map/ppermute | solution.py:37
  29.1 10.6 %collective-permute-start.7 = (bf16[4,256,128]{2,1,0:T(8,128)(2,1)S(1)}, bf16[4,256,128]{2,1,0:T(8,128)(2,1)S(1)}, u32[]{:S(2)}, u32[]{:S(2)}) collective-permute-start(bf16[4,256,128]{2,1,0:T(8,128)(2,1)S(1)} %get-tuple-element.27), channel_id=1, source_target_pairs={{0,4},{1,5},{2,6},{3,7},{4,8},{5,9},{6,10},{7,11},{8,12},{9,13},{1... | collective-permute-start | bytes 786440 | tf_op jit(solution)/shard_map/ppermute | solution.py:37
  39.9 15.3 %collective-permute-start.8 = (bf16[4,4,256,128]{3,2,1,0:T(8,128)(2,1)S(1)}, bf16[4,4,256,128]{3,2,1,0:T(8,128)(2,1)S(1)}, u32[]{:S(2)}, u32[]{:S(2)}) collective-permute-start(bf16[4,4,256,128]{3,2,1,0:T(8,128)(2,1)S(1)} %get-tuple-element.22), channel_id=1, source_target_pairs={{0,80},{1,81},{2,82},{3,83},{4,84},{5,85},{6,86},{7,87},{8,88},{9,... | collective-permute-start | bytes 3145736 | tf_op jit(solution)/shard_map/ppermute | solution.py:37
  42.9 16.1 %collective-permute-start.9 = (bf16[4,4,256,128]{3,2,1,0:T(8,128)(2,1)S(1)}, bf16[4,4,256,128]{3,2,1,0:T(8,128)(2,1)S(1)}, u32[]{:S(2)}, u32[]{:S(2)}) collective-permute-start(bf16[4,4,256,128]{3,2,1,0:T(8,128)(2,1)S(1)} %get-tuple-element.22), channel_id=1, source_target_pairs={{0,16},{1,17},{2,18},{3,19},{4,20},{5,21},{6,22},{7,23},{8,24},{9,... | collective-permute-start | bytes 3145736 | tf_op jit(solution)/shard_map/ppermute | solution.py:37
  55.3 10.5 %collective-permute-start.11 = (bf16[4,4,128,128]{3,2,1,0:T(8,128)(2,1)S(1)}, bf16[4,4,128,128]{3,2,1,0:T(8,128)(2,1)S(1)}, u32[]{:S(2)}, u32[]{:S(2)}) collective-permute-start(bf16[4,4,128,128]{3,2,1,0:T(8,128)(2,1)S(1)} %slice.104), channel_id=1, source_target_pairs={{0,80},{1,81},{2,82},{3,83},{4,84},{5,85},{6,86},{7,87},{8,88},{9,... | collective-permute-start | bytes 1572872 | tf_op jit(solution)/shard_map/ppermute | solution.py:37
  59.1 10.5 %collective-permute-start.10 = (bf16[4,4,128,128]{3,2,1,0:T(8,128)(2,1)S(1)}, bf16[4,4,128,128]{3,2,1,0:T(8,128)(2,1)S(1)}, u32[]{:S(2)}, u32[]{:S(2)}) collective-permute-start(bf16[4,4,128,128]{3,2,1,0:T(8,128)(2,1)S(1)} %slice.103), channel_id=1, source_target_pairs={{0,16},{1,17},{2,18},{3,19},{4,20},{5,21},{6,22},{7,23},{8,24},{9,... | collective-permute-start | bytes 1572872 | tf_op jit(solution)/shard_map/ppermute | solution.py:37
  71.9 7.5 %collective-permute-start.12 = (bf16[128,128,128]{2,1,0:T(8,128)(2,1)}, bf16[128,128,128]{2,1,0:T(8,128)(2,1)}, u32[]{:S(2)}, u32[]{:S(2)}) collective-permute-start(bf16[128,128,128]{2,1,0:T(8,128)(2,1)} %bitcast.16.proj_ref), channel_id=1, source_target_pairs={{0,32},{32,0},{64,96},{96,64},{1,33},{33,1},{65,97},{97,65},{2,34}... | collective-permute-start | bytes 12582920 | tf_op jit(solution)/shard_map/ppermute | solution.py:41
  79.4 6.7 %copy-start.1 = (f32[2,128,128]{2,1,0:T(8,128)S(1)}, f32[2,128,128]{2,1,0:T(8,128)}, u32[]{:S(2)}) copy-start(f32[2,128,128]{2,1,0:T(8,128)} %shard_map.85) | copy-start | bytes 393220
  79.4 7.6 %copy-start.2 = (bf16[256,128]{1,0:T(8,128)(2,1)S(1)}, bf16[256,128]{1,0:T(8,128)(2,1)}, u32[]{:S(2)}) copy-start(bf16[256,128]{1,0:T(8,128)(2,1)} %param.11) | copy-start | bytes 196612
  79.4 8.8 %copy-start.4 = (s32[8]{0:T(128)S(1)}, s32[8]{0:T(128)}, u32[]{:S(2)}) copy-start(s32[8]{0:T(128)} %count_ref.3) | copy-start | bytes 100
  87.9 1.3 collective-permute-start.14
  135.5 9.2 %collective-permute-start.17 = (bf16[4,4,128,128]{3,2,1,0:T(8,128)(2,1)S(1)}, bf16[4,4,128,128]{3,2,1,0:T(8,128)(2,1)S(1)}, u32[]{:S(2)}, u32[]{:S(2)}) collective-permute-start(bf16[4,4,128,128]{3,2,1,0:T(8,128)(2,1)S(1)} %get-tuple-element.20), channel_id=1, source_target_pairs={{0,80},{1,81},{2,82},{3,83},{4,84},{5,85},{6,86},{7,87},{8,88},{9,... | collective-permute-start | bytes 1572872 | tf_op jit(solution)/shard_map/ppermute | solution.py:37
  135.6 10.7 %collective-permute-start.15 = (bf16[4,4,128,128]{3,2,1,0:T(8,128)(2,1)S(1)}, bf16[4,4,128,128]{3,2,1,0:T(8,128)(2,1)S(1)}, u32[]{:S(2)}, u32[]{:S(2)}) collective-permute-start(bf16[4,4,128,128]{3,2,1,0:T(8,128)(2,1)S(1)} %get-tuple-element.19), channel_id=1, source_target_pairs={{0,16},{1,17},{2,18},{3,19},{4,20},{5,21},{6,22},{7,23},{8,24},{9,... | collective-permute-start | bytes 1572872 | tf_op jit(solution)/shard_map/ppermute | solution.py:37
  145.0 14.9 %collective-permute-start.18 = (bf16[4,4,256,128]{3,2,1,0:T(8,128)(2,1)S(1)}, bf16[4,4,256,128]{3,2,1,0:T(8,128)(2,1)S(1)}, u32[]{:S(2)}, u32[]{:S(2)}) collective-permute-start(bf16[4,4,256,128]{3,2,1,0:T(8,128)(2,1)S(1)} %pad_maximum_fusion.3), channel_id=1, source_target_pairs={{0,80},{1,81},{2,82},{3,83},{4,84},{5,85},{6,86},{7,87},{8,88},{9,... | collective-permute-start | bytes 3145736 | tf_op jit(solution)/shard_map/ppermute | solution.py:37
  146.5 16.1 %collective-permute-start.16 = (bf16[4,4,256,128]{3,2,1,0:T(8,128)(2,1)S(1)}, bf16[4,4,256,128]{3,2,1,0:T(8,128)(2,1)S(1)}, u32[]{:S(2)}, u32[]{:S(2)}) collective-permute-start(bf16[4,4,256,128]{3,2,1,0:T(8,128)(2,1)S(1)} %pad_maximum_fusion.2), channel_id=1, source_target_pairs={{0,16},{1,17},{2,18},{3,19},{4,20},{5,21},{6,22},{7,23},{8,24},{9,... | collective-permute-start | bytes 3145736 | tf_op jit(solution)/shard_map/ppermute | solution.py:37
  163.1 8.9 %collective-permute-start.19 = (bf16[4,256,128]{2,1,0:T(8,128)(2,1)S(1)}, bf16[4,256,128]{2,1,0:T(8,128)(2,1)S(1)}, u32[]{:S(2)}, u32[]{:S(2)}) collective-permute-start(bf16[4,256,128]{2,1,0:T(8,128)(2,1)S(1)} %get-tuple-element.16), channel_id=1, source_target_pairs={{0,4},{1,5},{2,6},{3,7},{4,8},{5,9},{6,10},{7,11},{8,12},{9,13},{1... | collective-permute-start | bytes 786440 | tf_op jit(solution)/shard_map/ppermute | solution.py:37
  163.7 14.5 %collective-permute-start.21 = (bf16[4,256,128]{2,1,0:T(8,128)(2,1)S(1)}, bf16[4,256,128]{2,1,0:T(8,128)(2,1)S(1)}, u32[]{:S(2)}, u32[]{:S(2)}) collective-permute-start(bf16[4,256,128]{2,1,0:T(8,128)(2,1)S(1)} %get-tuple-element.17), channel_id=1, source_target_pairs={{0,8},{1,9},{2,10},{3,11},{4,12},{5,13},{6,14},{7,15},{8,0},{9,1},... | collective-permute-start | bytes 786440 | tf_op jit(solution)/shard_map/ppermute | solution.py:37
  166.0 12.3 %collective-permute-start.20 = (bf16[4,256,128]{2,1,0:T(8,128)(2,1)S(1)}, bf16[4,256,128]{2,1,0:T(8,128)(2,1)S(1)}, u32[]{:S(2)}, u32[]{:S(2)}) collective-permute-start(bf16[4,256,128]{2,1,0:T(8,128)(2,1)S(1)} %get-tuple-element.18), channel_id=1, source_target_pairs={{0,12},{1,13},{2,14},{3,15},{4,0},{5,1},{6,2},{7,3},{8,4},{9,5},{1... | collective-permute-start | bytes 786440 | tf_op jit(solution)/shard_map/ppermute | solution.py:37
  178.4 6.2 %collective-permute-start.22 = (bf16[256,128]{1,0:T(8,128)(2,1)S(1)}, bf16[256,128]{1,0:T(8,128)(2,1)S(1)}, u32[]{:S(2)}, u32[]{:S(2)}) collective-permute-start(bf16[256,128]{1,0:T(8,128)(2,1)S(1)} %get-tuple-element.23), channel_id=1, source_target_pairs={{0,1},{1,2},{2,3},{3,0},{4,5},{5,6},{6,7},{7,4},{8,9},{9,10},{10,1... | collective-permute-start | bytes 196616 | tf_op jit(solution)/shard_map/ppermute | solution.py:37
  178.5 6.2 %collective-permute-start.24 = (bf16[256,128]{1,0:T(8,128)(2,1)S(1)}, bf16[256,128]{1,0:T(8,128)(2,1)S(1)}, u32[]{:S(2)}, u32[]{:S(2)}) collective-permute-start(bf16[256,128]{1,0:T(8,128)(2,1)S(1)} %get-tuple-element.24), channel_id=1, source_target_pairs={{0,2},{1,3},{2,0},{3,1},{4,6},{5,7},{6,4},{7,5},{8,10},{9,11},{10,... | collective-permute-start | bytes 196616 | tf_op jit(solution)/shard_map/ppermute | solution.py:37
  180.3 5.3 %collective-permute-start.23 = (bf16[256,128]{1,0:T(8,128)(2,1)S(1)}, bf16[256,128]{1,0:T(8,128)(2,1)S(1)}, u32[]{:S(2)}, u32[]{:S(2)}) collective-permute-start(bf16[256,128]{1,0:T(8,128)(2,1)S(1)} %get-tuple-element.25), channel_id=1, source_target_pairs={{0,3},{1,0},{2,1},{3,2},{4,7},{5,4},{6,5},{7,6},{8,11},{9,8},{10,9... | collective-permute-start | bytes 196616 | tf_op jit(solution)/shard_map/ppermute | solution.py:37
  200.8 1.2 collective-permute-start.25
  202.0 5.1 %collective-permute-start.26 = (f32[4,128]{1,0:T(4,128)S(1)}, f32[4,128]{1,0:T(4,128)S(1)}, u32[]{:S(2)}, u32[]{:S(2)}) collective-permute-start(f32[4,128]{1,0:T(4,128)S(1)} %add.221), channel_id=1, source_target_pairs={{0,64},{32,96},{64,0},{96,32},{1,65},{33,97},{65,1},{97,33},{2,66}... | collective-permute-start | bytes 6152 | tf_op jit(solution)/shard_map/ppermute | solution.py:46
  (2 other events, 2.9 us)

commit v18 on v17

--- a/solution.py
+++ b/solution.py
@@ -192,10 +192,7 @@
             for slot in range(slot_count):
                 spot = where_ref[(source * blocks * tile_rows + base) * slot_count + slot]
                 term = jnp.dot(grad_rows, tiles_ref[slot], preferred_element_type=jnp.float32)
-
-                @pl.when(slot < live)
-                def _():
-                    total_ref[spot] += term
+                total_ref[spot] += jnp.where(slot < live, term, jnp.zeros_like(term))
 
         pl.when(source == 0)(lambda: spread(own_ref))
         pl.when(source == 1)(lambda: spread(other_ref))

time: 208 us -> 178 us (0.86)
  Pallas kernels: 57 us -> 26.1 us
    pallas_call x1, Pallas kernels: 43.8 us -> 12.9 us  [spread_pair(): pl.pallas_call(kernel, grid_spec=grid_spec, out_shape=jax.ShapeDtypeStruc...]
  transfers between devices with their start and end apart: 28 -> 28, of which waited for: 21 -> 22; matrix products, arithmetic and copies ran while one was open for 5% -> 6% of each run, Pallas kernels for 6% -> 7%
where the time goes in v18:
time: 178 us; the launch traced here: 177 us
  waiting for transfers between devices  83.2 us (47%)
  starting transfers between devices  37.3 us (21%)
  Pallas kernels  26.1 us (15%)
  blocking collectives  14.6 us (8%)
  other arithmetic  7.84 us (4%)
  local copies, waits for them, and re-layouts  6.43 us (4%)
    ppermute x20, waiting for transfers between devices, ring_shift(): return lax.ppermute(block, BOTH, route)  70 us
    ppermute x20, starting transfers between devices, ring_shift(): return lax.ppermute(block, BOTH, route)  26.2 us
    all_to_all x1, blocking collectives, body(): lax.all_to_all(outgoing, 'feat', split_axis=0, concat_axis=0, tiled=True)  14.6 us
    pallas_call x2, Pallas kernels, aggregate_pair(): pl.pallas_call(aggregate_kernel, grid_spec=grid_spec, out_shape=jax.Shape...  13.2 us
    pallas_call x1, Pallas kernels, spread_pair(): pl.pallas_call(kernel, grid_spec=grid_spec, out_shape=jax.ShapeDtypeStruc...  12.9 us
    all_to_all x1, starting transfers between devices, body(): lax.all_to_all(features_t, 'feat', split_axis=1, concat_axis=0, tiled=True)  9.27 us
    all_to_all x1, waiting for transfers between devices, body(): lax.all_to_all(features_t, 'feat', split_axis=1, concat_axis=0, tiled=True)  7.74 us
    slice x2, local copies, waits for them, and re-layouts, term(): return total[k]  5.03 us
  transfers between devices with their start and end apart: 28, of which 22 were waited for; matrix products, arithmetic and copies ran while one was open for 6% of the time, Pallas kernels for 7%

profile of v18, /device:TPU:0, one launch (start us, length us, event | category | flops | bytes accessed | tf_op | source)
XLA Modules:
  0.0 177.0 jit_solution(11419275649677815225)
XLA Ops:
  0.7 9.3 %all-to-all-start = ((bf16[4,32,256]{2,0,1:T(4,128)(2,1)}), bf16[4,32,256]{2,0,1:T(4,128)(2,1)S(1)}, u32[]{:S(2)}, u32[]{:S(2)}) async-start(bf16[4,32,256]{2,0,1:T(4,128)(2,1)} %bitcast.128), calls=%async_computation | async-start | bytes 131072 | tf_op jit(solution)/shard_map/all_to_all | solution.py:274
  10.6 7.7 %all-to-all-done = bf16[4,32,256]{2,0,1:T(4,128)(2,1)S(1)} async-done(((bf16[4,32,256]{2,0,1:T(4,128)(2,1)}), bf16[4,32,256]{2,0,1:T(4,128)(2,1)S(1)}, u32[]{:S(2)}, u32[]{:S(2)}) %all-to-all-start) | async-done | bytes 65568 | tf_op jit(solution)/shard_map/all_to_all | solution.py:274
  19.2 2.3 %collective-permute-start.3 = (bf16[256,128]{1,0:T(8,128)(2,1)S(1)}, bf16[256,128]{1,0:T(8,128)(2,1)S(1)}, u32[]{:S(2)}, u32[]{:S(2)}) collective-permute-start(bf16[256,128]{1,0:T(8,128)(2,1)S(1)} %convolution_convert_fusion.1), channel_id=1, source_target_pairs={{0,2},{1,3},{2,0},{3,1},{4,6},{5,7},{6,4},{7,5},{8,10},{9,11},{10,... | collective-permute-start | bytes 196616 | tf_op jit(solution)/shard_map/ppermute | solution.py:37
  22.6 1.5 collective-permute-done.4
  25.8 1.4 collective-permute-start.6
  27.2 1.9 %collective-permute-start.5 = (bf16[4,256,128]{2,1,0:T(8,128)(2,1)S(1)}, bf16[4,256,128]{2,1,0:T(8,128)(2,1)S(1)}, u32[]{:S(2)}, u32[]{:S(2)}) collective-permute-start(bf16[4,256,128]{2,1,0:T(8,128)(2,1)S(1)} %get-tuple-element.27), channel_id=1, source_target_pairs={{0,12},{1,13},{2,14},{3,15},{4,0},{5,1},{6,2},{7,3},{8,4},{9,5},{1... | collective-permute-start | bytes 786440 | tf_op jit(solution)/shard_map/ppermute | solution.py:37
  29.3 7.4 %collective-permute-done.6 = bf16[4,256,128]{2,1,0:T(8,128)(2,1)S(1)} collective-permute-done((bf16[4,256,128]{2,1,0:T(8,128)(2,1)S(1)}, bf16[4,256,128]{2,1,0:T(8,128)(2,1)S(1)}, u32[]{:S(2)}, u32[]{:S(2)}) %collective-permute-start.6) | collective-permute-done | bytes 262176 | tf_op jit(solution)/shard_map/ppermute | solution.py:37
  36.6 1.9 %collective-permute-done.5 = bf16[4,256,128]{2,1,0:T(8,128)(2,1)S(1)} collective-permute-done((bf16[4,256,128]{2,1,0:T(8,128)(2,1)S(1)}, bf16[4,256,128]{2,1,0:T(8,128)(2,1)S(1)}, u32[]{:S(2)}, u32[]{:S(2)}) %collective-permute-start.5) | collective-permute-done | bytes 262176 | tf_op jit(solution)/shard_map/ppermute | solution.py:37
  39.9 3.0 %collective-permute-start.8 = (bf16[4,4,256,128]{3,2,1,0:T(8,128)(2,1)S(1)}, bf16[4,4,256,128]{3,2,1,0:T(8,128)(2,1)S(1)}, u32[]{:S(2)}, u32[]{:S(2)}) collective-permute-start(bf16[4,4,256,128]{3,2,1,0:T(8,128)(2,1)S(1)} %get-tuple-element.22), channel_id=1, source_target_pairs={{0,80},{1,81},{2,82},{3,83},{4,84},{5,85},{6,86},{7,87},{8,88},{9,... | collective-permute-start | bytes 3145736 | tf_op jit(solution)/shard_map/ppermute | solution.py:37
  42.9 12.3 %collective-permute-done.8 = bf16[4,4,256,128]{3,2,1,0:T(8,128)(2,1)S(1)} collective-permute-done((bf16[4,4,256,128]{3,2,1,0:T(8,128)(2,1)S(1)}, bf16[4,4,256,128]{3,2,1,0:T(8,128)(2,1)S(1)}, u32[]{:S(2)}, u32[]{:S(2)}) %collective-permute-start.8) | collective-permute-done | bytes 1048608 | tf_op jit(solution)/shard_map/ppermute | solution.py:37
  55.3 3.8 %collective-permute-start.11 = (bf16[4,4,128,128]{3,2,1,0:T(8,128)(2,1)S(1)}, bf16[4,4,128,128]{3,2,1,0:T(8,128)(2,1)S(1)}, u32[]{:S(2)}, u32[]{:S(2)}) collective-permute-start(bf16[4,4,128,128]{3,2,1,0:T(8,128)(2,1)S(1)} %slice.104), channel_id=1, source_target_pairs={{0,80},{1,81},{2,82},{3,83},{4,84},{5,85},{6,86},{7,87},{8,88},{9,... | collective-permute-start | bytes 1572872 | tf_op jit(solution)/shard_map/ppermute | solution.py:37
  59.2 6.6 %collective-permute-done.11 = bf16[4,4,128,128]{3,2,1,0:T(8,128)(2,1)S(1)} collective-permute-done((bf16[4,4,128,128]{3,2,1,0:T(8,128)(2,1)S(1)}, bf16[4,4,128,128]{3,2,1,0:T(8,128)(2,1)S(1)}, u32[]{:S(2)}, u32[]{:S(2)}) %collective-permute-start.11) | collective-permute-done | bytes 524320 | tf_op jit(solution)/shard_map/ppermute | solution.py:37
  65.7 3.8 %collective-permute-done.10 = bf16[4,4,128,128]{3,2,1,0:T(8,128)(2,1)S(1)} collective-permute-done((bf16[4,4,128,128]{3,2,1,0:T(8,128)(2,1)S(1)}, bf16[4,4,128,128]{3,2,1,0:T(8,128)(2,1)S(1)}, u32[]{:S(2)}, u32[]{:S(2)}) %collective-permute-start.10) | collective-permute-done | bytes 524320 | tf_op jit(solution)/shard_map/ppermute | solution.py:37
  69.6 2.3 %pad_maximum_fusion = bf16[4,4,4,256,128]{4,3,2,1,0:T(8,128)(2,1)} fusion(bf16[1,4,4,256,128]{4,3,2,1,0:T(8,128)(2,1)S(1)} %bitcast.112, bf16[1,4,4,256,128]{4,3,2,1,0:T(8,128)(2,1)S(1)} %maximum_bitcast_fusion, bf16[1,4,4,256,128]{4,3,2,1,0:T(8,128)(2,1)S(1)} %bitcast.111, bf16[1,4,4,256,128]{4,3,2,1,0:T(8,128)(2,1)S(1)} %get-tuple-element.21), kind=kLoop, calls=%fused_computation | loop fusion | flops 6291456 | bytes 8388608 | tf_op jit(solution)/shard_map/stack | solution.py:56
  72.6 6.5 %shard_map.85 = f32[2,128,128]{2,1,0:T(8,128)} custom-call(s32[1]{0:T(128)} %bitcast.core_ref, s32[256]{0:T(256)} %copy-done.3, s32[8]{0:T(128)} %count_ref.3, bf16[4,2,32,128,128]{4,3,2,1,0:T(8,128)(2,1)} %bitcast.102, bf16[128,128,128]{2,1,0:T(8,128)(2,1)} %bitcast.16.proj_ref), custom_call_target="tpu_custom_call" | custom-call | tf_op jit(solution)/shard_map/pallas_call | solution.py:155
  79.4 6.7 %shard_map.86 = f32[2,128,128]{2,1,0:T(8,128)} custom-call(s32[1]{0:T(128)} %bitcast.17.core_ref, s32[256]{0:T(256)} %copy-done.3, s32[8]{0:T(128)} %count_ref.3, bf16[4,2,32,128,128]{4,3,2,1,0:T(8,128)(2,1)} %bitcast.103, bf16[128,128,128]{2,1,0:T(8,128)(2,1)} %collective-permute-done.12.proj_ref), custom_call_target="tpu_custom_call" | custom-call | tf_op jit(solution)/shard_map/pallas_call | solution.py:155
  89.9 12.9 %shard_map.87 = f32[128,128,128]{2,1,0:T(8,128)} custom-call(s32[1]{0:T(128)} %bitcast.core_ref, s32[512]{0:T(512)} %pad_add_fusion.where_ref, s32[16]{0:T(128)} %pad_add_fusion.1.count_ref, bf16[4,2,32,128,128]{4,3,2,1,0:T(8,128)(2,1)} %bitcast.104, bf16[4,2,32,128,128]{4,3,2,1,0:T(8,128)(2,1)} %collective-permute-done.13.other_ref, ...), custom_call_target="tpu_custom_call" | custom-call | tf_op jit(solution)/shard_map/pallas_call | solution.py:222
  102.7 1.7 slice.158
  104.7 2.0 %collective-permute-start.15 = (bf16[4,4,128,128]{3,2,1,0:T(8,128)(2,1)S(1)}, bf16[4,4,128,128]{3,2,1,0:T(8,128)(2,1)S(1)}, u32[]{:S(2)}, u32[]{:S(2)}) collective-permute-start(bf16[4,4,128,128]{3,2,1,0:T(8,128)(2,1)S(1)} %get-tuple-element.19), channel_id=1, source_target_pairs={{0,16},{1,17},{2,18},{3,19},{4,20},{5,21},{6,22},{7,23},{8,24},{9,... | collective-permute-start | bytes 1572872 | tf_op jit(solution)/shard_map/ppermute | solution.py:37
  106.7 3.3 %fusion.39 = (f32[32,128,128]{2,1,0:T(8,128)S(1)}, f32[32,128,128]{2,1,0:T(8,128)S(1)}, f32[32,128,128]{2,1,0:T(8,128)S(1)}) fusion(f32[128,128,128]{2,1,0:T(8,128)} %shard_map.87), kind=kLoop, calls=%fused_computation.142 | loop fusion | bytes 12582912 | tf_op jit(solution)/shard_map/slice | solution.py:83
  110.2 3.7 %collective-permute-done.17 = bf16[4,4,128,128]{3,2,1,0:T(8,128)(2,1)S(1)} collective-permute-done((bf16[4,4,128,128]{3,2,1,0:T(8,128)(2,1)S(1)}, bf16[4,4,128,128]{3,2,1,0:T(8,128)(2,1)S(1)}, u32[]{:S(2)}, u32[]{:S(2)}) %collective-permute-start.17) | collective-permute-done | bytes 524320 | tf_op jit(solution)/shard_map/ppermute | solution.py:37
  114.1 1.3 collective-permute-start.18
  116.7 12.3 %collective-permute-done.18 = bf16[4,4,256,128]{3,2,1,0:T(8,128)(2,1)S(1)} collective-permute-done((bf16[4,4,256,128]{3,2,1,0:T(8,128)(2,1)S(1)}, bf16[4,4,256,128]{3,2,1,0:T(8,128)(2,1)S(1)}, u32[]{:S(2)}, u32[]{:S(2)}) %collective-permute-start.18) | collective-permute-done | bytes 1048608 | tf_op jit(solution)/shard_map/ppermute | solution.py:37
  129.0 2.9 %collective-permute-done.16 = bf16[4,4,256,128]{3,2,1,0:T(8,128)(2,1)S(1)} collective-permute-done((bf16[4,4,256,128]{3,2,1,0:T(8,128)(2,1)S(1)}, bf16[4,4,256,128]{3,2,1,0:T(8,128)(2,1)S(1)}, u32[]{:S(2)}, u32[]{:S(2)}) %collective-permute-start.16) | collective-permute-done | bytes 1048608 | tf_op jit(solution)/shard_map/ppermute | solution.py:37
  132.9 2.4 %collective-permute-start.21 = (bf16[4,256,128]{2,1,0:T(8,128)(2,1)S(1)}, bf16[4,256,128]{2,1,0:T(8,128)(2,1)S(1)}, u32[]{:S(2)}, u32[]{:S(2)}) collective-permute-start(bf16[4,256,128]{2,1,0:T(8,128)(2,1)S(1)} %get-tuple-element.17), channel_id=1, source_target_pairs={{0,8},{1,9},{2,10},{3,11},{4,12},{5,13},{6,14},{7,15},{8,0},{9,1},... | collective-permute-start | bytes 786440 | tf_op jit(solution)/shard_map/ppermute | solution.py:37
  136.6 4.8 %collective-permute-done.19 = bf16[4,256,128]{2,1,0:T(8,128)(2,1)S(1)} collective-permute-done((bf16[4,256,128]{2,1,0:T(8,128)(2,1)S(1)}, bf16[4,256,128]{2,1,0:T(8,128)(2,1)S(1)}, u32[]{:S(2)}, u32[]{:S(2)}) %collective-permute-start.19) | collective-permute-done | bytes 262176 | tf_op jit(solution)/shard_map/ppermute | solution.py:37
  141.4 6.1 %collective-permute-done.21 = bf16[4,256,128]{2,1,0:T(8,128)(2,1)S(1)} collective-permute-done((bf16[4,256,128]{2,1,0:T(8,128)(2,1)S(1)}, bf16[4,256,128]{2,1,0:T(8,128)(2,1)S(1)}, u32[]{:S(2)}, u32[]{:S(2)}) %collective-permute-start.21) | collective-permute-done | bytes 262176 | tf_op jit(solution)/shard_map/ppermute | solution.py:37
  147.8 1.5 collective-permute-start.24
  149.3 1.8 collective-permute-start.23
  151.0 2.9 %collective-permute-done.22 = bf16[256,128]{1,0:T(8,128)(2,1)S(1)} collective-permute-done((bf16[256,128]{1,0:T(8,128)(2,1)S(1)}, bf16[256,128]{1,0:T(8,128)(2,1)S(1)}, u32[]{:S(2)}, u32[]{:S(2)}) %collective-permute-start.22) | collective-permute-done | bytes 65568 | tf_op jit(solution)/shard_map/ppermute | solution.py:37
  155.4 14.6 %all_to_all.24 = f32[32,4,384]{2,1,0:T(4,128)S(1)} all-to-all(f32[32,4,384]{2,1,0:T(4,128)S(1)} %pad_maximum_fusion.5), channel_id=1, replica_groups=mesh['blk'=4,'feat'=32] {'feat'}, dimensions={0} | all-to-all | bytes 393216 | tf_op jit(solution)/shard_map/all_to_all | solution.py:336
  172.7 3.7 %collective-permute-done.26 = f32[4,128]{1,0:T(4,128)S(1)} collective-permute-done((f32[4,128]{1,0:T(4,128)S(1)}, f32[4,128]{1,0:T(4,128)S(1)}, u32[]{:S(2)}, u32[]{:S(2)}) %collective-permute-start.26) | collective-permute-done | bytes 2080 | tf_op jit(solution)/shard_map/ppermute | solution.py:46
  (79 shorter events, 19.9 us)
Async XLA Ops:
  0.6 17.7 %copy-start = (bf16[128,128]{1,0:T(8,128)(2,1)S(1)}, bf16[128,128]{1,0:T(8,128)(2,1)}, u32[]{:S(2)}) copy-start(bf16[128,128]{1,0:T(8,128)(2,1)} %param.7) | copy-start | bytes 98308
  0.6 89.2 %collective-permute-start.13 = (bf16[4,2,32,128,128]{4,3,2,1,0:T(8,128)(2,1)}, bf16[4,2,32,128,128]{4,3,2,1,0:T(8,128)(2,1)}, u32[]{:S(2)}, u32[]{:S(2)}) collective-permute-start(bf16[4,2,32,128,128]{4,3,2,1,0:T(8,128)(2,1)} %bitcast.101), channel_id=1, source_target_pairs={{0,32},{32,0},{64,96},{96,64},{1,33},{33,1},{65,97},{97,65},{2,34}... | collective-permute-start | bytes 25165832 | tf_op jit(solution)/shard_map/ppermute | solution.py:41
  0.7 17.6 %all-to-all-start = ((bf16[4,32,256]{2,0,1:T(4,128)(2,1)}), bf16[4,32,256]{2,0,1:T(4,128)(2,1)S(1)}, u32[]{:S(2)}, u32[]{:S(2)}) async-start(bf16[4,32,256]{2,0,1:T(4,128)(2,1)} %bitcast.128), calls=%async_computation | async-start | bytes 131072 | tf_op jit(solution)/shard_map/all_to_all | solution.py:274
  10.0 8.6 %collective-permute-start.1 = (s32[8]{0:T(128)}, s32[8]{0:T(128)S(1)}, u32[]{:S(2)}, u32[]{:S(2)}) collective-permute-start(s32[8]{0:T(128)} %count_ref.3), channel_id=1, source_target_pairs={{0,32},{32,0},{64,96},{96,64},{1,33},{33,1},{65,97},{97,65},{2,34}... | collective-permute-start | bytes 104 | tf_op jit(solution)/shard_map/ppermute | solution.py:41
  10.3 8.3 %collective-permute-start = (s32[256]{0:T(256)}, s32[256]{0:T(256)S(1)}, u32[]{:S(2)}, u32[]{:S(2)}) collective-permute-start(s32[256]{0:T(256)} %param.9), channel_id=1, source_target_pairs={{0,32},{32,0},{64,96},{96,64},{1,33},{33,1},{65,97},{97,65},{2,34}... | collective-permute-start | bytes 3080 | tf_op jit(solution)/shard_map/ppermute | solution.py:41
  18.6 5.5 %collective-permute-start.4 = (bf16[256,128]{1,0:T(8,128)(2,1)S(1)}, bf16[256,128]{1,0:T(8,128)(2,1)S(1)}, u32[]{:S(2)}, u32[]{:S(2)}) collective-permute-start(bf16[256,128]{1,0:T(8,128)(2,1)S(1)} %convolution_convert_fusion.1), channel_id=1, source_target_pairs={{0,1},{1,2},{2,3},{3,0},{4,5},{5,6},{6,7},{7,4},{8,9},{9,10},{10,1... | collective-permute-start | bytes 196616 | tf_op jit(solution)/shard_map/ppermute | solution.py:37
  19.2 5.8 %collective-permute-start.3 = (bf16[256,128]{1,0:T(8,128)(2,1)S(1)}, bf16[256,128]{1,0:T(8,128)(2,1)S(1)}, u32[]{:S(2)}, u32[]{:S(2)}) collective-permute-start(bf16[256,128]{1,0:T(8,128)(2,1)S(1)} %convolution_convert_fusion.1), channel_id=1, source_target_pairs={{0,2},{1,3},{2,0},{3,1},{4,6},{5,7},{6,4},{7,5},{8,10},{9,11},{10,... | collective-permute-start | bytes 196616 | tf_op jit(solution)/shard_map/ppermute | solution.py:37
  21.5 4.3 %collective-permute-start.2 = (bf16[256,128]{1,0:T(8,128)(2,1)S(1)}, bf16[256,128]{1,0:T(8,128)(2,1)S(1)}, u32[]{:S(2)}, u32[]{:S(2)}) collective-permute-start(bf16[256,128]{1,0:T(8,128)(2,1)S(1)} %convolution_convert_fusion.1), channel_id=1, source_target_pairs={{0,3},{1,0},{2,1},{3,2},{4,7},{5,4},{6,5},{7,6},{8,11},{9,8},{10,9... | collective-permute-start | bytes 196616 | tf_op jit(solution)/shard_map/ppermute | solution.py:37
  25.8 10.8 %collective-permute-start.6 = (bf16[4,256,128]{2,1,0:T(8,128)(2,1)S(1)}, bf16[4,256,128]{2,1,0:T(8,128)(2,1)S(1)}, u32[]{:S(2)}, u32[]{:S(2)}) collective-permute-start(bf16[4,256,128]{2,1,0:T(8,128)(2,1)S(1)} %get-tuple-element.27), channel_id=1, source_target_pairs={{0,8},{1,9},{2,10},{3,11},{4,12},{5,13},{6,14},{7,15},{8,0},{9,1},... | collective-permute-start | bytes 786440 | tf_op jit(solution)/shard_map/ppermute | solution.py:37
  27.2 11.3 %collective-permute-start.5 = (bf16[4,256,128]{2,1,0:T(8,128)(2,1)S(1)}, bf16[4,256,128]{2,1,0:T(8,128)(2,1)S(1)}, u32[]{:S(2)}, u32[]{:S(2)}) collective-permute-start(bf16[4,256,128]{2,1,0:T(8,128)(2,1)S(1)} %get-tuple-element.27), channel_id=1, source_target_pairs={{0,12},{1,13},{2,14},{3,15},{4,0},{5,1},{6,2},{7,3},{8,4},{9,5},{1... | collective-permute-start | bytes 786440 | tf_op jit(solution)/shard_map/ppermute | solution.py:37
  29.1 10.6 %collective-permute-start.7 = (bf16[4,256,128]{2,1,0:T(8,128)(2,1)S(1)}, bf16[4,256,128]{2,1,0:T(8,128)(2,1)S(1)}, u32[]{:S(2)}, u32[]{:S(2)}) collective-permute-start(bf16[4,256,128]{2,1,0:T(8,128)(2,1)S(1)} %get-tuple-element.27), channel_id=1, source_target_pairs={{0,4},{1,5},{2,6},{3,7},{4,8},{5,9},{6,10},{7,11},{8,12},{9,13},{1... | collective-permute-start | bytes 786440 | tf_op jit(solution)/shard_map/ppermute | solution.py:37
  39.9 15.3 %collective-permute-start.8 = (bf16[4,4,256,128]{3,2,1,0:T(8,128)(2,1)S(1)}, bf16[4,4,256,128]{3,2,1,0:T(8,128)(2,1)S(1)}, u32[]{:S(2)}, u32[]{:S(2)}) collective-permute-start(bf16[4,4,256,128]{3,2,1,0:T(8,128)(2,1)S(1)} %get-tuple-element.22), channel_id=1, source_target_pairs={{0,80},{1,81},{2,82},{3,83},{4,84},{5,85},{6,86},{7,87},{8,88},{9,... | collective-permute-start | bytes 3145736 | tf_op jit(solution)/shard_map/ppermute | solution.py:37
  42.9 16.1 %collective-permute-start.9 = (bf16[4,4,256,128]{3,2,1,0:T(8,128)(2,1)S(1)}, bf16[4,4,256,128]{3,2,1,0:T(8,128)(2,1)S(1)}, u32[]{:S(2)}, u32[]{:S(2)}) collective-permute-start(bf16[4,4,256,128]{3,2,1,0:T(8,128)(2,1)S(1)} %get-tuple-element.22), channel_id=1, source_target_pairs={{0,16},{1,17},{2,18},{3,19},{4,20},{5,21},{6,22},{7,23},{8,24},{9,... | collective-permute-start | bytes 3145736 | tf_op jit(solution)/shard_map/ppermute | solution.py:37
  55.3 10.5 %collective-permute-start.11 = (bf16[4,4,128,128]{3,2,1,0:T(8,128)(2,1)S(1)}, bf16[4,4,128,128]{3,2,1,0:T(8,128)(2,1)S(1)}, u32[]{:S(2)}, u32[]{:S(2)}) collective-permute-start(bf16[4,4,128,128]{3,2,1,0:T(8,128)(2,1)S(1)} %slice.104), channel_id=1, source_target_pairs={{0,80},{1,81},{2,82},{3,83},{4,84},{5,85},{6,86},{7,87},{8,88},{9,... | collective-permute-start | bytes 1572872 | tf_op jit(solution)/shard_map/ppermute | solution.py:37
  59.1 10.5 %collective-permute-start.10 = (bf16[4,4,128,128]{3,2,1,0:T(8,128)(2,1)S(1)}, bf16[4,4,128,128]{3,2,1,0:T(8,128)(2,1)S(1)}, u32[]{:S(2)}, u32[]{:S(2)}) collective-permute-start(bf16[4,4,128,128]{3,2,1,0:T(8,128)(2,1)S(1)} %slice.103), channel_id=1, source_target_pairs={{0,16},{1,17},{2,18},{3,19},{4,20},{5,21},{6,22},{7,23},{8,24},{9,... | collective-permute-start | bytes 1572872 | tf_op jit(solution)/shard_map/ppermute | solution.py:37
  71.9 7.5 %collective-permute-start.12 = (bf16[128,128,128]{2,1,0:T(8,128)(2,1)}, bf16[128,128,128]{2,1,0:T(8,128)(2,1)}, u32[]{:S(2)}, u32[]{:S(2)}) collective-permute-start(bf16[128,128,128]{2,1,0:T(8,128)(2,1)} %bitcast.16.proj_ref), channel_id=1, source_target_pairs={{0,32},{32,0},{64,96},{96,64},{1,33},{33,1},{65,97},{97,65},{2,34}... | collective-permute-start | bytes 12582920 | tf_op jit(solution)/shard_map/ppermute | solution.py:41
  79.4 6.7 %copy-start.1 = (f32[2,128,128]{2,1,0:T(8,128)S(1)}, f32[2,128,128]{2,1,0:T(8,128)}, u32[]{:S(2)}) copy-start(f32[2,128,128]{2,1,0:T(8,128)} %shard_map.85) | copy-start | bytes 393220
  79.4 7.6 %copy-start.2 = (bf16[256,128]{1,0:T(8,128)(2,1)S(1)}, bf16[256,128]{1,0:T(8,128)(2,1)}, u32[]{:S(2)}) copy-start(bf16[256,128]{1,0:T(8,128)(2,1)} %param.11) | copy-start | bytes 196612
  79.4 8.8 %copy-start.4 = (s32[8]{0:T(128)S(1)}, s32[8]{0:T(128)}, u32[]{:S(2)}) copy-start(s32[8]{0:T(128)} %count_ref.3) | copy-start | bytes 100
  87.9 1.3 collective-permute-start.14
  104.6 9.2 %collective-permute-start.17 = (bf16[4,4,128,128]{3,2,1,0:T(8,128)(2,1)S(1)}, bf16[4,4,128,128]{3,2,1,0:T(8,128)(2,1)S(1)}, u32[]{:S(2)}, u32[]{:S(2)}) collective-permute-start(bf16[4,4,128,128]{3,2,1,0:T(8,128)(2,1)S(1)} %get-tuple-element.20), channel_id=1, source_target_pairs={{0,80},{1,81},{2,82},{3,83},{4,84},{5,85},{6,86},{7,87},{8,88},{9,... | collective-permute-start | bytes 1572872 | tf_op jit(solution)/shard_map/ppermute | solution.py:37
  104.7 10.7 %collective-permute-start.15 = (bf16[4,4,128,128]{3,2,1,0:T(8,128)(2,1)S(1)}, bf16[4,4,128,128]{3,2,1,0:T(8,128)(2,1)S(1)}, u32[]{:S(2)}, u32[]{:S(2)}) collective-permute-start(bf16[4,4,128,128]{3,2,1,0:T(8,128)(2,1)S(1)} %get-tuple-element.19), channel_id=1, source_target_pairs={{0,16},{1,17},{2,18},{3,19},{4,20},{5,21},{6,22},{7,23},{8,24},{9,... | collective-permute-start | bytes 1572872 | tf_op jit(solution)/shard_map/ppermute | solution.py:37
  114.1 14.9 %collective-permute-start.18 = (bf16[4,4,256,128]{3,2,1,0:T(8,128)(2,1)S(1)}, bf16[4,4,256,128]{3,2,1,0:T(8,128)(2,1)S(1)}, u32[]{:S(2)}, u32[]{:S(2)}) collective-permute-start(bf16[4,4,256,128]{3,2,1,0:T(8,128)(2,1)S(1)} %pad_maximum_fusion.3), channel_id=1, source_target_pairs={{0,80},{1,81},{2,82},{3,83},{4,84},{5,85},{6,86},{7,87},{8,88},{9,... | collective-permute-start | bytes 3145736 | tf_op jit(solution)/shard_map/ppermute | solution.py:37
  115.6 16.3 %collective-permute-start.16 = (bf16[4,4,256,128]{3,2,1,0:T(8,128)(2,1)S(1)}, bf16[4,4,256,128]{3,2,1,0:T(8,128)(2,1)S(1)}, u32[]{:S(2)}, u32[]{:S(2)}) collective-permute-start(bf16[4,4,256,128]{3,2,1,0:T(8,128)(2,1)S(1)} %pad_maximum_fusion.2), channel_id=1, source_target_pairs={{0,16},{1,17},{2,18},{3,19},{4,20},{5,21},{6,22},{7,23},{8,24},{9,... | collective-permute-start | bytes 3145736 | tf_op jit(solution)/shard_map/ppermute | solution.py:37
  132.4 9.0 %collective-permute-start.19 = (bf16[4,256,128]{2,1,0:T(8,128)(2,1)S(1)}, bf16[4,256,128]{2,1,0:T(8,128)(2,1)S(1)}, u32[]{:S(2)}, u32[]{:S(2)}) collective-permute-start(bf16[4,256,128]{2,1,0:T(8,128)(2,1)S(1)} %get-tuple-element.16), channel_id=1, source_target_pairs={{0,4},{1,5},{2,6},{3,7},{4,8},{5,9},{6,10},{7,11},{8,12},{9,13},{1... | collective-permute-start | bytes 786440 | tf_op jit(solution)/shard_map/ppermute | solution.py:37
  132.9 14.5 %collective-permute-start.21 = (bf16[4,256,128]{2,1,0:T(8,128)(2,1)S(1)}, bf16[4,256,128]{2,1,0:T(8,128)(2,1)S(1)}, u32[]{:S(2)}, u32[]{:S(2)}) collective-permute-start(bf16[4,256,128]{2,1,0:T(8,128)(2,1)S(1)} %get-tuple-element.17), channel_id=1, source_target_pairs={{0,8},{1,9},{2,10},{3,11},{4,12},{5,13},{6,14},{7,15},{8,0},{9,1},... | collective-permute-start | bytes 786440 | tf_op jit(solution)/shard_map/ppermute | solution.py:37
  135.3 12.2 %collective-permute-start.20 = (bf16[4,256,128]{2,1,0:T(8,128)(2,1)S(1)}, bf16[4,256,128]{2,1,0:T(8,128)(2,1)S(1)}, u32[]{:S(2)}, u32[]{:S(2)}) collective-permute-start(bf16[4,256,128]{2,1,0:T(8,128)(2,1)S(1)} %get-tuple-element.18), channel_id=1, source_target_pairs={{0,12},{1,13},{2,14},{3,15},{4,0},{5,1},{6,2},{7,3},{8,4},{9,5},{1... | collective-permute-start | bytes 786440 | tf_op jit(solution)/shard_map/ppermute | solution.py:37
  147.7 6.2 %collective-permute-start.22 = (bf16[256,128]{1,0:T(8,128)(2,1)S(1)}, bf16[256,128]{1,0:T(8,128)(2,1)S(1)}, u32[]{:S(2)}, u32[]{:S(2)}) collective-permute-start(bf16[256,128]{1,0:T(8,128)(2,1)S(1)} %get-tuple-element.23), channel_id=1, source_target_pairs={{0,1},{1,2},{2,3},{3,0},{4,5},{5,6},{6,7},{7,4},{8,9},{9,10},{10,1... | collective-permute-start | bytes 196616 | tf_op jit(solution)/shard_map/ppermute | solution.py:37
  147.8 6.2 %collective-permute-start.24 = (bf16[256,128]{1,0:T(8,128)(2,1)S(1)}, bf16[256,128]{1,0:T(8,128)(2,1)S(1)}, u32[]{:S(2)}, u32[]{:S(2)}) collective-permute-start(bf16[256,128]{1,0:T(8,128)(2,1)S(1)} %get-tuple-element.24), channel_id=1, source_target_pairs={{0,2},{1,3},{2,0},{3,1},{4,6},{5,7},{6,4},{7,5},{8,10},{9,11},{10,... | collective-permute-start | bytes 196616 | tf_op jit(solution)/shard_map/ppermute | solution.py:37
  149.3 5.6 %collective-permute-start.23 = (bf16[256,128]{1,0:T(8,128)(2,1)S(1)}, bf16[256,128]{1,0:T(8,128)(2,1)S(1)}, u32[]{:S(2)}, u32[]{:S(2)}) collective-permute-start(bf16[256,128]{1,0:T(8,128)(2,1)S(1)} %get-tuple-element.25), channel_id=1, source_target_pairs={{0,3},{1,0},{2,1},{3,2},{4,7},{5,4},{6,5},{7,6},{8,11},{9,8},{10,9... | collective-permute-start | bytes 196616 | tf_op jit(solution)/shard_map/ppermute | solution.py:37
  170.1 1.2 collective-permute-start.25
  171.3 5.1 %collective-permute-start.26 = (f32[4,128]{1,0:T(4,128)S(1)}, f32[4,128]{1,0:T(4,128)S(1)}, u32[]{:S(2)}, u32[]{:S(2)}) collective-permute-start(f32[4,128]{1,0:T(4,128)S(1)} %add.221), channel_id=1, source_target_pairs={{0,64},{32,96},{64,0},{96,32},{1,65},{33,97},{65,1},{97,33},{2,66}... | collective-permute-start | bytes 6152 | tf_op jit(solution)/shard_map/ppermute | solution.py:46
  (2 other events, 2.9 us)

commit v19 on v18

--- a/solution.py
+++ b/solution.py
@@ -199,7 +199,7 @@
 
         @pl.when((source == 1) & (row == tile_rows - 1) & (half_id == halves - 1))
         def _():
-            out_ref[...] = total_ref[...]
+            out_ref[...] = total_ref[...].astype(out_ref.dtype)
 
     tile_spec = (None, None, slot_count, tile_size, tile_size)
     grid_spec = pltpu.PrefetchScalarGridSpec(
@@ -222,7 +222,7 @@
     return pl.pallas_call(
         kernel,
         grid_spec=grid_spec,
-        out_shape=jax.ShapeDtypeStruct((buffer_tiles, hidden_width, tile_size), jnp.float32),
+        out_shape=jax.ShapeDtypeStruct((buffer_tiles, hidden_width, tile_size), jnp.bfloat16),
         compiler_params=pltpu.CompilerParams(
             dimension_semantics=("arbitrary", "arbitrary", "arbitrary")
         ),

time: 178 us -> 177 us (level)
  waiting for transfers between devices: 83.2 us -> 86.7 us
  local copies, waits for them, and re-layouts: 6.43 us -> 4.03 us
    ppermute x20, waiting for transfers between devices: 70 us -> 73.4 us  [ring_shift(): return lax.ppermute(block, BOTH, route)]
    slice x2 -> x1, local copies, waits for them, and re-layouts: 5.03 us -> 2.75 us  [term(): return total[k]]
  transfers between devices with their start and end apart: 28 -> 28, of which waited for: 22 -> 22; matrix products, arithmetic and copies ran while one was open for 6% -> 4% of each run, Pallas kernels for 7% -> 7%
where the time goes in v19:
time: 177 us
  waiting for transfers between devices  86.7 us (49%)
  starting transfers between devices  37.3 us (21%)
  Pallas kernels  24.7 us (14%)
  blocking collectives  14.6 us (8%)
  other arithmetic  7.84 us (4%)
  local copies, waits for them, and re-layouts  4.03 us (2%)
    ppermute x20, waiting for transfers between devices, ring_shift(): return lax.ppermute(block, BOTH, route)  73.4 us
    ppermute x20, starting transfers between devices, ring_shift(): return lax.ppermute(block, BOTH, route)  26.2 us
    all_to_all x1, blocking collectives, body(): lax.all_to_all(outgoing, 'feat', split_axis=0, concat_axis=0, tiled=True)  14.6 us
    pallas_call x2, Pallas kernels, aggregate_pair(): pl.pallas_call(aggregate_kernel, grid_spec=grid_spec, out_shape=jax.Shape...  13.2 us
    pallas_call x1, Pallas kernels, spread_pair(): pl.pallas_call(kernel, grid_spec=grid_spec, out_shape=jax.ShapeDtypeStruc...  11.5 us
    all_to_all x1, starting transfers between devices, body(): lax.all_to_all(features_t, 'feat', split_axis=1, concat_axis=0, tiled=True)  9.27 us
    all_to_all x1, waiting for transfers between devices, body(): lax.all_to_all(features_t, 'feat', split_axis=1, concat_axis=0, tiled=True)  7.74 us
    ppermute x2, waiting for transfers between devices, swapped(): return lax.ppermute(block, axis, [(i, i ^ mask) for i in range(count)])  4.8 us
  transfers between devices with their start and end apart: 28, of which 22 were waited for; matrix products, arithmetic and copies ran while one was open for 4% of the time, Pallas kernels for 7%

profile of v19, /device:TPU:0, one launch (start us, length us, event | category | flops | bytes accessed | tf_op | source)
XLA Modules:
  0.0 176.6 jit_solution(813704865488693796)
XLA Ops:
  0.7 9.3 %all-to-all-start = ((bf16[4,32,256]{2,0,1:T(4,128)(2,1)}), bf16[4,32,256]{2,0,1:T(4,128)(2,1)S(1)}, u32[]{:S(2)}, u32[]{:S(2)}) async-start(bf16[4,32,256]{2,0,1:T(4,128)(2,1)} %bitcast.129), calls=%async_computation | async-start | bytes 131072 | tf_op jit(solution)/shard_map/all_to_all | solution.py:274
  10.6 7.7 %all-to-all-done = bf16[4,32,256]{2,0,1:T(4,128)(2,1)S(1)} async-done(((bf16[4,32,256]{2,0,1:T(4,128)(2,1)}), bf16[4,32,256]{2,0,1:T(4,128)(2,1)S(1)}, u32[]{:S(2)}, u32[]{:S(2)}) %all-to-all-start) | async-done | bytes 65568 | tf_op jit(solution)/shard_map/all_to_all | solution.py:274
  19.2 2.3 %collective-permute-start.3 = (bf16[256,128]{1,0:T(8,128)(2,1)S(1)}, bf16[256,128]{1,0:T(8,128)(2,1)S(1)}, u32[]{:S(2)}, u32[]{:S(2)}) collective-permute-start(bf16[256,128]{1,0:T(8,128)(2,1)S(1)} %convolution_convert_fusion.1), channel_id=1, source_target_pairs={{0,2},{1,3},{2,0},{3,1},{4,6},{5,7},{6,4},{7,5},{8,10},{9,11},{10,... | collective-permute-start | bytes 196616 | tf_op jit(solution)/shard_map/ppermute | solution.py:37
  22.6 1.5 collective-permute-done.4
  25.8 1.4 collective-permute-start.6
  27.2 1.9 %collective-permute-start.5 = (bf16[4,256,128]{2,1,0:T(8,128)(2,1)S(1)}, bf16[4,256,128]{2,1,0:T(8,128)(2,1)S(1)}, u32[]{:S(2)}, u32[]{:S(2)}) collective-permute-start(bf16[4,256,128]{2,1,0:T(8,128)(2,1)S(1)} %get-tuple-element.28), channel_id=1, source_target_pairs={{0,12},{1,13},{2,14},{3,15},{4,0},{5,1},{6,2},{7,3},{8,4},{9,5},{1... | collective-permute-start | bytes 786440 | tf_op jit(solution)/shard_map/ppermute | solution.py:37
  29.3 7.4 %collective-permute-done.6 = bf16[4,256,128]{2,1,0:T(8,128)(2,1)S(1)} collective-permute-done((bf16[4,256,128]{2,1,0:T(8,128)(2,1)S(1)}, bf16[4,256,128]{2,1,0:T(8,128)(2,1)S(1)}, u32[]{:S(2)}, u32[]{:S(2)}) %collective-permute-start.6) | collective-permute-done | bytes 262176 | tf_op jit(solution)/shard_map/ppermute | solution.py:37
  36.6 1.9 %collective-permute-done.5 = bf16[4,256,128]{2,1,0:T(8,128)(2,1)S(1)} collective-permute-done((bf16[4,256,128]{2,1,0:T(8,128)(2,1)S(1)}, bf16[4,256,128]{2,1,0:T(8,128)(2,1)S(1)}, u32[]{:S(2)}, u32[]{:S(2)}) %collective-permute-start.5) | collective-permute-done | bytes 262176 | tf_op jit(solution)/shard_map/ppermute | solution.py:37
  39.9 3.0 %collective-permute-start.8 = (bf16[4,4,256,128]{3,2,1,0:T(8,128)(2,1)S(1)}, bf16[4,4,256,128]{3,2,1,0:T(8,128)(2,1)S(1)}, u32[]{:S(2)}, u32[]{:S(2)}) collective-permute-start(bf16[4,4,256,128]{3,2,1,0:T(8,128)(2,1)S(1)} %get-tuple-element.23), channel_id=1, source_target_pairs={{0,80},{1,81},{2,82},{3,83},{4,84},{5,85},{6,86},{7,87},{8,88},{9,... | collective-permute-start | bytes 3145736 | tf_op jit(solution)/shard_map/ppermute | solution.py:37
  42.9 12.3 %collective-permute-done.8 = bf16[4,4,256,128]{3,2,1,0:T(8,128)(2,1)S(1)} collective-permute-done((bf16[4,4,256,128]{3,2,1,0:T(8,128)(2,1)S(1)}, bf16[4,4,256,128]{3,2,1,0:T(8,128)(2,1)S(1)}, u32[]{:S(2)}, u32[]{:S(2)}) %collective-permute-start.8) | collective-permute-done | bytes 1048608 | tf_op jit(solution)/shard_map/ppermute | solution.py:37
  55.3 3.8 %collective-permute-start.11 = (bf16[4,4,128,128]{3,2,1,0:T(8,128)(2,1)S(1)}, bf16[4,4,128,128]{3,2,1,0:T(8,128)(2,1)S(1)}, u32[]{:S(2)}, u32[]{:S(2)}) collective-permute-start(bf16[4,4,128,128]{3,2,1,0:T(8,128)(2,1)S(1)} %slice.100), channel_id=1, source_target_pairs={{0,80},{1,81},{2,82},{3,83},{4,84},{5,85},{6,86},{7,87},{8,88},{9,... | collective-permute-start | bytes 1572872 | tf_op jit(solution)/shard_map/ppermute | solution.py:37
  59.2 6.6 %collective-permute-done.11 = bf16[4,4,128,128]{3,2,1,0:T(8,128)(2,1)S(1)} collective-permute-done((bf16[4,4,128,128]{3,2,1,0:T(8,128)(2,1)S(1)}, bf16[4,4,128,128]{3,2,1,0:T(8,128)(2,1)S(1)}, u32[]{:S(2)}, u32[]{:S(2)}) %collective-permute-start.11) | collective-permute-done | bytes 524320 | tf_op jit(solution)/shard_map/ppermute | solution.py:37
  65.7 3.8 %collective-permute-done.10 = bf16[4,4,128,128]{3,2,1,0:T(8,128)(2,1)S(1)} collective-permute-done((bf16[4,4,128,128]{3,2,1,0:T(8,128)(2,1)S(1)}, bf16[4,4,128,128]{3,2,1,0:T(8,128)(2,1)S(1)}, u32[]{:S(2)}, u32[]{:S(2)}) %collective-permute-start.10) | collective-permute-done | bytes 524320 | tf_op jit(solution)/shard_map/ppermute | solution.py:37
  69.6 2.3 %pad_maximum_fusion = bf16[4,4,4,256,128]{4,3,2,1,0:T(8,128)(2,1)} fusion(bf16[1,4,4,256,128]{4,3,2,1,0:T(8,128)(2,1)S(1)} %bitcast.113, bf16[1,4,4,256,128]{4,3,2,1,0:T(8,128)(2,1)S(1)} %maximum_bitcast_fusion, bf16[1,4,4,256,128]{4,3,2,1,0:T(8,128)(2,1)S(1)} %bitcast.112, bf16[1,4,4,256,128]{4,3,2,1,0:T(8,128)(2,1)S(1)} %get-tuple-element.22), kind=kLoop, calls=%fused_computation | loop fusion | flops 6291456 | bytes 8388608 | tf_op jit(solution)/shard_map/stack | solution.py:56
  72.6 6.5 %shard_map.85 = f32[2,128,128]{2,1,0:T(8,128)} custom-call(s32[1]{0:T(128)} %bitcast.core_ref, s32[256]{0:T(256)} %copy-done.3, s32[8]{0:T(128)} %count_ref.3, bf16[4,2,32,128,128]{4,3,2,1,0:T(8,128)(2,1)} %bitcast.103, bf16[128,128,128]{2,1,0:T(8,128)(2,1)} %bitcast.16.proj_ref), custom_call_target="tpu_custom_call" | custom-call | tf_op jit(solution)/shard_map/pallas_call | solution.py:155
  79.4 6.7 %shard_map.86 = f32[2,128,128]{2,1,0:T(8,128)} custom-call(s32[1]{0:T(128)} %bitcast.17.core_ref, s32[256]{0:T(256)} %copy-done.3, s32[8]{0:T(128)} %count_ref.3, bf16[4,2,32,128,128]{4,3,2,1,0:T(8,128)(2,1)} %bitcast.104, bf16[128,128,128]{2,1,0:T(8,128)(2,1)} %collective-permute-done.12.proj_ref), custom_call_target="tpu_custom_call" | custom-call | tf_op jit(solution)/shard_map/pallas_call | solution.py:155
  89.9 11.5 %shard_map.87 = bf16[128,128,128]{2,1,0:T(8,128)(2,1)} custom-call(s32[1]{0:T(128)} %bitcast.core_ref, s32[512]{0:T(512)} %pad_add_fusion.where_ref, s32[16]{0:T(128)} %pad_add_fusion.1.count_ref, bf16[4,2,32,128,128]{4,3,2,1,0:T(8,128)(2,1)} %bitcast.105, bf16[4,2,32,128,128]{4,3,2,1,0:T(8,128)(2,1)} %collective-permute-done.13.other_ref, ...), custom_call_target="tpu_custom_call" | custom-call | tf_op jit(solution)/shard_map/pallas_call | solution.py:222
  101.4 2.7 %fusion.39 = (bf16[32,128,128]{2,1,0:T(8,128)(2,1)S(1)}, bf16[32,128,128]{2,1,0:T(8,128)(2,1)S(1)}, bf16[32,128,128]{2,1,0:T(8,128)(2,1)S(1)}, bf16[32,128,128]{2,1,0:T(8,128)(2,1)S(1)}) fusion(bf16[128,128,128]{2,1,0:T(8,128)(2,1)} %shard_map.87), kind=kLoop, calls=%fused_computation.138 | loop fusion | bytes 8388608 | tf_op jit(solution)/shard_map/slice | solution.py:83
  104.3 2.0 %collective-permute-start.15 = (bf16[4,4,128,128]{3,2,1,0:T(8,128)(2,1)S(1)}, bf16[4,4,128,128]{3,2,1,0:T(8,128)(2,1)S(1)}, u32[]{:S(2)}, u32[]{:S(2)}) collective-permute-start(bf16[4,4,128,128]{3,2,1,0:T(8,128)(2,1)S(1)} %get-tuple-element.20), channel_id=1, source_target_pairs={{0,16},{1,17},{2,18},{3,19},{4,20},{5,21},{6,22},{7,23},{8,24},{9,... | collective-permute-start | bytes 1572872 | tf_op jit(solution)/shard_map/ppermute | solution.py:37
  106.4 7.1 %collective-permute-done.17 = bf16[4,4,128,128]{3,2,1,0:T(8,128)(2,1)S(1)} collective-permute-done((bf16[4,4,128,128]{3,2,1,0:T(8,128)(2,1)S(1)}, bf16[4,4,128,128]{3,2,1,0:T(8,128)(2,1)S(1)}, u32[]{:S(2)}, u32[]{:S(2)}) %collective-permute-start.17) | collective-permute-done | bytes 524320 | tf_op jit(solution)/shard_map/ppermute | solution.py:37
  113.7 1.3 collective-permute-start.18
  116.3 12.3 %collective-permute-done.18 = bf16[4,4,256,128]{3,2,1,0:T(8,128)(2,1)S(1)} collective-permute-done((bf16[4,4,256,128]{3,2,1,0:T(8,128)(2,1)S(1)}, bf16[4,4,256,128]{3,2,1,0:T(8,128)(2,1)S(1)}, u32[]{:S(2)}, u32[]{:S(2)}) %collective-permute-start.18) | collective-permute-done | bytes 1048608 | tf_op jit(solution)/shard_map/ppermute | solution.py:37
  128.6 2.9 %collective-permute-done.16 = bf16[4,4,256,128]{3,2,1,0:T(8,128)(2,1)S(1)} collective-permute-done((bf16[4,4,256,128]{3,2,1,0:T(8,128)(2,1)S(1)}, bf16[4,4,256,128]{3,2,1,0:T(8,128)(2,1)S(1)}, u32[]{:S(2)}, u32[]{:S(2)}) %collective-permute-start.16) | collective-permute-done | bytes 1048608 | tf_op jit(solution)/shard_map/ppermute | solution.py:37
  132.5 2.4 %collective-permute-start.21 = (bf16[4,256,128]{2,1,0:T(8,128)(2,1)S(1)}, bf16[4,256,128]{2,1,0:T(8,128)(2,1)S(1)}, u32[]{:S(2)}, u32[]{:S(2)}) collective-permute-start(bf16[4,256,128]{2,1,0:T(8,128)(2,1)S(1)} %get-tuple-element.18), channel_id=1, source_target_pairs={{0,8},{1,9},{2,10},{3,11},{4,12},{5,13},{6,14},{7,15},{8,0},{9,1},... | collective-permute-start | bytes 786440 | tf_op jit(solution)/shard_map/ppermute | solution.py:37
  134.9 1.3 collective-permute-start.20
  136.2 4.8 %collective-permute-done.19 = bf16[4,256,128]{2,1,0:T(8,128)(2,1)S(1)} collective-permute-done((bf16[4,256,128]{2,1,0:T(8,128)(2,1)S(1)}, bf16[4,256,128]{2,1,0:T(8,128)(2,1)S(1)}, u32[]{:S(2)}, u32[]{:S(2)}) %collective-permute-start.19) | collective-permute-done | bytes 262176 | tf_op jit(solution)/shard_map/ppermute | solution.py:37
  141.0 6.1 %collective-permute-done.21 = bf16[4,256,128]{2,1,0:T(8,128)(2,1)S(1)} collective-permute-done((bf16[4,256,128]{2,1,0:T(8,128)(2,1)S(1)}, bf16[4,256,128]{2,1,0:T(8,128)(2,1)S(1)}, u32[]{:S(2)}, u32[]{:S(2)}) %collective-permute-start.21) | collective-permute-done | bytes 262176 | tf_op jit(solution)/shard_map/ppermute | solution.py:37
  147.4 1.5 collective-permute-start.24
  148.9 1.8 %collective-permute-start.23 = (bf16[256,128]{1,0:T(8,128)(2,1)S(1)}, bf16[256,128]{1,0:T(8,128)(2,1)S(1)}, u32[]{:S(2)}, u32[]{:S(2)}) collective-permute-start(bf16[256,128]{1,0:T(8,128)(2,1)S(1)} %get-tuple-element.26), channel_id=1, source_target_pairs={{0,3},{1,0},{2,1},{3,2},{4,7},{5,4},{6,5},{7,6},{8,11},{9,8},{10,9... | collective-permute-start | bytes 196616 | tf_op jit(solution)/shard_map/ppermute | solution.py:37
  150.7 2.9 %collective-permute-done.22 = bf16[256,128]{1,0:T(8,128)(2,1)S(1)} collective-permute-done((bf16[256,128]{1,0:T(8,128)(2,1)S(1)}, bf16[256,128]{1,0:T(8,128)(2,1)S(1)}, u32[]{:S(2)}, u32[]{:S(2)}) %collective-permute-start.22) | collective-permute-done | bytes 65568 | tf_op jit(solution)/shard_map/ppermute | solution.py:37
  155.0 14.6 %all_to_all.24 = f32[32,4,384]{2,1,0:T(4,128)S(1)} all-to-all(f32[32,4,384]{2,1,0:T(4,128)S(1)} %pad_maximum_fusion.5), channel_id=1, replica_groups=mesh['blk'=4,'feat'=32] {'feat'}, dimensions={0} | all-to-all | bytes 393216 | tf_op jit(solution)/shard_map/all_to_all | solution.py:336
  172.3 3.7 %collective-permute-done.26 = f32[4,128]{1,0:T(4,128)S(1)} collective-permute-done((f32[4,128]{1,0:T(4,128)S(1)}, f32[4,128]{1,0:T(4,128)S(1)}, u32[]{:S(2)}, u32[]{:S(2)}) %collective-permute-start.26) | collective-permute-done | bytes 2080 | tf_op jit(solution)/shard_map/ppermute | solution.py:46
  (78 shorter events, 18.5 us)
Async XLA Ops:
  0.6 17.7 %copy-start = (bf16[128,128]{1,0:T(8,128)(2,1)S(1)}, bf16[128,128]{1,0:T(8,128)(2,1)}, u32[]{:S(2)}) copy-start(bf16[128,128]{1,0:T(8,128)(2,1)} %param.7) | copy-start | bytes 98308
  0.6 89.2 %collective-permute-start.13 = (bf16[4,2,32,128,128]{4,3,2,1,0:T(8,128)(2,1)}, bf16[4,2,32,128,128]{4,3,2,1,0:T(8,128)(2,1)}, u32[]{:S(2)}, u32[]{:S(2)}) collective-permute-start(bf16[4,2,32,128,128]{4,3,2,1,0:T(8,128)(2,1)} %bitcast.102), channel_id=1, source_target_pairs={{0,32},{32,0},{64,96},{96,64},{1,33},{33,1},{65,97},{97,65},{2,34}... | collective-permute-start | bytes 25165832 | tf_op jit(solution)/shard_map/ppermute | solution.py:41
  0.7 17.6 %all-to-all-start = ((bf16[4,32,256]{2,0,1:T(4,128)(2,1)}), bf16[4,32,256]{2,0,1:T(4,128)(2,1)S(1)}, u32[]{:S(2)}, u32[]{:S(2)}) async-start(bf16[4,32,256]{2,0,1:T(4,128)(2,1)} %bitcast.129), calls=%async_computation | async-start | bytes 131072 | tf_op jit(solution)/shard_map/all_to_all | solution.py:274
  10.0 8.6 %collective-permute-start.1 = (s32[8]{0:T(128)}, s32[8]{0:T(128)S(1)}, u32[]{:S(2)}, u32[]{:S(2)}) collective-permute-start(s32[8]{0:T(128)} %count_ref.3), channel_id=1, source_target_pairs={{0,32},{32,0},{64,96},{96,64},{1,33},{33,1},{65,97},{97,65},{2,34}... | collective-permute-start | bytes 104 | tf_op jit(solution)/shard_map/ppermute | solution.py:41
  10.3 8.3 %collective-permute-start = (s32[256]{0:T(256)}, s32[256]{0:T(256)S(1)}, u32[]{:S(2)}, u32[]{:S(2)}) collective-permute-start(s32[256]{0:T(256)} %param.9), channel_id=1, source_target_pairs={{0,32},{32,0},{64,96},{96,64},{1,33},{33,1},{65,97},{97,65},{2,34}... | collective-permute-start | bytes 3080 | tf_op jit(solution)/shard_map/ppermute | solution.py:41
  18.6 5.5 %collective-permute-start.4 = (bf16[256,128]{1,0:T(8,128)(2,1)S(1)}, bf16[256,128]{1,0:T(8,128)(2,1)S(1)}, u32[]{:S(2)}, u32[]{:S(2)}) collective-permute-start(bf16[256,128]{1,0:T(8,128)(2,1)S(1)} %convolution_convert_fusion.1), channel_id=1, source_target_pairs={{0,1},{1,2},{2,3},{3,0},{4,5},{5,6},{6,7},{7,4},{8,9},{9,10},{10,1... | collective-permute-start | bytes 196616 | tf_op jit(solution)/shard_map/ppermute | solution.py:37
  19.2 5.8 %collective-permute-start.3 = (bf16[256,128]{1,0:T(8,128)(2,1)S(1)}, bf16[256,128]{1,0:T(8,128)(2,1)S(1)}, u32[]{:S(2)}, u32[]{:S(2)}) collective-permute-start(bf16[256,128]{1,0:T(8,128)(2,1)S(1)} %convolution_convert_fusion.1), channel_id=1, source_target_pairs={{0,2},{1,3},{2,0},{3,1},{4,6},{5,7},{6,4},{7,5},{8,10},{9,11},{10,... | collective-permute-start | bytes 196616 | tf_op jit(solution)/shard_map/ppermute | solution.py:37
  21.5 4.3 %collective-permute-start.2 = (bf16[256,128]{1,0:T(8,128)(2,1)S(1)}, bf16[256,128]{1,0:T(8,128)(2,1)S(1)}, u32[]{:S(2)}, u32[]{:S(2)}) collective-permute-start(bf16[256,128]{1,0:T(8,128)(2,1)S(1)} %convolution_convert_fusion.1), channel_id=1, source_target_pairs={{0,3},{1,0},{2,1},{3,2},{4,7},{5,4},{6,5},{7,6},{8,11},{9,8},{10,9... | collective-permute-start | bytes 196616 | tf_op jit(solution)/shard_map/ppermute | solution.py:37
  25.8 10.8 %collective-permute-start.6 = (bf16[4,256,128]{2,1,0:T(8,128)(2,1)S(1)}, bf16[4,256,128]{2,1,0:T(8,128)(2,1)S(1)}, u32[]{:S(2)}, u32[]{:S(2)}) collective-permute-start(bf16[4,256,128]{2,1,0:T(8,128)(2,1)S(1)} %get-tuple-element.28), channel_id=1, source_target_pairs={{0,8},{1,9},{2,10},{3,11},{4,12},{5,13},{6,14},{7,15},{8,0},{9,1},... | collective-permute-start | bytes 786440 | tf_op jit(solution)/shard_map/ppermute | solution.py:37
  27.2 11.3 %collective-permute-start.5 = (bf16[4,256,128]{2,1,0:T(8,128)(2,1)S(1)}, bf16[4,256,128]{2,1,0:T(8,128)(2,1)S(1)}, u32[]{:S(2)}, u32[]{:S(2)}) collective-permute-start(bf16[4,256,128]{2,1,0:T(8,128)(2,1)S(1)} %get-tuple-element.28), channel_id=1, source_target_pairs={{0,12},{1,13},{2,14},{3,15},{4,0},{5,1},{6,2},{7,3},{8,4},{9,5},{1... | collective-permute-start | bytes 786440 | tf_op jit(solution)/shard_map/ppermute | solution.py:37
  29.1 10.6 %collective-permute-start.7 = (bf16[4,256,128]{2,1,0:T(8,128)(2,1)S(1)}, bf16[4,256,128]{2,1,0:T(8,128)(2,1)S(1)}, u32[]{:S(2)}, u32[]{:S(2)}) collective-permute-start(bf16[4,256,128]{2,1,0:T(8,128)(2,1)S(1)} %get-tuple-element.28), channel_id=1, source_target_pairs={{0,4},{1,5},{2,6},{3,7},{4,8},{5,9},{6,10},{7,11},{8,12},{9,13},{1... | collective-permute-start | bytes 786440 | tf_op jit(solution)/shard_map/ppermute | solution.py:37
  39.9 15.3 %collective-permute-start.8 = (bf16[4,4,256,128]{3,2,1,0:T(8,128)(2,1)S(1)}, bf16[4,4,256,128]{3,2,1,0:T(8,128)(2,1)S(1)}, u32[]{:S(2)}, u32[]{:S(2)}) collective-permute-start(bf16[4,4,256,128]{3,2,1,0:T(8,128)(2,1)S(1)} %get-tuple-element.23), channel_id=1, source_target_pairs={{0,80},{1,81},{2,82},{3,83},{4,84},{5,85},{6,86},{7,87},{8,88},{9,... | collective-permute-start | bytes 3145736 | tf_op jit(solution)/shard_map/ppermute | solution.py:37
  42.9 16.1 %collective-permute-start.9 = (bf16[4,4,256,128]{3,2,1,0:T(8,128)(2,1)S(1)}, bf16[4,4,256,128]{3,2,1,0:T(8,128)(2,1)S(1)}, u32[]{:S(2)}, u32[]{:S(2)}) collective-permute-start(bf16[4,4,256,128]{3,2,1,0:T(8,128)(2,1)S(1)} %get-tuple-element.23), channel_id=1, source_target_pairs={{0,16},{1,17},{2,18},{3,19},{4,20},{5,21},{6,22},{7,23},{8,24},{9,... | collective-permute-start | bytes 3145736 | tf_op jit(solution)/shard_map/ppermute | solution.py:37
  55.3 10.5 %collective-permute-start.11 = (bf16[4,4,128,128]{3,2,1,0:T(8,128)(2,1)S(1)}, bf16[4,4,128,128]{3,2,1,0:T(8,128)(2,1)S(1)}, u32[]{:S(2)}, u32[]{:S(2)}) collective-permute-start(bf16[4,4,128,128]{3,2,1,0:T(8,128)(2,1)S(1)} %slice.100), channel_id=1, source_target_pairs={{0,80},{1,81},{2,82},{3,83},{4,84},{5,85},{6,86},{7,87},{8,88},{9,... | collective-permute-start | bytes 1572872 | tf_op jit(solution)/shard_map/ppermute | solution.py:37
  59.1 10.5 %collective-permute-start.10 = (bf16[4,4,128,128]{3,2,1,0:T(8,128)(2,1)S(1)}, bf16[4,4,128,128]{3,2,1,0:T(8,128)(2,1)S(1)}, u32[]{:S(2)}, u32[]{:S(2)}) collective-permute-start(bf16[4,4,128,128]{3,2,1,0:T(8,128)(2,1)S(1)} %slice.99), channel_id=1, source_target_pairs={{0,16},{1,17},{2,18},{3,19},{4,20},{5,21},{6,22},{7,23},{8,24},{9,... | collective-permute-start | bytes 1572872 | tf_op jit(solution)/shard_map/ppermute | solution.py:37
  71.9 7.5 %collective-permute-start.12 = (bf16[128,128,128]{2,1,0:T(8,128)(2,1)}, bf16[128,128,128]{2,1,0:T(8,128)(2,1)}, u32[]{:S(2)}, u32[]{:S(2)}) collective-permute-start(bf16[128,128,128]{2,1,0:T(8,128)(2,1)} %bitcast.16.proj_ref), channel_id=1, source_target_pairs={{0,32},{32,0},{64,96},{96,64},{1,33},{33,1},{65,97},{97,65},{2,34}... | collective-permute-start | bytes 12582920 | tf_op jit(solution)/shard_map/ppermute | solution.py:41
  79.4 6.7 %copy-start.1 = (f32[2,128,128]{2,1,0:T(8,128)S(1)}, f32[2,128,128]{2,1,0:T(8,128)}, u32[]{:S(2)}) copy-start(f32[2,128,128]{2,1,0:T(8,128)} %shard_map.85) | copy-start | bytes 393220
  79.4 7.6 %copy-start.2 = (bf16[256,128]{1,0:T(8,128)(2,1)S(1)}, bf16[256,128]{1,0:T(8,128)(2,1)}, u32[]{:S(2)}) copy-start(bf16[256,128]{1,0:T(8,128)(2,1)} %param.11) | copy-start | bytes 196612
  79.4 8.8 %copy-start.4 = (s32[8]{0:T(128)S(1)}, s32[8]{0:T(128)}, u32[]{:S(2)}) copy-start(s32[8]{0:T(128)} %count_ref.3) | copy-start | bytes 100
  87.9 1.3 collective-permute-start.14
  104.2 9.2 %collective-permute-start.17 = (bf16[4,4,128,128]{3,2,1,0:T(8,128)(2,1)S(1)}, bf16[4,4,128,128]{3,2,1,0:T(8,128)(2,1)S(1)}, u32[]{:S(2)}, u32[]{:S(2)}) collective-permute-start(bf16[4,4,128,128]{3,2,1,0:T(8,128)(2,1)S(1)} %get-tuple-element.21), channel_id=1, source_target_pairs={{0,80},{1,81},{2,82},{3,83},{4,84},{5,85},{6,86},{7,87},{8,88},{9,... | collective-permute-start | bytes 1572872 | tf_op jit(solution)/shard_map/ppermute | solution.py:37
  104.3 10.7 %collective-permute-start.15 = (bf16[4,4,128,128]{3,2,1,0:T(8,128)(2,1)S(1)}, bf16[4,4,128,128]{3,2,1,0:T(8,128)(2,1)S(1)}, u32[]{:S(2)}, u32[]{:S(2)}) collective-permute-start(bf16[4,4,128,128]{3,2,1,0:T(8,128)(2,1)S(1)} %get-tuple-element.20), channel_id=1, source_target_pairs={{0,16},{1,17},{2,18},{3,19},{4,20},{5,21},{6,22},{7,23},{8,24},{9,... | collective-permute-start | bytes 1572872 | tf_op jit(solution)/shard_map/ppermute | solution.py:37
  113.7 14.9 %collective-permute-start.18 = (bf16[4,4,256,128]{3,2,1,0:T(8,128)(2,1)S(1)}, bf16[4,4,256,128]{3,2,1,0:T(8,128)(2,1)S(1)}, u32[]{:S(2)}, u32[]{:S(2)}) collective-permute-start(bf16[4,4,256,128]{3,2,1,0:T(8,128)(2,1)S(1)} %pad_maximum_fusion.3), channel_id=1, source_target_pairs={{0,80},{1,81},{2,82},{3,83},{4,84},{5,85},{6,86},{7,87},{8,88},{9,... | collective-permute-start | bytes 3145736 | tf_op jit(solution)/shard_map/ppermute | solution.py:37
  115.2 16.3 %collective-permute-start.16 = (bf16[4,4,256,128]{3,2,1,0:T(8,128)(2,1)S(1)}, bf16[4,4,256,128]{3,2,1,0:T(8,128)(2,1)S(1)}, u32[]{:S(2)}, u32[]{:S(2)}) collective-permute-start(bf16[4,4,256,128]{3,2,1,0:T(8,128)(2,1)S(1)} %pad_maximum_fusion.2), channel_id=1, source_target_pairs={{0,16},{1,17},{2,18},{3,19},{4,20},{5,21},{6,22},{7,23},{8,24},{9,... | collective-permute-start | bytes 3145736 | tf_op jit(solution)/shard_map/ppermute | solution.py:37
  132.0 9.0 %collective-permute-start.19 = (bf16[4,256,128]{2,1,0:T(8,128)(2,1)S(1)}, bf16[4,256,128]{2,1,0:T(8,128)(2,1)S(1)}, u32[]{:S(2)}, u32[]{:S(2)}) collective-permute-start(bf16[4,256,128]{2,1,0:T(8,128)(2,1)S(1)} %get-tuple-element.17), channel_id=1, source_target_pairs={{0,4},{1,5},{2,6},{3,7},{4,8},{5,9},{6,10},{7,11},{8,12},{9,13},{1... | collective-permute-start | bytes 786440 | tf_op jit(solution)/shard_map/ppermute | solution.py:37
  132.5 14.6 %collective-permute-start.21 = (bf16[4,256,128]{2,1,0:T(8,128)(2,1)S(1)}, bf16[4,256,128]{2,1,0:T(8,128)(2,1)S(1)}, u32[]{:S(2)}, u32[]{:S(2)}) collective-permute-start(bf16[4,256,128]{2,1,0:T(8,128)(2,1)S(1)} %get-tuple-element.18), channel_id=1, source_target_pairs={{0,8},{1,9},{2,10},{3,11},{4,12},{5,13},{6,14},{7,15},{8,0},{9,1},... | collective-permute-start | bytes 786440 | tf_op jit(solution)/shard_map/ppermute | solution.py:37
  134.9 12.3 %collective-permute-start.20 = (bf16[4,256,128]{2,1,0:T(8,128)(2,1)S(1)}, bf16[4,256,128]{2,1,0:T(8,128)(2,1)S(1)}, u32[]{:S(2)}, u32[]{:S(2)}) collective-permute-start(bf16[4,256,128]{2,1,0:T(8,128)(2,1)S(1)} %get-tuple-element.19), channel_id=1, source_target_pairs={{0,12},{1,13},{2,14},{3,15},{4,0},{5,1},{6,2},{7,3},{8,4},{9,5},{1... | collective-permute-start | bytes 786440 | tf_op jit(solution)/shard_map/ppermute | solution.py:37
  147.3 6.2 %collective-permute-start.22 = (bf16[256,128]{1,0:T(8,128)(2,1)S(1)}, bf16[256,128]{1,0:T(8,128)(2,1)S(1)}, u32[]{:S(2)}, u32[]{:S(2)}) collective-permute-start(bf16[256,128]{1,0:T(8,128)(2,1)S(1)} %get-tuple-element.24), channel_id=1, source_target_pairs={{0,1},{1,2},{2,3},{3,0},{4,5},{5,6},{6,7},{7,4},{8,9},{9,10},{10,1... | collective-permute-start | bytes 196616 | tf_op jit(solution)/shard_map/ppermute | solution.py:37
  147.4 6.2 %collective-permute-start.24 = (bf16[256,128]{1,0:T(8,128)(2,1)S(1)}, bf16[256,128]{1,0:T(8,128)(2,1)S(1)}, u32[]{:S(2)}, u32[]{:S(2)}) collective-permute-start(bf16[256,128]{1,0:T(8,128)(2,1)S(1)} %get-tuple-element.25), channel_id=1, source_target_pairs={{0,2},{1,3},{2,0},{3,1},{4,6},{5,7},{6,4},{7,5},{8,10},{9,11},{10,... | collective-permute-start | bytes 196616 | tf_op jit(solution)/shard_map/ppermute | solution.py:37
  148.9 5.6 %collective-permute-start.23 = (bf16[256,128]{1,0:T(8,128)(2,1)S(1)}, bf16[256,128]{1,0:T(8,128)(2,1)S(1)}, u32[]{:S(2)}, u32[]{:S(2)}) collective-permute-start(bf16[256,128]{1,0:T(8,128)(2,1)S(1)} %get-tuple-element.26), channel_id=1, source_target_pairs={{0,3},{1,0},{2,1},{3,2},{4,7},{5,4},{6,5},{7,6},{8,11},{9,8},{10,9... | collective-permute-start | bytes 196616 | tf_op jit(solution)/shard_map/ppermute | solution.py:37
  169.7 1.2 collective-permute-start.25
  170.9 5.1 %collective-permute-start.26 = (f32[4,128]{1,0:T(4,128)S(1)}, f32[4,128]{1,0:T(4,128)S(1)}, u32[]{:S(2)}, u32[]{:S(2)}) collective-permute-start(f32[4,128]{1,0:T(4,128)S(1)} %add.221), channel_id=1, source_target_pairs={{0,64},{32,96},{64,0},{96,32},{1,65},{33,97},{65,1},{97,33},{2,66}... | collective-permute-start | bytes 6152 | tf_op jit(solution)/shard_map/ppermute | solution.py:46
  (2 other events, 2.9 us)
